TPU v7x, 32 devices: a whole 2x2x4 slice. The times are simulated.
32 devices in a mesh: groups: 2 (over x), seq: 16 (over z, y, core).
Axes of the slice: x: 2, y: 2, z: 4, core: 2. Of those that a mesh axis runs over, the one named last changes fastest.
Arguments:
- frames_in: bfloat16 [4096, 1024], P(('groups', 'seq')), parts along dimension 0, may hold values from -6 to 6
- query_proj: bfloat16 [4096, 512], P(('groups', 'seq')), parts along dimension 0, may hold values from -6 to 6
- key_proj: bfloat16 [4096, 512], P(('groups', 'seq')), parts along dimension 0, may hold values from -6 to 6
- value_proj: bfloat16 [4096, 512], P(('groups', 'seq')), parts along dimension 0, may hold values from -6 to 6
- utterance_lengths: int32 [32], P('groups'), parts along dimension 0, may hold values from 1 to 256, 2048 in all
- bucket_table: int32 [767], replicated, may hold values from 0 to 31
- bucket_bias: float32 [32, 8], replicated, may hold values from -4 to 4
- out_weight: bfloat16 [512, 1024], replicated, may hold values from -0.25 to 0.25
- norm_gain: float32 [1024], replicated, may hold values from 0.1 to 1.9
- expand_weight: bfloat16 [1024, 2048], replicated, may hold values from -0.1875 to 0.1875
- depth_taps: float32 [31, 1024], replicated, may hold values from -1 to 1
- inner_gain: float32 [1024], replicated, may hold values from 0.1 to 1.9
- shrink_weight: bfloat16 [1024, 1024], replicated, may hold values from -0.1875 to 0.1875
Outputs:
- block_out: bfloat16 [4096, 1024], P(('groups', 'seq')), parts along dimension 0
There are 2 independent parts, one for each index of `groups`. A program takes and returns all parts, laid end to end along the dimension named above; an argument that names none is the same for every part. Nothing has to cross between parts.
Inputs may be any that keep to these rules, and one draw needn't show every extreme that they name: `utterance_lengths`: they sum to 2048, and one is exactly 256.
All inputs are finite; a program needn't handle non-finite values.
Results may differ from a plain program's by a relative error of at most 0.014.
Values may be sent and summed in bfloat16 or wider, within the bound.
No kernel may reach another device: no remote copies, remote signals or barrier semaphores. Data moves between devices by JAX's collectives and lax.ppermute only.
A program may use at most 64 MiB of HBM per device.

v0:
```python
import jax
import jax.numpy as jnp
from jax import lax
from jax.sharding import PartitionSpec as P

KERNEL = 31
DILATION = 4
REACH = 2


norm_epsilon = 1e-05
masked_score = -1e30


def shifted(value, axis, steps):
    count = lax.axis_size(axis)
    leading, last = (max(0, -steps), min(count, count - steps))
    return lax.ppermute(value, axis, [(source, source + steps) for source in range(leading, last)])


def padded_2(cells, sides, width):
    for axis, dim in sides:
        count = lax.axis_size(axis)
        ends = count - 1
        head = lax.slice_in_dim(cells, 0, width, axis=dim)
        tail = lax.slice_in_dim(cells, cells.shape[dim] - width, cells.shape[dim], axis=dim)
        cells = jnp.concatenate(
            [
                lax.ppermute(tail, axis, [(i, (i + 1) % count) for i in range(ends)]),
                cells,
                lax.ppermute(head, axis, [((i + 1) % count, i) for i in range(ends)]),
            ],
            axis=dim,
        )
    return cells


def segment_of(positions, bounds):
    inside = jnp.sum((positions[:, None] >= bounds[None, :]).astype(jnp.int32), axis=1)
    return jnp.where(positions < 0, -1, inside)


def layer_norm(values, gain_vec):
    row_mean = jnp.mean(values, axis=-1, keepdims=True)
    centred = values - row_mean
    spread = jnp.mean(centred * centred, axis=-1, keepdims=True)
    return centred * lax.rsqrt(spread + norm_epsilon) * gain_vec


def gated_units(mid, norm_gain, expand_weight):
    model_width = mid.shape[1]
    normed = layer_norm(mid.astype(jnp.float32), norm_gain).astype(jnp.bfloat16)
    hidden = jnp.dot(normed, expand_weight, preferred_element_type=jnp.float32)
    return (hidden[:, :model_width] * jax.nn.sigmoid(hidden[:, model_width:])).astype(jnp.bfloat16)


def on_device(
    frames_in,
    query_proj,
    key_proj,
    value_proj,
    utterance_lengths,
    bucket_table,
    bucket_bias,
    out_weight,
    norm_gain,
    expand_weight,
    depth_taps,
    inner_gain,
    shrink_weight,
):
    row_count = query_proj.shape[0]
    head_count = bucket_bias.shape[1]
    att_width = query_proj.shape[1]
    head_width = att_width // head_count
    model_width = frames_in.shape[1]
    line_length = bucket_table.shape[0]
    window_cols = (2 * REACH + 1) * row_count
    device_index = lax.axis_index("seq")
    bounds = jnp.cumsum(utterance_lengths)
    offsets = jnp.arange(row_count, dtype=jnp.int32)
    query_segment = segment_of(device_index * row_count + offsets, bounds)
    bucket_hits = (
        bucket_table[:, None] == jnp.arange(bucket_bias.shape[0], dtype=jnp.int32)[None, :]
    ).astype(jnp.float32)
    bias_line = jnp.dot(bucket_hits, bucket_bias, precision=lax.Precision.HIGHEST).T
    repeated = jnp.tile(bias_line, (1, row_count + 1))
    skewed = repeated[:, row_count - 1 : row_count - 1 + row_count * (line_length - 1)]
    window_bias = skewed.reshape(head_count, row_count, line_length - 1)[:, :, :window_cols]
    queries = query_proj.reshape(row_count, head_count, head_width).transpose(1, 0, 2)
    scaling = head_width ** (-0.5)

    def absorb(state, packed_block, hop_count, key_segment):
        run_max, run_total, run_acc = state
        keys_here = packed_block[:, :att_width].reshape(row_count, head_count, head_width)
        values_here = packed_block[:, att_width:].reshape(row_count, head_count, head_width)
        scores = jnp.einsum("hrd,chd->hrc", queries, keys_here, preferred_element_type=jnp.float32)
        first_col = (hop_count + REACH) * row_count
        scores = scores * scaling + window_bias[:, :, first_col : first_col + row_count]
        same_utterance = (query_segment[:, None] == key_segment[None, :])[None]
        scores = jnp.where(same_utterance, scores, masked_score)
        new_max = jnp.maximum(run_max, jnp.max(scores, axis=2))
        weights = jnp.exp(scores - new_max[:, :, None])
        rescale = jnp.exp(run_max - new_max)
        new_total = run_total * rescale + jnp.sum(weights, axis=2)
        weighted = jnp.einsum(
            "hrc,chd->hrd",
            weights.astype(jnp.bfloat16),
            values_here,
            preferred_element_type=jnp.float32,
        )
        return (new_max, new_total, run_acc * rescale[:, :, None] + weighted)

    def visit(state, packed_block, hop_count):
        key_segment = segment_of((device_index + hop_count) * row_count + offsets, bounds)
        return absorb(state, packed_block, hop_count, key_segment)

    packed = jnp.concatenate([key_proj, value_proj], axis=1)
    state = (
        jnp.full((head_count, row_count), masked_score, jnp.float32),
        jnp.zeros((head_count, row_count), jnp.float32),
        jnp.zeros((head_count, row_count, head_width), jnp.float32),
    )
    state = visit(state, packed, 0)
    from_next = packed
    from_prev = packed
    for hop_count in range(1, REACH + 1):
        from_next = shifted(from_next, "seq", -1)
        from_prev = shifted(from_prev, "seq", 1)
        state = visit(state, from_next, hop_count)
        state = visit(state, from_prev, -hop_count)
    run_max, run_total, run_acc = state
    attended = (
        (run_acc / run_total[:, :, None])
        .astype(jnp.bfloat16)
        .transpose(1, 0, 2)
        .reshape(row_count, att_width)
    )
    mid = (
        frames_in.astype(jnp.float32)
        + jnp.dot(attended, out_weight, preferred_element_type=jnp.float32)
    ).astype(jnp.bfloat16)
    halo_rows = DILATION * (KERNEL - 1) // 2
    gated = gated_units(mid, norm_gain, expand_weight)
    padded = padded_2(gated, (("seq", 0),), halo_rows)
    phased = padded.reshape(-1, DILATION, model_width)
    step_rows = row_count // DILATION
    conv_sum = jnp.zeros((step_rows, DILATION, model_width), jnp.float32)
    for tap_index in range(KERNEL):
        conv_sum = conv_sum + depth_taps[tap_index] * phased[
            tap_index : tap_index + step_rows
        ].astype(jnp.float32)
    conv_sum = conv_sum.reshape(row_count, model_width)
    inner_normed = layer_norm(conv_sum, inner_gain)
    activated = (inner_normed * jax.nn.sigmoid(inner_normed)).astype(jnp.bfloat16)
    return (
        mid.astype(jnp.float32)
        + jnp.dot(activated, shrink_weight, preferred_element_type=jnp.float32)
    ).astype(jnp.bfloat16)


def solution(mesh):
    placed = (
        P(("groups", "seq"), None),
        P(("groups", "seq"), None),
        P(("groups", "seq"), None),
        P(("groups", "seq"), None),
        P("groups"),
        P(),
        P(),
        P(),
        P(),
        P(),
        P(),
        P(),
        P(),
    )
    return jax.shard_map(
        on_device, mesh=mesh, in_specs=placed, out_specs=P(("groups", "seq"), None), check_vma=False
    )
```

profile of v0, /device:TPU:21, one launch (start us, length us, event | category | flops | bytes accessed | tf_op | source)
XLA Modules:
  0.0 97.3 jit_solution(1213232763662413313)
XLA Ops:
  0.0 1.7 %constant_dynamic-update-slice_fusion.1 = bf16[128,1024]{1,0:T(8,128)(2,1)} fusion(bf16[128,512]{1,0:T(8,128)(2,1)} %param.15), kind=kLoop, calls=%fused_computation.179 | loop fusion | bytes 262144
  1.7 1.6 %constant_dynamic-update-slice_fusion = bf16[128,1024]{1,0:T(8,128)(2,1)} fusion(bf16[128,1024]{1,0:T(8,128)(2,1)} %constant_dynamic-update-slice_fusion.1, bf16[128,512]{1,0:T(8,128)(2,1)} %param.16), kind=kLoop, calls=%fused_computation.178 | loop fusion | bytes 262144 | tf_op jit(solution)/shard_map/concatenate | solution.py:118
  3.3 3.7 %collective-permute-start.1 = (bf16[128,1024]{1,0:T(8,128)(2,1)}, bf16[128,1024]{1,0:T(8,128)(2,1)}, u32[]{:S(2)}, u32[]{:S(2)}) collective-permute-start(bf16[128,1024]{1,0:T(8,128)(2,1)} %constant_dynamic-update-slice_fusion), channel_id=1, source_target_pairs={{0,1},{1,2},{2,3},{3,4},{4,5},{5,6},{6,7},{7,8},{8,9},{9,10},{10,1... | collective-permute-start | bytes 786440 | tf_op jit(solution)/shard_map/ppermute | solution.py:18
  7.0 1.9 %collective-permute-start = (bf16[128,1024]{1,0:T(8,128)(2,1)}, bf16[128,1024]{1,0:T(8,128)(2,1)}, u32[]{:S(2)}, u32[]{:S(2)}) collective-permute-start(bf16[128,1024]{1,0:T(8,128)(2,1)} %constant_dynamic-update-slice_fusion), channel_id=1, source_target_pairs={{1,0},{2,1},{3,2},{4,3},{5,4},{6,5},{7,6},{8,7},{9,8},{10,9},{11,1... | collective-permute-start | bytes 786440 | tf_op jit(solution)/shard_map/ppermute | solution.py:18
  9.0 0.7 copy.55
  9.8 0.1 reduce
  9.9 0.1 convert_reduce_fusion
  10.0 0.6 compare_select_fusion.4
  10.6 1.1 %convolution_bitcast_fusion.5 = f32[8,767]{1,0:T(8,128)S(1)} fusion(f32[32,8]{0,1:T(8,128)} %param.19, s32[767]{0:T(1024)} %param.18), kind=kOutput, calls=%fused_computation.68 | convolution fusion | flops 2380768 | bytes 28636 | tf_op jit(solution)/shard_map/dot_general | solution.py:86
  11.6 2.0 %tile.4 = f32[8,129,767]{2,1,0:T(8,128)} broadcast(f32[8,767]{1,0:T(8,128)S(1)} %convolution_bitcast_fusion.5), dimensions={0,2} | broadcast | bytes 3190720 | tf_op jit(solution)/shard_map/tile | solution.py:87
  13.6 4.7 %tile.10 = f32[8,98943]{1,0:T(8,128)} reshape(f32[8,129,767]{2,1,0:T(8,128)} %tile.4) | data formatting | bytes 6332352 | tf_op jit(solution)/shard_map/tile | solution.py:87
  18.3 4.5 %slice.384 = f32[8,98048]{1,0:T(8,128)} slice(f32[8,98943]{1,0:T(8,128)} %tile.10), slice={[0:8], [127:98175]} | slice | bytes 6275072 | tf_op jit(solution)/shard_map/slice | solution.py:88
  22.7 7.0 %reshape.468 = f32[8,128,766]{2,1,0:T(8,128)} reshape(f32[8,98048]{1,0:T(8,128)} %slice.384) | data formatting | bytes 6275072 | tf_op jit(solution)/shard_map/reshape | solution.py:89
  29.7 3.0 %fusion.104 = (f32[8,128,128]{2,1,0:T(8,128)}, f32[8,128,128]{2,1,0:T(8,128)}, f32[8,128,128]{2,1,0:T(8,128)S(1)}, f32[8,128,128]{2,1,0:T(8,128)S(1)}, f32[8,128,128]{2,1,0:T(8,128)}) fusion(f32[8,128,766]{2,1,0:T(8,128)} %reshape.468), kind=kLoop, calls=%fused_computation.220 | loop fusion | bytes 5242880 | tf_op jit(solution)/shard_map/slice | solution.py:99
  32.7 0.7 fusion.110
  33.4 0.8 broadcast_compare_fusion.2
  34.2 0.8 copy.57
  35.0 0.1 copy.60
  35.1 2.1 %copy.87 = f32[8,128,128]{1,2,0:T(8,128)} copy(f32[8,128,128]{2,1,0:T(8,128)} %get-tuple-element.24) | data formatting | bytes 1048576
  37.2 1.0 %copy.56 = bf16[128,512]{0,1:T(8,128)(2,1)S(1)} copy(bf16[128,512]{1,0:T(8,128)(2,1)} %param.14) | data formatting | bytes 262144 | tf_op args[1]
  38.2 2.0 %copy.86 = f32[8,128,128]{1,2,0:T(8,128)} copy(f32[8,128,128]{2,1,0:T(8,128)} %get-tuple-element.21) | data formatting | bytes 1048576
  40.2 2.0 %copy.85 = f32[8,128,128]{1,2,0:T(8,128)} copy(f32[8,128,128]{2,1,0:T(8,128)} %get-tuple-element.20) | data formatting | bytes 1048576
  42.3 1.0 %copy.84 = f32[8,128,128]{1,2,0:T(8,128)} copy(f32[8,128,128]{2,1,0:T(8,128)S(1)} %get-tuple-element.22) | data formatting | bytes 1048576
  43.3 0.2 copy.83
  43.5 1.6 %fusion.116 = (f32[8,128]{1,0:T(8,128)}, f32[8,128,128]{1,2,0:T(8,128)S(1)}) fusion(f32[8,128,128]{1,2,0:T(8,128)S(1)} %copy.83, bf16[8,128,64]{1,2,0:T(8,128)(2,1)S(1)} %bitcast.220, bf16[128,8,64]{0,2,1:T(8,128)(2,1)S(1)} %bitcast.231, pred[128,128]{0,1:T(8,128)(4,1)} %get-tuple-element.73), kind=kOutput, calls=%fused_computation.232 | convolution fusion | flops 17300480 | bytes 1331200 | tf_op jit(solution)/shard_map/hrd,chd->hrc/dot_general | solution.py:97
  45.1 1.6 %fusion.108 = (bf16[128,512]{1,0:T(8,128)(2,1)}, bf16[128,512]{1,0:T(8,128)(2,1)S(1)}) fusion(bf16[128,1024]{1,0:T(8,128)(2,1)} %collective-permute-done.1), kind=kLoop, calls=%fused_computation.224 | loop fusion | bytes 524288 | tf_op jit(solution)/shard_map/slice | solution.py:96
  46.8 0.1 copy.66
  46.9 4.5 %collective-permute-start.3 = (bf16[128,1024]{1,0:T(8,128)(2,1)}, bf16[128,1024]{1,0:T(8,128)(2,1)}, u32[]{:S(2)}, u32[]{:S(2)}) collective-permute-start(bf16[128,1024]{1,0:T(8,128)(2,1)} %collective-permute-done.1), channel_id=1, source_target_pairs={{0,1},{1,2},{2,3},{3,4},{4,5},{5,6},{6,7},{7,8},{8,9},{9,10},{10,1... | collective-permute-start | bytes 786440 | tf_op jit(solution)/shard_map/ppermute | solution.py:18
  51.4 1.9 %fusion.114 = (f32[8,128]{1,0:T(8,128)}, f32[8,128,128]{1,2,0:T(8,128)S(1)}) fusion(f32[8,128,128]{1,2,0:T(8,128)} %copy.85, bf16[128,8,64]{0,2,1:T(8,128)(2,1)S(1)} %bitcast.232, bf16[8,128,64]{1,2,0:T(8,128)(2,1)S(1)} %bitcast.221, pred[128,128]{0,1:T(8,128)(4,1)} %get-tuple-element.69), kind=kOutput, calls=%fused_computation.230 | convolution fusion | flops 17300480 | bytes 1331200 | tf_op jit(solution)/shard_map/hrd,chd->hrc/dot_general | solution.py:97
  53.4 1.6 %fusion.109 = (bf16[128,512]{1,0:T(8,128)(2,1)S(1)}, bf16[128,512]{1,0:T(8,128)(2,1)}) fusion(bf16[128,1024]{1,0:T(8,128)(2,1)} %collective-permute-done), kind=kLoop, calls=%fused_computation.225 | loop fusion | bytes 524288 | tf_op jit(solution)/shard_map/slice | solution.py:96
  55.0 1.7 %copy.62 = bf16[128,512]{0,1:T(8,128)(2,1)} copy(bf16[128,512]{1,0:T(8,128)(2,1)} %get-tuple-element.34) | data formatting | bytes 262144 | tf_op jit(solution)/shard_map/slice | solution.py:95
  56.7 1.9 %collective-permute-start.2 = (bf16[128,1024]{1,0:T(8,128)(2,1)}, bf16[128,1024]{1,0:T(8,128)(2,1)}, u32[]{:S(2)}, u32[]{:S(2)}) collective-permute-start(bf16[128,1024]{1,0:T(8,128)(2,1)} %collective-permute-done), channel_id=1, source_target_pairs={{1,0},{2,1},{3,2},{4,3},{5,4},{6,5},{7,6},{8,7},{9,8},{10,9},{11,1... | collective-permute-start | bytes 786440 | tf_op jit(solution)/shard_map/ppermute | solution.py:18
  58.6 2.8 %fusion.115 = (f32[8,128]{1,0:T(8,128)}, f32[8,128,128]{1,2,0:T(8,128)}) fusion(f32[8,128,128]{1,2,0:T(8,128)} %copy.84, bf16[128,8,64]{0,2,1:T(8,128)(2,1)} %bitcast.233, bf16[8,128,64]{1,2,0:T(8,128)(2,1)S(1)} %bitcast.222, pred[128,128]{0,1:T(8,128)(4,1)} %get-tuple-element.72), kind=kOutput, calls=%fused_computation.231 | convolution fusion | flops 17300480 | bytes 1331200 | tf_op jit(solution)/shard_map/hrd,chd->hrc/dot_general | solution.py:97
  61.4 0.8 copy.64
  62.1 1.0 %copy.68 = bf16[128,512]{0,1:T(8,128)(2,1)S(1)} copy(bf16[128,512]{1,0:T(8,128)(2,1)} %get-tuple-element.31) | data formatting | bytes 262144 | tf_op jit(solution)/shard_map/slice | solution.py:96
  63.2 1.7 %fusion.106 = (bf16[128,512]{1,0:T(8,128)(2,1)}, bf16[128,512]{1,0:T(8,128)(2,1)}) fusion(bf16[128,1024]{1,0:T(8,128)(2,1)} %collective-permute-done.3), kind=kLoop, calls=%fused_computation.222 | loop fusion | bytes 524288 | tf_op jit(solution)/shard_map/slice | solution.py:96
  64.9 1.7 %copy.74 = bf16[128,512]{0,1:T(8,128)(2,1)} copy(bf16[128,512]{1,0:T(8,128)(2,1)} %get-tuple-element.28) | data formatting | bytes 262144 | tf_op jit(solution)/shard_map/slice | solution.py:95
  66.5 1.7 %fusion.107 = (bf16[128,512]{1,0:T(8,128)(2,1)}, bf16[128,512]{1,0:T(8,128)(2,1)}) fusion(bf16[128,1024]{1,0:T(8,128)(2,1)} %collective-permute-done.2), kind=kLoop, calls=%fused_computation.223 | loop fusion | bytes 524288 | tf_op jit(solution)/shard_map/slice | solution.py:96
  68.2 1.7 %copy.70 = bf16[128,512]{0,1:T(8,128)(2,1)} copy(bf16[128,512]{1,0:T(8,128)(2,1)} %get-tuple-element.30) | data formatting | bytes 262144 | tf_op jit(solution)/shard_map/slice | solution.py:95
  69.9 1.7 %copy.72 = bf16[128,512]{0,1:T(8,128)(2,1)} copy(bf16[128,512]{1,0:T(8,128)(2,1)} %get-tuple-element.29) | data formatting | bytes 262144 | tf_op jit(solution)/shard_map/slice | solution.py:96
  71.5 1.7 %copy.76 = bf16[128,512]{0,1:T(8,128)(2,1)} copy(bf16[128,512]{1,0:T(8,128)(2,1)} %get-tuple-element.27) | data formatting | bytes 262144 | tf_op jit(solution)/shard_map/slice | solution.py:96
  73.2 1.4 %fusion.112 = (f32[8,128]{1,0:T(8,128)S(1)}, f32[8,128,128]{1,2,0:T(8,128)S(1)}) fusion(f32[8,128,128]{1,2,0:T(8,128)} %copy.87, bf16[128,8,64]{0,2,1:T(8,128)(2,1)} %bitcast.229, bf16[8,128,64]{1,2,0:T(8,128)(2,1)S(1)} %bitcast.223, pred[128,128]{0,1:T(8,128)(4,1)} %get-tuple-element.71), kind=kOutput, calls=%fused_computation.228 | convolution fusion | flops 17300480 | bytes 1331200 | tf_op jit(solution)/shard_map/hrd,chd->hrc/dot_general | solution.py:97
  74.6 1.4 %fusion.113 = (f32[8,128]{1,0:T(8,128)S(1)}, f32[8,128,128]{1,2,0:T(8,128)S(1)}) fusion(f32[8,128,128]{1,2,0:T(8,128)} %copy.86, bf16[128,8,64]{0,2,1:T(8,128)(2,1)} %bitcast.230, bf16[8,128,64]{1,2,0:T(8,128)(2,1)S(1)} %bitcast.224, pred[128,128]{0,1:T(8,128)(4,1)S(1)} %get-tuple-element.70), kind=kOutput, calls=%fused_computation.229 | convolution fusion | flops 17300480 | bytes 1331200 | tf_op jit(solution)/shard_map/hrd,chd->hrc/dot_general | solution.py:97
  76.1 0.7 fusion.102
  76.8 0.1 fusion.33
  76.9 0.1 fusion.35
  77.0 0.1 fusion.37
  77.4 0.2 fusion.26
  77.6 0.2 fusion.24
  77.9 0.2 fusion.22
  78.1 0.2 fusion.20
  78.3 0.2 fusion.27
  78.6 0.4 fusion.117
  79.0 0.2 multiply_reduce_fusion.1
  79.2 0.9 copy-done.2
  80.3 0.8 fusion.48
  81.1 0.1 fusion.32
  81.3 4.5 %collective-permute-start.4 = (bf16[60,1024]{1,0:T(8,128)(2,1)S(1)}, bf16[60,1024]{1,0:T(8,128)(2,1)S(1)}, u32[]{:S(2)}, u32[]{:S(2)}) collective-permute-start(bf16[60,1024]{1,0:T(8,128)(2,1)S(1)} %get-tuple-element.25), channel_id=1, source_target_pairs={{0,1},{1,2},{2,3},{3,4},{4,5},{5,6},{6,7},{7,8},{8,9},{9,10},{10,1... | collective-permute-start | bytes 368648 | tf_op jit(solution)/shard_map/ppermute | solution.py:29
  85.9 1.9 %collective-permute-start.5 = (bf16[60,1024]{1,0:T(8,128)(2,1)S(1)}, bf16[60,1024]{1,0:T(8,128)(2,1)S(1)}, u32[]{:S(2)}, u32[]{:S(2)}) collective-permute-start(bf16[60,1024]{1,0:T(8,128)(2,1)S(1)} %get-tuple-element.26), channel_id=1, source_target_pairs={{1,0},{2,1},{3,2},{4,3},{5,4},{6,5},{7,6},{8,7},{9,8},{10,9},{11,1... | collective-permute-start | bytes 368648 | tf_op jit(solution)/shard_map/ppermute | solution.py:31
  87.8 1.1 %fusion.111 = (f32[1,1024]{1,0:T(1,128)S(1)}, f32[1,1024]{1,0:T(1,128)S(1)}, f32[1,1024]{1,0:T(1,128)S(1)}, f32[1,1024]{1,0:T(1,128)S(1)}, f32[1,1024]{1,0:T(1,1...) fusion(f32[31,1024]{1,0:T(8,128)} %param.23), kind=kLoop, calls=%fused_computation.227 | loop fusion | bytes 98304 | tf_op jit(solution)/shard_map/slice | solution.py:150
  89.0 4.1 %collective-permute-done.5 = bf16[60,1024]{1,0:T(8,128)(2,1)S(1)} collective-permute-done((bf16[60,1024]{1,0:T(8,128)(2,1)S(1)}, bf16[60,1024]{1,0:T(8,128)(2,1)S(1)}, u32[]{:S(2)}, u32[]{:S(2)}) %collective-permute-start.5) | collective-permute-done | bytes 122912 | tf_op jit(solution)/shard_map/ppermute | solution.py:31
  93.2 2.5 %fusion.100 = (f32[128]{0:T(128)S(1)}, f32[128,1024]{1,0:T(8,128)S(1)}) fusion(bf16[60,1024]{1,0:T(8,128)(2,1)S(1)} %collective-permute-done.5, bf16[128,1024]{1,0:T(8,128)(2,1)S(1)} %fusion.32, f32[1024]{0:T(1024)S(1)} %bitcast.265, f32[1024]{0:T(1024)S(1)} %bitcast.266, f32[1024]{0:T(1024)S(1)} %bitcast.237, f32[1024]{0:T(1024)S(1)} %bitcast.238, ...), kind=kLoop, calls=%fused_computation.218 | loop fusion | flops 23986048 | bytes 1159680 | tf_op jit(solution)/shard_map/reduce_sum | solution.py:44
  95.8 0.2 multiply_reduce_fusion
  96.0 1.3 %fusion.16 = bf16[128,1024]{1,0:T(8,128)(2,1)} fusion(f32[128,1024]{1,0:T(8,128)S(1)} %get-tuple-element.85, bf16[1024,1024]{1,0:T(8,128)(2,1)S(1)} %copy-done, f32[128,1024]{1,0:T(8,128)S(1)} %get-tuple-element.11, f32[1024]{0:T(1024)S(1)} %copy-done.36, f32[128]{0:T(128)S(1)} %add_rsqrt_fusion, f32[128]{0:T(128)S(1)} %broadcast_multiply_fusion), kind=kOutput, calls=%fused_computation.51 | convolution fusion | flops 269746176 | bytes 3412992 | tf_op jit(solution)/shard_map/dot_general | solution.py:158
  (94 shorter events, 0.5 us)
Async XLA Ops:
  0.0 96.0 %copy-start = (bf16[1024,1024]{1,0:T(8,128)(2,1)S(1)}, bf16[1024,1024]{1,0:T(8,128)(2,1)}, u32[]{:S(2)}) copy-start(bf16[1024,1024]{1,0:T(8,128)(2,1)} %param.25) | copy-start | bytes 6291460
  3.3 41.8 %collective-permute-start.1 = (bf16[128,1024]{1,0:T(8,128)(2,1)}, bf16[128,1024]{1,0:T(8,128)(2,1)}, u32[]{:S(2)}, u32[]{:S(2)}) collective-permute-start(bf16[128,1024]{1,0:T(8,128)(2,1)} %constant_dynamic-update-slice_fusion), channel_id=1, source_target_pairs={{0,1},{1,2},{2,3},{3,4},{4,5},{5,6},{6,7},{7,8},{8,9},{9,10},{10,1... | collective-permute-start | bytes 786440 | tf_op jit(solution)/shard_map/ppermute | solution.py:18
  7.0 46.4 %collective-permute-start = (bf16[128,1024]{1,0:T(8,128)(2,1)}, bf16[128,1024]{1,0:T(8,128)(2,1)}, u32[]{:S(2)}, u32[]{:S(2)}) collective-permute-start(bf16[128,1024]{1,0:T(8,128)(2,1)} %constant_dynamic-update-slice_fusion), channel_id=1, source_target_pairs={{1,0},{2,1},{3,2},{4,3},{5,4},{6,5},{7,6},{8,7},{9,8},{10,9},{11,1... | collective-permute-start | bytes 786440 | tf_op jit(solution)/shard_map/ppermute | solution.py:18
  29.7 3.0 %copy-start.11 = (f32[31,1024]{1,0:T(8,128)S(1)}, f32[31,1024]{1,0:T(8,128)}, u32[]{:S(2)}) copy-start(f32[31,1024]{1,0:T(8,128)} %param.23) | copy-start | bytes 380932
  29.7 3.7 %copy-start.35 = (s32[128]{0:T(128)S(1)}, s32[128]{0:T(128)}, u32[]{:S(2)}) copy-start(s32[128]{0:T(128)} %compare_select_fusion.4) | copy-start | bytes 1540
  29.7 4.5 %copy-start.6 = (bf16[128,512]{1,0:T(8,128)(2,1)S(1)}, bf16[128,512]{1,0:T(8,128)(2,1)}, u32[]{:S(2)}) copy-start(bf16[128,512]{1,0:T(8,128)(2,1)} %param.15) | copy-start | bytes 393220
  29.7 5.3 %copy-start.7 = (bf16[128,512]{1,0:T(8,128)(2,1)S(1)}, bf16[128,512]{1,0:T(8,128)(2,1)}, u32[]{:S(2)}) copy-start(bf16[128,512]{1,0:T(8,128)(2,1)} %param.16) | copy-start | bytes 393220
  35.1 8.4 %copy-start.8 = (bf16[128,512]{0,1:T(8,128)(2,1)S(1)}, bf16[128,512]{0,1:T(8,128)(2,1)}, u32[]{:S(2)}) copy-start(bf16[128,512]{0,1:T(8,128)(2,1)} %copy.57) | copy-start | bytes 393220
  46.9 16.3 %collective-permute-start.3 = (bf16[128,1024]{1,0:T(8,128)(2,1)}, bf16[128,1024]{1,0:T(8,128)(2,1)}, u32[]{:S(2)}, u32[]{:S(2)}) collective-permute-start(bf16[128,1024]{1,0:T(8,128)(2,1)} %collective-permute-done.1), channel_id=1, source_target_pairs={{0,1},{1,2},{2,3},{3,4},{4,5},{5,6},{6,7},{7,8},{8,9},{9,10},{10,1... | collective-permute-start | bytes 786440 | tf_op jit(solution)/shard_map/ppermute | solution.py:18
  56.7 9.8 %collective-permute-start.2 = (bf16[128,1024]{1,0:T(8,128)(2,1)}, bf16[128,1024]{1,0:T(8,128)(2,1)}, u32[]{:S(2)}, u32[]{:S(2)}) collective-permute-start(bf16[128,1024]{1,0:T(8,128)(2,1)} %collective-permute-done), channel_id=1, source_target_pairs={{1,0},{2,1},{3,2},{4,3},{5,4},{6,5},{7,6},{8,7},{9,8},{10,9},{11,1... | collective-permute-start | bytes 786440 | tf_op jit(solution)/shard_map/ppermute | solution.py:18
  73.2 3.7 %copy-start.1 = (f32[8,128,128]{1,2,0:T(8,128)S(1)}, f32[8,128,128]{1,2,0:T(8,128)}, u32[]{:S(2)}) copy-start(f32[8,128,128]{1,2,0:T(8,128)} %get-tuple-element.81) | copy-start | bytes 1572868
  73.2 4.1 %copy-start.12 = (f32[8,128]{1,0:T(8,128)S(1)}, f32[8,128]{1,0:T(8,128)}, u32[]{:S(2)}) copy-start(f32[8,128]{1,0:T(8,128)} %get-tuple-element.82) | copy-start | bytes 12292
  73.2 4.1 %copy-start.13 = (f32[8,128]{1,0:T(8,128)S(1)}, f32[8,128]{1,0:T(8,128)}, u32[]{:S(2)}) copy-start(f32[8,128]{1,0:T(8,128)} %get-tuple-element.78) | copy-start | bytes 12292
  73.2 4.1 %copy-start.14 = (f32[8,128]{1,0:T(8,128)S(1)}, f32[8,128]{1,0:T(8,128)}, u32[]{:S(2)}) copy-start(f32[8,128]{1,0:T(8,128)} %get-tuple-element.80) | copy-start | bytes 12292
  73.2 4.4 %copy-start.4 = (bf16[128,512]{0,1:T(8,128)(2,1)S(1)}, bf16[128,512]{0,1:T(8,128)(2,1)}, u32[]{:S(2)}) copy-start(bf16[128,512]{0,1:T(8,128)(2,1)} %copy.64) | copy-start | bytes 393220
  76.1 2.0 %copy-start.5 = (bf16[128,512]{0,1:T(8,128)(2,1)S(1)}, bf16[128,512]{0,1:T(8,128)(2,1)}, u32[]{:S(2)}) copy-start(bf16[128,512]{0,1:T(8,128)(2,1)} %copy.72) | copy-start | bytes 393220
  77.0 1.3 %copy-start.10 = (bf16[128,512]{0,1:T(8,128)(2,1)S(1)}, bf16[128,512]{0,1:T(8,128)(2,1)}, u32[]{:S(2)}) copy-start(bf16[128,512]{0,1:T(8,128)(2,1)} %copy.76) | copy-start | bytes 393220
  77.2 1.4 %copy-start.3 = (bf16[512,1024]{1,0:T(8,128)(2,1)S(1)}, bf16[512,1024]{1,0:T(8,128)(2,1)}, u32[]{:S(2)}) copy-start(bf16[512,1024]{1,0:T(8,128)(2,1)} %param.20) | copy-start | bytes 3145732
  77.2 1.4 %copy-start.9 = (bf16[128,1024]{1,0:T(8,128)(2,1)S(1)}, bf16[128,1024]{1,0:T(8,128)(2,1)}, u32[]{:S(2)}) copy-start(bf16[128,1024]{1,0:T(8,128)(2,1)} %param.13) | copy-start | bytes 786436
  77.8 2.3 %copy-start.2 = (bf16[1024,2048]{1,0:T(8,128)(2,1)S(1)}, bf16[1024,2048]{1,0:T(8,128)(2,1)}, u32[]{:S(2)}) copy-start(bf16[1024,2048]{1,0:T(8,128)(2,1)} %param.22) | copy-start | bytes 12582916
  77.9 2.3 %copy-start.34 = (f32[1024]{0:T(1024)S(1)}, f32[1024]{0:T(1024)}, u32[]{:S(2)}) copy-start(f32[1024]{0:T(1024)} %param.21) | copy-start | bytes 12292
  80.1 12.9 %copy-start.15 = (f32[1,1024]{1,0:T(1,128)S(1)}, f32[1,1024]{1,0:T(1,128)}, u32[]{:S(2)}) copy-start(f32[1,1024]{1,0:T(1,128)} %get-tuple-element.35) | copy-start | bytes 12292
  80.2 12.9 %copy-start.16 = (f32[1,1024]{1,0:T(1,128)S(1)}, f32[1,1024]{1,0:T(1,128)}, u32[]{:S(2)}) copy-start(f32[1,1024]{1,0:T(1,128)} %get-tuple-element.36) | copy-start | bytes 12292
  80.2 12.9 %copy-start.17 = (f32[1,1024]{1,0:T(1,128)S(1)}, f32[1,1024]{1,0:T(1,128)}, u32[]{:S(2)}) copy-start(f32[1,1024]{1,0:T(1,128)} %get-tuple-element.37) | copy-start | bytes 12292
  80.2 12.9 %copy-start.18 = (f32[1,1024]{1,0:T(1,128)S(1)}, f32[1,1024]{1,0:T(1,128)}, u32[]{:S(2)}) copy-start(f32[1,1024]{1,0:T(1,128)} %get-tuple-element.38) | copy-start | bytes 12292
  80.2 12.9 %copy-start.19 = (f32[1,1024]{1,0:T(1,128)S(1)}, f32[1,1024]{1,0:T(1,128)}, u32[]{:S(2)}) copy-start(f32[1,1024]{1,0:T(1,128)} %get-tuple-element.39) | copy-start | bytes 12292
  80.2 12.9 %copy-start.20 = (f32[1,1024]{1,0:T(1,128)S(1)}, f32[1,1024]{1,0:T(1,128)}, u32[]{:S(2)}) copy-start(f32[1,1024]{1,0:T(1,128)} %get-tuple-element.40) | copy-start | bytes 12292
  80.2 12.9 %copy-start.21 = (f32[1,1024]{1,0:T(1,128)S(1)}, f32[1,1024]{1,0:T(1,128)}, u32[]{:S(2)}) copy-start(f32[1,1024]{1,0:T(1,128)} %get-tuple-element.41) | copy-start | bytes 12292
  80.2 12.9 %copy-start.22 = (f32[1,1024]{1,0:T(1,128)S(1)}, f32[1,1024]{1,0:T(1,128)}, u32[]{:S(2)}) copy-start(f32[1,1024]{1,0:T(1,128)} %get-tuple-element.42) | copy-start | bytes 12292
  80.2 12.9 %copy-start.23 = (f32[1,1024]{1,0:T(1,128)S(1)}, f32[1,1024]{1,0:T(1,128)}, u32[]{:S(2)}) copy-start(f32[1,1024]{1,0:T(1,128)} %get-tuple-element.43) | copy-start | bytes 12292
  80.2 12.9 %copy-start.24 = (f32[1,1024]{1,0:T(1,128)S(1)}, f32[1,1024]{1,0:T(1,128)}, u32[]{:S(2)}) copy-start(f32[1,1024]{1,0:T(1,128)} %get-tuple-element.44) | copy-start | bytes 12292
  80.2 12.9 %copy-start.25 = (f32[1,1024]{1,0:T(1,128)S(1)}, f32[1,1024]{1,0:T(1,128)}, u32[]{:S(2)}) copy-start(f32[1,1024]{1,0:T(1,128)} %get-tuple-element.45) | copy-start | bytes 12292
  80.2 12.9 %copy-start.26 = (f32[1,1024]{1,0:T(1,128)S(1)}, f32[1,1024]{1,0:T(1,128)}, u32[]{:S(2)}) copy-start(f32[1,1024]{1,0:T(1,128)} %get-tuple-element.46) | copy-start | bytes 12292
  80.2 12.9 %copy-start.27 = (f32[1,1024]{1,0:T(1,128)S(1)}, f32[1,1024]{1,0:T(1,128)}, u32[]{:S(2)}) copy-start(f32[1,1024]{1,0:T(1,128)} %get-tuple-element.47) | copy-start | bytes 12292
  80.3 12.9 %copy-start.28 = (f32[1,1024]{1,0:T(1,128)S(1)}, f32[1,1024]{1,0:T(1,128)}, u32[]{:S(2)}) copy-start(f32[1,1024]{1,0:T(1,128)} %get-tuple-element.48) | copy-start | bytes 12292
  80.3 12.9 %copy-start.29 = (f32[1,1024]{1,0:T(1,128)S(1)}, f32[1,1024]{1,0:T(1,128)}, u32[]{:S(2)}) copy-start(f32[1,1024]{1,0:T(1,128)} %get-tuple-element.49) | copy-start | bytes 12292
  80.3 12.9 %copy-start.30 = (f32[1,1024]{1,0:T(1,128)S(1)}, f32[1,1024]{1,0:T(1,128)}, u32[]{:S(2)}) copy-start(f32[1,1024]{1,0:T(1,128)} %get-tuple-element.50) | copy-start | bytes 12292
  80.3 12.9 %copy-start.31 = (f32[1,1024]{1,0:T(1,128)S(1)}, f32[1,1024]{1,0:T(1,128)}, u32[]{:S(2)}) copy-start(f32[1,1024]{1,0:T(1,128)} %get-tuple-element.51) | copy-start | bytes 12292
  80.3 12.9 %copy-start.32 = (f32[1,1024]{1,0:T(1,128)S(1)}, f32[1,1024]{1,0:T(1,128)}, u32[]{:S(2)}) copy-start(f32[1,1024]{1,0:T(1,128)} %get-tuple-element.52) | copy-start | bytes 12292
  80.3 12.9 %copy-start.33 = (f32[1,1024]{1,0:T(1,128)S(1)}, f32[1,1024]{1,0:T(1,128)}, u32[]{:S(2)}) copy-start(f32[1,1024]{1,0:T(1,128)} %get-tuple-element.53) | copy-start | bytes 12292
  81.1 14.9 %copy-start.36 = (f32[1024]{0:T(1024)S(1)}, f32[1024]{0:T(1024)}, u32[]{:S(2)}) copy-start(f32[1024]{0:T(1024)} %param.24) | copy-start | bytes 12292
  81.3 7.6 %collective-permute-start.4 = (bf16[60,1024]{1,0:T(8,128)(2,1)S(1)}, bf16[60,1024]{1,0:T(8,128)(2,1)S(1)}, u32[]{:S(2)}, u32[]{:S(2)}) collective-permute-start(bf16[60,1024]{1,0:T(8,128)(2,1)S(1)} %get-tuple-element.25), channel_id=1, source_target_pairs={{0,1},{1,2},{2,3},{3,4},{4,5},{5,6},{6,7},{7,8},{8,9},{9,10},{10,1... | collective-permute-start | bytes 368648 | tf_op jit(solution)/shard_map/ppermute | solution.py:29
  85.9 7.2 %collective-permute-start.5 = (bf16[60,1024]{1,0:T(8,128)(2,1)S(1)}, bf16[60,1024]{1,0:T(8,128)(2,1)S(1)}, u32[]{:S(2)}, u32[]{:S(2)}) collective-permute-start(bf16[60,1024]{1,0:T(8,128)(2,1)S(1)} %get-tuple-element.26), channel_id=1, source_target_pairs={{1,0},{2,1},{3,2},{4,3},{5,4},{6,5},{7,6},{8,7},{9,8},{10,9},{11,1... | collective-permute-start | bytes 368648 | tf_op jit(solution)/shard_map/ppermute | solution.py:31
where the time goes:
time: 98.3 us; the launch traced here: 97.3 us
  local copies, waits for them, and re-layouts  54.2 us (55%)
  starting transfers between devices  18.5 us (19%)
  matrix products  13.8 us (14%)
  other arithmetic  5.88 us (6%)
  waiting for transfers between devices  4.11 us (4%)
    unnamed x83, local copies, waits for them, and re-layouts  12.1 us
    ppermute x4, starting transfers between devices, shifted(): lax.ppermute(value, axis, [(source, source + steps) for source in range(l...  12.1 us
    slice x8, local copies, waits for them, and re-layouts, absorb(): packed_block[:, att_width:].reshape(row_count, head_count, head_width)  11.7 us
    dot_general x5, matrix products, absorb(): jnp.einsum('hrd,chd->hrc', queries, keys_here, preferred_element_type=jnp...  9.14 us
    reshape x1, local copies, waits for them, and re-layouts, on_device(): skewed.reshape(head_count, row_count, line_length - 1)[:, :, :window_cols]  6.98 us
    another operation x2, local copies, waits for them, and re-layouts, on_device(): repeated = jnp.tile(bias_line, (1, row_count + 1))  6.62 us
    slice x4, local copies, waits for them, and re-layouts, absorb(): packed_block[:, :att_width].reshape(row_count, head_count, head_width)  5.12 us
    ppermute x1, starting transfers between devices, padded_2(): lax.ppermute(tail, axis, [(i, (i + 1) % count) for i in range(ends)])  4.54 us
  transfers between devices with their start and end apart: 6, of which 1 were waited for; matrix products, arithmetic and copies ran while one was open for 54% of the time, Pallas kernels for 0%

commit v1 on v0

v1 whole, which is shorter than its diff:
```python
import jax
import jax.numpy as jnp
from jax import lax
from jax.experimental import pallas as pl
from jax.experimental.pallas import tpu as pltpu
from jax.sharding import PartitionSpec as P

KERNEL = 31
DILATION = 4
REACH = 2
LANES = 128

norm_epsilon = 1e-05
masked_score = -1e30


def shifted(value, axis, steps):
    count = lax.axis_size(axis)
    leading, last = (max(0, -steps), min(count, count - steps))
    return lax.ppermute(value, axis, [(source, source + steps) for source in range(leading, last)])


def layer_norm(values, gain_vec):
    row_mean = jnp.mean(values, axis=-1, keepdims=True)
    centred = values - row_mean
    spread = jnp.mean(centred * centred, axis=-1, keepdims=True)
    return centred * lax.rsqrt(spread + norm_epsilon) * gain_vec


def sigmoid(values):
    return 1.0 / (1.0 + jnp.exp(-values))


def attention_kernel(
    meta_ref, len_ref, table_ref, bias_t_ref, q_ref,
    k0, k1, k2, k3, k4, v0, v1, v2, v3, v4,
    x_ref, gain_ref, ow_hbm, ew_hbm,
    mid_ref, head_ref, tail_ref,
    ow_vmem, ew_vmem, sems, att_ref,
):
    ow_copy = pltpu.make_async_copy(ow_hbm, ow_vmem, sems.at[0])
    ew_copy = pltpu.make_async_copy(ew_hbm, ew_vmem, sems.at[1])
    ow_copy.start()
    ew_copy.start()
    k_refs = (k0, k1, k2, k3, k4)
    v_refs = (v0, v1, v2, v3, v4)
    rows, att_width = q_ref.shape
    heads = bias_t_ref.shape[0]
    buckets = bias_t_ref.shape[1]
    head_width = att_width // heads
    width = len(k_refs) * rows
    line_len = table_ref.shape[1]

    base = meta_ref[0]
    qpos = base + lax.broadcasted_iota(jnp.int32, (rows, 1), 0)
    kpos = base - REACH * rows + lax.broadcasted_iota(jnp.int32, (1, width), 1)

    def seg_step(u, carry):
        run, qs, ks = carry
        run = run + len_ref[u]
        return run, qs + (qpos >= run).astype(jnp.int32), ks + (kpos >= run).astype(jnp.int32)

    _, qseg, kseg = lax.fori_loop(
        0, len_ref.shape[0], seg_step,
        (jnp.int32(0), jnp.zeros((rows, 1), jnp.int32), jnp.zeros((1, width), jnp.int32)),
    )
    kseg = jnp.where(kpos < 0, -1, kseg)
    same = qseg == kseg

    table = table_ref[...]
    bias_t = bias_t_ref[...]
    line = jnp.zeros((heads, line_len), jnp.float32)
    for b in range(buckets):
        line = jnp.where(table == b, bias_t[:, b:b + 1], line)

    scaling = head_width ** (-0.5)
    lane = lax.broadcasted_iota(jnp.int32, (rows, LANES), 1)
    per_pair = LANES // head_width
    for pair in range(att_width // LANES):
        cols = slice(pair * LANES, (pair + 1) * LANES)
        q_pair = q_ref[:, cols]
        k_pair = jnp.concatenate([r[:, cols] for r in k_refs], axis=0)
        v_pair = jnp.concatenate([r[:, cols] for r in v_refs], axis=0)
        result = None
        for sub in range(per_pair):
            head = pair * per_pair + sub
            in_head = (lane >= sub * head_width) & (lane < (sub + 1) * head_width)
            q_head = jnp.where(in_head, q_pair, jnp.zeros_like(q_pair))
            spread = jnp.broadcast_to(line[head:head + 1, :], (rows, line_len))
            skew = pltpu.roll(spread, line_len - rows + 1, 1, stride=1, stride_axis=0)[:, :width]
            bias = jnp.where(same, skew, masked_score)
            scores = lax.dot_general(
                q_head, k_pair, (((1,), (1,)), ((), ())), preferred_element_type=jnp.float32
            )
            scores = scores * scaling + bias
            top = jnp.max(scores, axis=1, keepdims=True)
            weights = jnp.exp(scores - top)
            total = jnp.sum(weights, axis=1, keepdims=True)
            summed = jnp.dot(weights.astype(jnp.bfloat16), v_pair, preferred_element_type=jnp.float32)
            part = summed / total
            result = part if result is None else jnp.where(in_head, part, result)
        att_ref[:, cols] = result.astype(jnp.bfloat16)

    ow_copy.wait()
    projected = jnp.dot(att_ref[...], ow_vmem[...], preferred_element_type=jnp.float32)
    mid = (x_ref[...].astype(jnp.float32) + projected).astype(jnp.bfloat16)
    mid_ref[...] = mid
    normed = layer_norm(mid.astype(jnp.float32), gain_ref[...]).astype(jnp.bfloat16)
    model_width = mid.shape[1]
    ew_copy.wait()
    value_half = jnp.dot(normed, ew_vmem[:, :model_width], preferred_element_type=jnp.float32)
    gate_half = jnp.dot(normed, ew_vmem[:, model_width:], preferred_element_type=jnp.float32)
    gated = (value_half * sigmoid(gate_half)).astype(jnp.bfloat16)
    half = head_ref.shape[0]
    head_ref[...] = gated[:half]
    tail_ref[...] = gated[half:]


def conv_kernel(
    prev_ref, head_ref, tail_ref, next_ref, taps_ref, gain_ref, mid_ref, sw_hbm,
    out_ref, win_ref, conv_ref, sw_vmem, sems,
):
    sw_copy = pltpu.make_async_copy(sw_hbm, sw_vmem, sems.at[0])
    sw_copy.start()
    half = head_ref.shape[0]
    rows, model_width = mid_ref.shape
    win_ref[0:half, :] = prev_ref[...].astype(jnp.float32)
    win_ref[half:2 * half, :] = head_ref[...].astype(jnp.float32)
    win_ref[2 * half:3 * half, :] = tail_ref[...].astype(jnp.float32)
    win_ref[3 * half:4 * half, :] = next_ref[...].astype(jnp.float32)
    reach = DILATION * (KERNEL - 1) // 2
    start = half - reach

    def chunk(c, carry):
        lanes = pl.ds(pl.multiple_of(c * LANES, LANES), LANES)
        acc = jnp.zeros((rows, LANES), jnp.float32)
        for tap in range(KERNEL):
            first = start + DILATION * tap
            acc = acc + taps_ref[tap:tap + 1, lanes] * win_ref[first:first + rows, lanes]
        conv_ref[:, lanes] = acc
        return carry

    lax.fori_loop(0, model_width // LANES, chunk, 0)
    inner = layer_norm(conv_ref[...], gain_ref[...])
    activated = (inner * sigmoid(inner)).astype(jnp.bfloat16)
    sw_copy.wait()
    shrunk = jnp.dot(activated, sw_vmem[...], preferred_element_type=jnp.float32)
    out_ref[...] = (mid_ref[...].astype(jnp.float32) + shrunk).astype(out_ref.dtype)


def on_device(
    frames_in,
    query_proj,
    key_proj,
    value_proj,
    utterance_lengths,
    bucket_table,
    bucket_bias,
    out_weight,
    norm_gain,
    expand_weight,
    depth_taps,
    inner_gain,
    shrink_weight,
):
    rows, att_width = query_proj.shape
    model_width = frames_in.shape[1]
    heads = bucket_bias.shape[1]
    device_index = lax.axis_index("seq")
    meta = (device_index * rows).astype(jnp.int32).reshape(1)
    line_len = -(-bucket_table.shape[0] // LANES) * LANES
    table = jnp.pad(bucket_table, (0, line_len - bucket_table.shape[0])).reshape(1, line_len)
    bias_t = bucket_bias.T

    received = {0: (key_proj, value_proj)}
    for hop in range(1, REACH + 1):
        received[hop] = shifted((key_proj, value_proj), "seq", -hop)
        received[-hop] = shifted((key_proj, value_proj), "seq", hop)
    order = list(range(-REACH, REACH + 1))
    k_blocks = [received[h][0] for h in order]
    v_blocks = [received[h][1] for h in order]

    half = rows // 2
    vmem = pl.BlockSpec(memory_space=pltpu.VMEM)
    smem = pl.BlockSpec(memory_space=pltpu.SMEM)
    anywhere = pl.BlockSpec(memory_space=pl.ANY)
    window = len(order) * rows
    attn_flops = 2 * 2 * heads * rows * window * LANES + 2 * rows * att_width * model_width + 2 * rows * model_width * 2 * model_width
    attn_bytes = 2 * (rows * att_width * (1 + 2 * len(order)) + rows * model_width * 2 + att_width * model_width + model_width * 2 * model_width)
    mid, g_head, g_tail = pl.pallas_call(
        attention_kernel,
        out_shape=(
            jax.ShapeDtypeStruct((rows, model_width), jnp.bfloat16),
            jax.ShapeDtypeStruct((half, model_width), jnp.bfloat16),
            jax.ShapeDtypeStruct((rows - half, model_width), jnp.bfloat16),
        ),
        in_specs=[smem, smem] + [vmem] * (3 + 2 * len(order)) + [vmem, vmem, anywhere, anywhere],
        out_specs=(vmem, vmem, vmem),
        scratch_shapes=[
            pltpu.VMEM((att_width, model_width), jnp.bfloat16),
            pltpu.VMEM((model_width, 2 * model_width), jnp.bfloat16),
            pltpu.SemaphoreType.DMA((2,)),
            pltpu.VMEM((rows, att_width), jnp.bfloat16),
        ],
        cost_estimate=pl.CostEstimate(
            flops=attn_flops, transcendentals=heads * rows * window + rows * model_width, bytes_accessed=attn_bytes
        ),
        name="attention_glu",
    )(
        meta, utterance_lengths, table, bias_t, query_proj, *k_blocks, *v_blocks,
        frames_in, norm_gain.reshape(1, -1), out_weight, expand_weight,
    )

    prev_tail = shifted(g_tail, "seq", 1)
    next_head = shifted(g_head, "seq", -1)
    conv_flops = 2 * KERNEL * rows * model_width + 2 * rows * model_width * model_width
    conv_bytes = 2 * (4 * half * model_width + rows * model_width * 2 + model_width * model_width) + 4 * KERNEL * model_width
    return pl.pallas_call(
        conv_kernel,
        out_shape=jax.ShapeDtypeStruct((rows, model_width), jnp.bfloat16),
        in_specs=[vmem] * 7 + [anywhere],
        out_specs=vmem,
        scratch_shapes=[
            pltpu.VMEM((4 * half, model_width), jnp.float32),
            pltpu.VMEM((rows, model_width), jnp.float32),
            pltpu.VMEM((model_width, model_width), jnp.bfloat16),
            pltpu.SemaphoreType.DMA((1,)),
        ],
        cost_estimate=pl.CostEstimate(
            flops=conv_flops, transcendentals=rows * model_width, bytes_accessed=conv_bytes
        ),
        name="conv_shrink",
    )(prev_tail, g_head, g_tail, next_head, depth_taps, inner_gain.reshape(1, -1), mid, shrink_weight)


def solution(mesh):
    placed = (
        P(("groups", "seq"), None),
        P(("groups", "seq"), None),
        P(("groups", "seq"), None),
        P(("groups", "seq"), None),
        P("groups"),
        P(),
        P(),
        P(),
        P(),
        P(),
        P(),
        P(),
        P(),
    )
    return jax.shard_map(
        on_device, mesh=mesh, in_specs=placed, out_specs=P(("groups", "seq"), None), check_vma=False
    )
```

time: 98.3 us -> 53.3 us (0.54)
  local copies, waits for them, and re-layouts: 54.2 us -> 2.56 us
  matrix products: 13.8 us -> 0 us
  Pallas kernels: 0 us -> 11.6 us
  starting transfers between devices: 18.5 us -> 28.9 us
  other arithmetic: 5.88 us -> 0 us
  waiting for transfers between devices: 4.11 us -> 9.31 us
    slice x17 -> x0, local copies, waits for them, and re-layouts: 26.2 us -> none  [the longest x8 11.7 us: absorb(): packed_block[:, att_width:].reshape(row_count, head_count, head_width)]
    ppermute x4 -> x10, starting transfers between devices: 12.1 us -> 28.9 us  [shifted(): lax.ppermute(value, axis, [(source, source + steps) for source in range(l...]
    dot_general x14 -> x0, matrix products: 13.8 us -> none  [the longest x5 9.14 us: absorb(): jnp.einsum('hrd,chd->hrc', queries, keys_here, preferred_element_type=jnp...]
    pallas_call x0 -> x2, Pallas kernels: none -> 11.6 us  [the longest x1 6.66 us: on_device(): pl.pallas_call(attention_kernel, out_shape=(jax.ShapeDtypeStruct((rows, m...]
    unnamed x83 -> x20, local copies, waits for them, and re-layouts: 12.1 us -> 1.29 us
    ppermute x4 -> x10, waiting for transfers between devices: 0.01 us -> 9.31 us  [shifted(): lax.ppermute(value, axis, [(source, source + steps) for source in range(l...]
    another operation x3 -> x0, local copies, waits for them, and re-layouts: 7.36 us -> none  [the longest x2 6.62 us: on_device(): repeated = jnp.tile(bias_line, (1, row_count + 1))]
    ppermute x2 -> x0, starting transfers between devices: 6.46 us -> none  [the longest x1 4.54 us: padded_2(): lax.ppermute(tail, axis, [(i, (i + 1) % count) for i in range(ends)])]
  transfers between devices with their start and end apart: 6 -> 10, of which waited for: 1 -> 3; matrix products, arithmetic and copies ran while one was open for 54% -> 2% of each run, Pallas kernels for 0% -> 0%
where the time goes in v1:
time: 53.3 us; the launch traced here: 52.5 us
  starting transfers between devices  28.9 us (54%)
  Pallas kernels  11.6 us (22%)
  waiting for transfers between devices  9.31 us (17%)
  local copies, waits for them, and re-layouts  2.56 us (5%)
    ppermute x10, starting transfers between devices, shifted(): lax.ppermute(value, axis, [(source, source + steps) for source in range(l...  28.9 us
    ppermute x10, waiting for transfers between devices, shifted(): lax.ppermute(value, axis, [(source, source + steps) for source in range(l...  9.31 us
    pallas_call x1, Pallas kernels, on_device(): pl.pallas_call(attention_kernel, out_shape=(jax.ShapeDtypeStruct((rows, m...  6.66 us
    pallas_call x1, Pallas kernels, on_device(): pl.pallas_call(conv_kernel, out_shape=jax.ShapeDtypeStruct((rows, model_w...  4.91 us
    unnamed x20, local copies, waits for them, and re-layouts  1.29 us
  transfers between devices with their start and end apart: 10, of which 3 were waited for; matrix products, arithmetic and copies ran while one was open for 2% of the time, Pallas kernels for 0%

profile of v1, /device:TPU:21, one launch (start us, length us, event | category | flops | bytes accessed | tf_op | source)
XLA Modules:
  0.0 52.5 jit_solution(9354990170293993444)
XLA Ops:
  0.0 2.6 %collective-permute-start.2 = (bf16[128,512]{1,0:T(8,128)(2,1)}, bf16[128,512]{1,0:T(8,128)(2,1)S(1)}, u32[]{:S(2)}, u32[]{:S(2)}) collective-permute-start(bf16[128,512]{1,0:T(8,128)(2,1)} %k2.1), channel_id=1, source_target_pairs={{1,0},{2,1},{3,2},{4,3},{5,4},{6,5},{7,6},{8,7},{9,8},{10,9},{11,1... | collective-permute-start | bytes 393224 | tf_op jit(solution)/shard_map/ppermute | solution.py:20
  2.6 3.9 %collective-permute-start.1 = (bf16[128,512]{1,0:T(8,128)(2,1)}, bf16[128,512]{1,0:T(8,128)(2,1)S(1)}, u32[]{:S(2)}, u32[]{:S(2)}) collective-permute-start(bf16[128,512]{1,0:T(8,128)(2,1)} %k2.1), channel_id=1, source_target_pairs={{0,1},{1,2},{2,3},{3,4},{4,5},{5,6},{6,7},{7,8},{8,9},{9,10},{10,1... | collective-permute-start | bytes 393224 | tf_op jit(solution)/shard_map/ppermute | solution.py:20
  6.5 2.3 %collective-permute-start = (bf16[128,512]{1,0:T(8,128)(2,1)}, bf16[128,512]{1,0:T(8,128)(2,1)S(1)}, u32[]{:S(2)}, u32[]{:S(2)}) collective-permute-start(bf16[128,512]{1,0:T(8,128)(2,1)} %k2.1), channel_id=1, source_target_pairs={{0,2},{1,3},{2,4},{3,5},{4,6},{5,7},{6,8},{7,9},{8,10},{9,11},{10,... | collective-permute-start | bytes 393224 | tf_op jit(solution)/shard_map/ppermute | solution.py:20
  8.8 3.0 %collective-permute-start.3 = (bf16[128,512]{1,0:T(8,128)(2,1)}, bf16[128,512]{1,0:T(8,128)(2,1)S(1)}, u32[]{:S(2)}, u32[]{:S(2)}) collective-permute-start(bf16[128,512]{1,0:T(8,128)(2,1)} %k2.1), channel_id=1, source_target_pairs={{2,0},{3,1},{4,2},{5,3},{6,4},{7,5},{8,6},{9,7},{10,8},{11,9},{12,... | collective-permute-start | bytes 393224 | tf_op jit(solution)/shard_map/ppermute | solution.py:20
  11.8 1.9 %collective-permute-start.6 = (bf16[128,512]{1,0:T(8,128)(2,1)}, bf16[128,512]{1,0:T(8,128)(2,1)S(1)}, u32[]{:S(2)}, u32[]{:S(2)}) collective-permute-start(bf16[128,512]{1,0:T(8,128)(2,1)} %v2.1), channel_id=1, source_target_pairs={{1,0},{2,1},{3,2},{4,3},{5,4},{6,5},{7,6},{8,7},{9,8},{10,9},{11,1... | collective-permute-start | bytes 393224 | tf_op jit(solution)/shard_map/ppermute | solution.py:20
  13.7 0.0 collective-permute-done.2.k3
  13.7 0.0 copy-start
  13.7 4.5 %collective-permute-start.5 = (bf16[128,512]{1,0:T(8,128)(2,1)}, bf16[128,512]{1,0:T(8,128)(2,1)S(1)}, u32[]{:S(2)}, u32[]{:S(2)}) collective-permute-start(bf16[128,512]{1,0:T(8,128)(2,1)} %v2.1), channel_id=1, source_target_pairs={{0,1},{1,2},{2,3},{3,4},{4,5},{5,6},{6,7},{7,8},{8,9},{9,10},{10,1... | collective-permute-start | bytes 393224 | tf_op jit(solution)/shard_map/ppermute | solution.py:20
  18.3 0.0 collective-permute-done.1.k1
  18.3 0.0 copy-start.1
  18.3 2.3 %collective-permute-start.4 = (bf16[128,512]{1,0:T(8,128)(2,1)}, bf16[128,512]{1,0:T(8,128)(2,1)S(1)}, u32[]{:S(2)}, u32[]{:S(2)}) collective-permute-start(bf16[128,512]{1,0:T(8,128)(2,1)} %v2.1), channel_id=1, source_target_pairs={{0,2},{1,3},{2,4},{3,5},{4,6},{5,7},{6,8},{7,9},{8,10},{9,11},{10,... | collective-permute-start | bytes 393224 | tf_op jit(solution)/shard_map/ppermute | solution.py:20
  20.6 0.0 collective-permute-done.k0
  20.6 0.0 copy-start.2
  20.6 3.0 %collective-permute-start.7 = (bf16[128,512]{1,0:T(8,128)(2,1)}, bf16[128,512]{1,0:T(8,128)(2,1)S(1)}, u32[]{:S(2)}, u32[]{:S(2)}) collective-permute-start(bf16[128,512]{1,0:T(8,128)(2,1)} %v2.1), channel_id=1, source_target_pairs={{2,0},{3,1},{4,2},{5,3},{6,4},{7,5},{8,6},{9,7},{10,8},{11,9},{12,... | collective-permute-start | bytes 393224 | tf_op jit(solution)/shard_map/ppermute | solution.py:20
  23.6 0.7 %pad.4 = s32[768]{0:T(1024)S(1)} pad(s32[767]{0:T(1024)} %param.18, s32[]{:T(128)} %constant.2.clone.1), padding=0_1 | pad | bytes 6144 | tf_op jit(solution)/shard_map/jit(_pad)/pad | solution.py:172
  24.3 0.6 %reshape.13.table_ref = s32[1,768]{1,0:T(1,128)} reshape(s32[768]{0:T(1024)S(1)} %pad.4) | data formatting | bytes 6144 | tf_op jit(solution)/shard_map/reshape | solution.py:172
  24.9 0.0 collective-permute-done.3.k4
  24.9 0.0 copy-start.3
  24.9 0.0 collective-permute-done.6.v3
  24.9 0.0 copy-start.4
  24.9 0.0 collective-permute-done.5.v1
  24.9 0.0 copy-start.5
  24.9 0.0 collective-permute-done.4.v0
  24.9 0.0 copy-start.6
  25.0 3.8 %collective-permute-done.7.v4 = bf16[128,512]{1,0:T(8,128)(2,1)S(1)} collective-permute-done((bf16[128,512]{1,0:T(8,128)(2,1)}, bf16[128,512]{1,0:T(8,128)(2,1)S(1)}, u32[]{:S(2)}, u32[]{:S(2)}) %collective-permute-start.7) | collective-permute-done | bytes 131104 | tf_op jit(solution)/shard_map/ppermute | solution.py:20
  28.8 0.0 copy-start.7
  28.8 0.0 copy-done
  28.8 0.0 copy-done.1
  28.8 0.0 copy-done.2
  28.8 0.0 copy-done.3
  28.8 0.0 copy-done.4
  28.8 0.0 copy-done.5
  28.8 0.0 copy-done.6
  28.8 0.6 %copy-done.7 = bf16[128,512]{1,0:T(8,128)(2,1)} copy-done((bf16[128,512]{1,0:T(8,128)(2,1)}, bf16[128,512]{1,0:T(8,128)(2,1)S(1)}, u32[]{:S(2)}) %copy-start.7) | copy-done | bytes 131096
  29.4 6.7 %attention_glu.1 = (bf16[128,1024]{1,0:T(8,128)(2,1)}, bf16[64,1024]{1,0:T(8,128)(2,1)}, bf16[64,1024]{1,0:T(8,128)(2,1)}) custom-call(s32[1]{0:T(128)} %bitcast.meta_ref, s32[16]{0:T(128)} %len_ref.1, s32[1,768]{1,0:T(1,128)} %reshape.13.table_ref, f32[8,32]{1,0:T(8,128)} %bitcast.4, bf16[128,512]{1,0:T(8,128)(2,1)} %q_ref.1, bf16[128,512]{1,0:T(8,128)(2,1)} %copy-done.2, ...), custom_call_target="tpu_custom_call" | custom-call | flops 1006632960 | bytes 7208960 | tf_op jit(solution)/shard_map/attention_glu/pallas_call | solution.py:190
  36.1 3.4 %collective-permute-start.8 = (bf16[64,1024]{1,0:T(8,128)(2,1)}, bf16[64,1024]{1,0:T(8,128)(2,1)S(1)}, u32[]{:S(2)}, u32[]{:S(2)}) collective-permute-start(bf16[64,1024]{1,0:T(8,128)(2,1)} %get-tuple-element.8.tail_ref), channel_id=1, source_target_pairs={{0,1},{1,2},{2,3},{3,4},{4,5},{5,6},{6,7},{7,8},{8,9},{9,10},{10,1... | collective-permute-start | bytes 393224 | tf_op jit(solution)/shard_map/ppermute | solution.py:20
  39.5 1.9 %collective-permute-start.9 = (bf16[64,1024]{1,0:T(8,128)(2,1)}, bf16[64,1024]{1,0:T(8,128)(2,1)S(1)}, u32[]{:S(2)}, u32[]{:S(2)}) collective-permute-start(bf16[64,1024]{1,0:T(8,128)(2,1)} %get-tuple-element.9.head_ref), channel_id=1, source_target_pairs={{1,0},{2,1},{3,2},{4,3},{5,4},{6,5},{7,6},{8,7},{9,8},{10,9},{11,1... | collective-permute-start | bytes 393224 | tf_op jit(solution)/shard_map/ppermute | solution.py:20
  41.5 0.3 collective-permute-done.8.prev_ref
  41.8 0.0 copy-start.8
  41.8 5.2 %collective-permute-done.9.next_ref = bf16[64,1024]{1,0:T(8,128)(2,1)S(1)} collective-permute-done((bf16[64,1024]{1,0:T(8,128)(2,1)}, bf16[64,1024]{1,0:T(8,128)(2,1)S(1)}, u32[]{:S(2)}, u32[]{:S(2)}) %collective-permute-start.9) | collective-permute-done | bytes 131104 | tf_op jit(solution)/shard_map/ppermute | solution.py:20
  46.9 0.0 copy-start.9
  46.9 0.0 copy-done.8
  47.0 0.7 %copy-done.9 = bf16[64,1024]{1,0:T(8,128)(2,1)} copy-done((bf16[64,1024]{1,0:T(8,128)(2,1)}, bf16[64,1024]{1,0:T(8,128)(2,1)S(1)}, u32[]{:S(2)}) %copy-start.9) | copy-done | bytes 131096
  47.6 4.9 %conv_shrink.1 = bf16[128,1024]{1,0:T(8,128)(2,1)} custom-call(bf16[64,1024]{1,0:T(8,128)(2,1)} %copy-done.8, bf16[64,1024]{1,0:T(8,128)(2,1)} %get-tuple-element.9.head_ref, bf16[64,1024]{1,0:T(8,128)(2,1)} %get-tuple-element.8.tail_ref, bf16[64,1024]{1,0:T(8,128)(2,1)} %copy-done.9, f32[31,1024]{1,0:T(8,128)} %taps_ref.1, f32[1,1024]{1,0:T(1,128)} %bitcast.6, ...), custom_call_target="tpu_custom_call" | custom-call | flops 276561920 | bytes 3272704 | tf_op jit(solution)/shard_map/conv_shrink/pallas_call | solution.py:218
Async XLA Ops:
  0.0 13.7 %collective-permute-start.2 = (bf16[128,512]{1,0:T(8,128)(2,1)}, bf16[128,512]{1,0:T(8,128)(2,1)S(1)}, u32[]{:S(2)}, u32[]{:S(2)}) collective-permute-start(bf16[128,512]{1,0:T(8,128)(2,1)} %k2.1), channel_id=1, source_target_pairs={{1,0},{2,1},{3,2},{4,3},{5,4},{6,5},{7,6},{8,7},{9,8},{10,9},{11,1... | collective-permute-start | bytes 393224 | tf_op jit(solution)/shard_map/ppermute | solution.py:20
  2.6 15.7 %collective-permute-start.1 = (bf16[128,512]{1,0:T(8,128)(2,1)}, bf16[128,512]{1,0:T(8,128)(2,1)S(1)}, u32[]{:S(2)}, u32[]{:S(2)}) collective-permute-start(bf16[128,512]{1,0:T(8,128)(2,1)} %k2.1), channel_id=1, source_target_pairs={{0,1},{1,2},{2,3},{3,4},{4,5},{5,6},{6,7},{7,8},{8,9},{9,10},{10,1... | collective-permute-start | bytes 393224 | tf_op jit(solution)/shard_map/ppermute | solution.py:20
  6.5 14.2 %collective-permute-start = (bf16[128,512]{1,0:T(8,128)(2,1)}, bf16[128,512]{1,0:T(8,128)(2,1)S(1)}, u32[]{:S(2)}, u32[]{:S(2)}) collective-permute-start(bf16[128,512]{1,0:T(8,128)(2,1)} %k2.1), channel_id=1, source_target_pairs={{0,2},{1,3},{2,4},{3,5},{4,6},{5,7},{6,8},{7,9},{8,10},{9,11},{10,... | collective-permute-start | bytes 393224 | tf_op jit(solution)/shard_map/ppermute | solution.py:20
  8.8 16.1 %collective-permute-start.3 = (bf16[128,512]{1,0:T(8,128)(2,1)}, bf16[128,512]{1,0:T(8,128)(2,1)S(1)}, u32[]{:S(2)}, u32[]{:S(2)}) collective-permute-start(bf16[128,512]{1,0:T(8,128)(2,1)} %k2.1), channel_id=1, source_target_pairs={{2,0},{3,1},{4,2},{5,3},{6,4},{7,5},{8,6},{9,7},{10,8},{11,9},{12,... | collective-permute-start | bytes 393224 | tf_op jit(solution)/shard_map/ppermute | solution.py:20
  11.8 13.1 %collective-permute-start.6 = (bf16[128,512]{1,0:T(8,128)(2,1)}, bf16[128,512]{1,0:T(8,128)(2,1)S(1)}, u32[]{:S(2)}, u32[]{:S(2)}) collective-permute-start(bf16[128,512]{1,0:T(8,128)(2,1)} %v2.1), channel_id=1, source_target_pairs={{1,0},{2,1},{3,2},{4,3},{5,4},{6,5},{7,6},{8,7},{9,8},{10,9},{11,1... | collective-permute-start | bytes 393224 | tf_op jit(solution)/shard_map/ppermute | solution.py:20
  13.7 15.1 %copy-start = (bf16[128,512]{1,0:T(8,128)(2,1)}, bf16[128,512]{1,0:T(8,128)(2,1)S(1)}, u32[]{:S(2)}) copy-start(bf16[128,512]{1,0:T(8,128)(2,1)S(1)} %collective-permute-done.2.k3) | copy-start | bytes 393220
  13.7 11.2 %collective-permute-start.5 = (bf16[128,512]{1,0:T(8,128)(2,1)}, bf16[128,512]{1,0:T(8,128)(2,1)S(1)}, u32[]{:S(2)}, u32[]{:S(2)}) collective-permute-start(bf16[128,512]{1,0:T(8,128)(2,1)} %v2.1), channel_id=1, source_target_pairs={{0,1},{1,2},{2,3},{3,4},{4,5},{5,6},{6,7},{7,8},{8,9},{9,10},{10,1... | collective-permute-start | bytes 393224 | tf_op jit(solution)/shard_map/ppermute | solution.py:20
  18.3 10.5 %copy-start.1 = (bf16[128,512]{1,0:T(8,128)(2,1)}, bf16[128,512]{1,0:T(8,128)(2,1)S(1)}, u32[]{:S(2)}) copy-start(bf16[128,512]{1,0:T(8,128)(2,1)S(1)} %collective-permute-done.1.k1) | copy-start | bytes 393220
  18.3 6.6 %collective-permute-start.4 = (bf16[128,512]{1,0:T(8,128)(2,1)}, bf16[128,512]{1,0:T(8,128)(2,1)S(1)}, u32[]{:S(2)}, u32[]{:S(2)}) collective-permute-start(bf16[128,512]{1,0:T(8,128)(2,1)} %v2.1), channel_id=1, source_target_pairs={{0,2},{1,3},{2,4},{3,5},{4,6},{5,7},{6,8},{7,9},{8,10},{9,11},{10,... | collective-permute-start | bytes 393224 | tf_op jit(solution)/shard_map/ppermute | solution.py:20
  20.6 8.2 %copy-start.2 = (bf16[128,512]{1,0:T(8,128)(2,1)}, bf16[128,512]{1,0:T(8,128)(2,1)S(1)}, u32[]{:S(2)}) copy-start(bf16[128,512]{1,0:T(8,128)(2,1)S(1)} %collective-permute-done.k0) | copy-start | bytes 393220
  20.6 8.1 %collective-permute-start.7 = (bf16[128,512]{1,0:T(8,128)(2,1)}, bf16[128,512]{1,0:T(8,128)(2,1)S(1)}, u32[]{:S(2)}, u32[]{:S(2)}) collective-permute-start(bf16[128,512]{1,0:T(8,128)(2,1)} %v2.1), channel_id=1, source_target_pairs={{2,0},{3,1},{4,2},{5,3},{6,4},{7,5},{8,6},{9,7},{10,8},{11,9},{12,... | collective-permute-start | bytes 393224 | tf_op jit(solution)/shard_map/ppermute | solution.py:20
  24.9 3.9 %copy-start.3 = (bf16[128,512]{1,0:T(8,128)(2,1)}, bf16[128,512]{1,0:T(8,128)(2,1)S(1)}, u32[]{:S(2)}) copy-start(bf16[128,512]{1,0:T(8,128)(2,1)S(1)} %collective-permute-done.3.k4) | copy-start | bytes 393220
  24.9 3.9 %copy-start.4 = (bf16[128,512]{1,0:T(8,128)(2,1)}, bf16[128,512]{1,0:T(8,128)(2,1)S(1)}, u32[]{:S(2)}) copy-start(bf16[128,512]{1,0:T(8,128)(2,1)S(1)} %collective-permute-done.6.v3) | copy-start | bytes 393220
  24.9 3.9 %copy-start.5 = (bf16[128,512]{1,0:T(8,128)(2,1)}, bf16[128,512]{1,0:T(8,128)(2,1)S(1)}, u32[]{:S(2)}) copy-start(bf16[128,512]{1,0:T(8,128)(2,1)S(1)} %collective-permute-done.5.v1) | copy-start | bytes 393220
  24.9 3.9 %copy-start.6 = (bf16[128,512]{1,0:T(8,128)(2,1)}, bf16[128,512]{1,0:T(8,128)(2,1)S(1)}, u32[]{:S(2)}) copy-start(bf16[128,512]{1,0:T(8,128)(2,1)S(1)} %collective-permute-done.4.v0) | copy-start | bytes 393220
  28.8 0.7 %copy-start.7 = (bf16[128,512]{1,0:T(8,128)(2,1)}, bf16[128,512]{1,0:T(8,128)(2,1)S(1)}, u32[]{:S(2)}) copy-start(bf16[128,512]{1,0:T(8,128)(2,1)S(1)} %collective-permute-done.7.v4) | copy-start | bytes 393220
  36.1 5.7 %collective-permute-start.8 = (bf16[64,1024]{1,0:T(8,128)(2,1)}, bf16[64,1024]{1,0:T(8,128)(2,1)S(1)}, u32[]{:S(2)}, u32[]{:S(2)}) collective-permute-start(bf16[64,1024]{1,0:T(8,128)(2,1)} %get-tuple-element.8.tail_ref), channel_id=1, source_target_pairs={{0,1},{1,2},{2,3},{3,4},{4,5},{5,6},{6,7},{7,8},{8,9},{9,10},{10,1... | collective-permute-start | bytes 393224 | tf_op jit(solution)/shard_map/ppermute | solution.py:20
  39.5 7.4 %collective-permute-start.9 = (bf16[64,1024]{1,0:T(8,128)(2,1)}, bf16[64,1024]{1,0:T(8,128)(2,1)S(1)}, u32[]{:S(2)}, u32[]{:S(2)}) collective-permute-start(bf16[64,1024]{1,0:T(8,128)(2,1)} %get-tuple-element.9.head_ref), channel_id=1, source_target_pairs={{1,0},{2,1},{3,2},{4,3},{5,4},{6,5},{7,6},{8,7},{9,8},{10,9},{11,1... | collective-permute-start | bytes 393224 | tf_op jit(solution)/shard_map/ppermute | solution.py:20
  41.8 5.2 %copy-start.8 = (bf16[64,1024]{1,0:T(8,128)(2,1)}, bf16[64,1024]{1,0:T(8,128)(2,1)S(1)}, u32[]{:S(2)}) copy-start(bf16[64,1024]{1,0:T(8,128)(2,1)S(1)} %collective-permute-done.8.prev_ref) | copy-start | bytes 393220
  46.9 0.7 %copy-start.9 = (bf16[64,1024]{1,0:T(8,128)(2,1)}, bf16[64,1024]{1,0:T(8,128)(2,1)S(1)}, u32[]{:S(2)}) copy-start(bf16[64,1024]{1,0:T(8,128)(2,1)S(1)} %collective-permute-done.9.next_ref) | copy-start | bytes 393220

commit v2 on v1

--- a/solution.py
+++ b/solution.py
@@ -33,7 +33,7 @@
 
 def attention_kernel(
     meta_ref, len_ref, table_ref, bias_t_ref, q_ref,
-    k0, k1, k2, k3, k4, v0, v1, v2, v3, v4,
+    kv0, kv1, kv2, kv3, kv4,
     x_ref, gain_ref, ow_hbm, ew_hbm,
     mid_ref, head_ref, tail_ref,
     ow_vmem, ew_vmem, sems, att_ref,
@@ -42,13 +42,12 @@
     ew_copy = pltpu.make_async_copy(ew_hbm, ew_vmem, sems.at[1])
     ow_copy.start()
     ew_copy.start()
-    k_refs = (k0, k1, k2, k3, k4)
-    v_refs = (v0, v1, v2, v3, v4)
+    kv_refs = (kv0, kv1, kv2, kv3, kv4)
     rows, att_width = q_ref.shape
     heads = bias_t_ref.shape[0]
     buckets = bias_t_ref.shape[1]
     head_width = att_width // heads
-    width = len(k_refs) * rows
+    width = len(kv_refs) * rows
     line_len = table_ref.shape[1]
 
     base = meta_ref[0]
@@ -79,8 +78,9 @@
     for pair in range(att_width // LANES):
         cols = slice(pair * LANES, (pair + 1) * LANES)
         q_pair = q_ref[:, cols]
-        k_pair = jnp.concatenate([r[:, cols] for r in k_refs], axis=0)
-        v_pair = jnp.concatenate([r[:, cols] for r in v_refs], axis=0)
+        v_cols = slice(att_width + pair * LANES, att_width + (pair + 1) * LANES)
+        k_pair = jnp.concatenate([r[:, cols] for r in kv_refs], axis=0)
+        v_pair = jnp.concatenate([r[:, v_cols] for r in kv_refs], axis=0)
         result = None
         for sub in range(per_pair):
             head = pair * per_pair + sub
@@ -172,13 +172,13 @@
     table = jnp.pad(bucket_table, (0, line_len - bucket_table.shape[0])).reshape(1, line_len)
     bias_t = bucket_bias.T
 
-    received = {0: (key_proj, value_proj)}
-    for hop in range(1, REACH + 1):
-        received[hop] = shifted((key_proj, value_proj), "seq", -hop)
-        received[-hop] = shifted((key_proj, value_proj), "seq", hop)
+    packed = jnp.concatenate([key_proj, value_proj], axis=1)
+    received = {0: packed}
+    for hop in range(REACH, 0, -1):
+        received[hop] = shifted(packed, "seq", -hop)
+        received[-hop] = shifted(packed, "seq", hop)
     order = list(range(-REACH, REACH + 1))
-    k_blocks = [received[h][0] for h in order]
-    v_blocks = [received[h][1] for h in order]
+    kv_blocks = [received[h] for h in order]
 
     half = rows // 2
     vmem = pl.BlockSpec(memory_space=pltpu.VMEM)
@@ -194,7 +194,7 @@
             jax.ShapeDtypeStruct((half, model_width), jnp.bfloat16),
             jax.ShapeDtypeStruct((rows - half, model_width), jnp.bfloat16),
         ),
-        in_specs=[smem, smem] + [vmem] * (3 + 2 * len(order)) + [vmem, vmem, anywhere, anywhere],
+        in_specs=[smem, smem] + [vmem] * (3 + len(order)) + [vmem, vmem, anywhere, anywhere],
         out_specs=(vmem, vmem, vmem),
         scratch_shapes=[
             pltpu.VMEM((att_width, model_width), jnp.bfloat16),
@@ -207,7 +207,7 @@
         ),
         name="attention_glu",
     )(
-        meta, utterance_lengths, table, bias_t, query_proj, *k_blocks, *v_blocks,
+        meta, utterance_lengths, table, bias_t, query_proj, *kv_blocks,
         frames_in, norm_gain.reshape(1, -1), out_weight, expand_weight,
     )
 

time: 53.3 us -> 46.4 us (0.87)
  starting transfers between devices: 28.9 us -> 16.1 us
  waiting for transfers between devices: 9.31 us -> 13.9 us
  local copies, waits for them, and re-layouts: 2.56 us -> 4.46 us
    ppermute x10 -> x6, starting transfers between devices: 28.9 us -> 16.1 us  [shifted(): lax.ppermute(value, axis, [(source, source + steps) for source in range(l...]
    ppermute x10 -> x6, waiting for transfers between devices: 9.31 us -> 13.9 us  [shifted(): lax.ppermute(value, axis, [(source, source + steps) for source in range(l...]
    unnamed x20 -> x15, local copies, waits for them, and re-layouts: 1.29 us -> 2.26 us
    concatenate x0 -> x1, local copies, waits for them, and re-layouts: none -> 0.92 us  [on_device(): packed = jnp.concatenate([key_proj, value_proj], axis=1)]
  transfers between devices with their start and end apart: 10 -> 6, of which waited for: 3 -> 3; matrix products, arithmetic and copies ran while one was open for 2% -> 3% of each run, Pallas kernels for 0% -> 0%
where the time goes in v2:
time: 46.4 us; the launch traced here: 46.1 us
  starting transfers between devices  16.1 us (35%)
  waiting for transfers between devices  13.9 us (30%)
  Pallas kernels  11.5 us (25%)
  local copies, waits for them, and re-layouts  4.46 us (10%)
    ppermute x6, starting transfers between devices, shifted(): lax.ppermute(value, axis, [(source, source + steps) for source in range(l...  16.1 us
    ppermute x6, waiting for transfers between devices, shifted(): lax.ppermute(value, axis, [(source, source + steps) for source in range(l...  13.9 us
    pallas_call x1, Pallas kernels, on_device(): pl.pallas_call(attention_kernel, out_shape=(jax.ShapeDtypeStruct((rows, m...  6.59 us
    pallas_call x1, Pallas kernels, on_device(): pl.pallas_call(conv_kernel, out_shape=jax.ShapeDtypeStruct((rows, model_w...  4.91 us
    unnamed x15, local copies, waits for them, and re-layouts  2.26 us
  transfers between devices with their start and end apart: 6, of which 3 were waited for; matrix products, arithmetic and copies ran while one was open for 3% of the time, Pallas kernels for 0%

profile of v2, /device:TPU:21, one launch (start us, length us, event | category | flops | bytes accessed | tf_op | source)
XLA Modules:
  0.0 46.1 jit_solution(9514222281314815948)
XLA Ops:
  0.0 0.9 %constant_dynamic-update-slice_fusion.1 = bf16[128,1024]{1,0:T(8,128)(2,1)S(1)} fusion(bf16[128,512]{1,0:T(8,128)(2,1)} %param.15), kind=kLoop, calls=%fused_computation.1 | loop fusion | bytes 262144
  0.9 0.9 %constant_dynamic-update-slice_fusion.kv2 = bf16[128,1024]{1,0:T(8,128)(2,1)S(1)} fusion(bf16[128,1024]{1,0:T(8,128)(2,1)S(1)} %constant_dynamic-update-slice_fusion.1, bf16[128,512]{1,0:T(8,128)(2,1)} %param.16), kind=kLoop, calls=%fused_computation | loop fusion | bytes 262144 | tf_op jit(solution)/shard_map/concatenate | solution.py:175
  1.8 0.0 copy-start
  1.8 2.1 %collective-permute-start.3 = (bf16[128,1024]{1,0:T(8,128)(2,1)S(1)}, bf16[128,1024]{1,0:T(8,128)(2,1)S(1)}, u32[]{:S(2)}, u32[]{:S(2)}) collective-permute-start(bf16[128,1024]{1,0:T(8,128)(2,1)S(1)} %constant_dynamic-update-slice_fusion.kv2), channel_id=1, source_target_pairs={{2,0},{3,1},{4,2},{5,3},{6,4},{7,5},{8,6},{9,7},{10,8},{11,9},{12,... | collective-permute-start | bytes 786440 | tf_op jit(solution)/shard_map/ppermute | solution.py:20
  4.0 2.9 %collective-permute-start.2 = (bf16[128,1024]{1,0:T(8,128)(2,1)S(1)}, bf16[128,1024]{1,0:T(8,128)(2,1)S(1)}, u32[]{:S(2)}, u32[]{:S(2)}) collective-permute-start(bf16[128,1024]{1,0:T(8,128)(2,1)S(1)} %constant_dynamic-update-slice_fusion.kv2), channel_id=1, source_target_pairs={{1,0},{2,1},{3,2},{4,3},{5,4},{6,5},{7,6},{8,7},{9,8},{10,9},{11,1... | collective-permute-start | bytes 786440 | tf_op jit(solution)/shard_map/ppermute | solution.py:20
  6.9 3.9 %collective-permute-start.1 = (bf16[128,1024]{1,0:T(8,128)(2,1)S(1)}, bf16[128,1024]{1,0:T(8,128)(2,1)S(1)}, u32[]{:S(2)}, u32[]{:S(2)}) collective-permute-start(bf16[128,1024]{1,0:T(8,128)(2,1)S(1)} %constant_dynamic-update-slice_fusion.kv2), channel_id=1, source_target_pairs={{0,1},{1,2},{2,3},{3,4},{4,5},{5,6},{6,7},{7,8},{8,9},{9,10},{10,1... | collective-permute-start | bytes 786440 | tf_op jit(solution)/shard_map/ppermute | solution.py:20
  10.8 2.8 %collective-permute-start = (bf16[128,1024]{1,0:T(8,128)(2,1)S(1)}, bf16[128,1024]{1,0:T(8,128)(2,1)S(1)}, u32[]{:S(2)}, u32[]{:S(2)}) collective-permute-start(bf16[128,1024]{1,0:T(8,128)(2,1)S(1)} %constant_dynamic-update-slice_fusion.kv2), channel_id=1, source_target_pairs={{0,2},{1,3},{2,4},{3,5},{4,6},{5,7},{6,8},{7,9},{8,10},{9,11},{10,... | collective-permute-start | bytes 786440 | tf_op jit(solution)/shard_map/ppermute | solution.py:20
  13.6 0.7 %pad.4 = s32[768]{0:T(1024)S(1)} pad(s32[767]{0:T(1024)} %param.18, s32[]{:T(128)} %constant.2.clone.1), padding=0_1 | pad | bytes 6144 | tf_op jit(solution)/shard_map/jit(_pad)/pad | solution.py:172
  14.3 0.6 %reshape.13.table_ref = s32[1,768]{1,0:T(1,128)} reshape(s32[768]{0:T(1024)S(1)} %pad.4) | data formatting | bytes 6144 | tf_op jit(solution)/shard_map/reshape | solution.py:172
  14.9 0.0 collective-permute-done.3.kv4
  14.9 0.0 copy-start.1
  14.9 0.7 %collective-permute-done.2.kv3 = bf16[128,1024]{1,0:T(8,128)(2,1)S(1)} collective-permute-done((bf16[128,1024]{1,0:T(8,128)(2,1)S(1)}, bf16[128,1024]{1,0:T(8,128)(2,1)S(1)}, u32[]{:S(2)}, u32[]{:S(2)}) %collective-permute-start.2) | collective-permute-done | bytes 262176 | tf_op jit(solution)/shard_map/ppermute | solution.py:20
  15.6 0.0 copy-start.2
  15.6 0.0 collective-permute-done.1.kv1
  15.6 0.0 copy-start.3
  15.6 8.3 %collective-permute-done.kv0 = bf16[128,1024]{1,0:T(8,128)(2,1)S(1)} collective-permute-done((bf16[128,1024]{1,0:T(8,128)(2,1)S(1)}, bf16[128,1024]{1,0:T(8,128)(2,1)S(1)}, u32[]{:S(2)}, u32[]{:S(2)}) %collective-permute-start) | collective-permute-done | bytes 262176 | tf_op jit(solution)/shard_map/ppermute | solution.py:20
  23.9 0.0 copy-start.4
  23.9 0.0 copy-done
  23.9 0.0 copy-done.1
  23.9 0.0 copy-done.2
  23.9 0.0 copy-done.3
  23.9 0.7 %copy-done.4 = bf16[128,1024]{1,0:T(8,128)(2,1)} copy-done((bf16[128,1024]{1,0:T(8,128)(2,1)}, bf16[128,1024]{1,0:T(8,128)(2,1)S(1)}, u32[]{:S(2)}) %copy-start.4) | copy-done | bytes 262168
  24.6 6.6 %attention_glu.1 = (bf16[128,1024]{1,0:T(8,128)(2,1)}, bf16[64,1024]{1,0:T(8,128)(2,1)}, bf16[64,1024]{1,0:T(8,128)(2,1)}) custom-call(s32[1]{0:T(128)} %bitcast.meta_ref, s32[16]{0:T(128)} %len_ref.1, s32[1,768]{1,0:T(1,128)} %reshape.13.table_ref, f32[8,32]{1,0:T(8,128)} %bitcast.4, bf16[128,512]{1,0:T(8,128)(2,1)} %q_ref.1, bf16[128,1024]{1,0:T(8,128)(2,1)} %copy-done.4, ...), custom_call_target="tpu_custom_call" | custom-call | flops 1006632960 | bytes 7208960 | tf_op jit(solution)/shard_map/attention_glu/pallas_call | solution.py:190
  31.2 1.9 %collective-permute-start.4 = (bf16[64,1024]{1,0:T(8,128)(2,1)}, bf16[64,1024]{1,0:T(8,128)(2,1)S(1)}, u32[]{:S(2)}, u32[]{:S(2)}) collective-permute-start(bf16[64,1024]{1,0:T(8,128)(2,1)} %get-tuple-element.8.tail_ref), channel_id=1, source_target_pairs={{0,1},{1,2},{2,3},{3,4},{4,5},{5,6},{6,7},{7,8},{8,9},{9,10},{10,1... | collective-permute-start | bytes 393224 | tf_op jit(solution)/shard_map/ppermute | solution.py:20
  33.1 2.4 %collective-permute-start.5 = (bf16[64,1024]{1,0:T(8,128)(2,1)}, bf16[64,1024]{1,0:T(8,128)(2,1)S(1)}, u32[]{:S(2)}, u32[]{:S(2)}) collective-permute-start(bf16[64,1024]{1,0:T(8,128)(2,1)} %get-tuple-element.9.head_ref), channel_id=1, source_target_pairs={{1,0},{2,1},{3,2},{4,3},{5,4},{6,5},{7,6},{8,7},{9,8},{10,9},{11,1... | collective-permute-start | bytes 393224 | tf_op jit(solution)/shard_map/ppermute | solution.py:20
  35.6 0.0 collective-permute-done.4.prev_ref
  35.6 0.0 copy-start.5
  35.6 5.0 %collective-permute-done.5.next_ref = bf16[64,1024]{1,0:T(8,128)(2,1)S(1)} collective-permute-done((bf16[64,1024]{1,0:T(8,128)(2,1)}, bf16[64,1024]{1,0:T(8,128)(2,1)S(1)}, u32[]{:S(2)}, u32[]{:S(2)}) %collective-permute-start.5) | collective-permute-done | bytes 131104 | tf_op jit(solution)/shard_map/ppermute | solution.py:20
  40.5 0.0 copy-start.6
  40.5 0.0 copy-done.5
  40.5 0.6 %copy-done.6 = bf16[64,1024]{1,0:T(8,128)(2,1)} copy-done((bf16[64,1024]{1,0:T(8,128)(2,1)}, bf16[64,1024]{1,0:T(8,128)(2,1)S(1)}, u32[]{:S(2)}) %copy-start.6) | copy-done | bytes 131096
  41.2 4.9 %conv_shrink.1 = bf16[128,1024]{1,0:T(8,128)(2,1)} custom-call(bf16[64,1024]{1,0:T(8,128)(2,1)} %copy-done.5, bf16[64,1024]{1,0:T(8,128)(2,1)} %get-tuple-element.9.head_ref, bf16[64,1024]{1,0:T(8,128)(2,1)} %get-tuple-element.8.tail_ref, bf16[64,1024]{1,0:T(8,128)(2,1)} %copy-done.6, f32[31,1024]{1,0:T(8,128)} %taps_ref.1, f32[1,1024]{1,0:T(1,128)} %bitcast.6, ...), custom_call_target="tpu_custom_call" | custom-call | flops 276561920 | bytes 3272704 | tf_op jit(solution)/shard_map/conv_shrink/pallas_call | solution.py:218
Async XLA Ops:
  1.8 22.1 %copy-start = (bf16[128,1024]{1,0:T(8,128)(2,1)}, bf16[128,1024]{1,0:T(8,128)(2,1)S(1)}, u32[]{:S(2)}) copy-start(bf16[128,1024]{1,0:T(8,128)(2,1)S(1)} %constant_dynamic-update-slice_fusion.kv2) | copy-start | bytes 786436
  1.8 13.1 %collective-permute-start.3 = (bf16[128,1024]{1,0:T(8,128)(2,1)S(1)}, bf16[128,1024]{1,0:T(8,128)(2,1)S(1)}, u32[]{:S(2)}, u32[]{:S(2)}) collective-permute-start(bf16[128,1024]{1,0:T(8,128)(2,1)S(1)} %constant_dynamic-update-slice_fusion.kv2), channel_id=1, source_target_pairs={{2,0},{3,1},{4,2},{5,3},{6,4},{7,5},{8,6},{9,7},{10,8},{11,9},{12,... | collective-permute-start | bytes 786440 | tf_op jit(solution)/shard_map/ppermute | solution.py:20
  4.0 11.6 %collective-permute-start.2 = (bf16[128,1024]{1,0:T(8,128)(2,1)S(1)}, bf16[128,1024]{1,0:T(8,128)(2,1)S(1)}, u32[]{:S(2)}, u32[]{:S(2)}) collective-permute-start(bf16[128,1024]{1,0:T(8,128)(2,1)S(1)} %constant_dynamic-update-slice_fusion.kv2), channel_id=1, source_target_pairs={{1,0},{2,1},{3,2},{4,3},{5,4},{6,5},{7,6},{8,7},{9,8},{10,9},{11,1... | collective-permute-start | bytes 786440 | tf_op jit(solution)/shard_map/ppermute | solution.py:20
  6.9 8.7 %collective-permute-start.1 = (bf16[128,1024]{1,0:T(8,128)(2,1)S(1)}, bf16[128,1024]{1,0:T(8,128)(2,1)S(1)}, u32[]{:S(2)}, u32[]{:S(2)}) collective-permute-start(bf16[128,1024]{1,0:T(8,128)(2,1)S(1)} %constant_dynamic-update-slice_fusion.kv2), channel_id=1, source_target_pairs={{0,1},{1,2},{2,3},{3,4},{4,5},{5,6},{6,7},{7,8},{8,9},{9,10},{10,1... | collective-permute-start | bytes 786440 | tf_op jit(solution)/shard_map/ppermute | solution.py:20
  10.8 13.1 %collective-permute-start = (bf16[128,1024]{1,0:T(8,128)(2,1)S(1)}, bf16[128,1024]{1,0:T(8,128)(2,1)S(1)}, u32[]{:S(2)}, u32[]{:S(2)}) collective-permute-start(bf16[128,1024]{1,0:T(8,128)(2,1)S(1)} %constant_dynamic-update-slice_fusion.kv2), channel_id=1, source_target_pairs={{0,2},{1,3},{2,4},{3,5},{4,6},{5,7},{6,8},{7,9},{8,10},{9,11},{10,... | collective-permute-start | bytes 786440 | tf_op jit(solution)/shard_map/ppermute | solution.py:20
  14.9 9.0 %copy-start.1 = (bf16[128,1024]{1,0:T(8,128)(2,1)}, bf16[128,1024]{1,0:T(8,128)(2,1)S(1)}, u32[]{:S(2)}) copy-start(bf16[128,1024]{1,0:T(8,128)(2,1)S(1)} %collective-permute-done.3.kv4) | copy-start | bytes 786436
  15.6 8.3 %copy-start.2 = (bf16[128,1024]{1,0:T(8,128)(2,1)}, bf16[128,1024]{1,0:T(8,128)(2,1)S(1)}, u32[]{:S(2)}) copy-start(bf16[128,1024]{1,0:T(8,128)(2,1)S(1)} %collective-permute-done.2.kv3) | copy-start | bytes 786436
  15.6 8.3 %copy-start.3 = (bf16[128,1024]{1,0:T(8,128)(2,1)}, bf16[128,1024]{1,0:T(8,128)(2,1)S(1)}, u32[]{:S(2)}) copy-start(bf16[128,1024]{1,0:T(8,128)(2,1)S(1)} %collective-permute-done.1.kv1) | copy-start | bytes 786436
  23.9 0.7 %copy-start.4 = (bf16[128,1024]{1,0:T(8,128)(2,1)}, bf16[128,1024]{1,0:T(8,128)(2,1)S(1)}, u32[]{:S(2)}) copy-start(bf16[128,1024]{1,0:T(8,128)(2,1)S(1)} %collective-permute-done.kv0) | copy-start | bytes 786436
  31.2 4.3 %collective-permute-start.4 = (bf16[64,1024]{1,0:T(8,128)(2,1)}, bf16[64,1024]{1,0:T(8,128)(2,1)S(1)}, u32[]{:S(2)}, u32[]{:S(2)}) collective-permute-start(bf16[64,1024]{1,0:T(8,128)(2,1)} %get-tuple-element.8.tail_ref), channel_id=1, source_target_pairs={{0,1},{1,2},{2,3},{3,4},{4,5},{5,6},{6,7},{7,8},{8,9},{9,10},{10,1... | collective-permute-start | bytes 393224 | tf_op jit(solution)/shard_map/ppermute | solution.py:20
  33.1 7.4 %collective-permute-start.5 = (bf16[64,1024]{1,0:T(8,128)(2,1)}, bf16[64,1024]{1,0:T(8,128)(2,1)S(1)}, u32[]{:S(2)}, u32[]{:S(2)}) collective-permute-start(bf16[64,1024]{1,0:T(8,128)(2,1)} %get-tuple-element.9.head_ref), channel_id=1, source_target_pairs={{1,0},{2,1},{3,2},{4,3},{5,4},{6,5},{7,6},{8,7},{9,8},{10,9},{11,1... | collective-permute-start | bytes 393224 | tf_op jit(solution)/shard_map/ppermute | solution.py:20
  35.6 5.0 %copy-start.5 = (bf16[64,1024]{1,0:T(8,128)(2,1)}, bf16[64,1024]{1,0:T(8,128)(2,1)S(1)}, u32[]{:S(2)}) copy-start(bf16[64,1024]{1,0:T(8,128)(2,1)S(1)} %collective-permute-done.4.prev_ref) | copy-start | bytes 393220
  40.5 0.6 %copy-start.6 = (bf16[64,1024]{1,0:T(8,128)(2,1)}, bf16[64,1024]{1,0:T(8,128)(2,1)S(1)}, u32[]{:S(2)}) copy-start(bf16[64,1024]{1,0:T(8,128)(2,1)S(1)} %collective-permute-done.5.next_ref) | copy-start | bytes 393220

commit v3 on v2

--- a/solution.py
+++ b/solution.py
@@ -33,24 +33,34 @@
 
 def attention_kernel(
     meta_ref, len_ref, table_ref, bias_t_ref, q_ref,
-    kv0, kv1, kv2, kv3, kv4,
+    pair_hbm, far_hbm,
     x_ref, gain_ref, ow_hbm, ew_hbm,
-    mid_ref, head_ref, tail_ref,
-    ow_vmem, ew_vmem, sems, att_ref,
+    mid_ref, gated_ref, cross_ref, partner_ref,
+    ow_vmem, ew_vmem, sems, att_ref, win_ref,
 ):
+    rows, att_width = q_ref.shape
+    chip_rows = pair_hbm.shape[0]
+    side = far_hbm.shape[0] // 2
+    copies = [
+        pltpu.make_async_copy(far_hbm.at[0:side], win_ref.at[0:side], sems.at[2]),
+        pltpu.make_async_copy(pair_hbm, win_ref.at[side:side + chip_rows], sems.at[3]),
+        pltpu.make_async_copy(far_hbm.at[side:2 * side], win_ref.at[side + chip_rows:2 * side + chip_rows], sems.at[4]),
+    ]
+    for copy in copies:
+        copy.start()
     ow_copy = pltpu.make_async_copy(ow_hbm, ow_vmem, sems.at[0])
     ew_copy = pltpu.make_async_copy(ew_hbm, ew_vmem, sems.at[1])
     ow_copy.start()
     ew_copy.start()
-    kv_refs = (kv0, kv1, kv2, kv3, kv4)
-    rows, att_width = q_ref.shape
     heads = bias_t_ref.shape[0]
     buckets = bias_t_ref.shape[1]
     head_width = att_width // heads
-    width = len(kv_refs) * rows
+    width = (2 * REACH + 1) * rows
     line_len = table_ref.shape[1]
 
     base = meta_ref[0]
+    core = meta_ref[1]
+    first_row = pl.multiple_of(core * rows, rows)
     qpos = base + lax.broadcasted_iota(jnp.int32, (rows, 1), 0)
     kpos = base - REACH * rows + lax.broadcasted_iota(jnp.int32, (1, width), 1)
 
@@ -72,6 +82,8 @@
     for b in range(buckets):
         line = jnp.where(table == b, bias_t[:, b:b + 1], line)
 
+    for copy in copies:
+        copy.wait()
     scaling = head_width ** (-0.5)
     lane = lax.broadcasted_iota(jnp.int32, (rows, LANES), 1)
     per_pair = LANES // head_width
@@ -79,8 +91,8 @@
         cols = slice(pair * LANES, (pair + 1) * LANES)
         q_pair = q_ref[:, cols]
         v_cols = slice(att_width + pair * LANES, att_width + (pair + 1) * LANES)
-        k_pair = jnp.concatenate([r[:, cols] for r in kv_refs], axis=0)
-        v_pair = jnp.concatenate([r[:, v_cols] for r in kv_refs], axis=0)
+        k_pair = win_ref[pl.ds(first_row, width), cols]
+        v_pair = win_ref[pl.ds(first_row, width), v_cols]
         result = None
         for sub in range(per_pair):
             head = pair * per_pair + sub
@@ -111,23 +123,25 @@
     value_half = jnp.dot(normed, ew_vmem[:, :model_width], preferred_element_type=jnp.float32)
     gate_half = jnp.dot(normed, ew_vmem[:, model_width:], preferred_element_type=jnp.float32)
     gated = (value_half * sigmoid(gate_half)).astype(jnp.bfloat16)
-    half = head_ref.shape[0]
-    head_ref[...] = gated[:half]
-    tail_ref[...] = gated[half:]
+    gated_ref[...] = gated
+    half = cross_ref.shape[0]
+    cross_ref[...] = gated_ref[pl.ds(pl.multiple_of(core * half, half), half), :]
+    partner_ref[...] = gated_ref[pl.ds(pl.multiple_of((1 - core) * half, half), half), :]
 
 
 def conv_kernel(
-    prev_ref, head_ref, tail_ref, next_ref, taps_ref, gain_ref, mid_ref, sw_hbm,
+    meta_ref, gated_ref, cross_ref, pairg_ref, taps_ref, gain_ref, mid_ref, sw_hbm,
     out_ref, win_ref, conv_ref, sw_vmem, sems,
 ):
     sw_copy = pltpu.make_async_copy(sw_hbm, sw_vmem, sems.at[0])
     sw_copy.start()
-    half = head_ref.shape[0]
+    half = cross_ref.shape[0]
     rows, model_width = mid_ref.shape
-    win_ref[0:half, :] = prev_ref[...].astype(jnp.float32)
-    win_ref[half:2 * half, :] = head_ref[...].astype(jnp.float32)
-    win_ref[2 * half:3 * half, :] = tail_ref[...].astype(jnp.float32)
-    win_ref[3 * half:4 * half, :] = next_ref[...].astype(jnp.float32)
+    first_core = meta_ref[1] == 0
+    cross = cross_ref[...]
+    win_ref[0:half, :] = jnp.where(first_core, cross, pairg_ref[0:half, :]).astype(jnp.float32)
+    win_ref[half:half + rows, :] = gated_ref[...].astype(jnp.float32)
+    win_ref[half + rows:2 * half + rows, :] = jnp.where(first_core, pairg_ref[half:2 * half, :], cross).astype(jnp.float32)
     reach = DILATION * (KERNEL - 1) // 2
     start = half - reach
 
@@ -166,19 +180,21 @@
     rows, att_width = query_proj.shape
     model_width = frames_in.shape[1]
     heads = bucket_bias.shape[1]
-    device_index = lax.axis_index("seq")
-    meta = (device_index * rows).astype(jnp.int32).reshape(1)
+    chip = lax.axis_index("chip")
+    core = lax.axis_index("core")
+    chips = lax.axis_size("chip")
+    cores = lax.axis_size("core")
+    meta = jnp.stack([(chip * cores + core) * rows, core]).astype(jnp.int32)
     line_len = -(-bucket_table.shape[0] // LANES) * LANES
     table = jnp.pad(bucket_table, (0, line_len - bucket_table.shape[0])).reshape(1, line_len)
     bias_t = bucket_bias.T
 
     packed = jnp.concatenate([key_proj, value_proj], axis=1)
-    received = {0: packed}
-    for hop in range(REACH, 0, -1):
-        received[hop] = shifted(packed, "seq", -hop)
-        received[-hop] = shifted(packed, "seq", hop)
+    pair = lax.all_gather(packed, "core", tiled=True)
+    outward = [(2 * (c - 1), 2 * c) for c in range(1, chips)] + [(2 * (c + 1) + 1, 2 * c + 1) for c in range(chips - 1)]
+    far = lax.ppermute(pair, ("chip", "core"), outward)
+    far = lax.all_gather(far, "core", tiled=True)
     order = list(range(-REACH, REACH + 1))
-    kv_blocks = [received[h] for h in order]
 
     half = rows // 2
     vmem = pl.BlockSpec(memory_space=pltpu.VMEM)
@@ -187,41 +203,44 @@
     window = len(order) * rows
     attn_flops = 2 * 2 * heads * rows * window * LANES + 2 * rows * att_width * model_width + 2 * rows * model_width * 2 * model_width
     attn_bytes = 2 * (rows * att_width * (1 + 2 * len(order)) + rows * model_width * 2 + att_width * model_width + model_width * 2 * model_width)
-    mid, g_head, g_tail = pl.pallas_call(
+    mid, gated, cross_send, partner_send = pl.pallas_call(
         attention_kernel,
         out_shape=(
             jax.ShapeDtypeStruct((rows, model_width), jnp.bfloat16),
+            jax.ShapeDtypeStruct((rows, model_width), jnp.bfloat16),
             jax.ShapeDtypeStruct((half, model_width), jnp.bfloat16),
-            jax.ShapeDtypeStruct((rows - half, model_width), jnp.bfloat16),
+            jax.ShapeDtypeStruct((half, model_width), jnp.bfloat16),
         ),
-        in_specs=[smem, smem] + [vmem] * (3 + len(order)) + [vmem, vmem, anywhere, anywhere],
-        out_specs=(vmem, vmem, vmem),
+        in_specs=[smem, smem, vmem, vmem, vmem, anywhere, anywhere, vmem, vmem, anywhere, anywhere],
+        out_specs=(vmem, vmem, vmem, vmem),
         scratch_shapes=[
             pltpu.VMEM((att_width, model_width), jnp.bfloat16),
             pltpu.VMEM((model_width, 2 * model_width), jnp.bfloat16),
-            pltpu.SemaphoreType.DMA((2,)),
+            pltpu.SemaphoreType.DMA((5,)),
             pltpu.VMEM((rows, att_width), jnp.bfloat16),
+            pltpu.VMEM((pair.shape[0] + far.shape[0], 2 * att_width), jnp.bfloat16),
         ],
         cost_estimate=pl.CostEstimate(
             flops=attn_flops, transcendentals=heads * rows * window + rows * model_width, bytes_accessed=attn_bytes
         ),
         name="attention_glu",
     )(
-        meta, utterance_lengths, table, bias_t, query_proj, *kv_blocks,
+        meta, utterance_lengths, table, bias_t, query_proj, pair, far,
         frames_in, norm_gain.reshape(1, -1), out_weight, expand_weight,
     )
 
-    prev_tail = shifted(g_tail, "seq", 1)
-    next_head = shifted(g_head, "seq", -1)
+    inward = [(2 * c + 1, 2 * c + 2) for c in range(chips - 1)] + [(2 * c, 2 * c - 1) for c in range(1, chips)]
+    cross_recv = lax.ppermute(cross_send, ("chip", "core"), inward)
+    partner_recv = lax.all_gather(partner_send, "core", tiled=True)
     conv_flops = 2 * KERNEL * rows * model_width + 2 * rows * model_width * model_width
     conv_bytes = 2 * (4 * half * model_width + rows * model_width * 2 + model_width * model_width) + 4 * KERNEL * model_width
     return pl.pallas_call(
         conv_kernel,
         out_shape=jax.ShapeDtypeStruct((rows, model_width), jnp.bfloat16),
-        in_specs=[vmem] * 7 + [anywhere],
+        in_specs=[smem] + [vmem] * 6 + [anywhere],
         out_specs=vmem,
         scratch_shapes=[
-            pltpu.VMEM((4 * half, model_width), jnp.float32),
+            pltpu.VMEM((rows + 2 * half, model_width), jnp.float32),
             pltpu.VMEM((rows, model_width), jnp.float32),
             pltpu.VMEM((model_width, model_width), jnp.bfloat16),
             pltpu.SemaphoreType.DMA((1,)),
@@ -230,15 +249,18 @@
             flops=conv_flops, transcendentals=rows * model_width, bytes_accessed=conv_bytes
         ),
         name="conv_shrink",
-    )(prev_tail, g_head, g_tail, next_head, depth_taps, inner_gain.reshape(1, -1), mid, shrink_weight)
+    )(meta, gated, cross_recv, partner_recv, depth_taps, inner_gain.reshape(1, -1), mid, shrink_weight)
 
 
 def solution(mesh):
+    groups, seq = mesh.devices.shape
+    chip_mesh = jax.sharding.Mesh(mesh.devices.reshape(groups, seq // 2, 2), ("groups", "chip", "core"))
+    rows_spec = P(("groups", "chip", "core"), None)
     placed = (
-        P(("groups", "seq"), None),
-        P(("groups", "seq"), None),
-        P(("groups", "seq"), None),
-        P(("groups", "seq"), None),
+        rows_spec,
+        rows_spec,
+        rows_spec,
+        rows_spec,
         P("groups"),
         P(),
         P(),
@@ -250,5 +272,5 @@
         P(),
     )
     return jax.shard_map(
-        on_device, mesh=mesh, in_specs=placed, out_specs=P(("groups", "seq"), None), check_vma=False
-    )
+        on_device, mesh=chip_mesh, in_specs=placed, out_specs=rows_spec, check_vma=False
+    )

time: 46.4 us -> 65.3 us (1.41); the launches traced: 46.1 us -> 64.3 us
  between operations: 0.11 us -> 13.5 us
  starting transfers between devices: 16.1 us -> 5.31 us
  waiting for transfers between devices: 13.9 us -> 22.9 us
  blocking collectives: 0 us -> 6.03 us
  local copies, waits for them, and re-layouts: 4.46 us -> 2.72 us
  other arithmetic: 0 us -> 1.65 us
  Pallas kernels: 11.5 us -> 12.2 us
    ppermute x6 -> x2, starting transfers between devices: 16.1 us -> 5.31 us  [the longest x1 3.19 us: on_device(): cross_recv = lax.ppermute(cross_send, ('chip', 'core'), inward)]
    all_gather x0 -> x1, waiting for transfers between devices: none -> 10.5 us  [on_device(): far = lax.all_gather(far, 'core', tiled=True)]
    all_gather x0 -> x2, blocking collectives: none -> 6.03 us  [the longest x1 3.55 us: on_device(): partner_recv = lax.all_gather(partner_send, 'core', tiled=True)]
    ppermute x6 -> x2, waiting for transfers between devices: 13.9 us -> 12.4 us  [the longest x1 11.7 us: on_device(): far = lax.ppermute(pair, ('chip', 'core'), outward)]
    concatenate x0 -> x1, other arithmetic: none -> 0.99 us  [on_device(): packed = jnp.concatenate([key_proj, value_proj], axis=1)]
    concatenate x1 -> x0, local copies, waits for them, and re-layouts: 0.92 us -> none  [on_device(): packed = jnp.concatenate([key_proj, value_proj], axis=1)]
    unnamed x15 -> x6, local copies, waits for them, and re-layouts: 2.26 us -> 1.44 us
    pallas_call x1, Pallas kernels: 6.59 us -> 7.29 us  [on_device(): pl.pallas_call(attention_kernel, out_shape=(jax.ShapeDtypeStruct((rows, m...]
  transfers between devices with their start and end apart: 6 -> 3, of which waited for: 3 -> 3; matrix products, arithmetic and copies ran while one was open for 3% -> 3% of each run, Pallas kernels for 0% -> 0%
where the time goes in v3:
time: 65.3 us; the launch traced here: 64.3 us
  waiting for transfers between devices  22.9 us (35%)
  between operations  13.5 us (21%)
  Pallas kernels  12.2 us (19%)
  blocking collectives  6.03 us (9%)
  starting transfers between devices  5.31 us (8%)
  local copies, waits for them, and re-layouts  2.72 us (4%)
  other arithmetic  1.65 us (3%)
    ppermute x1, waiting for transfers between devices, on_device(): far = lax.ppermute(pair, ('chip', 'core'), outward)  11.7 us
    all_gather x1, waiting for transfers between devices, on_device(): far = lax.all_gather(far, 'core', tiled=True)  10.5 us
    pallas_call x1, Pallas kernels, on_device(): pl.pallas_call(attention_kernel, out_shape=(jax.ShapeDtypeStruct((rows, m...  7.29 us
    pallas_call x1, Pallas kernels, on_device(): pl.pallas_call(conv_kernel, out_shape=jax.ShapeDtypeStruct((rows, model_w...  4.92 us
    all_gather x1, blocking collectives, on_device(): partner_recv = lax.all_gather(partner_send, 'core', tiled=True)  3.55 us
    ppermute x1, starting transfers between devices, on_device(): cross_recv = lax.ppermute(cross_send, ('chip', 'core'), inward)  3.19 us
    all_gather x1, blocking collectives, on_device(): pair = lax.all_gather(packed, 'core', tiled=True)  2.48 us
    ppermute x1, starting transfers between devices, on_device(): far = lax.ppermute(pair, ('chip', 'core'), outward)  2.12 us
  transfers between devices with their start and end apart: 3, of which 3 were waited for; matrix products, arithmetic and copies ran while one was open for 3% of the time, Pallas kernels for 0%

profile of v3, /device:TPU:21, one launch (start us, length us, event | category | flops | bytes accessed | tf_op | source)
XLA Modules:
  0.0 64.3 jit_solution(11477187436718616099)
XLA Ops:
  6.5 0.0 all-gather.2.cloned.1.call-start
  6.5 1.0 %pad_maximum_fusion = bf16[128,1024]{1,0:T(8,128)(2,1)S(1)} fusion(bf16[128,512]{1,0:T(8,128)(2,1)} %param.16, bf16[128,512]{1,0:T(8,128)(2,1)} %param.15), kind=kLoop, calls=%fused_computation | loop fusion | flops 524288 | bytes 524288 | tf_op jit(solution)/shard_map/concatenate | solution.py:192
  7.5 2.5 %all_gather.9.pair_hbm = bf16[256,1024]{1,0:T(8,128)(2,1)S(1)} all-gather(bf16[128,1024]{1,0:T(8,128)(2,1)S(1)} %pad_maximum_fusion), channel_id=1, replica_groups=mesh['groups'=2,'chip'=8,'core'=2] {'core'}, dimensions={0}, use_global_device_ids=true | all-gather | bytes 786432 | tf_op jit(solution)/shard_map/all_gather | solution.py:193
  10.0 0.0 copy-start
  10.0 2.1 %collective-permute-start = (bf16[256,1024]{1,0:T(8,128)(2,1)S(1)}, bf16[256,1024]{1,0:T(8,128)(2,1)S(1)}, u32[]{:S(2)}, u32[]{:S(2)}) collective-permute-start(bf16[256,1024]{1,0:T(8,128)(2,1)S(1)} %all_gather.9.pair_hbm), channel_id=1, source_target_pairs={{0,2},{2,4},{4,6},{6,8},{8,10},{10,12},{12,14},{3,1},{5,3},{7,5},{... | collective-permute-start | bytes 1572872 | tf_op jit(solution)/shard_map/ppermute | solution.py:195
  12.1 11.7 %collective-permute-done = bf16[256,1024]{1,0:T(8,128)(2,1)S(1)} collective-permute-done((bf16[256,1024]{1,0:T(8,128)(2,1)S(1)}, bf16[256,1024]{1,0:T(8,128)(2,1)S(1)}, u32[]{:S(2)}, u32[]{:S(2)}) %collective-permute-start) | collective-permute-done | bytes 524320 | tf_op jit(solution)/shard_map/ppermute | solution.py:195
  23.9 0.0 copy-start.1
  23.9 0.8 %copy-done.1 = bf16[256,1024]{1,0:T(8,128)(2,1)} copy-done((bf16[256,1024]{1,0:T(8,128)(2,1)}, bf16[256,1024]{1,0:T(8,128)(2,1)S(1)}, u32[]{:S(2)}) %copy-start.1) | copy-done | bytes 524312
  24.7 0.0 all-gather.2.cloned.1.call-update
  24.7 0.7 %pad.4 = s32[768]{0:T(1024)S(1)} pad(s32[767]{0:T(1024)} %param.18, s32[]{:T(128)} %constant.13.clone.1), padding=0_1 | pad | bytes 6144 | tf_op jit(solution)/shard_map/jit(_pad)/pad | solution.py:189
  25.4 0.6 reshape.9.table_ref
  26.0 0.7 %pad_add_fusion.meta_ref = s32[2]{0:T(128)} fusion(s32[1]{0:T(128)} %bitcast.1, s32[1]{0:T(128)} %bitcast), kind=kLoop, calls=%fused_computation.1 | loop fusion | flops 2 | bytes 16 | tf_op jit(solution)/shard_map/stack | solution.py:187
  26.6 10.5 %all-gather.2.cloned.1.call-done.far_hbm = bf16[512,1024]{1,0:T(8,128)(2,1)} async-done(((bf16[256,1024]{1,0:T(8,128)(2,1)}), bf16[512,1024]{1,0:T(8,128)(2,1)}) %all-gather.2.cloned.1.call-update) | async-done | bytes 1048592 | tf_op jit(solution)/shard_map/all_gather | solution.py:196
  37.1 0.0 copy-done
  37.1 7.3 %attention_glu.1 = (bf16[128,1024]{1,0:T(8,128)(2,1)}, bf16[128,1024]{1,0:T(8,128)(2,1)}, bf16[64,1024]{1,0:T(8,128)(2,1)}, bf16[64,1024]{1,0:T(8,128)(2,1)}) custom-call(s32[2]{0:T(128)} %pad_add_fusion.meta_ref, s32[16]{0:T(128)} %len_ref.1, s32[1,768]{1,0:T(1,128)} %reshape.9.table_ref, f32[8,32]{1,0:T(8,128)} %bitcast.5, bf16[128,512]{1,0:T(8,128)(2,1)} %q_ref.1, ...), custom_call_target="tpu_custom_call" | custom-call | flops 1006632960 | bytes 7208960 | tf_op jit(solution)/shard_map/attention_glu/pallas_call | solution.py:206
  44.4 3.2 %collective-permute-start.1 = (bf16[64,1024]{1,0:T(8,128)(2,1)}, bf16[64,1024]{1,0:T(8,128)(2,1)S(1)}, u32[]{:S(2)}, u32[]{:S(2)}) collective-permute-start(bf16[64,1024]{1,0:T(8,128)(2,1)} %get-tuple-element.10), channel_id=1, source_target_pairs={{1,2},{3,4},{5,6},{7,8},{9,10},{11,12},{13,14},{2,1},{4,3},{6,5},{... | collective-permute-start | bytes 393224 | tf_op jit(solution)/shard_map/ppermute | solution.py:233
  47.6 3.5 %all_gather.11.pairg_ref = bf16[128,1024]{1,0:T(8,128)(2,1)} all-gather(bf16[64,1024]{1,0:T(8,128)(2,1)} %get-tuple-element.11), channel_id=1, replica_groups=mesh['groups'=2,'chip'=8,'core'=2] {'core'}, dimensions={0}, use_global_device_ids=true | all-gather | bytes 393216 | tf_op jit(solution)/shard_map/all_gather | solution.py:234
  51.2 0.7 %collective-permute-done.1.cross_ref = bf16[64,1024]{1,0:T(8,128)(2,1)S(1)} collective-permute-done((bf16[64,1024]{1,0:T(8,128)(2,1)}, bf16[64,1024]{1,0:T(8,128)(2,1)S(1)}, u32[]{:S(2)}, u32[]{:S(2)}) %collective-permute-start.1) | collective-permute-done | bytes 131104 | tf_op jit(solution)/shard_map/ppermute | solution.py:233
  51.9 0.0 copy-start.2
  51.9 0.6 copy-done.2
  52.5 4.9 %conv_shrink.1 = bf16[128,1024]{1,0:T(8,128)(2,1)} custom-call(s32[2]{0:T(128)} %pad_add_fusion.meta_ref, bf16[128,1024]{1,0:T(8,128)(2,1)} %get-tuple-element.9.gated_ref, bf16[64,1024]{1,0:T(8,128)(2,1)} %copy-done.2, bf16[128,1024]{1,0:T(8,128)(2,1)} %all_gather.11.pairg_ref, f32[31,1024]{1,0:T(8,128)} %taps_ref.1, f32[1,1024]{1,0:T(1,128)} %bitcast.7, ...), custom_call_target="tpu_custom_call" | custom-call | flops 276561920 | bytes 3272704 | tf_op jit(solution)/shard_map/conv_shrink/pallas_call | solution.py:237
Async XLA Ops:
  6.5 30.6 %all-gather.2.cloned.1.call-start = ((), (), s32[]{:S(2)}) async-start(), calls=%async_computation | async-start | bytes 1572864 | tf_op jit(solution)/shard_map/all_gather | solution.py:196
  10.0 27.1 %copy-start = (bf16[256,1024]{1,0:T(8,128)(2,1)}, bf16[256,1024]{1,0:T(8,128)(2,1)S(1)}, u32[]{:S(2)}) copy-start(bf16[256,1024]{1,0:T(8,128)(2,1)S(1)} %all_gather.9.pair_hbm) | copy-start | bytes 1572868
  10.0 13.9 %collective-permute-start = (bf16[256,1024]{1,0:T(8,128)(2,1)S(1)}, bf16[256,1024]{1,0:T(8,128)(2,1)S(1)}, u32[]{:S(2)}, u32[]{:S(2)}) collective-permute-start(bf16[256,1024]{1,0:T(8,128)(2,1)S(1)} %all_gather.9.pair_hbm), channel_id=1, source_target_pairs={{0,2},{2,4},{4,6},{6,8},{8,10},{10,12},{12,14},{3,1},{5,3},{7,5},{... | collective-permute-start | bytes 1572872 | tf_op jit(solution)/shard_map/ppermute | solution.py:195
  23.9 0.8 %copy-start.1 = (bf16[256,1024]{1,0:T(8,128)(2,1)}, bf16[256,1024]{1,0:T(8,128)(2,1)S(1)}, u32[]{:S(2)}) copy-start(bf16[256,1024]{1,0:T(8,128)(2,1)S(1)} %collective-permute-done) | copy-start | bytes 1572868
  44.4 7.4 %collective-permute-start.1 = (bf16[64,1024]{1,0:T(8,128)(2,1)}, bf16[64,1024]{1,0:T(8,128)(2,1)S(1)}, u32[]{:S(2)}, u32[]{:S(2)}) collective-permute-start(bf16[64,1024]{1,0:T(8,128)(2,1)} %get-tuple-element.10), channel_id=1, source_target_pairs={{1,2},{3,4},{5,6},{7,8},{9,10},{11,12},{13,14},{2,1},{4,3},{6,5},{... | collective-permute-start | bytes 393224 | tf_op jit(solution)/shard_map/ppermute | solution.py:233
  51.9 0.6 copy-start.2
Sparse Core Ops, SparseCore 0:
  24.8 12.2 all-gather.1

commit v4 on v2

--- a/solution.py
+++ b/solution.py
@@ -33,24 +33,41 @@
 
 def attention_kernel(
     meta_ref, len_ref, table_ref, bias_t_ref, q_ref,
-    kv0, kv1, kv2, kv3, kv4,
+    prev_hbm, next_hbm, own_hbm, sel_hbm,
     x_ref, gain_ref, ow_hbm, ew_hbm,
     mid_ref, head_ref, tail_ref,
-    ow_vmem, ew_vmem, sems, att_ref,
+    ow_vmem, ew_vmem, sems, att_ref, win_ref,
 ):
+    base = meta_ref[0]
+    core = meta_ref[1]
+    planes = prev_hbm.shape[0]
+    mine = pl.ds(pl.multiple_of(core * planes, planes), planes)
+    other = pl.ds(pl.multiple_of((1 - core) * planes, planes), planes)
+    copies = [
+        pltpu.make_async_copy(prev_hbm, win_ref.at[pl.ds(0, planes)], sems.at[2]),
+        pltpu.make_async_copy(own_hbm.at[mine], win_ref.at[pl.ds(2 * planes, planes)], sems.at[3]),
+        pltpu.make_async_copy(next_hbm, win_ref.at[pl.ds(4 * planes, planes)], sems.at[4]),
+        pltpu.make_async_copy(
+            sel_hbm.at[other], win_ref.at[pl.ds(pl.multiple_of((1 + 2 * core) * planes, planes), planes)], sems.at[5]
+        ),
+        pltpu.make_async_copy(
+            own_hbm.at[other], win_ref.at[pl.ds(pl.multiple_of((3 - 2 * core) * planes, planes), planes)], sems.at[6]
+        ),
+    ]
+    for copy in copies:
+        copy.start()
     ow_copy = pltpu.make_async_copy(ow_hbm, ow_vmem, sems.at[0])
     ew_copy = pltpu.make_async_copy(ew_hbm, ew_vmem, sems.at[1])
     ow_copy.start()
     ew_copy.start()
-    kv_refs = (kv0, kv1, kv2, kv3, kv4)
+    blocks = win_ref.shape[0] // planes
     rows, att_width = q_ref.shape
     heads = bias_t_ref.shape[0]
     buckets = bias_t_ref.shape[1]
     head_width = att_width // heads
-    width = len(kv_refs) * rows
+    width = blocks * rows
     line_len = table_ref.shape[1]
 
-    base = meta_ref[0]
     qpos = base + lax.broadcasted_iota(jnp.int32, (rows, 1), 0)
     kpos = base - REACH * rows + lax.broadcasted_iota(jnp.int32, (1, width), 1)
 
@@ -72,15 +89,16 @@
     for b in range(buckets):
         line = jnp.where(table == b, bias_t[:, b:b + 1], line)
 
+    for copy in copies:
+        copy.wait()
     scaling = head_width ** (-0.5)
     lane = lax.broadcasted_iota(jnp.int32, (rows, LANES), 1)
     per_pair = LANES // head_width
     for pair in range(att_width // LANES):
         cols = slice(pair * LANES, (pair + 1) * LANES)
         q_pair = q_ref[:, cols]
-        v_cols = slice(att_width + pair * LANES, att_width + (pair + 1) * LANES)
-        k_pair = jnp.concatenate([r[:, cols] for r in kv_refs], axis=0)
-        v_pair = jnp.concatenate([r[:, v_cols] for r in kv_refs], axis=0)
+        k_pair = jnp.concatenate([win_ref[planes * j, :, cols] for j in range(blocks)], axis=0)
+        v_pair = jnp.concatenate([win_ref[planes * j + 1, :, cols] for j in range(blocks)], axis=0)
         result = None
         for sub in range(per_pair):
             head = pair * per_pair + sub
@@ -166,19 +184,27 @@
     rows, att_width = query_proj.shape
     model_width = frames_in.shape[1]
     heads = bucket_bias.shape[1]
-    device_index = lax.axis_index("seq")
-    meta = (device_index * rows).astype(jnp.int32).reshape(1)
+    core = lax.axis_index("core")
+    cores = lax.axis_size("core")
+    count = lax.axis_size("chip") * cores
+    device_index = lax.axis_index("chip") * cores + core
+    meta = jnp.stack([device_index * rows, core]).astype(jnp.int32)
+
+    def lin_shift(value, steps):
+        leading, last = (max(0, -steps), min(count, count - steps))
+        return lax.ppermute(value, ("chip", "core"), [(s, s + steps) for s in range(leading, last)])
+
     line_len = -(-bucket_table.shape[0] // LANES) * LANES
     table = jnp.pad(bucket_table, (0, line_len - bucket_table.shape[0])).reshape(1, line_len)
     bias_t = bucket_bias.T
 
-    packed = jnp.concatenate([key_proj, value_proj], axis=1)
-    received = {0: packed}
-    for hop in range(REACH, 0, -1):
-        received[hop] = shifted(packed, "seq", -hop)
-        received[-hop] = shifted(packed, "seq", hop)
+    packed = jnp.stack([key_proj, value_proj])
+    from_prev = lin_shift(packed, REACH)
+    from_next = lin_shift(packed, -REACH)
+    own_pair = lax.all_gather(packed, "core", tiled=True)
+    sel = jnp.where(core == 0, from_next, from_prev)
+    sel_pair = lax.all_gather(sel, "core", tiled=True)
     order = list(range(-REACH, REACH + 1))
-    kv_blocks = [received[h] for h in order]
 
     half = rows // 2
     vmem = pl.BlockSpec(memory_space=pltpu.VMEM)
@@ -194,25 +220,26 @@
             jax.ShapeDtypeStruct((half, model_width), jnp.bfloat16),
             jax.ShapeDtypeStruct((rows - half, model_width), jnp.bfloat16),
         ),
-        in_specs=[smem, smem] + [vmem] * (3 + len(order)) + [vmem, vmem, anywhere, anywhere],
+        in_specs=[smem, smem, vmem, vmem, vmem] + [anywhere] * 4 + [vmem, vmem, anywhere, anywhere],
         out_specs=(vmem, vmem, vmem),
         scratch_shapes=[
             pltpu.VMEM((att_width, model_width), jnp.bfloat16),
             pltpu.VMEM((model_width, 2 * model_width), jnp.bfloat16),
-            pltpu.SemaphoreType.DMA((2,)),
+            pltpu.SemaphoreType.DMA((7,)),
             pltpu.VMEM((rows, att_width), jnp.bfloat16),
+            pltpu.VMEM((len(order) * packed.shape[0], rows, att_width), jnp.bfloat16),
         ],
         cost_estimate=pl.CostEstimate(
             flops=attn_flops, transcendentals=heads * rows * window + rows * model_width, bytes_accessed=attn_bytes
         ),
         name="attention_glu",
     )(
-        meta, utterance_lengths, table, bias_t, query_proj, *kv_blocks,
+        meta, utterance_lengths, table, bias_t, query_proj, from_prev, from_next, own_pair, sel_pair,
         frames_in, norm_gain.reshape(1, -1), out_weight, expand_weight,
     )
 
-    prev_tail = shifted(g_tail, "seq", 1)
-    next_head = shifted(g_head, "seq", -1)
+    prev_tail = lin_shift(g_tail, 1)
+    next_head = lin_shift(g_head, -1)
     conv_flops = 2 * KERNEL * rows * model_width + 2 * rows * model_width * model_width
     conv_bytes = 2 * (4 * half * model_width + rows * model_width * 2 + model_width * model_width) + 4 * KERNEL * model_width
     return pl.pallas_call(
@@ -234,11 +261,14 @@
 
 
 def solution(mesh):
+    groups, seq = mesh.devices.shape
+    chip_mesh = jax.sharding.Mesh(mesh.devices.reshape(groups, seq // 2, 2), ("groups", "chip", "core"))
+    rows_spec = P(("groups", "chip", "core"), None)
     placed = (
-        P(("groups", "seq"), None),
-        P(("groups", "seq"), None),
-        P(("groups", "seq"), None),
-        P(("groups", "seq"), None),
+        rows_spec,
+        rows_spec,
+        rows_spec,
+        rows_spec,
         P("groups"),
         P(),
         P(),
@@ -250,5 +280,5 @@
         P(),
     )
     return jax.shard_map(
-        on_device, mesh=mesh, in_specs=placed, out_specs=P(("groups", "seq"), None), check_vma=False
-    )
+        on_device, mesh=chip_mesh, in_specs=placed, out_specs=rows_spec, check_vma=False
+    )

time: 46.4 us -> 43.8 us (0.944)
  the two profiles are of different devices: /device:TPU:21 before, /device:TPU:1 now
where the time goes in v4:
time: 43.8 us; the launch traced here: 43.5 us
  starting transfers between devices  12.2 us (28%)
  Pallas kernels  12 us (27%)
  waiting for transfers between devices  10.4 us (24%)
  blocking collectives  5.32 us (12%)
  local copies, waits for them, and re-layouts  1.93 us (4%)
  other arithmetic  1.64 us (4%)
    ppermute x4, starting transfers between devices, lin_shift(): lax.ppermute(value, ('chip', 'core'), [(s, s + steps) for s in range(lead...  12.2 us
    ppermute x4, waiting for transfers between devices, lin_shift(): lax.ppermute(value, ('chip', 'core'), [(s, s + steps) for s in range(lead...  10.4 us
    pallas_call x1, Pallas kernels, on_device(): pl.pallas_call(attention_kernel, out_shape=(jax.ShapeDtypeStruct((rows, m...  7.03 us
    pallas_call x1, Pallas kernels, on_device(): pl.pallas_call(conv_kernel, out_shape=jax.ShapeDtypeStruct((rows, model_w...  4.92 us
    all_gather x1, blocking collectives, on_device(): own_pair = lax.all_gather(packed, 'core', tiled=True)  2.88 us
    all_gather x1, blocking collectives, on_device(): sel_pair = lax.all_gather(sel, 'core', tiled=True)  2.43 us
    another operation x1, other arithmetic, on_device(): packed = jnp.stack([key_proj, value_proj])  0.99 us
  transfers between devices with their start and end apart: 4, of which 3 were waited for; matrix products, arithmetic and copies ran while one was open for 4% of the time, Pallas kernels for 0%

profile of v4, /device:TPU:1, one launch (start us, length us, event | category | flops | bytes accessed | tf_op | source)
XLA Modules:
  0.0 43.5 jit_solution(17749116652414811181)
XLA Ops:
  0.0 1.0 %pad_maximum_fusion = bf16[2,128,512]{2,1,0:T(8,128)(2,1)S(1)} fusion(bf16[1,128,512]{2,1,0:T(8,128)(2,1)} %bitcast.7, bf16[1,128,512]{2,1,0:T(8,128)(2,1)} %bitcast.8), kind=kLoop, calls=%fused_computation | loop fusion | flops 131072 | bytes 524288 | tf_op jit(solution)/shard_map/stack | solution.py:201
  1.0 1.3 %collective-permute-start.1 = (bf16[2,128,512]{2,1,0:T(8,128)(2,1)S(1)}, bf16[2,128,512]{2,1,0:T(8,128)(2,1)S(1)}, u32[]{:S(2)}, u32[]{:S(2)}) collective-permute-start(bf16[2,128,512]{2,1,0:T(8,128)(2,1)S(1)} %pad_maximum_fusion), channel_id=1, source_target_pairs={{2,0},{3,1},{4,2},{5,3},{6,4},{7,5},{8,6},{9,7},{10,8},{11,9},{12,... | collective-permute-start | bytes 786440 | tf_op jit(solution)/shard_map/ppermute | solution.py:195
  2.3 4.6 %collective-permute-start = (bf16[2,128,512]{2,1,0:T(8,128)(2,1)S(1)}, bf16[2,128,512]{2,1,0:T(8,128)(2,1)S(1)}, u32[]{:S(2)}, u32[]{:S(2)}) collective-permute-start(bf16[2,128,512]{2,1,0:T(8,128)(2,1)S(1)} %pad_maximum_fusion), channel_id=1, source_target_pairs={{0,2},{1,3},{2,4},{3,5},{4,6},{5,7},{6,8},{7,9},{8,10},{9,11},{10,... | collective-permute-start | bytes 786440 | tf_op jit(solution)/shard_map/ppermute | solution.py:195
  6.9 0.7 %pad.4 = s32[768]{0:T(1024)S(1)} pad(s32[767]{0:T(1024)} %param.18, s32[]{:T(128)} %constant.13.clone.1), padding=0_1 | pad | bytes 6144 | tf_op jit(solution)/shard_map/jit(_pad)/pad | solution.py:198
  7.6 0.6 %reshape.9.table_ref = s32[1,768]{1,0:T(1,128)} reshape(s32[768]{0:T(1024)S(1)} %pad.4) | data formatting | bytes 6144 | tf_op jit(solution)/shard_map/reshape | solution.py:198
  8.2 0.6 %pad_add_fusion.meta_ref = s32[2]{0:T(128)} fusion(s32[1]{0:T(128)} %bitcast.1, s32[1]{0:T(128)} %bitcast), kind=kLoop, calls=%fused_computation.2 | loop fusion | flops 2 | bytes 16 | tf_op jit(solution)/shard_map/stack | solution.py:191
  8.8 2.9 %all_gather.6.own_hbm = bf16[4,128,512]{2,1,0:T(8,128)(2,1)} all-gather(bf16[2,128,512]{2,1,0:T(8,128)(2,1)S(1)} %pad_maximum_fusion), channel_id=1, replica_groups=mesh['groups'=2,'chip'=8,'core'=2] {'core'}, dimensions={0}, use_global_device_ids=true | all-gather | bytes 786432 | tf_op jit(solution)/shard_map/all_gather | solution.py:204
  11.7 0.0 collective-permute-done.1.next_hbm
  11.7 0.0 copy-start
  11.7 5.8 %collective-permute-done.prev_hbm = bf16[2,128,512]{2,1,0:T(8,128)(2,1)S(1)} collective-permute-done((bf16[2,128,512]{2,1,0:T(8,128)(2,1)S(1)}, bf16[2,128,512]{2,1,0:T(8,128)(2,1)S(1)}, u32[]{:S(2)}, u32[]{:S(2)}) %collective-permute-start) | collective-permute-done | bytes 262176 | tf_op jit(solution)/shard_map/ppermute | solution.py:195
  17.5 0.0 copy-start.1
  17.5 2.4 %all_gather.7.sel_hbm = bf16[4,128,512]{2,1,0:T(8,128)(2,1)} all-gather(bf16[2,128,512]{2,1,0:T(8,128)(2,1)S(1)} %broadcast_select_fusion), channel_id=1, replica_groups=mesh['groups'=2,'chip'=8,'core'=2] {'core'}, dimensions={0}, use_global_device_ids=true | all-gather | bytes 786432 | tf_op jit(solution)/shard_map/all_gather | solution.py:206
  20.0 0.0 copy-done
  20.0 0.0 copy-done.1
  20.0 7.0 %attention_glu.1 = (bf16[128,1024]{1,0:T(8,128)(2,1)}, bf16[64,1024]{1,0:T(8,128)(2,1)}, bf16[64,1024]{1,0:T(8,128)(2,1)}) custom-call(s32[2]{0:T(128)} %pad_add_fusion.meta_ref, s32[16]{0:T(128)} %len_ref.1, s32[1,768]{1,0:T(1,128)} %reshape.9.table_ref, f32[8,32]{1,0:T(8,128)} %bitcast.9, bf16[128,512]{1,0:T(8,128)(2,1)} %q_ref.1, ...), custom_call_target="tpu_custom_call" | custom-call | flops 1006632960 | bytes 7208960 | tf_op jit(solution)/shard_map/attention_glu/pallas_call | solution.py:216
  27.0 4.4 %collective-permute-start.2 = (bf16[64,1024]{1,0:T(8,128)(2,1)}, bf16[64,1024]{1,0:T(8,128)(2,1)S(1)}, u32[]{:S(2)}, u32[]{:S(2)}) collective-permute-start(bf16[64,1024]{1,0:T(8,128)(2,1)} %get-tuple-element.8.tail_ref), channel_id=1, source_target_pairs={{0,1},{1,2},{2,3},{3,4},{4,5},{5,6},{6,7},{7,8},{8,9},{9,10},{10,1... | collective-permute-start | bytes 393224 | tf_op jit(solution)/shard_map/ppermute | solution.py:195
  31.4 1.9 %collective-permute-start.3 = (bf16[64,1024]{1,0:T(8,128)(2,1)}, bf16[64,1024]{1,0:T(8,128)(2,1)S(1)}, u32[]{:S(2)}, u32[]{:S(2)}) collective-permute-start(bf16[64,1024]{1,0:T(8,128)(2,1)} %get-tuple-element.9.head_ref), channel_id=1, source_target_pairs={{1,0},{2,1},{3,2},{4,3},{5,4},{6,5},{7,6},{8,7},{9,8},{10,9},{11,1... | collective-permute-start | bytes 393224 | tf_op jit(solution)/shard_map/ppermute | solution.py:195
  33.3 0.3 collective-permute-done.2.prev_ref
  33.6 0.0 copy-start.2
  33.6 4.3 %collective-permute-done.3.next_ref = bf16[64,1024]{1,0:T(8,128)(2,1)S(1)} collective-permute-done((bf16[64,1024]{1,0:T(8,128)(2,1)}, bf16[64,1024]{1,0:T(8,128)(2,1)S(1)}, u32[]{:S(2)}, u32[]{:S(2)}) %collective-permute-start.3) | collective-permute-done | bytes 131104 | tf_op jit(solution)/shard_map/ppermute | solution.py:195
  37.9 0.0 copy-start.3
  37.9 0.0 copy-done.2
  37.9 0.6 %copy-done.3 = bf16[64,1024]{1,0:T(8,128)(2,1)} copy-done((bf16[64,1024]{1,0:T(8,128)(2,1)}, bf16[64,1024]{1,0:T(8,128)(2,1)S(1)}, u32[]{:S(2)}) %copy-start.3) | copy-done | bytes 131096
  38.5 4.9 %conv_shrink.1 = bf16[128,1024]{1,0:T(8,128)(2,1)} custom-call(bf16[64,1024]{1,0:T(8,128)(2,1)} %copy-done.2, bf16[64,1024]{1,0:T(8,128)(2,1)} %get-tuple-element.9.head_ref, bf16[64,1024]{1,0:T(8,128)(2,1)} %get-tuple-element.8.tail_ref, bf16[64,1024]{1,0:T(8,128)(2,1)} %copy-done.3, f32[31,1024]{1,0:T(8,128)} %taps_ref.1, f32[1,1024]{1,0:T(1,128)} %bitcast.11, ...), custom_call_target="tpu_custom_call" | custom-call | flops 276561920 | bytes 3272704 | tf_op jit(solution)/shard_map/conv_shrink/pallas_call | solution.py:245
  (1 shorter events, 0.0 us)
Async XLA Ops:
  1.0 10.7 %collective-permute-start.1 = (bf16[2,128,512]{2,1,0:T(8,128)(2,1)S(1)}, bf16[2,128,512]{2,1,0:T(8,128)(2,1)S(1)}, u32[]{:S(2)}, u32[]{:S(2)}) collective-permute-start(bf16[2,128,512]{2,1,0:T(8,128)(2,1)S(1)} %pad_maximum_fusion), channel_id=1, source_target_pairs={{2,0},{3,1},{4,2},{5,3},{6,4},{7,5},{8,6},{9,7},{10,8},{11,9},{12,... | collective-permute-start | bytes 786440 | tf_op jit(solution)/shard_map/ppermute | solution.py:195
  2.3 15.2 %collective-permute-start = (bf16[2,128,512]{2,1,0:T(8,128)(2,1)S(1)}, bf16[2,128,512]{2,1,0:T(8,128)(2,1)S(1)}, u32[]{:S(2)}, u32[]{:S(2)}) collective-permute-start(bf16[2,128,512]{2,1,0:T(8,128)(2,1)S(1)} %pad_maximum_fusion), channel_id=1, source_target_pairs={{0,2},{1,3},{2,4},{3,5},{4,6},{5,7},{6,8},{7,9},{8,10},{9,11},{10,... | collective-permute-start | bytes 786440 | tf_op jit(solution)/shard_map/ppermute | solution.py:195
  11.7 8.3 %copy-start = (bf16[2,128,512]{2,1,0:T(8,128)(2,1)}, bf16[2,128,512]{2,1,0:T(8,128)(2,1)S(1)}, u32[]{:S(2)}) copy-start(bf16[2,128,512]{2,1,0:T(8,128)(2,1)S(1)} %collective-permute-done.1.next_hbm) | copy-start | bytes 786436
  17.5 2.5 %copy-start.1 = (bf16[2,128,512]{2,1,0:T(8,128)(2,1)}, bf16[2,128,512]{2,1,0:T(8,128)(2,1)S(1)}, u32[]{:S(2)}) copy-start(bf16[2,128,512]{2,1,0:T(8,128)(2,1)S(1)} %collective-permute-done.prev_hbm) | copy-start | bytes 786436
  27.0 6.6 %collective-permute-start.2 = (bf16[64,1024]{1,0:T(8,128)(2,1)}, bf16[64,1024]{1,0:T(8,128)(2,1)S(1)}, u32[]{:S(2)}, u32[]{:S(2)}) collective-permute-start(bf16[64,1024]{1,0:T(8,128)(2,1)} %get-tuple-element.8.tail_ref), channel_id=1, source_target_pairs={{0,1},{1,2},{2,3},{3,4},{4,5},{5,6},{6,7},{7,8},{8,9},{9,10},{10,1... | collective-permute-start | bytes 393224 | tf_op jit(solution)/shard_map/ppermute | solution.py:195
  31.4 6.5 %collective-permute-start.3 = (bf16[64,1024]{1,0:T(8,128)(2,1)}, bf16[64,1024]{1,0:T(8,128)(2,1)S(1)}, u32[]{:S(2)}, u32[]{:S(2)}) collective-permute-start(bf16[64,1024]{1,0:T(8,128)(2,1)} %get-tuple-element.9.head_ref), channel_id=1, source_target_pairs={{1,0},{2,1},{3,2},{4,3},{5,4},{6,5},{7,6},{8,7},{9,8},{10,9},{11,1... | collective-permute-start | bytes 393224 | tf_op jit(solution)/shard_map/ppermute | solution.py:195
  33.6 4.3 %copy-start.2 = (bf16[64,1024]{1,0:T(8,128)(2,1)}, bf16[64,1024]{1,0:T(8,128)(2,1)S(1)}, u32[]{:S(2)}) copy-start(bf16[64,1024]{1,0:T(8,128)(2,1)S(1)} %collective-permute-done.2.prev_ref) | copy-start | bytes 393220
  37.9 0.6 %copy-start.3 = (bf16[64,1024]{1,0:T(8,128)(2,1)}, bf16[64,1024]{1,0:T(8,128)(2,1)S(1)}, u32[]{:S(2)}) copy-start(bf16[64,1024]{1,0:T(8,128)(2,1)S(1)} %collective-permute-done.3.next_ref) | copy-start | bytes 393220

commit v5 on v4

--- a/solution.py
+++ b/solution.py
@@ -35,7 +35,7 @@
     meta_ref, len_ref, table_ref, bias_t_ref, q_ref,
     prev_hbm, next_hbm, own_hbm, sel_hbm,
     x_ref, gain_ref, ow_hbm, ew_hbm,
-    mid_ref, head_ref, tail_ref,
+    mid_ref, gated_ref, cross_ref, partner_ref,
     ow_vmem, ew_vmem, sems, att_ref, win_ref,
 ):
     base = meta_ref[0]
@@ -129,23 +129,25 @@
     value_half = jnp.dot(normed, ew_vmem[:, :model_width], preferred_element_type=jnp.float32)
     gate_half = jnp.dot(normed, ew_vmem[:, model_width:], preferred_element_type=jnp.float32)
     gated = (value_half * sigmoid(gate_half)).astype(jnp.bfloat16)
-    half = head_ref.shape[0]
-    head_ref[...] = gated[:half]
-    tail_ref[...] = gated[half:]
+    gated_ref[...] = gated
+    half = cross_ref.shape[0]
+    cross_ref[...] = gated_ref[pl.ds(pl.multiple_of(core * half, half), half), :]
+    partner_ref[...] = gated_ref[pl.ds(pl.multiple_of((1 - core) * half, half), half), :]
 
 
 def conv_kernel(
-    prev_ref, head_ref, tail_ref, next_ref, taps_ref, gain_ref, mid_ref, sw_hbm,
+    meta_ref, gated_ref, cross_ref, pairg_ref, taps_ref, gain_ref, mid_ref, sw_hbm,
     out_ref, win_ref, conv_ref, sw_vmem, sems,
 ):
     sw_copy = pltpu.make_async_copy(sw_hbm, sw_vmem, sems.at[0])
     sw_copy.start()
-    half = head_ref.shape[0]
+    half = cross_ref.shape[0]
     rows, model_width = mid_ref.shape
-    win_ref[0:half, :] = prev_ref[...].astype(jnp.float32)
-    win_ref[half:2 * half, :] = head_ref[...].astype(jnp.float32)
-    win_ref[2 * half:3 * half, :] = tail_ref[...].astype(jnp.float32)
-    win_ref[3 * half:4 * half, :] = next_ref[...].astype(jnp.float32)
+    first_core = meta_ref[1] == 0
+    cross = cross_ref[...]
+    win_ref[0:half, :] = jnp.where(first_core, cross, pairg_ref[0:half, :]).astype(jnp.float32)
+    win_ref[half:half + rows, :] = gated_ref[...].astype(jnp.float32)
+    win_ref[half + rows:2 * half + rows, :] = jnp.where(first_core, pairg_ref[half:2 * half, :], cross).astype(jnp.float32)
     reach = DILATION * (KERNEL - 1) // 2
     start = half - reach
 
@@ -213,15 +215,16 @@
     window = len(order) * rows
     attn_flops = 2 * 2 * heads * rows * window * LANES + 2 * rows * att_width * model_width + 2 * rows * model_width * 2 * model_width
     attn_bytes = 2 * (rows * att_width * (1 + 2 * len(order)) + rows * model_width * 2 + att_width * model_width + model_width * 2 * model_width)
-    mid, g_head, g_tail = pl.pallas_call(
+    mid, gated, cross_send, partner_send = pl.pallas_call(
         attention_kernel,
         out_shape=(
             jax.ShapeDtypeStruct((rows, model_width), jnp.bfloat16),
+            jax.ShapeDtypeStruct((rows, model_width), jnp.bfloat16),
             jax.ShapeDtypeStruct((half, model_width), jnp.bfloat16),
-            jax.ShapeDtypeStruct((rows - half, model_width), jnp.bfloat16),
+            jax.ShapeDtypeStruct((half, model_width), jnp.bfloat16),
         ),
         in_specs=[smem, smem, vmem, vmem, vmem] + [anywhere] * 4 + [vmem, vmem, anywhere, anywhere],
-        out_specs=(vmem, vmem, vmem),
+        out_specs=(vmem, vmem, vmem, vmem),
         scratch_shapes=[
             pltpu.VMEM((att_width, model_width), jnp.bfloat16),
             pltpu.VMEM((model_width, 2 * model_width), jnp.bfloat16),
@@ -238,17 +241,19 @@
         frames_in, norm_gain.reshape(1, -1), out_weight, expand_weight,
     )
 
-    prev_tail = lin_shift(g_tail, 1)
-    next_head = lin_shift(g_head, -1)
+    chips = count // cores
+    inward = [(2 * c + 1, 2 * c + 2) for c in range(chips - 1)] + [(2 * c, 2 * c - 1) for c in range(1, chips)]
+    cross_recv = lax.ppermute(cross_send, ("chip", "core"), inward)
+    partner_recv = lax.all_gather(partner_send, "core", tiled=True)
     conv_flops = 2 * KERNEL * rows * model_width + 2 * rows * model_width * model_width
     conv_bytes = 2 * (4 * half * model_width + rows * model_width * 2 + model_width * model_width) + 4 * KERNEL * model_width
     return pl.pallas_call(
         conv_kernel,
         out_shape=jax.ShapeDtypeStruct((rows, model_width), jnp.bfloat16),
-        in_specs=[vmem] * 7 + [anywhere],
+        in_specs=[smem] + [vmem] * 6 + [anywhere],
         out_specs=vmem,
         scratch_shapes=[
-            pltpu.VMEM((4 * half, model_width), jnp.float32),
+            pltpu.VMEM((rows + 2 * half, model_width), jnp.float32),
             pltpu.VMEM((rows, model_width), jnp.float32),
             pltpu.VMEM((model_width, model_width), jnp.bfloat16),
             pltpu.SemaphoreType.DMA((1,)),
@@ -257,7 +262,7 @@
             flops=conv_flops, transcendentals=rows * model_width, bytes_accessed=conv_bytes
         ),
         name="conv_shrink",
-    )(prev_tail, g_head, g_tail, next_head, depth_taps, inner_gain.reshape(1, -1), mid, shrink_weight)
+    )(meta, gated, cross_recv, partner_recv, depth_taps, inner_gain.reshape(1, -1), mid, shrink_weight)
 
 
 def solution(mesh):

time: 43.8 us -> 41.3 us (0.943)
  the two profiles are of different devices: /device:TPU:1 before, /device:TPU:0 now
where the time goes in v5:
time: 41.3 us; the launch traced here: 41 us
  Pallas kernels  12.1 us (29%)
  blocking collectives  11.8 us (29%)
  starting transfers between devices  7.48 us (18%)
  waiting for transfers between devices  5.88 us (14%)
  local copies, waits for them, and re-layouts  1.93 us (5%)
  other arithmetic  1.67 us (4%)
    all_gather x1, blocking collectives, on_device(): partner_recv = lax.all_gather(partner_send, 'core', tiled=True)  7.22 us
    pallas_call x1, Pallas kernels, on_device(): pl.pallas_call(attention_kernel, out_shape=(jax.ShapeDtypeStruct((rows, m...  7.19 us
    ppermute x2, starting transfers between devices, lin_shift(): lax.ppermute(value, ('chip', 'core'), [(s, s + steps) for s in range(lead...  6.81 us
    ppermute x2, waiting for transfers between devices, lin_shift(): lax.ppermute(value, ('chip', 'core'), [(s, s + steps) for s in range(lead...  5.88 us
    pallas_call x1, Pallas kernels, on_device(): pl.pallas_call(conv_kernel, out_shape=jax.ShapeDtypeStruct((rows, model_w...  4.92 us
    all_gather x1, blocking collectives, on_device(): sel_pair = lax.all_gather(sel, 'core', tiled=True)  2.31 us
    all_gather x1, blocking collectives, on_device(): own_pair = lax.all_gather(packed, 'core', tiled=True)  2.3 us
    another operation x1, other arithmetic, on_device(): packed = jnp.stack([key_proj, value_proj])  0.99 us
  transfers between devices with their start and end apart: 3, of which 2 were waited for; matrix products, arithmetic and copies ran while one was open for 5% of the time, Pallas kernels for 0%

profile of v5, /device:TPU:0, one launch (start us, length us, event | category | flops | bytes accessed | tf_op | source)
XLA Modules:
  0.0 41.0 jit_solution(12607131210290543412)
XLA Ops:
  0.0 1.0 %pad_maximum_fusion = bf16[2,128,512]{2,1,0:T(8,128)(2,1)S(1)} fusion(bf16[1,128,512]{2,1,0:T(8,128)(2,1)} %bitcast.7, bf16[1,128,512]{2,1,0:T(8,128)(2,1)} %bitcast.8), kind=kLoop, calls=%fused_computation | loop fusion | flops 131072 | bytes 524288 | tf_op jit(solution)/shard_map/stack | solution.py:203
  1.0 1.3 %collective-permute-start.1 = (bf16[2,128,512]{2,1,0:T(8,128)(2,1)S(1)}, bf16[2,128,512]{2,1,0:T(8,128)(2,1)S(1)}, u32[]{:S(2)}, u32[]{:S(2)}) collective-permute-start(bf16[2,128,512]{2,1,0:T(8,128)(2,1)S(1)} %pad_maximum_fusion), channel_id=1, source_target_pairs={{2,0},{3,1},{4,2},{5,3},{6,4},{7,5},{8,6},{9,7},{10,8},{11,9},{12,... | collective-permute-start | bytes 786440 | tf_op jit(solution)/shard_map/ppermute | solution.py:197
  2.3 5.5 %collective-permute-start = (bf16[2,128,512]{2,1,0:T(8,128)(2,1)S(1)}, bf16[2,128,512]{2,1,0:T(8,128)(2,1)S(1)}, u32[]{:S(2)}, u32[]{:S(2)}) collective-permute-start(bf16[2,128,512]{2,1,0:T(8,128)(2,1)S(1)} %pad_maximum_fusion), channel_id=1, source_target_pairs={{0,2},{1,3},{2,4},{3,5},{4,6},{5,7},{6,8},{7,9},{8,10},{9,11},{10,... | collective-permute-start | bytes 786440 | tf_op jit(solution)/shard_map/ppermute | solution.py:197
  7.8 0.7 %pad.4 = s32[768]{0:T(1024)S(1)} pad(s32[767]{0:T(1024)} %param.18, s32[]{:T(128)} %constant.13.clone.1), padding=0_1 | pad | bytes 6144 | tf_op jit(solution)/shard_map/jit(_pad)/pad | solution.py:200
  8.5 0.6 %reshape.9.table_ref = s32[1,768]{1,0:T(1,128)} reshape(s32[768]{0:T(1024)S(1)} %pad.4) | data formatting | bytes 6144 | tf_op jit(solution)/shard_map/reshape | solution.py:200
  9.1 0.7 %pad_add_fusion.meta_ref = s32[2]{0:T(128)} fusion(s32[1]{0:T(128)} %bitcast.1, s32[1]{0:T(128)} %bitcast), kind=kLoop, calls=%fused_computation.2 | loop fusion | flops 2 | bytes 16 | tf_op jit(solution)/shard_map/stack | solution.py:193
  9.8 2.3 %all_gather.9.own_hbm = bf16[4,128,512]{2,1,0:T(8,128)(2,1)} all-gather(bf16[2,128,512]{2,1,0:T(8,128)(2,1)S(1)} %pad_maximum_fusion), channel_id=1, replica_groups=mesh['groups'=2,'chip'=8,'core'=2] {'core'}, dimensions={0}, use_global_device_ids=true | all-gather | bytes 786432 | tf_op jit(solution)/shard_map/all_gather | solution.py:206
  12.1 0.1 collective-permute-done.1.next_hbm
  12.2 0.0 copy-start
  12.2 5.8 %collective-permute-done.prev_hbm = bf16[2,128,512]{2,1,0:T(8,128)(2,1)S(1)} collective-permute-done((bf16[2,128,512]{2,1,0:T(8,128)(2,1)S(1)}, bf16[2,128,512]{2,1,0:T(8,128)(2,1)S(1)}, u32[]{:S(2)}, u32[]{:S(2)}) %collective-permute-start) | collective-permute-done | bytes 262176 | tf_op jit(solution)/shard_map/ppermute | solution.py:197
  17.9 0.0 copy-start.1
  18.0 2.3 %all_gather.10.sel_hbm = bf16[4,128,512]{2,1,0:T(8,128)(2,1)} all-gather(bf16[2,128,512]{2,1,0:T(8,128)(2,1)S(1)} %broadcast_select_fusion), channel_id=1, replica_groups=mesh['groups'=2,'chip'=8,'core'=2] {'core'}, dimensions={0}, use_global_device_ids=true | all-gather | bytes 786432 | tf_op jit(solution)/shard_map/all_gather | solution.py:208
  20.3 0.0 copy-done
  20.3 0.0 copy-done.1
  20.3 7.2 %attention_glu.1 = (bf16[128,1024]{1,0:T(8,128)(2,1)}, bf16[128,1024]{1,0:T(8,128)(2,1)}, bf16[64,1024]{1,0:T(8,128)(2,1)}, bf16[64,1024]{1,0:T(8,128)(2,1)}) custom-call(s32[2]{0:T(128)} %pad_add_fusion.meta_ref, s32[16]{0:T(128)} %len_ref.1, s32[1,768]{1,0:T(1,128)} %reshape.9.table_ref, f32[8,32]{1,0:T(8,128)} %bitcast.9, bf16[128,512]{1,0:T(8,128)(2,1)} %q_ref.1, ...), custom_call_target="tpu_custom_call" | custom-call | flops 1006632960 | bytes 7208960 | tf_op jit(solution)/shard_map/attention_glu/pallas_call | solution.py:218
  27.5 0.7 %collective-permute-start.2 = (bf16[64,1024]{1,0:T(8,128)(2,1)}, bf16[64,1024]{1,0:T(8,128)(2,1)S(1)}, u32[]{:S(2)}, u32[]{:S(2)}) collective-permute-start(bf16[64,1024]{1,0:T(8,128)(2,1)} %get-tuple-element.10), channel_id=1, source_target_pairs={{1,2},{3,4},{5,6},{7,8},{9,10},{11,12},{13,14},{2,1},{4,3},{6,5},{... | collective-permute-start | bytes 393224 | tf_op jit(solution)/shard_map/ppermute | solution.py:246
  28.2 7.2 %all_gather.11.pairg_ref = bf16[128,1024]{1,0:T(8,128)(2,1)} all-gather(bf16[64,1024]{1,0:T(8,128)(2,1)} %get-tuple-element.11), channel_id=1, replica_groups=mesh['groups'=2,'chip'=8,'core'=2] {'core'}, dimensions={0}, use_global_device_ids=true | all-gather | bytes 393216 | tf_op jit(solution)/shard_map/all_gather | solution.py:247
  35.4 0.0 collective-permute-done.2.cross_ref
  35.4 0.0 copy-start.2
  35.4 0.6 %copy-done.2 = bf16[64,1024]{1,0:T(8,128)(2,1)} copy-done((bf16[64,1024]{1,0:T(8,128)(2,1)}, bf16[64,1024]{1,0:T(8,128)(2,1)S(1)}, u32[]{:S(2)}) %copy-start.2) | copy-done | bytes 131096
  36.0 4.9 %conv_shrink.1 = bf16[128,1024]{1,0:T(8,128)(2,1)} custom-call(s32[2]{0:T(128)} %pad_add_fusion.meta_ref, bf16[128,1024]{1,0:T(8,128)(2,1)} %get-tuple-element.9.gated_ref, bf16[64,1024]{1,0:T(8,128)(2,1)} %copy-done.2, bf16[128,1024]{1,0:T(8,128)(2,1)} %all_gather.11.pairg_ref, f32[31,1024]{1,0:T(8,128)} %taps_ref.1, f32[1,1024]{1,0:T(1,128)} %bitcast.11, ...), custom_call_target="tpu_custom_call" | custom-call | flops 276561920 | bytes 3272704 | tf_op jit(solution)/shard_map/conv_shrink/pallas_call | solution.py:250
  (1 shorter events, 0.0 us)
Async XLA Ops:
  1.0 11.2 %collective-permute-start.1 = (bf16[2,128,512]{2,1,0:T(8,128)(2,1)S(1)}, bf16[2,128,512]{2,1,0:T(8,128)(2,1)S(1)}, u32[]{:S(2)}, u32[]{:S(2)}) collective-permute-start(bf16[2,128,512]{2,1,0:T(8,128)(2,1)S(1)} %pad_maximum_fusion), channel_id=1, source_target_pairs={{2,0},{3,1},{4,2},{5,3},{6,4},{7,5},{8,6},{9,7},{10,8},{11,9},{12,... | collective-permute-start | bytes 786440 | tf_op jit(solution)/shard_map/ppermute | solution.py:197
  2.3 15.6 %collective-permute-start = (bf16[2,128,512]{2,1,0:T(8,128)(2,1)S(1)}, bf16[2,128,512]{2,1,0:T(8,128)(2,1)S(1)}, u32[]{:S(2)}, u32[]{:S(2)}) collective-permute-start(bf16[2,128,512]{2,1,0:T(8,128)(2,1)S(1)} %pad_maximum_fusion), channel_id=1, source_target_pairs={{0,2},{1,3},{2,4},{3,5},{4,6},{5,7},{6,8},{7,9},{8,10},{9,11},{10,... | collective-permute-start | bytes 786440 | tf_op jit(solution)/shard_map/ppermute | solution.py:197
  12.2 8.1 %copy-start = (bf16[2,128,512]{2,1,0:T(8,128)(2,1)}, bf16[2,128,512]{2,1,0:T(8,128)(2,1)S(1)}, u32[]{:S(2)}) copy-start(bf16[2,128,512]{2,1,0:T(8,128)(2,1)S(1)} %collective-permute-done.1.next_hbm) | copy-start | bytes 786436
  17.9 2.4 %copy-start.1 = (bf16[2,128,512]{2,1,0:T(8,128)(2,1)}, bf16[2,128,512]{2,1,0:T(8,128)(2,1)S(1)}, u32[]{:S(2)}) copy-start(bf16[2,128,512]{2,1,0:T(8,128)(2,1)S(1)} %collective-permute-done.prev_hbm) | copy-start | bytes 786436
  27.5 7.9 %collective-permute-start.2 = (bf16[64,1024]{1,0:T(8,128)(2,1)}, bf16[64,1024]{1,0:T(8,128)(2,1)S(1)}, u32[]{:S(2)}, u32[]{:S(2)}) collective-permute-start(bf16[64,1024]{1,0:T(8,128)(2,1)} %get-tuple-element.10), channel_id=1, source_target_pairs={{1,2},{3,4},{5,6},{7,8},{9,10},{11,12},{13,14},{2,1},{4,3},{6,5},{... | collective-permute-start | bytes 393224 | tf_op jit(solution)/shard_map/ppermute | solution.py:246
  35.4 0.7 %copy-start.2 = (bf16[64,1024]{1,0:T(8,128)(2,1)}, bf16[64,1024]{1,0:T(8,128)(2,1)S(1)}, u32[]{:S(2)}) copy-start(bf16[64,1024]{1,0:T(8,128)(2,1)S(1)} %collective-permute-done.2.cross_ref) | copy-start | bytes 393220

commit v6 on v5

--- a/solution.py
+++ b/solution.py
@@ -33,7 +33,7 @@
 
 def attention_kernel(
     meta_ref, len_ref, table_ref, bias_t_ref, q_ref,
-    prev_hbm, next_hbm, own_hbm, sel_hbm,
+    prev_hbm, next_hbm, own_hbm, partner_hbm, sel_hbm,
     x_ref, gain_ref, ow_hbm, ew_hbm,
     mid_ref, gated_ref, cross_ref, partner_ref,
     ow_vmem, ew_vmem, sems, att_ref, win_ref,
@@ -41,17 +41,15 @@
     base = meta_ref[0]
     core = meta_ref[1]
     planes = prev_hbm.shape[0]
-    mine = pl.ds(pl.multiple_of(core * planes, planes), planes)
-    other = pl.ds(pl.multiple_of((1 - core) * planes, planes), planes)
     copies = [
         pltpu.make_async_copy(prev_hbm, win_ref.at[pl.ds(0, planes)], sems.at[2]),
-        pltpu.make_async_copy(own_hbm.at[mine], win_ref.at[pl.ds(2 * planes, planes)], sems.at[3]),
+        pltpu.make_async_copy(own_hbm, win_ref.at[pl.ds(2 * planes, planes)], sems.at[3]),
         pltpu.make_async_copy(next_hbm, win_ref.at[pl.ds(4 * planes, planes)], sems.at[4]),
         pltpu.make_async_copy(
-            sel_hbm.at[other], win_ref.at[pl.ds(pl.multiple_of((1 + 2 * core) * planes, planes), planes)], sems.at[5]
+            sel_hbm, win_ref.at[pl.ds(pl.multiple_of((1 + 2 * core) * planes, planes), planes)], sems.at[5]
         ),
         pltpu.make_async_copy(
-            own_hbm.at[other], win_ref.at[pl.ds(pl.multiple_of((3 - 2 * core) * planes, planes), planes)], sems.at[6]
+            partner_hbm, win_ref.at[pl.ds(pl.multiple_of((3 - 2 * core) * planes, planes), planes)], sems.at[6]
         ),
     ]
     for copy in copies:
@@ -145,9 +143,10 @@
     rows, model_width = mid_ref.shape
     first_core = meta_ref[1] == 0
     cross = cross_ref[...]
-    win_ref[0:half, :] = jnp.where(first_core, cross, pairg_ref[0:half, :]).astype(jnp.float32)
+    partner = pairg_ref[...]
+    win_ref[0:half, :] = jnp.where(first_core, cross, partner).astype(jnp.float32)
     win_ref[half:half + rows, :] = gated_ref[...].astype(jnp.float32)
-    win_ref[half + rows:2 * half + rows, :] = jnp.where(first_core, pairg_ref[half:2 * half, :], cross).astype(jnp.float32)
+    win_ref[half + rows:2 * half + rows, :] = jnp.where(first_core, partner, cross).astype(jnp.float32)
     reach = DILATION * (KERNEL - 1) // 2
     start = half - reach
 
@@ -203,9 +202,10 @@
     packed = jnp.stack([key_proj, value_proj])
     from_prev = lin_shift(packed, REACH)
     from_next = lin_shift(packed, -REACH)
-    own_pair = lax.all_gather(packed, "core", tiled=True)
+    swap = [(0, 1), (1, 0)]
+    partner = lax.ppermute(packed, "core", swap)
     sel = jnp.where(core == 0, from_next, from_prev)
-    sel_pair = lax.all_gather(sel, "core", tiled=True)
+    partner_sel = lax.ppermute(sel, "core", swap)
     order = list(range(-REACH, REACH + 1))
 
     half = rows // 2
@@ -223,7 +223,7 @@
             jax.ShapeDtypeStruct((half, model_width), jnp.bfloat16),
             jax.ShapeDtypeStruct((half, model_width), jnp.bfloat16),
         ),
-        in_specs=[smem, smem, vmem, vmem, vmem] + [anywhere] * 4 + [vmem, vmem, anywhere, anywhere],
+        in_specs=[smem, smem, vmem, vmem, vmem] + [anywhere] * 5 + [vmem, vmem, anywhere, anywhere],
         out_specs=(vmem, vmem, vmem, vmem),
         scratch_shapes=[
             pltpu.VMEM((att_width, model_width), jnp.bfloat16),
@@ -237,14 +237,14 @@
         ),
         name="attention_glu",
     )(
-        meta, utterance_lengths, table, bias_t, query_proj, from_prev, from_next, own_pair, sel_pair,
+        meta, utterance_lengths, table, bias_t, query_proj, from_prev, from_next, packed, partner, partner_sel,
         frames_in, norm_gain.reshape(1, -1), out_weight, expand_weight,
     )
 
     chips = count // cores
     inward = [(2 * c + 1, 2 * c + 2) for c in range(chips - 1)] + [(2 * c, 2 * c - 1) for c in range(1, chips)]
     cross_recv = lax.ppermute(cross_send, ("chip", "core"), inward)
-    partner_recv = lax.all_gather(partner_send, "core", tiled=True)
+    partner_recv = lax.ppermute(partner_send, "core", swap)
     conv_flops = 2 * KERNEL * rows * model_width + 2 * rows * model_width * model_width
     conv_bytes = 2 * (4 * half * model_width + rows * model_width * 2 + model_width * model_width) + 4 * KERNEL * model_width
     return pl.pallas_call(

time: 41.3 us -> 41.4 us (level)
  the two profiles are of different devices: /device:TPU:0 before, /device:TPU:21 now
where the time goes in v6:
time: 41.4 us; the launch traced here: 41.1 us
  waiting for transfers between devices  14.2 us (34%)
  Pallas kernels  12.1 us (29%)
  starting transfers between devices  10.3 us (25%)
  local copies, waits for them, and re-layouts  2.77 us (7%)
  other arithmetic  1.6 us (4%)
    ppermute x2, waiting for transfers between devices, lin_shift(): lax.ppermute(value, ('chip', 'core'), [(s, s + steps) for s in range(lead...  9.14 us
    pallas_call x1, Pallas kernels, on_device(): pl.pallas_call(attention_kernel, out_shape=(jax.ShapeDtypeStruct((rows, m...  7.2 us
    ppermute x2, starting transfers between devices, lin_shift(): lax.ppermute(value, ('chip', 'core'), [(s, s + steps) for s in range(lead...  6.18 us
    ppermute x1, waiting for transfers between devices, on_device(): cross_recv = lax.ppermute(cross_send, ('chip', 'core'), inward)  5.1 us
    pallas_call x1, Pallas kernels, on_device(): pl.pallas_call(conv_kernel, out_shape=jax.ShapeDtypeStruct((rows, model_w...  4.88 us
    ppermute x1, starting transfers between devices, on_device(): cross_recv = lax.ppermute(cross_send, ('chip', 'core'), inward)  2.21 us
    unnamed x14, local copies, waits for them, and re-layouts  1.49 us
    ppermute x1, starting transfers between devices, on_device(): partner = lax.ppermute(packed, 'core', swap)  1.3 us
  transfers between devices with their start and end apart: 6, of which 3 were waited for; matrix products, arithmetic and copies ran while one was open for 5% of the time, Pallas kernels for 0%

profile of v6, /device:TPU:21, one launch (start us, length us, event | category | flops | bytes accessed | tf_op | source)
XLA Modules:
  0.0 41.1 jit_solution(5359247426437948858)
XLA Ops:
  0.0 1.0 %pad_maximum_fusion.own_hbm = bf16[2,128,512]{2,1,0:T(8,128)(2,1)S(1)} fusion(bf16[1,128,512]{2,1,0:T(8,128)(2,1)} %bitcast.7, bf16[1,128,512]{2,1,0:T(8,128)(2,1)} %bitcast.8), kind=kLoop, calls=%fused_computation | loop fusion | flops 131072 | bytes 524288 | tf_op jit(solution)/shard_map/stack | solution.py:202
  1.0 0.0 copy-start
  1.0 2.1 %collective-permute-start.1 = (bf16[2,128,512]{2,1,0:T(8,128)(2,1)S(1)}, bf16[2,128,512]{2,1,0:T(8,128)(2,1)S(1)}, u32[]{:S(2)}, u32[]{:S(2)}) collective-permute-start(bf16[2,128,512]{2,1,0:T(8,128)(2,1)S(1)} %pad_maximum_fusion.own_hbm), channel_id=1, source_target_pairs={{2,0},{3,1},{4,2},{5,3},{6,4},{7,5},{8,6},{9,7},{10,8},{11,9},{12,... | collective-permute-start | bytes 786440 | tf_op jit(solution)/shard_map/ppermute | solution.py:196
  3.1 4.0 %collective-permute-start = (bf16[2,128,512]{2,1,0:T(8,128)(2,1)S(1)}, bf16[2,128,512]{2,1,0:T(8,128)(2,1)S(1)}, u32[]{:S(2)}, u32[]{:S(2)}) collective-permute-start(bf16[2,128,512]{2,1,0:T(8,128)(2,1)S(1)} %pad_maximum_fusion.own_hbm), channel_id=1, source_target_pairs={{0,2},{1,3},{2,4},{3,5},{4,6},{5,7},{6,8},{7,9},{8,10},{9,11},{10,... | collective-permute-start | bytes 786440 | tf_op jit(solution)/shard_map/ppermute | solution.py:196
  7.2 1.3 %collective-permute-start.2 = (bf16[2,128,512]{2,1,0:T(8,128)(2,1)S(1)}, bf16[2,128,512]{2,1,0:T(8,128)(2,1)S(1)}, u32[]{:S(2)}, u32[]{:S(2)}) collective-permute-start(bf16[2,128,512]{2,1,0:T(8,128)(2,1)S(1)} %pad_maximum_fusion.own_hbm), channel_id=1, source_target_pairs={{0,1},{1,0},{2,3},{3,2},{4,5},{5,4},{6,7},{7,6},{8,9},{9,8},{10,11... | collective-permute-start | bytes 786440 | tf_op jit(solution)/shard_map/ppermute | solution.py:206
  8.5 5.1 %collective-permute-done.1.next_hbm = bf16[2,128,512]{2,1,0:T(8,128)(2,1)S(1)} collective-permute-done((bf16[2,128,512]{2,1,0:T(8,128)(2,1)S(1)}, bf16[2,128,512]{2,1,0:T(8,128)(2,1)S(1)}, u32[]{:S(2)}, u32[]{:S(2)}) %collective-permute-start.1) | collective-permute-done | bytes 262176 | tf_op jit(solution)/shard_map/ppermute | solution.py:196
  13.6 0.0 copy-start.1
  13.6 4.1 %collective-permute-done.prev_hbm = bf16[2,128,512]{2,1,0:T(8,128)(2,1)S(1)} collective-permute-done((bf16[2,128,512]{2,1,0:T(8,128)(2,1)S(1)}, bf16[2,128,512]{2,1,0:T(8,128)(2,1)S(1)}, u32[]{:S(2)}, u32[]{:S(2)}) %collective-permute-start) | collective-permute-done | bytes 262176 | tf_op jit(solution)/shard_map/ppermute | solution.py:196
  17.6 0.0 copy-start.2
  17.7 0.6 %collective-permute-start.3 = (bf16[2,128,512]{2,1,0:T(8,128)(2,1)S(1)}, bf16[2,128,512]{2,1,0:T(8,128)(2,1)S(1)}, u32[]{:S(2)}, u32[]{:S(2)}) collective-permute-start(bf16[2,128,512]{2,1,0:T(8,128)(2,1)S(1)} %broadcast_select_fusion), channel_id=1, source_target_pairs={{0,1},{1,0},{2,3},{3,2},{4,5},{5,4},{6,7},{7,6},{8,9},{9,8},{10,11... | collective-permute-start | bytes 786440 | tf_op jit(solution)/shard_map/ppermute | solution.py:208
  18.2 0.7 %pad.4 = s32[768]{0:T(1024)S(1)} pad(s32[767]{0:T(1024)} %param.18, s32[]{:T(128)} %constant.13.clone.1), padding=0_1 | pad | bytes 6144 | tf_op jit(solution)/shard_map/jit(_pad)/pad | solution.py:199
  18.9 0.6 %reshape.9.table_ref = s32[1,768]{1,0:T(1,128)} reshape(s32[768]{0:T(1024)S(1)} %pad.4) | data formatting | bytes 6144 | tf_op jit(solution)/shard_map/reshape | solution.py:199
  19.5 0.6 %pad_add_fusion.meta_ref = s32[2]{0:T(128)} fusion(s32[1]{0:T(128)} %bitcast.1, s32[1]{0:T(128)} %bitcast), kind=kLoop, calls=%fused_computation.2 | loop fusion | flops 2 | bytes 16 | tf_op jit(solution)/shard_map/stack | solution.py:192
  20.1 0.0 collective-permute-done.2.partner_hbm
  20.1 0.0 copy-start.3
  20.1 0.0 collective-permute-done.3.sel_hbm
  20.1 0.0 copy-start.4
  20.1 0.0 copy-done
  20.1 0.0 copy-done.1
  20.1 0.0 copy-done.2
  20.2 0.7 %copy-done.3 = bf16[2,128,512]{2,1,0:T(8,128)(2,1)} copy-done((bf16[2,128,512]{2,1,0:T(8,128)(2,1)}, bf16[2,128,512]{2,1,0:T(8,128)(2,1)S(1)}, u32[]{:S(2)}) %copy-start.3) | copy-done | bytes 262168
  20.8 0.1 copy-done.4
  20.9 7.2 %attention_glu.1 = (bf16[128,1024]{1,0:T(8,128)(2,1)}, bf16[128,1024]{1,0:T(8,128)(2,1)}, bf16[64,1024]{1,0:T(8,128)(2,1)}, bf16[64,1024]{1,0:T(8,128)(2,1)}) custom-call(s32[2]{0:T(128)} %pad_add_fusion.meta_ref, s32[16]{0:T(128)} %len_ref.1, s32[1,768]{1,0:T(1,128)} %reshape.9.table_ref, f32[8,32]{1,0:T(8,128)} %bitcast.9, bf16[128,512]{1,0:T(8,128)(2,1)} %q_ref.1, ...), custom_call_target="tpu_custom_call" | custom-call | flops 1006632960 | bytes 7208960 | tf_op jit(solution)/shard_map/attention_glu/pallas_call | solution.py:218
  28.1 2.2 %collective-permute-start.4 = (bf16[64,1024]{1,0:T(8,128)(2,1)}, bf16[64,1024]{1,0:T(8,128)(2,1)S(1)}, u32[]{:S(2)}, u32[]{:S(2)}) collective-permute-start(bf16[64,1024]{1,0:T(8,128)(2,1)} %get-tuple-element.10), channel_id=1, source_target_pairs={{1,2},{3,4},{5,6},{7,8},{9,10},{11,12},{13,14},{2,1},{4,3},{6,5},{... | collective-permute-start | bytes 393224 | tf_op jit(solution)/shard_map/ppermute | solution.py:246
  30.4 0.1 collective-permute-start.5
  30.4 5.1 %collective-permute-done.4.cross_ref = bf16[64,1024]{1,0:T(8,128)(2,1)S(1)} collective-permute-done((bf16[64,1024]{1,0:T(8,128)(2,1)}, bf16[64,1024]{1,0:T(8,128)(2,1)S(1)}, u32[]{:S(2)}, u32[]{:S(2)}) %collective-permute-start.4) | collective-permute-done | bytes 131104 | tf_op jit(solution)/shard_map/ppermute | solution.py:246
  35.5 0.0 copy-start.5
  35.5 0.0 collective-permute-done.5.pairg_ref
  35.5 0.0 copy-start.6
  35.5 0.6 %copy-done.5 = bf16[64,1024]{1,0:T(8,128)(2,1)} copy-done((bf16[64,1024]{1,0:T(8,128)(2,1)}, bf16[64,1024]{1,0:T(8,128)(2,1)S(1)}, u32[]{:S(2)}) %copy-start.5) | copy-done | bytes 131096
  36.2 0.0 copy-done.6
  36.2 4.9 %conv_shrink.1 = bf16[128,1024]{1,0:T(8,128)(2,1)} custom-call(s32[2]{0:T(128)} %pad_add_fusion.meta_ref, bf16[128,1024]{1,0:T(8,128)(2,1)} %get-tuple-element.9.gated_ref, bf16[64,1024]{1,0:T(8,128)(2,1)} %copy-done.5, bf16[64,1024]{1,0:T(8,128)(2,1)} %copy-done.6, f32[31,1024]{1,0:T(8,128)} %taps_ref.1, f32[1,1024]{1,0:T(1,128)} %bitcast.11, ...), custom_call_target="tpu_custom_call" | custom-call | flops 276561920 | bytes 3272704 | tf_op jit(solution)/shard_map/conv_shrink/pallas_call | solution.py:250
  (1 shorter events, 0.0 us)
Async XLA Ops:
  1.0 19.1 %copy-start = (bf16[2,128,512]{2,1,0:T(8,128)(2,1)}, bf16[2,128,512]{2,1,0:T(8,128)(2,1)S(1)}, u32[]{:S(2)}) copy-start(bf16[2,128,512]{2,1,0:T(8,128)(2,1)S(1)} %pad_maximum_fusion.own_hbm) | copy-start | bytes 786436
  1.0 12.6 %collective-permute-start.1 = (bf16[2,128,512]{2,1,0:T(8,128)(2,1)S(1)}, bf16[2,128,512]{2,1,0:T(8,128)(2,1)S(1)}, u32[]{:S(2)}, u32[]{:S(2)}) collective-permute-start(bf16[2,128,512]{2,1,0:T(8,128)(2,1)S(1)} %pad_maximum_fusion.own_hbm), channel_id=1, source_target_pairs={{2,0},{3,1},{4,2},{5,3},{6,4},{7,5},{8,6},{9,7},{10,8},{11,9},{12,... | collective-permute-start | bytes 786440 | tf_op jit(solution)/shard_map/ppermute | solution.py:196
  3.1 14.5 %collective-permute-start = (bf16[2,128,512]{2,1,0:T(8,128)(2,1)S(1)}, bf16[2,128,512]{2,1,0:T(8,128)(2,1)S(1)}, u32[]{:S(2)}, u32[]{:S(2)}) collective-permute-start(bf16[2,128,512]{2,1,0:T(8,128)(2,1)S(1)} %pad_maximum_fusion.own_hbm), channel_id=1, source_target_pairs={{0,2},{1,3},{2,4},{3,5},{4,6},{5,7},{6,8},{7,9},{8,10},{9,11},{10,... | collective-permute-start | bytes 786440 | tf_op jit(solution)/shard_map/ppermute | solution.py:196
  7.2 12.9 %collective-permute-start.2 = (bf16[2,128,512]{2,1,0:T(8,128)(2,1)S(1)}, bf16[2,128,512]{2,1,0:T(8,128)(2,1)S(1)}, u32[]{:S(2)}, u32[]{:S(2)}) collective-permute-start(bf16[2,128,512]{2,1,0:T(8,128)(2,1)S(1)} %pad_maximum_fusion.own_hbm), channel_id=1, source_target_pairs={{0,1},{1,0},{2,3},{3,2},{4,5},{5,4},{6,7},{7,6},{8,9},{9,8},{10,11... | collective-permute-start | bytes 786440 | tf_op jit(solution)/shard_map/ppermute | solution.py:206
  13.6 6.6 %copy-start.1 = (bf16[2,128,512]{2,1,0:T(8,128)(2,1)}, bf16[2,128,512]{2,1,0:T(8,128)(2,1)S(1)}, u32[]{:S(2)}) copy-start(bf16[2,128,512]{2,1,0:T(8,128)(2,1)S(1)} %collective-permute-done.1.next_hbm) | copy-start | bytes 786436
  17.6 2.5 %copy-start.2 = (bf16[2,128,512]{2,1,0:T(8,128)(2,1)}, bf16[2,128,512]{2,1,0:T(8,128)(2,1)S(1)}, u32[]{:S(2)}) copy-start(bf16[2,128,512]{2,1,0:T(8,128)(2,1)S(1)} %collective-permute-done.prev_hbm) | copy-start | bytes 786436
  17.7 2.4 %collective-permute-start.3 = (bf16[2,128,512]{2,1,0:T(8,128)(2,1)S(1)}, bf16[2,128,512]{2,1,0:T(8,128)(2,1)S(1)}, u32[]{:S(2)}, u32[]{:S(2)}) collective-permute-start(bf16[2,128,512]{2,1,0:T(8,128)(2,1)S(1)} %broadcast_select_fusion), channel_id=1, source_target_pairs={{0,1},{1,0},{2,3},{3,2},{4,5},{5,4},{6,7},{7,6},{8,9},{9,8},{10,11... | collective-permute-start | bytes 786440 | tf_op jit(solution)/shard_map/ppermute | solution.py:208
  20.1 0.7 %copy-start.3 = (bf16[2,128,512]{2,1,0:T(8,128)(2,1)}, bf16[2,128,512]{2,1,0:T(8,128)(2,1)S(1)}, u32[]{:S(2)}) copy-start(bf16[2,128,512]{2,1,0:T(8,128)(2,1)S(1)} %collective-permute-done.2.partner_hbm) | copy-start | bytes 786436
  20.1 0.8 %copy-start.4 = (bf16[2,128,512]{2,1,0:T(8,128)(2,1)}, bf16[2,128,512]{2,1,0:T(8,128)(2,1)S(1)}, u32[]{:S(2)}) copy-start(bf16[2,128,512]{2,1,0:T(8,128)(2,1)S(1)} %collective-permute-done.3.sel_hbm) | copy-start | bytes 786436
  28.1 7.4 %collective-permute-start.4 = (bf16[64,1024]{1,0:T(8,128)(2,1)}, bf16[64,1024]{1,0:T(8,128)(2,1)S(1)}, u32[]{:S(2)}, u32[]{:S(2)}) collective-permute-start(bf16[64,1024]{1,0:T(8,128)(2,1)} %get-tuple-element.10), channel_id=1, source_target_pairs={{1,2},{3,4},{5,6},{7,8},{9,10},{11,12},{13,14},{2,1},{4,3},{6,5},{... | collective-permute-start | bytes 393224 | tf_op jit(solution)/shard_map/ppermute | solution.py:246
  30.4 5.2 %collective-permute-start.5 = (bf16[64,1024]{1,0:T(8,128)(2,1)}, bf16[64,1024]{1,0:T(8,128)(2,1)S(1)}, u32[]{:S(2)}, u32[]{:S(2)}) collective-permute-start(bf16[64,1024]{1,0:T(8,128)(2,1)} %get-tuple-element.11), channel_id=1, source_target_pairs={{0,1},{1,0},{2,3},{3,2},{4,5},{5,4},{6,7},{7,6},{8,9},{9,8},{10,11... | collective-permute-start | bytes 393224 | tf_op jit(solution)/shard_map/ppermute | solution.py:247
  35.5 0.7 %copy-start.5 = (bf16[64,1024]{1,0:T(8,128)(2,1)}, bf16[64,1024]{1,0:T(8,128)(2,1)S(1)}, u32[]{:S(2)}) copy-start(bf16[64,1024]{1,0:T(8,128)(2,1)S(1)} %collective-permute-done.4.cross_ref) | copy-start | bytes 393220
  35.5 0.7 %copy-start.6 = (bf16[64,1024]{1,0:T(8,128)(2,1)}, bf16[64,1024]{1,0:T(8,128)(2,1)S(1)}, u32[]{:S(2)}) copy-start(bf16[64,1024]{1,0:T(8,128)(2,1)S(1)} %collective-permute-done.5.pairg_ref) | copy-start | bytes 393220

commit v7 on v6

--- a/solution.py
+++ b/solution.py
@@ -32,12 +32,14 @@
 
 
 def attention_kernel(
-    meta_ref, len_ref, table_ref, bias_t_ref, q_ref,
+    meta_ref, len_ref, table_ref, bias_t_ref, q_hbm,
     prev_hbm, next_hbm, own_hbm, partner_hbm, sel_hbm,
-    x_ref, gain_ref, ow_hbm, ew_hbm,
+    x_hbm, gain_ref, ow_hbm, ew_hbm,
     mid_ref, gated_ref, cross_ref, partner_ref,
-    ow_vmem, ew_vmem, sems, att_ref, win_ref,
+    ow_vmem, ew_vmem, sems, att_ref, win_ref, q_ref, x_ref,
 ):
+    q_copy = pltpu.make_async_copy(q_hbm, q_ref, sems.at[7])
+    q_copy.start()
     base = meta_ref[0]
     core = meta_ref[1]
     planes = prev_hbm.shape[0]
@@ -56,7 +58,9 @@
         copy.start()
     ow_copy = pltpu.make_async_copy(ow_hbm, ow_vmem, sems.at[0])
     ew_copy = pltpu.make_async_copy(ew_hbm, ew_vmem, sems.at[1])
+    x_copy = pltpu.make_async_copy(x_hbm, x_ref, sems.at[8])
     ow_copy.start()
+    x_copy.start()
     ew_copy.start()
     blocks = win_ref.shape[0] // planes
     rows, att_width = q_ref.shape
@@ -89,6 +93,7 @@
 
     for copy in copies:
         copy.wait()
+    q_copy.wait()
     scaling = head_width ** (-0.5)
     lane = lax.broadcasted_iota(jnp.int32, (rows, LANES), 1)
     per_pair = LANES // head_width
@@ -118,6 +123,7 @@
         att_ref[:, cols] = result.astype(jnp.bfloat16)
 
     ow_copy.wait()
+    x_copy.wait()
     projected = jnp.dot(att_ref[...], ow_vmem[...], preferred_element_type=jnp.float32)
     mid = (x_ref[...].astype(jnp.float32) + projected).astype(jnp.bfloat16)
     mid_ref[...] = mid
@@ -134,11 +140,22 @@
 
 
 def conv_kernel(
-    meta_ref, gated_ref, cross_ref, pairg_ref, taps_ref, gain_ref, mid_ref, sw_hbm,
-    out_ref, win_ref, conv_ref, sw_vmem, sems,
+    meta_ref, gated_hbm, cross_hbm, pairg_hbm, taps_ref, gain_ref, mid_hbm, sw_hbm,
+    out_ref, win_ref, conv_ref, sw_vmem, sems, gated_ref, cross_ref, pairg_ref, mid_ref,
 ):
+    loads = [
+        pltpu.make_async_copy(gated_hbm, gated_ref, sems.at[1]),
+        pltpu.make_async_copy(cross_hbm, cross_ref, sems.at[2]),
+        pltpu.make_async_copy(pairg_hbm, pairg_ref, sems.at[3]),
+    ]
+    for load in loads:
+        load.start()
     sw_copy = pltpu.make_async_copy(sw_hbm, sw_vmem, sems.at[0])
+    mid_copy = pltpu.make_async_copy(mid_hbm, mid_ref, sems.at[4])
     sw_copy.start()
+    mid_copy.start()
+    for load in loads:
+        load.wait()
     half = cross_ref.shape[0]
     rows, model_width = mid_ref.shape
     first_core = meta_ref[1] == 0
@@ -163,6 +180,7 @@
     inner = layer_norm(conv_ref[...], gain_ref[...])
     activated = (inner * sigmoid(inner)).astype(jnp.bfloat16)
     sw_copy.wait()
+    mid_copy.wait()
     shrunk = jnp.dot(activated, sw_vmem[...], preferred_element_type=jnp.float32)
     out_ref[...] = (mid_ref[...].astype(jnp.float32) + shrunk).astype(out_ref.dtype)
 
@@ -223,14 +241,16 @@
             jax.ShapeDtypeStruct((half, model_width), jnp.bfloat16),
             jax.ShapeDtypeStruct((half, model_width), jnp.bfloat16),
         ),
-        in_specs=[smem, smem, vmem, vmem, vmem] + [anywhere] * 5 + [vmem, vmem, anywhere, anywhere],
+        in_specs=[smem, smem, vmem, vmem, anywhere] + [anywhere] * 5 + [anywhere, vmem, anywhere, anywhere],
         out_specs=(vmem, vmem, vmem, vmem),
         scratch_shapes=[
             pltpu.VMEM((att_width, model_width), jnp.bfloat16),
             pltpu.VMEM((model_width, 2 * model_width), jnp.bfloat16),
-            pltpu.SemaphoreType.DMA((7,)),
+            pltpu.SemaphoreType.DMA((9,)),
             pltpu.VMEM((rows, att_width), jnp.bfloat16),
             pltpu.VMEM((len(order) * packed.shape[0], rows, att_width), jnp.bfloat16),
+            pltpu.VMEM((rows, att_width), jnp.bfloat16),
+            pltpu.VMEM((rows, model_width), jnp.bfloat16),
         ],
         cost_estimate=pl.CostEstimate(
             flops=attn_flops, transcendentals=heads * rows * window + rows * model_width, bytes_accessed=attn_bytes
@@ -250,13 +270,17 @@
     return pl.pallas_call(
         conv_kernel,
         out_shape=jax.ShapeDtypeStruct((rows, model_width), jnp.bfloat16),
-        in_specs=[smem] + [vmem] * 6 + [anywhere],
+        in_specs=[smem, anywhere, anywhere, anywhere, vmem, vmem, anywhere, anywhere],
         out_specs=vmem,
         scratch_shapes=[
             pltpu.VMEM((rows + 2 * half, model_width), jnp.float32),
             pltpu.VMEM((rows, model_width), jnp.float32),
             pltpu.VMEM((model_width, model_width), jnp.bfloat16),
-            pltpu.SemaphoreType.DMA((1,)),
+            pltpu.SemaphoreType.DMA((5,)),
+            pltpu.VMEM((rows, model_width), jnp.bfloat16),
+            pltpu.VMEM((half, model_width), jnp.bfloat16),
+            pltpu.VMEM((half, model_width), jnp.bfloat16),
+            pltpu.VMEM((rows, model_width), jnp.bfloat16),
         ],
         cost_estimate=pl.CostEstimate(
             flops=conv_flops, transcendentals=rows * model_width, bytes_accessed=conv_bytes

time: 41.4 us -> 42 us (1.014)
  Pallas kernels: 12.1 us -> 12.7 us
    pallas_call x1, Pallas kernels: 4.88 us -> 5.65 us  [on_device(): pl.pallas_call(conv_kernel, out_shape=jax.ShapeDtypeStruct((rows, model_w...]
where the time goes in v7:
time: 42 us; the launch traced here: 41.7 us
  waiting for transfers between devices  14.2 us (34%)
  Pallas kernels  12.7 us (30%)
  starting transfers between devices  10.3 us (25%)
  local copies, waits for them, and re-layouts  2.77 us (7%)
  other arithmetic  1.6 us (4%)
    ppermute x2, waiting for transfers between devices, lin_shift(): lax.ppermute(value, ('chip', 'core'), [(s, s + steps) for s in range(lead...  9.14 us
    pallas_call x1, Pallas kernels, on_device(): pl.pallas_call(attention_kernel, out_shape=(jax.ShapeDtypeStruct((rows, m...  7.06 us
    ppermute x2, starting transfers between devices, lin_shift(): lax.ppermute(value, ('chip', 'core'), [(s, s + steps) for s in range(lead...  6.18 us
    pallas_call x1, Pallas kernels, on_device(): pl.pallas_call(conv_kernel, out_shape=jax.ShapeDtypeStruct((rows, model_w...  5.65 us
    ppermute x1, waiting for transfers between devices, on_device(): cross_recv = lax.ppermute(cross_send, ('chip', 'core'), inward)  5.1 us
    ppermute x1, starting transfers between devices, on_device(): cross_recv = lax.ppermute(cross_send, ('chip', 'core'), inward)  2.21 us
    unnamed x14, local copies, waits for them, and re-layouts  1.49 us
    ppermute x1, starting transfers between devices, on_device(): partner = lax.ppermute(packed, 'core', swap)  1.3 us
  transfers between devices with their start and end apart: 6, of which 3 were waited for; matrix products, arithmetic and copies ran while one was open for 5% of the time, Pallas kernels for 0%

profile of v7, /device:TPU:21, one launch (start us, length us, event | category | flops | bytes accessed | tf_op | source)
XLA Modules:
  0.0 41.7 jit_solution(18418458776070540063)
XLA Ops:
  0.0 1.0 %pad_maximum_fusion.own_hbm = bf16[2,128,512]{2,1,0:T(8,128)(2,1)S(1)} fusion(bf16[1,128,512]{2,1,0:T(8,128)(2,1)} %bitcast.7, bf16[1,128,512]{2,1,0:T(8,128)(2,1)} %bitcast.8), kind=kLoop, calls=%fused_computation | loop fusion | flops 131072 | bytes 524288 | tf_op jit(solution)/shard_map/stack | solution.py:220
  1.0 0.0 copy-start
  1.0 2.1 %collective-permute-start.1 = (bf16[2,128,512]{2,1,0:T(8,128)(2,1)S(1)}, bf16[2,128,512]{2,1,0:T(8,128)(2,1)S(1)}, u32[]{:S(2)}, u32[]{:S(2)}) collective-permute-start(bf16[2,128,512]{2,1,0:T(8,128)(2,1)S(1)} %pad_maximum_fusion.own_hbm), channel_id=1, source_target_pairs={{2,0},{3,1},{4,2},{5,3},{6,4},{7,5},{8,6},{9,7},{10,8},{11,9},{12,... | collective-permute-start | bytes 786440 | tf_op jit(solution)/shard_map/ppermute | solution.py:214
  3.1 4.0 %collective-permute-start = (bf16[2,128,512]{2,1,0:T(8,128)(2,1)S(1)}, bf16[2,128,512]{2,1,0:T(8,128)(2,1)S(1)}, u32[]{:S(2)}, u32[]{:S(2)}) collective-permute-start(bf16[2,128,512]{2,1,0:T(8,128)(2,1)S(1)} %pad_maximum_fusion.own_hbm), channel_id=1, source_target_pairs={{0,2},{1,3},{2,4},{3,5},{4,6},{5,7},{6,8},{7,9},{8,10},{9,11},{10,... | collective-permute-start | bytes 786440 | tf_op jit(solution)/shard_map/ppermute | solution.py:214
  7.2 1.3 %collective-permute-start.2 = (bf16[2,128,512]{2,1,0:T(8,128)(2,1)S(1)}, bf16[2,128,512]{2,1,0:T(8,128)(2,1)S(1)}, u32[]{:S(2)}, u32[]{:S(2)}) collective-permute-start(bf16[2,128,512]{2,1,0:T(8,128)(2,1)S(1)} %pad_maximum_fusion.own_hbm), channel_id=1, source_target_pairs={{0,1},{1,0},{2,3},{3,2},{4,5},{5,4},{6,7},{7,6},{8,9},{9,8},{10,11... | collective-permute-start | bytes 786440 | tf_op jit(solution)/shard_map/ppermute | solution.py:224
  8.5 5.1 %collective-permute-done.1.next_hbm = bf16[2,128,512]{2,1,0:T(8,128)(2,1)S(1)} collective-permute-done((bf16[2,128,512]{2,1,0:T(8,128)(2,1)S(1)}, bf16[2,128,512]{2,1,0:T(8,128)(2,1)S(1)}, u32[]{:S(2)}, u32[]{:S(2)}) %collective-permute-start.1) | collective-permute-done | bytes 262176 | tf_op jit(solution)/shard_map/ppermute | solution.py:214
  13.6 0.0 copy-start.1
  13.6 4.1 %collective-permute-done.prev_hbm = bf16[2,128,512]{2,1,0:T(8,128)(2,1)S(1)} collective-permute-done((bf16[2,128,512]{2,1,0:T(8,128)(2,1)S(1)}, bf16[2,128,512]{2,1,0:T(8,128)(2,1)S(1)}, u32[]{:S(2)}, u32[]{:S(2)}) %collective-permute-start) | collective-permute-done | bytes 262176 | tf_op jit(solution)/shard_map/ppermute | solution.py:214
  17.6 0.0 copy-start.2
  17.7 0.6 %collective-permute-start.3 = (bf16[2,128,512]{2,1,0:T(8,128)(2,1)S(1)}, bf16[2,128,512]{2,1,0:T(8,128)(2,1)S(1)}, u32[]{:S(2)}, u32[]{:S(2)}) collective-permute-start(bf16[2,128,512]{2,1,0:T(8,128)(2,1)S(1)} %broadcast_select_fusion), channel_id=1, source_target_pairs={{0,1},{1,0},{2,3},{3,2},{4,5},{5,4},{6,7},{7,6},{8,9},{9,8},{10,11... | collective-permute-start | bytes 786440 | tf_op jit(solution)/shard_map/ppermute | solution.py:226
  18.2 0.7 %pad.4 = s32[768]{0:T(1024)S(1)} pad(s32[767]{0:T(1024)} %param.18, s32[]{:T(128)} %constant.13.clone.1), padding=0_1 | pad | bytes 6144 | tf_op jit(solution)/shard_map/jit(_pad)/pad | solution.py:217
  18.9 0.6 %reshape.9.table_ref = s32[1,768]{1,0:T(1,128)} reshape(s32[768]{0:T(1024)S(1)} %pad.4) | data formatting | bytes 6144 | tf_op jit(solution)/shard_map/reshape | solution.py:217
  19.5 0.6 %pad_add_fusion.meta_ref = s32[2]{0:T(128)} fusion(s32[1]{0:T(128)} %bitcast.1, s32[1]{0:T(128)} %bitcast), kind=kLoop, calls=%fused_computation.2 | loop fusion | flops 2 | bytes 16 | tf_op jit(solution)/shard_map/stack | solution.py:210
  20.1 0.0 collective-permute-done.2.partner_hbm
  20.1 0.0 copy-start.3
  20.1 0.0 collective-permute-done.3.sel_hbm
  20.1 0.0 copy-start.4
  20.1 0.0 copy-done
  20.1 0.0 copy-done.1
  20.1 0.0 copy-done.2
  20.2 0.7 %copy-done.3 = bf16[2,128,512]{2,1,0:T(8,128)(2,1)} copy-done((bf16[2,128,512]{2,1,0:T(8,128)(2,1)}, bf16[2,128,512]{2,1,0:T(8,128)(2,1)S(1)}, u32[]{:S(2)}) %copy-start.3) | copy-done | bytes 262168
  20.8 0.1 copy-done.4
  20.9 7.1 %attention_glu.1 = (bf16[128,1024]{1,0:T(8,128)(2,1)}, bf16[128,1024]{1,0:T(8,128)(2,1)}, bf16[64,1024]{1,0:T(8,128)(2,1)}, bf16[64,1024]{1,0:T(8,128)(2,1)}) custom-call(s32[2]{0:T(128)} %pad_add_fusion.meta_ref, s32[16]{0:T(128)} %len_ref.1, s32[1,768]{1,0:T(1,128)} %reshape.9.table_ref, f32[8,32]{1,0:T(8,128)} %bitcast.9, bf16[128,512]{1,0:T(8,128)(2,1)} %q_hbm.1, ...), custom_call_target="tpu_custom_call" | custom-call | flops 1006632960 | bytes 7208960 | tf_op jit(solution)/shard_map/attention_glu/pallas_call | solution.py:236
  28.0 2.2 %collective-permute-start.4 = (bf16[64,1024]{1,0:T(8,128)(2,1)}, bf16[64,1024]{1,0:T(8,128)(2,1)S(1)}, u32[]{:S(2)}, u32[]{:S(2)}) collective-permute-start(bf16[64,1024]{1,0:T(8,128)(2,1)} %get-tuple-element.10), channel_id=1, source_target_pairs={{1,2},{3,4},{5,6},{7,8},{9,10},{11,12},{13,14},{2,1},{4,3},{6,5},{... | collective-permute-start | bytes 393224 | tf_op jit(solution)/shard_map/ppermute | solution.py:266
  30.2 0.1 collective-permute-start.5
  30.3 5.1 %collective-permute-done.4.cross_hbm = bf16[64,1024]{1,0:T(8,128)(2,1)S(1)} collective-permute-done((bf16[64,1024]{1,0:T(8,128)(2,1)}, bf16[64,1024]{1,0:T(8,128)(2,1)S(1)}, u32[]{:S(2)}, u32[]{:S(2)}) %collective-permute-start.4) | collective-permute-done | bytes 131104 | tf_op jit(solution)/shard_map/ppermute | solution.py:266
  35.4 0.0 copy-start.5
  35.4 0.0 collective-permute-done.5.pairg_hbm
  35.4 0.0 copy-start.6
  35.4 0.6 %copy-done.5 = bf16[64,1024]{1,0:T(8,128)(2,1)} copy-done((bf16[64,1024]{1,0:T(8,128)(2,1)}, bf16[64,1024]{1,0:T(8,128)(2,1)S(1)}, u32[]{:S(2)}) %copy-start.5) | copy-done | bytes 131096
  36.0 0.0 copy-done.6
  36.1 5.7 %conv_shrink.1 = bf16[128,1024]{1,0:T(8,128)(2,1)} custom-call(s32[2]{0:T(128)} %pad_add_fusion.meta_ref, bf16[128,1024]{1,0:T(8,128)(2,1)} %get-tuple-element.9.gated_hbm, bf16[64,1024]{1,0:T(8,128)(2,1)} %copy-done.5, bf16[64,1024]{1,0:T(8,128)(2,1)} %copy-done.6, f32[31,1024]{1,0:T(8,128)} %taps_ref.1, f32[1,1024]{1,0:T(1,128)} %bitcast.11, ...), custom_call_target="tpu_custom_call" | custom-call | flops 276561920 | bytes 3272704 | tf_op jit(solution)/shard_map/conv_shrink/pallas_call | solution.py:270
  (1 shorter events, 0.0 us)
Async XLA Ops:
  1.0 19.1 %copy-start = (bf16[2,128,512]{2,1,0:T(8,128)(2,1)}, bf16[2,128,512]{2,1,0:T(8,128)(2,1)S(1)}, u32[]{:S(2)}) copy-start(bf16[2,128,512]{2,1,0:T(8,128)(2,1)S(1)} %pad_maximum_fusion.own_hbm) | copy-start | bytes 786436
  1.0 12.6 %collective-permute-start.1 = (bf16[2,128,512]{2,1,0:T(8,128)(2,1)S(1)}, bf16[2,128,512]{2,1,0:T(8,128)(2,1)S(1)}, u32[]{:S(2)}, u32[]{:S(2)}) collective-permute-start(bf16[2,128,512]{2,1,0:T(8,128)(2,1)S(1)} %pad_maximum_fusion.own_hbm), channel_id=1, source_target_pairs={{2,0},{3,1},{4,2},{5,3},{6,4},{7,5},{8,6},{9,7},{10,8},{11,9},{12,... | collective-permute-start | bytes 786440 | tf_op jit(solution)/shard_map/ppermute | solution.py:214
  3.1 14.5 %collective-permute-start = (bf16[2,128,512]{2,1,0:T(8,128)(2,1)S(1)}, bf16[2,128,512]{2,1,0:T(8,128)(2,1)S(1)}, u32[]{:S(2)}, u32[]{:S(2)}) collective-permute-start(bf16[2,128,512]{2,1,0:T(8,128)(2,1)S(1)} %pad_maximum_fusion.own_hbm), channel_id=1, source_target_pairs={{0,2},{1,3},{2,4},{3,5},{4,6},{5,7},{6,8},{7,9},{8,10},{9,11},{10,... | collective-permute-start | bytes 786440 | tf_op jit(solution)/shard_map/ppermute | solution.py:214
  7.2 12.9 %collective-permute-start.2 = (bf16[2,128,512]{2,1,0:T(8,128)(2,1)S(1)}, bf16[2,128,512]{2,1,0:T(8,128)(2,1)S(1)}, u32[]{:S(2)}, u32[]{:S(2)}) collective-permute-start(bf16[2,128,512]{2,1,0:T(8,128)(2,1)S(1)} %pad_maximum_fusion.own_hbm), channel_id=1, source_target_pairs={{0,1},{1,0},{2,3},{3,2},{4,5},{5,4},{6,7},{7,6},{8,9},{9,8},{10,11... | collective-permute-start | bytes 786440 | tf_op jit(solution)/shard_map/ppermute | solution.py:224
  13.6 6.6 %copy-start.1 = (bf16[2,128,512]{2,1,0:T(8,128)(2,1)}, bf16[2,128,512]{2,1,0:T(8,128)(2,1)S(1)}, u32[]{:S(2)}) copy-start(bf16[2,128,512]{2,1,0:T(8,128)(2,1)S(1)} %collective-permute-done.1.next_hbm) | copy-start | bytes 786436
  17.6 2.5 %copy-start.2 = (bf16[2,128,512]{2,1,0:T(8,128)(2,1)}, bf16[2,128,512]{2,1,0:T(8,128)(2,1)S(1)}, u32[]{:S(2)}) copy-start(bf16[2,128,512]{2,1,0:T(8,128)(2,1)S(1)} %collective-permute-done.prev_hbm) | copy-start | bytes 786436
  17.7 2.4 %collective-permute-start.3 = (bf16[2,128,512]{2,1,0:T(8,128)(2,1)S(1)}, bf16[2,128,512]{2,1,0:T(8,128)(2,1)S(1)}, u32[]{:S(2)}, u32[]{:S(2)}) collective-permute-start(bf16[2,128,512]{2,1,0:T(8,128)(2,1)S(1)} %broadcast_select_fusion), channel_id=1, source_target_pairs={{0,1},{1,0},{2,3},{3,2},{4,5},{5,4},{6,7},{7,6},{8,9},{9,8},{10,11... | collective-permute-start | bytes 786440 | tf_op jit(solution)/shard_map/ppermute | solution.py:226
  20.1 0.7 %copy-start.3 = (bf16[2,128,512]{2,1,0:T(8,128)(2,1)}, bf16[2,128,512]{2,1,0:T(8,128)(2,1)S(1)}, u32[]{:S(2)}) copy-start(bf16[2,128,512]{2,1,0:T(8,128)(2,1)S(1)} %collective-permute-done.2.partner_hbm) | copy-start | bytes 786436
  20.1 0.8 %copy-start.4 = (bf16[2,128,512]{2,1,0:T(8,128)(2,1)}, bf16[2,128,512]{2,1,0:T(8,128)(2,1)S(1)}, u32[]{:S(2)}) copy-start(bf16[2,128,512]{2,1,0:T(8,128)(2,1)S(1)} %collective-permute-done.3.sel_hbm) | copy-start | bytes 786436
  28.0 7.4 %collective-permute-start.4 = (bf16[64,1024]{1,0:T(8,128)(2,1)}, bf16[64,1024]{1,0:T(8,128)(2,1)S(1)}, u32[]{:S(2)}, u32[]{:S(2)}) collective-permute-start(bf16[64,1024]{1,0:T(8,128)(2,1)} %get-tuple-element.10), channel_id=1, source_target_pairs={{1,2},{3,4},{5,6},{7,8},{9,10},{11,12},{13,14},{2,1},{4,3},{6,5},{... | collective-permute-start | bytes 393224 | tf_op jit(solution)/shard_map/ppermute | solution.py:266
  30.2 5.2 %collective-permute-start.5 = (bf16[64,1024]{1,0:T(8,128)(2,1)}, bf16[64,1024]{1,0:T(8,128)(2,1)S(1)}, u32[]{:S(2)}, u32[]{:S(2)}) collective-permute-start(bf16[64,1024]{1,0:T(8,128)(2,1)} %get-tuple-element.11), channel_id=1, source_target_pairs={{0,1},{1,0},{2,3},{3,2},{4,5},{5,4},{6,7},{7,6},{8,9},{9,8},{10,11... | collective-permute-start | bytes 393224 | tf_op jit(solution)/shard_map/ppermute | solution.py:267
  35.4 0.7 %copy-start.5 = (bf16[64,1024]{1,0:T(8,128)(2,1)}, bf16[64,1024]{1,0:T(8,128)(2,1)S(1)}, u32[]{:S(2)}) copy-start(bf16[64,1024]{1,0:T(8,128)(2,1)S(1)} %collective-permute-done.4.cross_hbm) | copy-start | bytes 393220
  35.4 0.7 %copy-start.6 = (bf16[64,1024]{1,0:T(8,128)(2,1)}, bf16[64,1024]{1,0:T(8,128)(2,1)S(1)}, u32[]{:S(2)}) copy-start(bf16[64,1024]{1,0:T(8,128)(2,1)S(1)} %collective-permute-done.5.pairg_hbm) | copy-start | bytes 393220

commit v8 on v6

--- a/solution.py
+++ b/solution.py
@@ -38,6 +38,10 @@
     mid_ref, gated_ref, cross_ref, partner_ref,
     ow_vmem, ew_vmem, sems, att_ref, win_ref,
 ):
+    ow_copy = pltpu.make_async_copy(ow_hbm, ow_vmem, sems.at[0])
+    ew_copy = pltpu.make_async_copy(ew_hbm, ew_vmem, sems.at[1])
+    ow_copy.start()
+    ew_copy.start()
     base = meta_ref[0]
     core = meta_ref[1]
     planes = prev_hbm.shape[0]
@@ -54,10 +58,6 @@
     ]
     for copy in copies:
         copy.start()
-    ow_copy = pltpu.make_async_copy(ow_hbm, ow_vmem, sems.at[0])
-    ew_copy = pltpu.make_async_copy(ew_hbm, ew_vmem, sems.at[1])
-    ow_copy.start()
-    ew_copy.start()
     blocks = win_ref.shape[0] // planes
     rows, att_width = q_ref.shape
     heads = bias_t_ref.shape[0]
@@ -134,11 +134,9 @@
 
 
 def conv_kernel(
-    meta_ref, gated_ref, cross_ref, pairg_ref, taps_ref, gain_ref, mid_ref, sw_hbm,
-    out_ref, win_ref, conv_ref, sw_vmem, sems,
+    meta_ref, gated_ref, cross_ref, pairg_ref, taps_ref, gain_ref, mid_ref, sw_vmem,
+    out_ref, win_ref, conv_ref,
 ):
-    sw_copy = pltpu.make_async_copy(sw_hbm, sw_vmem, sems.at[0])
-    sw_copy.start()
     half = cross_ref.shape[0]
     rows, model_width = mid_ref.shape
     first_core = meta_ref[1] == 0
@@ -162,7 +160,6 @@
     lax.fori_loop(0, model_width // LANES, chunk, 0)
     inner = layer_norm(conv_ref[...], gain_ref[...])
     activated = (inner * sigmoid(inner)).astype(jnp.bfloat16)
-    sw_copy.wait()
     shrunk = jnp.dot(activated, sw_vmem[...], preferred_element_type=jnp.float32)
     out_ref[...] = (mid_ref[...].astype(jnp.float32) + shrunk).astype(out_ref.dtype)
 
@@ -238,7 +235,8 @@
         name="attention_glu",
     )(
         meta, utterance_lengths, table, bias_t, query_proj, from_prev, from_next, packed, partner, partner_sel,
-        frames_in, norm_gain.reshape(1, -1), out_weight, expand_weight,
+        frames_in, norm_gain.reshape(1, -1),
+        out_weight, expand_weight,
     )
 
     chips = count // cores
@@ -250,19 +248,20 @@
     return pl.pallas_call(
         conv_kernel,
         out_shape=jax.ShapeDtypeStruct((rows, model_width), jnp.bfloat16),
-        in_specs=[smem] + [vmem] * 6 + [anywhere],
+        in_specs=[smem] + [vmem] * 7,
         out_specs=vmem,
         scratch_shapes=[
             pltpu.VMEM((rows + 2 * half, model_width), jnp.float32),
             pltpu.VMEM((rows, model_width), jnp.float32),
-            pltpu.VMEM((model_width, model_width), jnp.bfloat16),
-            pltpu.SemaphoreType.DMA((1,)),
         ],
         cost_estimate=pl.CostEstimate(
             flops=conv_flops, transcendentals=rows * model_width, bytes_accessed=conv_bytes
         ),
         name="conv_shrink",
-    )(meta, gated, cross_recv, partner_recv, depth_taps, inner_gain.reshape(1, -1), mid, shrink_weight)
+    )(
+        meta, gated, cross_recv, partner_recv, depth_taps, inner_gain.reshape(1, -1), mid,
+        pltpu.with_memory_space_constraint(shrink_weight, pltpu.VMEM),
+    )
 
 
 def solution(mesh):

time: 41.4 us -> 43.7 us (1.056)
  Pallas kernels: 12.1 us -> 13.5 us
  other arithmetic: 1.6 us -> 2.53 us
    pallas_call x1, Pallas kernels: 7.2 us -> 8.73 us  [on_device(): pl.pallas_call(attention_kernel, out_shape=(jax.ShapeDtypeStruct((rows, m...]
    select_n x1, other arithmetic: 0.03 us -> 0.79 us  [on_device(): sel = jnp.where(core == 0, from_next, from_prev)]
    unnamed x14 -> x16, local copies, waits for them, and re-layouts: 1.49 us -> 1.5 us
  transfers between devices with their start and end apart: 6 -> 6, of which waited for: 3 -> 3; matrix products, arithmetic and copies ran while one was open for 5% -> 6% of each run, Pallas kernels for 0% -> 0%
where the time goes in v8:
time: 43.7 us; the launch traced here: 43.4 us
  waiting for transfers between devices  14.3 us (33%)
  Pallas kernels  13.5 us (31%)
  starting transfers between devices  10.2 us (23%)
  local copies, waits for them, and re-layouts  2.79 us (6%)
  other arithmetic  2.53 us (6%)
    ppermute x2, waiting for transfers between devices, lin_shift(): lax.ppermute(value, ('chip', 'core'), [(s, s + steps) for s in range(lead...  9.14 us
    pallas_call x1, Pallas kernels, on_device(): pl.pallas_call(attention_kernel, out_shape=(jax.ShapeDtypeStruct((rows, m...  8.73 us
    ppermute x2, starting transfers between devices, lin_shift(): lax.ppermute(value, ('chip', 'core'), [(s, s + steps) for s in range(lead...  6.18 us
    ppermute x1, waiting for transfers between devices, on_device(): cross_recv = lax.ppermute(cross_send, ('chip', 'core'), inward)  5.14 us
    pallas_call x1, Pallas kernels, on_device(): pl.pallas_call(conv_kernel, out_shape=jax.ShapeDtypeStruct((rows, model_w...  4.75 us
    ppermute x1, starting transfers between devices, on_device(): cross_recv = lax.ppermute(cross_send, ('chip', 'core'), inward)  2.17 us
    unnamed x16, local copies, waits for them, and re-layouts  1.5 us
    ppermute x1, starting transfers between devices, on_device(): partner = lax.ppermute(packed, 'core', swap)  1.3 us
  transfers between devices with their start and end apart: 6, of which 3 were waited for; matrix products, arithmetic and copies ran while one was open for 6% of the time, Pallas kernels for 0%

profile of v8, /device:TPU:21, one launch (start us, length us, event | category | flops | bytes accessed | tf_op | source)
XLA Modules:
  0.0 43.4 jit_solution(516291619410802724)
XLA Ops:
  0.0 0.0 copy-start
  0.0 1.1 %pad_maximum_fusion.own_hbm = bf16[2,128,512]{2,1,0:T(8,128)(2,1)S(1)} fusion(bf16[1,128,512]{2,1,0:T(8,128)(2,1)} %bitcast.7, bf16[1,128,512]{2,1,0:T(8,128)(2,1)} %bitcast.8), kind=kLoop, calls=%fused_computation | loop fusion | flops 131072 | bytes 524288 | tf_op jit(solution)/shard_map/stack | solution.py:199
  1.1 0.0 copy-start.1
  1.2 2.1 %collective-permute-start.1 = (bf16[2,128,512]{2,1,0:T(8,128)(2,1)S(1)}, bf16[2,128,512]{2,1,0:T(8,128)(2,1)S(1)}, u32[]{:S(2)}, u32[]{:S(2)}) collective-permute-start(bf16[2,128,512]{2,1,0:T(8,128)(2,1)S(1)} %pad_maximum_fusion.own_hbm), channel_id=1, source_target_pairs={{2,0},{3,1},{4,2},{5,3},{6,4},{7,5},{8,6},{9,7},{10,8},{11,9},{12,... | collective-permute-start | bytes 786440 | tf_op jit(solution)/shard_map/ppermute | solution.py:193
  3.3 4.0 %collective-permute-start = (bf16[2,128,512]{2,1,0:T(8,128)(2,1)S(1)}, bf16[2,128,512]{2,1,0:T(8,128)(2,1)S(1)}, u32[]{:S(2)}, u32[]{:S(2)}) collective-permute-start(bf16[2,128,512]{2,1,0:T(8,128)(2,1)S(1)} %pad_maximum_fusion.own_hbm), channel_id=1, source_target_pairs={{0,2},{1,3},{2,4},{3,5},{4,6},{5,7},{6,8},{7,9},{8,10},{9,11},{10,... | collective-permute-start | bytes 786440 | tf_op jit(solution)/shard_map/ppermute | solution.py:193
  7.4 1.3 %collective-permute-start.2 = (bf16[2,128,512]{2,1,0:T(8,128)(2,1)S(1)}, bf16[2,128,512]{2,1,0:T(8,128)(2,1)S(1)}, u32[]{:S(2)}, u32[]{:S(2)}) collective-permute-start(bf16[2,128,512]{2,1,0:T(8,128)(2,1)S(1)} %pad_maximum_fusion.own_hbm), channel_id=1, source_target_pairs={{0,1},{1,0},{2,3},{3,2},{4,5},{5,4},{6,7},{7,6},{8,9},{9,8},{10,11... | collective-permute-start | bytes 786440 | tf_op jit(solution)/shard_map/ppermute | solution.py:203
  8.7 5.1 %collective-permute-done.1.next_hbm = bf16[2,128,512]{2,1,0:T(8,128)(2,1)S(1)} collective-permute-done((bf16[2,128,512]{2,1,0:T(8,128)(2,1)S(1)}, bf16[2,128,512]{2,1,0:T(8,128)(2,1)S(1)}, u32[]{:S(2)}, u32[]{:S(2)}) %collective-permute-start.1) | collective-permute-done | bytes 262176 | tf_op jit(solution)/shard_map/ppermute | solution.py:193
  13.7 0.0 copy-start.2
  13.7 4.1 %collective-permute-done.prev_hbm = bf16[2,128,512]{2,1,0:T(8,128)(2,1)S(1)} collective-permute-done((bf16[2,128,512]{2,1,0:T(8,128)(2,1)S(1)}, bf16[2,128,512]{2,1,0:T(8,128)(2,1)S(1)}, u32[]{:S(2)}, u32[]{:S(2)}) %collective-permute-start) | collective-permute-done | bytes 262176 | tf_op jit(solution)/shard_map/ppermute | solution.py:193
  17.8 0.0 copy-start.3
  17.8 0.8 %broadcast_select_fusion = bf16[2,128,512]{2,1,0:T(8,128)(2,1)} fusion(bf16[2,128,512]{2,1,0:T(8,128)(2,1)S(1)} %collective-permute-done.1.next_hbm, bf16[2,128,512]{2,1,0:T(8,128)(2,1)S(1)} %collective-permute-done.prev_hbm, pred[]{:T(512)S(6)} %eq.3), kind=kLoop, calls=%fused_computation.1 | loop fusion | flops 131072 | bytes 786433 | tf_op jit(solution)/shard_map/jit(_where)/select_n | solution.py:204
  18.6 0.5 %collective-permute-start.3 = (bf16[2,128,512]{2,1,0:T(8,128)(2,1)}, bf16[2,128,512]{2,1,0:T(8,128)(2,1)S(1)}, u32[]{:S(2)}, u32[]{:S(2)}) collective-permute-start(bf16[2,128,512]{2,1,0:T(8,128)(2,1)} %broadcast_select_fusion), channel_id=1, source_target_pairs={{0,1},{1,0},{2,3},{3,2},{4,5},{5,4},{6,7},{7,6},{8,9},{9,8},{10,11... | collective-permute-start | bytes 786440 | tf_op jit(solution)/shard_map/ppermute | solution.py:205
  19.1 0.7 %pad.4 = s32[768]{0:T(1024)S(1)} pad(s32[767]{0:T(1024)} %param.18, s32[]{:T(128)} %constant.13.clone.1), padding=0_1 | pad | bytes 6144 | tf_op jit(solution)/shard_map/jit(_pad)/pad | solution.py:196
  19.8 0.6 %reshape.9.table_ref = s32[1,768]{1,0:T(1,128)} reshape(s32[768]{0:T(1024)S(1)} %pad.4) | data formatting | bytes 6144 | tf_op jit(solution)/shard_map/reshape | solution.py:196
  20.4 0.6 %pad_add_fusion.meta_ref = s32[2]{0:T(128)} fusion(s32[1]{0:T(128)} %bitcast.1, s32[1]{0:T(128)} %bitcast), kind=kLoop, calls=%fused_computation.2 | loop fusion | flops 2 | bytes 16 | tf_op jit(solution)/shard_map/stack | solution.py:189
  21.0 0.0 collective-permute-done.2.partner_hbm
  21.0 0.0 copy-start.4
  21.0 0.0 collective-permute-done.3.sel_hbm
  21.0 0.0 copy-start.5
  21.0 0.0 copy-done.1
  21.0 0.0 copy-done.2
  21.0 0.0 copy-done.3
  21.0 0.7 %copy-done.4 = bf16[2,128,512]{2,1,0:T(8,128)(2,1)} copy-done((bf16[2,128,512]{2,1,0:T(8,128)(2,1)}, bf16[2,128,512]{2,1,0:T(8,128)(2,1)S(1)}, u32[]{:S(2)}) %copy-start.4) | copy-done | bytes 262168
  21.7 0.1 copy-done.5
  21.8 8.7 %attention_glu.1 = (bf16[128,1024]{1,0:T(8,128)(2,1)}, bf16[128,1024]{1,0:T(8,128)(2,1)}, bf16[64,1024]{1,0:T(8,128)(2,1)}, bf16[64,1024]{1,0:T(8,128)(2,1)}) custom-call(s32[2]{0:T(128)} %pad_add_fusion.meta_ref, s32[16]{0:T(128)} %len_ref.1, s32[1,768]{1,0:T(1,128)} %reshape.9.table_ref, f32[8,32]{1,0:T(8,128)} %bitcast.9, bf16[128,512]{1,0:T(8,128)(2,1)} %q_ref.1, ...), custom_call_target="tpu_custom_call" | custom-call | flops 1006632960 | bytes 7208960 | tf_op jit(solution)/shard_map/attention_glu/pallas_call | solution.py:215
  30.5 2.2 %collective-permute-start.4 = (bf16[64,1024]{1,0:T(8,128)(2,1)}, bf16[64,1024]{1,0:T(8,128)(2,1)S(1)}, u32[]{:S(2)}, u32[]{:S(2)}) collective-permute-start(bf16[64,1024]{1,0:T(8,128)(2,1)} %get-tuple-element.10), channel_id=1, source_target_pairs={{1,2},{3,4},{5,6},{7,8},{9,10},{11,12},{13,14},{2,1},{4,3},{6,5},{... | collective-permute-start | bytes 393224 | tf_op jit(solution)/shard_map/ppermute | solution.py:244
  32.7 0.1 collective-permute-start.5
  32.8 5.1 %collective-permute-done.4.cross_ref = bf16[64,1024]{1,0:T(8,128)(2,1)S(1)} collective-permute-done((bf16[64,1024]{1,0:T(8,128)(2,1)}, bf16[64,1024]{1,0:T(8,128)(2,1)S(1)}, u32[]{:S(2)}, u32[]{:S(2)}) %collective-permute-start.4) | collective-permute-done | bytes 131104 | tf_op jit(solution)/shard_map/ppermute | solution.py:244
  37.9 0.0 copy-start.6
  37.9 0.0 collective-permute-done.5.pairg_ref
  37.9 0.0 copy-start.7
  37.9 0.6 %copy-done.6 = bf16[64,1024]{1,0:T(8,128)(2,1)} copy-done((bf16[64,1024]{1,0:T(8,128)(2,1)}, bf16[64,1024]{1,0:T(8,128)(2,1)S(1)}, u32[]{:S(2)}) %copy-start.6) | copy-done | bytes 131096
  38.6 0.1 copy-done.7
  38.6 0.0 copy-done
  38.6 4.7 %conv_shrink.1 = bf16[128,1024]{1,0:T(8,128)(2,1)} custom-call(s32[2]{0:T(128)} %pad_add_fusion.meta_ref, bf16[128,1024]{1,0:T(8,128)(2,1)} %get-tuple-element.9.gated_ref, bf16[64,1024]{1,0:T(8,128)(2,1)} %copy-done.6, bf16[64,1024]{1,0:T(8,128)(2,1)} %copy-done.7, f32[31,1024]{1,0:T(8,128)} %taps_ref.1, f32[1,1024]{1,0:T(1,128)} %bitcast.11, ...), custom_call_target="tpu_custom_call" | custom-call | flops 276561920 | bytes 3272704 | tf_op jit(solution)/shard_map/conv_shrink/pallas_call | solution.py:248
Async XLA Ops:
  0.0 38.6 %copy-start = (bf16[1024,1024]{1,0:T(8,128)(2,1)S(1)}, bf16[1024,1024]{1,0:T(8,128)(2,1)}, u32[]{:S(2)}) copy-start(bf16[1024,1024]{1,0:T(8,128)(2,1)} %sw_vmem.1) | copy-start | bytes 6291460
  1.1 19.8 %copy-start.1 = (bf16[2,128,512]{2,1,0:T(8,128)(2,1)}, bf16[2,128,512]{2,1,0:T(8,128)(2,1)S(1)}, u32[]{:S(2)}) copy-start(bf16[2,128,512]{2,1,0:T(8,128)(2,1)S(1)} %pad_maximum_fusion.own_hbm) | copy-start | bytes 786436
  1.2 12.6 %collective-permute-start.1 = (bf16[2,128,512]{2,1,0:T(8,128)(2,1)S(1)}, bf16[2,128,512]{2,1,0:T(8,128)(2,1)S(1)}, u32[]{:S(2)}, u32[]{:S(2)}) collective-permute-start(bf16[2,128,512]{2,1,0:T(8,128)(2,1)S(1)} %pad_maximum_fusion.own_hbm), channel_id=1, source_target_pairs={{2,0},{3,1},{4,2},{5,3},{6,4},{7,5},{8,6},{9,7},{10,8},{11,9},{12,... | collective-permute-start | bytes 786440 | tf_op jit(solution)/shard_map/ppermute | solution.py:193
  3.3 14.5 %collective-permute-start = (bf16[2,128,512]{2,1,0:T(8,128)(2,1)S(1)}, bf16[2,128,512]{2,1,0:T(8,128)(2,1)S(1)}, u32[]{:S(2)}, u32[]{:S(2)}) collective-permute-start(bf16[2,128,512]{2,1,0:T(8,128)(2,1)S(1)} %pad_maximum_fusion.own_hbm), channel_id=1, source_target_pairs={{0,2},{1,3},{2,4},{3,5},{4,6},{5,7},{6,8},{7,9},{8,10},{9,11},{10,... | collective-permute-start | bytes 786440 | tf_op jit(solution)/shard_map/ppermute | solution.py:193
  7.4 13.6 %collective-permute-start.2 = (bf16[2,128,512]{2,1,0:T(8,128)(2,1)S(1)}, bf16[2,128,512]{2,1,0:T(8,128)(2,1)S(1)}, u32[]{:S(2)}, u32[]{:S(2)}) collective-permute-start(bf16[2,128,512]{2,1,0:T(8,128)(2,1)S(1)} %pad_maximum_fusion.own_hbm), channel_id=1, source_target_pairs={{0,1},{1,0},{2,3},{3,2},{4,5},{5,4},{6,7},{7,6},{8,9},{9,8},{10,11... | collective-permute-start | bytes 786440 | tf_op jit(solution)/shard_map/ppermute | solution.py:203
  13.7 7.3 %copy-start.2 = (bf16[2,128,512]{2,1,0:T(8,128)(2,1)}, bf16[2,128,512]{2,1,0:T(8,128)(2,1)S(1)}, u32[]{:S(2)}) copy-start(bf16[2,128,512]{2,1,0:T(8,128)(2,1)S(1)} %collective-permute-done.1.next_hbm) | copy-start | bytes 786436
  17.8 3.2 %copy-start.3 = (bf16[2,128,512]{2,1,0:T(8,128)(2,1)}, bf16[2,128,512]{2,1,0:T(8,128)(2,1)S(1)}, u32[]{:S(2)}) copy-start(bf16[2,128,512]{2,1,0:T(8,128)(2,1)S(1)} %collective-permute-done.prev_hbm) | copy-start | bytes 786436
  18.6 2.4 %collective-permute-start.3 = (bf16[2,128,512]{2,1,0:T(8,128)(2,1)}, bf16[2,128,512]{2,1,0:T(8,128)(2,1)S(1)}, u32[]{:S(2)}, u32[]{:S(2)}) collective-permute-start(bf16[2,128,512]{2,1,0:T(8,128)(2,1)} %broadcast_select_fusion), channel_id=1, source_target_pairs={{0,1},{1,0},{2,3},{3,2},{4,5},{5,4},{6,7},{7,6},{8,9},{9,8},{10,11... | collective-permute-start | bytes 786440 | tf_op jit(solution)/shard_map/ppermute | solution.py:205
  21.0 0.7 %copy-start.4 = (bf16[2,128,512]{2,1,0:T(8,128)(2,1)}, bf16[2,128,512]{2,1,0:T(8,128)(2,1)S(1)}, u32[]{:S(2)}) copy-start(bf16[2,128,512]{2,1,0:T(8,128)(2,1)S(1)} %collective-permute-done.2.partner_hbm) | copy-start | bytes 786436
  21.0 0.8 %copy-start.5 = (bf16[2,128,512]{2,1,0:T(8,128)(2,1)}, bf16[2,128,512]{2,1,0:T(8,128)(2,1)S(1)}, u32[]{:S(2)}) copy-start(bf16[2,128,512]{2,1,0:T(8,128)(2,1)S(1)} %collective-permute-done.3.sel_hbm) | copy-start | bytes 786436
  30.5 7.4 %collective-permute-start.4 = (bf16[64,1024]{1,0:T(8,128)(2,1)}, bf16[64,1024]{1,0:T(8,128)(2,1)S(1)}, u32[]{:S(2)}, u32[]{:S(2)}) collective-permute-start(bf16[64,1024]{1,0:T(8,128)(2,1)} %get-tuple-element.10), channel_id=1, source_target_pairs={{1,2},{3,4},{5,6},{7,8},{9,10},{11,12},{13,14},{2,1},{4,3},{6,5},{... | collective-permute-start | bytes 393224 | tf_op jit(solution)/shard_map/ppermute | solution.py:244
  32.7 5.2 %collective-permute-start.5 = (bf16[64,1024]{1,0:T(8,128)(2,1)}, bf16[64,1024]{1,0:T(8,128)(2,1)S(1)}, u32[]{:S(2)}, u32[]{:S(2)}) collective-permute-start(bf16[64,1024]{1,0:T(8,128)(2,1)} %get-tuple-element.11), channel_id=1, source_target_pairs={{0,1},{1,0},{2,3},{3,2},{4,5},{5,4},{6,7},{7,6},{8,9},{9,8},{10,11... | collective-permute-start | bytes 393224 | tf_op jit(solution)/shard_map/ppermute | solution.py:245
  37.9 0.7 %copy-start.6 = (bf16[64,1024]{1,0:T(8,128)(2,1)}, bf16[64,1024]{1,0:T(8,128)(2,1)S(1)}, u32[]{:S(2)}) copy-start(bf16[64,1024]{1,0:T(8,128)(2,1)S(1)} %collective-permute-done.4.cross_ref) | copy-start | bytes 393220
  37.9 0.7 %copy-start.7 = (bf16[64,1024]{1,0:T(8,128)(2,1)}, bf16[64,1024]{1,0:T(8,128)(2,1)S(1)}, u32[]{:S(2)}) copy-start(bf16[64,1024]{1,0:T(8,128)(2,1)S(1)} %collective-permute-done.5.pairg_ref) | copy-start | bytes 393220

commit v9 on v6

--- a/solution.py
+++ b/solution.py
@@ -55,9 +55,19 @@
     for copy in copies:
         copy.start()
     ow_copy = pltpu.make_async_copy(ow_hbm, ow_vmem, sems.at[0])
-    ew_copy = pltpu.make_async_copy(ew_hbm, ew_vmem, sems.at[1])
     ow_copy.start()
-    ew_copy.start()
+    model_width = ew_hbm.shape[0]
+    pieces = 2
+    piece = model_width // pieces
+    ew_copies = []
+    for j in range(pieces):
+        pair_copies = []
+        for part in range(2):
+            cols = pl.ds(part * model_width + j * piece, piece)
+            copy = pltpu.make_async_copy(ew_hbm.at[:, cols], ew_vmem.at[:, cols], sems.at[7 + 2 * j + part])
+            copy.start()
+            pair_copies.append(copy)
+        ew_copies.append(pair_copies)
     blocks = win_ref.shape[0] // planes
     rows, att_width = q_ref.shape
     heads = bias_t_ref.shape[0]
@@ -122,12 +132,14 @@
     mid = (x_ref[...].astype(jnp.float32) + projected).astype(jnp.bfloat16)
     mid_ref[...] = mid
     normed = layer_norm(mid.astype(jnp.float32), gain_ref[...]).astype(jnp.bfloat16)
-    model_width = mid.shape[1]
-    ew_copy.wait()
-    value_half = jnp.dot(normed, ew_vmem[:, :model_width], preferred_element_type=jnp.float32)
-    gate_half = jnp.dot(normed, ew_vmem[:, model_width:], preferred_element_type=jnp.float32)
-    gated = (value_half * sigmoid(gate_half)).astype(jnp.bfloat16)
-    gated_ref[...] = gated
+    for j in range(pieces):
+        for copy in ew_copies[j]:
+            copy.wait()
+        cols = slice(j * piece, (j + 1) * piece)
+        gate_cols = slice(model_width + j * piece, model_width + (j + 1) * piece)
+        value_half = jnp.dot(normed, ew_vmem[:, cols], preferred_element_type=jnp.float32)
+        gate_half = jnp.dot(normed, ew_vmem[:, gate_cols], preferred_element_type=jnp.float32)
+        gated_ref[:, cols] = (value_half * sigmoid(gate_half)).astype(jnp.bfloat16)
     half = cross_ref.shape[0]
     cross_ref[...] = gated_ref[pl.ds(pl.multiple_of(core * half, half), half), :]
     partner_ref[...] = gated_ref[pl.ds(pl.multiple_of((1 - core) * half, half), half), :]
@@ -137,8 +149,14 @@
     meta_ref, gated_ref, cross_ref, pairg_ref, taps_ref, gain_ref, mid_ref, sw_hbm,
     out_ref, win_ref, conv_ref, sw_vmem, sems,
 ):
-    sw_copy = pltpu.make_async_copy(sw_hbm, sw_vmem, sems.at[0])
-    sw_copy.start()
+    pieces = 2
+    piece = sw_hbm.shape[1] // pieces
+    sw_copies = []
+    for j in range(pieces):
+        cols = pl.ds(j * piece, piece)
+        copy = pltpu.make_async_copy(sw_hbm.at[:, cols], sw_vmem.at[:, cols], sems.at[j])
+        copy.start()
+        sw_copies.append(copy)
     half = cross_ref.shape[0]
     rows, model_width = mid_ref.shape
     first_core = meta_ref[1] == 0
@@ -162,9 +180,11 @@
     lax.fori_loop(0, model_width // LANES, chunk, 0)
     inner = layer_norm(conv_ref[...], gain_ref[...])
     activated = (inner * sigmoid(inner)).astype(jnp.bfloat16)
-    sw_copy.wait()
-    shrunk = jnp.dot(activated, sw_vmem[...], preferred_element_type=jnp.float32)
-    out_ref[...] = (mid_ref[...].astype(jnp.float32) + shrunk).astype(out_ref.dtype)
+    for j in range(pieces):
+        sw_copies[j].wait()
+        cols = slice(j * piece, (j + 1) * piece)
+        shrunk = jnp.dot(activated, sw_vmem[:, cols], preferred_element_type=jnp.float32)
+        out_ref[:, cols] = (mid_ref[:, cols].astype(jnp.float32) + shrunk).astype(out_ref.dtype)
 
 
 def on_device(
@@ -228,7 +248,7 @@
         scratch_shapes=[
             pltpu.VMEM((att_width, model_width), jnp.bfloat16),
             pltpu.VMEM((model_width, 2 * model_width), jnp.bfloat16),
-            pltpu.SemaphoreType.DMA((7,)),
+            pltpu.SemaphoreType.DMA((11,)),
             pltpu.VMEM((rows, att_width), jnp.bfloat16),
             pltpu.VMEM((len(order) * packed.shape[0], rows, att_width), jnp.bfloat16),
         ],
@@ -256,7 +276,7 @@
             pltpu.VMEM((rows + 2 * half, model_width), jnp.float32),
             pltpu.VMEM((rows, model_width), jnp.float32),
             pltpu.VMEM((model_width, model_width), jnp.bfloat16),
-            pltpu.SemaphoreType.DMA((1,)),
+            pltpu.SemaphoreType.DMA((2,)),
         ],
         cost_estimate=pl.CostEstimate(
             flops=conv_flops, transcendentals=rows * model_width, bytes_accessed=conv_bytes

time: 41.4 us -> 41.8 us (level)
  no operation moved by 1% of the time
where the time goes in v9:
time: 41.8 us; the launch traced here: 41.6 us
  waiting for transfers between devices  14.2 us (34%)
  Pallas kernels  12.5 us (30%)
  starting transfers between devices  10.3 us (25%)
  local copies, waits for them, and re-layouts  2.77 us (7%)
  other arithmetic  1.6 us (4%)
    ppermute x2, waiting for transfers between devices, lin_shift(): lax.ppermute(value, ('chip', 'core'), [(s, s + steps) for s in range(lead...  9.14 us
    pallas_call x1, Pallas kernels, on_device(): pl.pallas_call(attention_kernel, out_shape=(jax.ShapeDtypeStruct((rows, m...  7.46 us
    ppermute x2, starting transfers between devices, lin_shift(): lax.ppermute(value, ('chip', 'core'), [(s, s + steps) for s in range(lead...  6.18 us
    ppermute x1, waiting for transfers between devices, on_device(): cross_recv = lax.ppermute(cross_send, ('chip', 'core'), inward)  5.1 us
    pallas_call x1, Pallas kernels, on_device(): pl.pallas_call(conv_kernel, out_shape=jax.ShapeDtypeStruct((rows, model_w...  5.07 us
    ppermute x1, starting transfers between devices, on_device(): cross_recv = lax.ppermute(cross_send, ('chip', 'core'), inward)  2.21 us
    unnamed x14, local copies, waits for them, and re-layouts  1.49 us
    ppermute x1, starting transfers between devices, on_device(): partner = lax.ppermute(packed, 'core', swap)  1.3 us
  transfers between devices with their start and end apart: 6, of which 3 were waited for; matrix products, arithmetic and copies ran while one was open for 5% of the time, Pallas kernels for 0%

profile of v9, /device:TPU:21, one launch (start us, length us, event | category | flops | bytes accessed | tf_op | source)
XLA Modules:
  0.0 41.6 jit_solution(622478775863455563)
XLA Ops:
  0.0 1.0 %pad_maximum_fusion.own_hbm = bf16[2,128,512]{2,1,0:T(8,128)(2,1)S(1)} fusion(bf16[1,128,512]{2,1,0:T(8,128)(2,1)} %bitcast.7, bf16[1,128,512]{2,1,0:T(8,128)(2,1)} %bitcast.8), kind=kLoop, calls=%fused_computation | loop fusion | flops 131072 | bytes 524288 | tf_op jit(solution)/shard_map/stack | solution.py:222
  1.0 0.0 copy-start
  1.0 2.1 %collective-permute-start.1 = (bf16[2,128,512]{2,1,0:T(8,128)(2,1)S(1)}, bf16[2,128,512]{2,1,0:T(8,128)(2,1)S(1)}, u32[]{:S(2)}, u32[]{:S(2)}) collective-permute-start(bf16[2,128,512]{2,1,0:T(8,128)(2,1)S(1)} %pad_maximum_fusion.own_hbm), channel_id=1, source_target_pairs={{2,0},{3,1},{4,2},{5,3},{6,4},{7,5},{8,6},{9,7},{10,8},{11,9},{12,... | collective-permute-start | bytes 786440 | tf_op jit(solution)/shard_map/ppermute | solution.py:216
  3.1 4.0 %collective-permute-start = (bf16[2,128,512]{2,1,0:T(8,128)(2,1)S(1)}, bf16[2,128,512]{2,1,0:T(8,128)(2,1)S(1)}, u32[]{:S(2)}, u32[]{:S(2)}) collective-permute-start(bf16[2,128,512]{2,1,0:T(8,128)(2,1)S(1)} %pad_maximum_fusion.own_hbm), channel_id=1, source_target_pairs={{0,2},{1,3},{2,4},{3,5},{4,6},{5,7},{6,8},{7,9},{8,10},{9,11},{10,... | collective-permute-start | bytes 786440 | tf_op jit(solution)/shard_map/ppermute | solution.py:216
  7.2 1.3 %collective-permute-start.2 = (bf16[2,128,512]{2,1,0:T(8,128)(2,1)S(1)}, bf16[2,128,512]{2,1,0:T(8,128)(2,1)S(1)}, u32[]{:S(2)}, u32[]{:S(2)}) collective-permute-start(bf16[2,128,512]{2,1,0:T(8,128)(2,1)S(1)} %pad_maximum_fusion.own_hbm), channel_id=1, source_target_pairs={{0,1},{1,0},{2,3},{3,2},{4,5},{5,4},{6,7},{7,6},{8,9},{9,8},{10,11... | collective-permute-start | bytes 786440 | tf_op jit(solution)/shard_map/ppermute | solution.py:226
  8.5 5.1 %collective-permute-done.1.next_hbm = bf16[2,128,512]{2,1,0:T(8,128)(2,1)S(1)} collective-permute-done((bf16[2,128,512]{2,1,0:T(8,128)(2,1)S(1)}, bf16[2,128,512]{2,1,0:T(8,128)(2,1)S(1)}, u32[]{:S(2)}, u32[]{:S(2)}) %collective-permute-start.1) | collective-permute-done | bytes 262176 | tf_op jit(solution)/shard_map/ppermute | solution.py:216
  13.6 0.0 copy-start.1
  13.6 4.1 %collective-permute-done.prev_hbm = bf16[2,128,512]{2,1,0:T(8,128)(2,1)S(1)} collective-permute-done((bf16[2,128,512]{2,1,0:T(8,128)(2,1)S(1)}, bf16[2,128,512]{2,1,0:T(8,128)(2,1)S(1)}, u32[]{:S(2)}, u32[]{:S(2)}) %collective-permute-start) | collective-permute-done | bytes 262176 | tf_op jit(solution)/shard_map/ppermute | solution.py:216
  17.6 0.0 copy-start.2
  17.7 0.6 %collective-permute-start.3 = (bf16[2,128,512]{2,1,0:T(8,128)(2,1)S(1)}, bf16[2,128,512]{2,1,0:T(8,128)(2,1)S(1)}, u32[]{:S(2)}, u32[]{:S(2)}) collective-permute-start(bf16[2,128,512]{2,1,0:T(8,128)(2,1)S(1)} %broadcast_select_fusion), channel_id=1, source_target_pairs={{0,1},{1,0},{2,3},{3,2},{4,5},{5,4},{6,7},{7,6},{8,9},{9,8},{10,11... | collective-permute-start | bytes 786440 | tf_op jit(solution)/shard_map/ppermute | solution.py:228
  18.2 0.7 %pad.4 = s32[768]{0:T(1024)S(1)} pad(s32[767]{0:T(1024)} %param.18, s32[]{:T(128)} %constant.13.clone.1), padding=0_1 | pad | bytes 6144 | tf_op jit(solution)/shard_map/jit(_pad)/pad | solution.py:219
  18.9 0.6 %reshape.9.table_ref = s32[1,768]{1,0:T(1,128)} reshape(s32[768]{0:T(1024)S(1)} %pad.4) | data formatting | bytes 6144 | tf_op jit(solution)/shard_map/reshape | solution.py:219
  19.5 0.6 %pad_add_fusion.meta_ref = s32[2]{0:T(128)} fusion(s32[1]{0:T(128)} %bitcast.1, s32[1]{0:T(128)} %bitcast), kind=kLoop, calls=%fused_computation.2 | loop fusion | flops 2 | bytes 16 | tf_op jit(solution)/shard_map/stack | solution.py:212
  20.1 0.0 collective-permute-done.2.partner_hbm
  20.1 0.0 copy-start.3
  20.1 0.0 collective-permute-done.3.sel_hbm
  20.1 0.0 copy-start.4
  20.1 0.0 copy-done
  20.1 0.0 copy-done.1
  20.1 0.0 copy-done.2
  20.2 0.7 %copy-done.3 = bf16[2,128,512]{2,1,0:T(8,128)(2,1)} copy-done((bf16[2,128,512]{2,1,0:T(8,128)(2,1)}, bf16[2,128,512]{2,1,0:T(8,128)(2,1)S(1)}, u32[]{:S(2)}) %copy-start.3) | copy-done | bytes 262168
  20.8 0.1 copy-done.4
  20.9 7.5 %attention_glu.1 = (bf16[128,1024]{1,0:T(8,128)(2,1)}, bf16[128,1024]{1,0:T(8,128)(2,1)}, bf16[64,1024]{1,0:T(8,128)(2,1)}, bf16[64,1024]{1,0:T(8,128)(2,1)}) custom-call(s32[2]{0:T(128)} %pad_add_fusion.meta_ref, s32[16]{0:T(128)} %len_ref.1, s32[1,768]{1,0:T(1,128)} %reshape.9.table_ref, f32[8,32]{1,0:T(8,128)} %bitcast.9, bf16[128,512]{1,0:T(8,128)(2,1)} %q_ref.1, ...), custom_call_target="tpu_custom_call" | custom-call | flops 1006632960 | bytes 7208960 | tf_op jit(solution)/shard_map/attention_glu/pallas_call | solution.py:238
  28.4 2.2 %collective-permute-start.4 = (bf16[64,1024]{1,0:T(8,128)(2,1)}, bf16[64,1024]{1,0:T(8,128)(2,1)S(1)}, u32[]{:S(2)}, u32[]{:S(2)}) collective-permute-start(bf16[64,1024]{1,0:T(8,128)(2,1)} %get-tuple-element.10), channel_id=1, source_target_pairs={{1,2},{3,4},{5,6},{7,8},{9,10},{11,12},{13,14},{2,1},{4,3},{6,5},{... | collective-permute-start | bytes 393224 | tf_op jit(solution)/shard_map/ppermute | solution.py:266
  30.6 0.1 collective-permute-start.5
  30.7 5.1 %collective-permute-done.4.cross_ref = bf16[64,1024]{1,0:T(8,128)(2,1)S(1)} collective-permute-done((bf16[64,1024]{1,0:T(8,128)(2,1)}, bf16[64,1024]{1,0:T(8,128)(2,1)S(1)}, u32[]{:S(2)}, u32[]{:S(2)}) %collective-permute-start.4) | collective-permute-done | bytes 131104 | tf_op jit(solution)/shard_map/ppermute | solution.py:266
  35.8 0.0 copy-start.5
  35.8 0.0 collective-permute-done.5.pairg_ref
  35.8 0.0 copy-start.6
  35.8 0.6 %copy-done.5 = bf16[64,1024]{1,0:T(8,128)(2,1)} copy-done((bf16[64,1024]{1,0:T(8,128)(2,1)}, bf16[64,1024]{1,0:T(8,128)(2,1)S(1)}, u32[]{:S(2)}) %copy-start.5) | copy-done | bytes 131096
  36.5 0.0 copy-done.6
  36.5 5.1 %conv_shrink.1 = bf16[128,1024]{1,0:T(8,128)(2,1)} custom-call(s32[2]{0:T(128)} %pad_add_fusion.meta_ref, bf16[128,1024]{1,0:T(8,128)(2,1)} %get-tuple-element.9.gated_ref, bf16[64,1024]{1,0:T(8,128)(2,1)} %copy-done.5, bf16[64,1024]{1,0:T(8,128)(2,1)} %copy-done.6, f32[31,1024]{1,0:T(8,128)} %taps_ref.1, f32[1,1024]{1,0:T(1,128)} %bitcast.11, ...), custom_call_target="tpu_custom_call" | custom-call | flops 276561920 | bytes 3272704 | tf_op jit(solution)/shard_map/conv_shrink/pallas_call | solution.py:270
  (1 shorter events, 0.0 us)
Async XLA Ops:
  1.0 19.1 %copy-start = (bf16[2,128,512]{2,1,0:T(8,128)(2,1)}, bf16[2,128,512]{2,1,0:T(8,128)(2,1)S(1)}, u32[]{:S(2)}) copy-start(bf16[2,128,512]{2,1,0:T(8,128)(2,1)S(1)} %pad_maximum_fusion.own_hbm) | copy-start | bytes 786436
  1.0 12.6 %collective-permute-start.1 = (bf16[2,128,512]{2,1,0:T(8,128)(2,1)S(1)}, bf16[2,128,512]{2,1,0:T(8,128)(2,1)S(1)}, u32[]{:S(2)}, u32[]{:S(2)}) collective-permute-start(bf16[2,128,512]{2,1,0:T(8,128)(2,1)S(1)} %pad_maximum_fusion.own_hbm), channel_id=1, source_target_pairs={{2,0},{3,1},{4,2},{5,3},{6,4},{7,5},{8,6},{9,7},{10,8},{11,9},{12,... | collective-permute-start | bytes 786440 | tf_op jit(solution)/shard_map/ppermute | solution.py:216
  3.1 14.5 %collective-permute-start = (bf16[2,128,512]{2,1,0:T(8,128)(2,1)S(1)}, bf16[2,128,512]{2,1,0:T(8,128)(2,1)S(1)}, u32[]{:S(2)}, u32[]{:S(2)}) collective-permute-start(bf16[2,128,512]{2,1,0:T(8,128)(2,1)S(1)} %pad_maximum_fusion.own_hbm), channel_id=1, source_target_pairs={{0,2},{1,3},{2,4},{3,5},{4,6},{5,7},{6,8},{7,9},{8,10},{9,11},{10,... | collective-permute-start | bytes 786440 | tf_op jit(solution)/shard_map/ppermute | solution.py:216
  7.2 12.9 %collective-permute-start.2 = (bf16[2,128,512]{2,1,0:T(8,128)(2,1)S(1)}, bf16[2,128,512]{2,1,0:T(8,128)(2,1)S(1)}, u32[]{:S(2)}, u32[]{:S(2)}) collective-permute-start(bf16[2,128,512]{2,1,0:T(8,128)(2,1)S(1)} %pad_maximum_fusion.own_hbm), channel_id=1, source_target_pairs={{0,1},{1,0},{2,3},{3,2},{4,5},{5,4},{6,7},{7,6},{8,9},{9,8},{10,11... | collective-permute-start | bytes 786440 | tf_op jit(solution)/shard_map/ppermute | solution.py:226
  13.6 6.6 %copy-start.1 = (bf16[2,128,512]{2,1,0:T(8,128)(2,1)}, bf16[2,128,512]{2,1,0:T(8,128)(2,1)S(1)}, u32[]{:S(2)}) copy-start(bf16[2,128,512]{2,1,0:T(8,128)(2,1)S(1)} %collective-permute-done.1.next_hbm) | copy-start | bytes 786436
  17.6 2.5 %copy-start.2 = (bf16[2,128,512]{2,1,0:T(8,128)(2,1)}, bf16[2,128,512]{2,1,0:T(8,128)(2,1)S(1)}, u32[]{:S(2)}) copy-start(bf16[2,128,512]{2,1,0:T(8,128)(2,1)S(1)} %collective-permute-done.prev_hbm) | copy-start | bytes 786436
  17.7 2.4 %collective-permute-start.3 = (bf16[2,128,512]{2,1,0:T(8,128)(2,1)S(1)}, bf16[2,128,512]{2,1,0:T(8,128)(2,1)S(1)}, u32[]{:S(2)}, u32[]{:S(2)}) collective-permute-start(bf16[2,128,512]{2,1,0:T(8,128)(2,1)S(1)} %broadcast_select_fusion), channel_id=1, source_target_pairs={{0,1},{1,0},{2,3},{3,2},{4,5},{5,4},{6,7},{7,6},{8,9},{9,8},{10,11... | collective-permute-start | bytes 786440 | tf_op jit(solution)/shard_map/ppermute | solution.py:228
  20.1 0.7 %copy-start.3 = (bf16[2,128,512]{2,1,0:T(8,128)(2,1)}, bf16[2,128,512]{2,1,0:T(8,128)(2,1)S(1)}, u32[]{:S(2)}) copy-start(bf16[2,128,512]{2,1,0:T(8,128)(2,1)S(1)} %collective-permute-done.2.partner_hbm) | copy-start | bytes 786436
  20.1 0.8 %copy-start.4 = (bf16[2,128,512]{2,1,0:T(8,128)(2,1)}, bf16[2,128,512]{2,1,0:T(8,128)(2,1)S(1)}, u32[]{:S(2)}) copy-start(bf16[2,128,512]{2,1,0:T(8,128)(2,1)S(1)} %collective-permute-done.3.sel_hbm) | copy-start | bytes 786436
  28.4 7.4 %collective-permute-start.4 = (bf16[64,1024]{1,0:T(8,128)(2,1)}, bf16[64,1024]{1,0:T(8,128)(2,1)S(1)}, u32[]{:S(2)}, u32[]{:S(2)}) collective-permute-start(bf16[64,1024]{1,0:T(8,128)(2,1)} %get-tuple-element.10), channel_id=1, source_target_pairs={{1,2},{3,4},{5,6},{7,8},{9,10},{11,12},{13,14},{2,1},{4,3},{6,5},{... | collective-permute-start | bytes 393224 | tf_op jit(solution)/shard_map/ppermute | solution.py:266
  30.6 5.2 %collective-permute-start.5 = (bf16[64,1024]{1,0:T(8,128)(2,1)}, bf16[64,1024]{1,0:T(8,128)(2,1)S(1)}, u32[]{:S(2)}, u32[]{:S(2)}) collective-permute-start(bf16[64,1024]{1,0:T(8,128)(2,1)} %get-tuple-element.11), channel_id=1, source_target_pairs={{0,1},{1,0},{2,3},{3,2},{4,5},{5,4},{6,7},{7,6},{8,9},{9,8},{10,11... | collective-permute-start | bytes 393224 | tf_op jit(solution)/shard_map/ppermute | solution.py:267
  35.8 0.7 %copy-start.5 = (bf16[64,1024]{1,0:T(8,128)(2,1)}, bf16[64,1024]{1,0:T(8,128)(2,1)S(1)}, u32[]{:S(2)}) copy-start(bf16[64,1024]{1,0:T(8,128)(2,1)S(1)} %collective-permute-done.4.cross_ref) | copy-start | bytes 393220
  35.8 0.7 %copy-start.6 = (bf16[64,1024]{1,0:T(8,128)(2,1)}, bf16[64,1024]{1,0:T(8,128)(2,1)S(1)}, u32[]{:S(2)}) copy-start(bf16[64,1024]{1,0:T(8,128)(2,1)S(1)} %collective-permute-done.5.pairg_ref) | copy-start | bytes 393220

commit v10 on v6

--- a/solution.py
+++ b/solution.py
@@ -203,7 +203,8 @@
     from_prev = lin_shift(packed, REACH)
     from_next = lin_shift(packed, -REACH)
     swap = [(0, 1), (1, 0)]
-    partner = lax.ppermute(packed, "core", swap)
+    gated_input, table, meta, bias_t = lax.optimization_barrier((packed, table, meta, bias_t))
+    partner = lax.ppermute(gated_input, "core", swap)
     sel = jnp.where(core == 0, from_next, from_prev)
     partner_sel = lax.ppermute(sel, "core", swap)
     order = list(range(-REACH, REACH + 1))

time: 41.4 us -> 40.7 us (0.983)
  waiting for transfers between devices: 14.2 us -> 13.4 us
    ppermute x2, waiting for transfers between devices: 9.14 us -> 7.33 us  [lin_shift(): lax.ppermute(value, ('chip', 'core'), [(s, s + steps) for s in range(lead...]
    ppermute x1, waiting for transfers between devices: 0.01 us -> 1.16 us  [on_device(): partner_sel = lax.ppermute(sel, 'core', swap)]
  transfers between devices with their start and end apart: 6 -> 6, of which waited for: 3 -> 4; matrix products, arithmetic and copies ran while one was open for 5% -> 5% of each run, Pallas kernels for 0% -> 0%
where the time goes in v10:
time: 40.7 us; the launch traced here: 40.4 us
  waiting for transfers between devices  13.4 us (33%)
  Pallas kernels  12.1 us (30%)
  starting transfers between devices  10.5 us (26%)
  local copies, waits for them, and re-layouts  2.67 us (7%)
  other arithmetic  1.6 us (4%)
    ppermute x2, waiting for transfers between devices, lin_shift(): lax.ppermute(value, ('chip', 'core'), [(s, s + steps) for s in range(lead...  7.33 us
    pallas_call x1, Pallas kernels, on_device(): pl.pallas_call(attention_kernel, out_shape=(jax.ShapeDtypeStruct((rows, m...  7.19 us
    ppermute x2, starting transfers between devices, lin_shift(): lax.ppermute(value, ('chip', 'core'), [(s, s + steps) for s in range(lead...  6.18 us
    ppermute x1, waiting for transfers between devices, on_device(): cross_recv = lax.ppermute(cross_send, ('chip', 'core'), inward)  4.91 us
    pallas_call x1, Pallas kernels, on_device(): pl.pallas_call(conv_kernel, out_shape=jax.ShapeDtypeStruct((rows, model_w...  4.88 us
    ppermute x1, starting transfers between devices, on_device(): cross_recv = lax.ppermute(cross_send, ('chip', 'core'), inward)  2.5 us
    unnamed x14, local copies, waits for them, and re-layouts  1.38 us
    ppermute x1, starting transfers between devices, on_device(): partner = lax.ppermute(gated_input, 'core', swap)  1.24 us
  transfers between devices with their start and end apart: 6, of which 4 were waited for; matrix products, arithmetic and copies ran while one was open for 5% of the time, Pallas kernels for 0%

profile of v10, /device:TPU:21, one launch (start us, length us, event | category | flops | bytes accessed | tf_op | source)
XLA Modules:
  0.0 40.4 jit_solution(1663792937834574045)
XLA Ops:
  0.0 1.0 %pad_maximum_fusion.own_hbm = bf16[2,128,512]{2,1,0:T(8,128)(2,1)S(1)} fusion(bf16[1,128,512]{2,1,0:T(8,128)(2,1)} %bitcast.7, bf16[1,128,512]{2,1,0:T(8,128)(2,1)} %bitcast.8), kind=kLoop, calls=%fused_computation | loop fusion | flops 131072 | bytes 524288 | tf_op jit(solution)/shard_map/stack | solution.py:202
  1.0 0.0 copy-start
  1.0 2.1 %collective-permute-start.1 = (bf16[2,128,512]{2,1,0:T(8,128)(2,1)S(1)}, bf16[2,128,512]{2,1,0:T(8,128)(2,1)S(1)}, u32[]{:S(2)}, u32[]{:S(2)}) collective-permute-start(bf16[2,128,512]{2,1,0:T(8,128)(2,1)S(1)} %pad_maximum_fusion.own_hbm), channel_id=1, source_target_pairs={{2,0},{3,1},{4,2},{5,3},{6,4},{7,5},{8,6},{9,7},{10,8},{11,9},{12,... | collective-permute-start | bytes 786440 | tf_op jit(solution)/shard_map/ppermute | solution.py:196
  3.1 4.0 %collective-permute-start = (bf16[2,128,512]{2,1,0:T(8,128)(2,1)S(1)}, bf16[2,128,512]{2,1,0:T(8,128)(2,1)S(1)}, u32[]{:S(2)}, u32[]{:S(2)}) collective-permute-start(bf16[2,128,512]{2,1,0:T(8,128)(2,1)S(1)} %pad_maximum_fusion.own_hbm), channel_id=1, source_target_pairs={{0,2},{1,3},{2,4},{3,5},{4,6},{5,7},{6,8},{7,9},{8,10},{9,11},{10,... | collective-permute-start | bytes 786440 | tf_op jit(solution)/shard_map/ppermute | solution.py:196
  7.2 0.7 %pad.4 = s32[768]{0:T(1024)S(1)} pad(s32[767]{0:T(1024)} %param.18, s32[]{:T(128)} %constant.5.clone.1), padding=0_1 | pad | bytes 6144 | tf_op jit(solution)/shard_map/jit(_pad)/pad | solution.py:199
  7.9 0.6 %reshape.9.table_ref = s32[1,768]{1,0:T(1,128)} reshape(s32[768]{0:T(1024)S(1)} %pad.4) | data formatting | bytes 6144 | tf_op jit(solution)/shard_map/reshape | solution.py:199
  8.5 0.6 %pad_add_fusion.meta_ref = s32[2]{0:T(128)} fusion(s32[1]{0:T(128)} %bitcast.3, s32[1]{0:T(128)} %bitcast.2), kind=kLoop, calls=%fused_computation.2 | loop fusion | flops 2 | bytes 16 | tf_op jit(solution)/shard_map/stack | solution.py:192
  9.1 1.2 %collective-permute-start.2 = (bf16[2,128,512]{2,1,0:T(8,128)(2,1)S(1)}, bf16[2,128,512]{2,1,0:T(8,128)(2,1)S(1)}, u32[]{:S(2)}, u32[]{:S(2)}) collective-permute-start(bf16[2,128,512]{2,1,0:T(8,128)(2,1)S(1)} %pad_maximum_fusion.own_hbm), channel_id=1, source_target_pairs={{0,1},{1,0},{2,3},{3,2},{4,5},{5,4},{6,7},{7,6},{8,9},{9,8},{10,11... | collective-permute-start | bytes 786440 | tf_op jit(solution)/shard_map/ppermute | solution.py:207
  10.3 3.3 %collective-permute-done.1.next_hbm = bf16[2,128,512]{2,1,0:T(8,128)(2,1)S(1)} collective-permute-done((bf16[2,128,512]{2,1,0:T(8,128)(2,1)S(1)}, bf16[2,128,512]{2,1,0:T(8,128)(2,1)S(1)}, u32[]{:S(2)}, u32[]{:S(2)}) %collective-permute-start.1) | collective-permute-done | bytes 262176 | tf_op jit(solution)/shard_map/ppermute | solution.py:196
  13.6 0.0 copy-start.1
  13.6 4.1 %collective-permute-done.prev_hbm = bf16[2,128,512]{2,1,0:T(8,128)(2,1)S(1)} collective-permute-done((bf16[2,128,512]{2,1,0:T(8,128)(2,1)S(1)}, bf16[2,128,512]{2,1,0:T(8,128)(2,1)S(1)}, u32[]{:S(2)}, u32[]{:S(2)}) %collective-permute-start) | collective-permute-done | bytes 262176 | tf_op jit(solution)/shard_map/ppermute | solution.py:196
  17.6 0.0 copy-start.2
  17.7 0.6 %collective-permute-start.3 = (bf16[2,128,512]{2,1,0:T(8,128)(2,1)S(1)}, bf16[2,128,512]{2,1,0:T(8,128)(2,1)S(1)}, u32[]{:S(2)}, u32[]{:S(2)}) collective-permute-start(bf16[2,128,512]{2,1,0:T(8,128)(2,1)S(1)} %broadcast_select_fusion), channel_id=1, source_target_pairs={{0,1},{1,0},{2,3},{3,2},{4,5},{5,4},{6,7},{7,6},{8,9},{9,8},{10,11... | collective-permute-start | bytes 786440 | tf_op jit(solution)/shard_map/ppermute | solution.py:209
  18.2 0.0 collective-permute-done.2.partner_hbm
  18.2 0.0 copy-start.3
  18.2 1.2 %collective-permute-done.3.sel_hbm = bf16[2,128,512]{2,1,0:T(8,128)(2,1)S(1)} collective-permute-done((bf16[2,128,512]{2,1,0:T(8,128)(2,1)S(1)}, bf16[2,128,512]{2,1,0:T(8,128)(2,1)S(1)}, u32[]{:S(2)}, u32[]{:S(2)}) %collective-permute-start.3) | collective-permute-done | bytes 262176 | tf_op jit(solution)/shard_map/ppermute | solution.py:209
  19.4 0.0 copy-start.4
  19.4 0.0 copy-done
  19.4 0.0 copy-done.1
  19.4 0.0 copy-done.2
  19.4 0.0 copy-done.3
  19.4 0.7 %copy-done.4 = bf16[2,128,512]{2,1,0:T(8,128)(2,1)} copy-done((bf16[2,128,512]{2,1,0:T(8,128)(2,1)}, bf16[2,128,512]{2,1,0:T(8,128)(2,1)S(1)}, u32[]{:S(2)}) %copy-start.4) | copy-done | bytes 262168
  20.1 7.2 %attention_glu.1 = (bf16[128,1024]{1,0:T(8,128)(2,1)}, bf16[128,1024]{1,0:T(8,128)(2,1)}, bf16[64,1024]{1,0:T(8,128)(2,1)}, bf16[64,1024]{1,0:T(8,128)(2,1)}) custom-call(s32[2]{0:T(128)} %pad_add_fusion.meta_ref, s32[16]{0:T(128)} %len_ref.1, s32[1,768]{1,0:T(1,128)} %reshape.9.table_ref, f32[8,32]{1,0:T(8,128)} %bitcast.9, bf16[128,512]{1,0:T(8,128)(2,1)} %q_ref.1, ...), custom_call_target="tpu_custom_call" | custom-call | flops 1006632960 | bytes 7208960 | tf_op jit(solution)/shard_map/attention_glu/pallas_call | solution.py:219
  27.3 2.5 %collective-permute-start.4 = (bf16[64,1024]{1,0:T(8,128)(2,1)}, bf16[64,1024]{1,0:T(8,128)(2,1)S(1)}, u32[]{:S(2)}, u32[]{:S(2)}) collective-permute-start(bf16[64,1024]{1,0:T(8,128)(2,1)} %get-tuple-element.18), channel_id=1, source_target_pairs={{1,2},{3,4},{5,6},{7,8},{9,10},{11,12},{13,14},{2,1},{4,3},{6,5},{... | collective-permute-start | bytes 393224 | tf_op jit(solution)/shard_map/ppermute | solution.py:247
  29.8 0.1 collective-permute-start.5
  29.9 4.9 %collective-permute-done.4.cross_ref = bf16[64,1024]{1,0:T(8,128)(2,1)S(1)} collective-permute-done((bf16[64,1024]{1,0:T(8,128)(2,1)}, bf16[64,1024]{1,0:T(8,128)(2,1)S(1)}, u32[]{:S(2)}, u32[]{:S(2)}) %collective-permute-start.4) | collective-permute-done | bytes 131104 | tf_op jit(solution)/shard_map/ppermute | solution.py:247
  34.8 0.0 copy-start.5
  34.8 0.0 collective-permute-done.5.pairg_ref
  34.8 0.0 copy-start.6
  34.8 0.6 %copy-done.5 = bf16[64,1024]{1,0:T(8,128)(2,1)} copy-done((bf16[64,1024]{1,0:T(8,128)(2,1)}, bf16[64,1024]{1,0:T(8,128)(2,1)S(1)}, u32[]{:S(2)}) %copy-start.5) | copy-done | bytes 131096
  35.5 0.0 copy-done.6
  35.5 4.9 %conv_shrink.1 = bf16[128,1024]{1,0:T(8,128)(2,1)} custom-call(s32[2]{0:T(128)} %pad_add_fusion.meta_ref, bf16[128,1024]{1,0:T(8,128)(2,1)} %get-tuple-element.17.gated_ref, bf16[64,1024]{1,0:T(8,128)(2,1)} %copy-done.5, bf16[64,1024]{1,0:T(8,128)(2,1)} %copy-done.6, f32[31,1024]{1,0:T(8,128)} %taps_ref.1, f32[1,1024]{1,0:T(1,128)} %bitcast.11, ...), custom_call_target="tpu_custom_call" | custom-call | flops 276561920 | bytes 3272704 | tf_op jit(solution)/shard_map/conv_shrink/pallas_call | solution.py:251
  (1 shorter events, 0.0 us)
Async XLA Ops:
  1.0 18.4 %copy-start = (bf16[2,128,512]{2,1,0:T(8,128)(2,1)}, bf16[2,128,512]{2,1,0:T(8,128)(2,1)S(1)}, u32[]{:S(2)}) copy-start(bf16[2,128,512]{2,1,0:T(8,128)(2,1)S(1)} %pad_maximum_fusion.own_hbm) | copy-start | bytes 786436
  1.0 12.6 %collective-permute-start.1 = (bf16[2,128,512]{2,1,0:T(8,128)(2,1)S(1)}, bf16[2,128,512]{2,1,0:T(8,128)(2,1)S(1)}, u32[]{:S(2)}, u32[]{:S(2)}) collective-permute-start(bf16[2,128,512]{2,1,0:T(8,128)(2,1)S(1)} %pad_maximum_fusion.own_hbm), channel_id=1, source_target_pairs={{2,0},{3,1},{4,2},{5,3},{6,4},{7,5},{8,6},{9,7},{10,8},{11,9},{12,... | collective-permute-start | bytes 786440 | tf_op jit(solution)/shard_map/ppermute | solution.py:196
  3.1 14.5 %collective-permute-start = (bf16[2,128,512]{2,1,0:T(8,128)(2,1)S(1)}, bf16[2,128,512]{2,1,0:T(8,128)(2,1)S(1)}, u32[]{:S(2)}, u32[]{:S(2)}) collective-permute-start(bf16[2,128,512]{2,1,0:T(8,128)(2,1)S(1)} %pad_maximum_fusion.own_hbm), channel_id=1, source_target_pairs={{0,2},{1,3},{2,4},{3,5},{4,6},{5,7},{6,8},{7,9},{8,10},{9,11},{10,... | collective-permute-start | bytes 786440 | tf_op jit(solution)/shard_map/ppermute | solution.py:196
  9.1 9.2 %collective-permute-start.2 = (bf16[2,128,512]{2,1,0:T(8,128)(2,1)S(1)}, bf16[2,128,512]{2,1,0:T(8,128)(2,1)S(1)}, u32[]{:S(2)}, u32[]{:S(2)}) collective-permute-start(bf16[2,128,512]{2,1,0:T(8,128)(2,1)S(1)} %pad_maximum_fusion.own_hbm), channel_id=1, source_target_pairs={{0,1},{1,0},{2,3},{3,2},{4,5},{5,4},{6,7},{7,6},{8,9},{9,8},{10,11... | collective-permute-start | bytes 786440 | tf_op jit(solution)/shard_map/ppermute | solution.py:207
  13.6 5.8 %copy-start.1 = (bf16[2,128,512]{2,1,0:T(8,128)(2,1)}, bf16[2,128,512]{2,1,0:T(8,128)(2,1)S(1)}, u32[]{:S(2)}) copy-start(bf16[2,128,512]{2,1,0:T(8,128)(2,1)S(1)} %collective-permute-done.1.next_hbm) | copy-start | bytes 786436
  17.6 1.8 %copy-start.2 = (bf16[2,128,512]{2,1,0:T(8,128)(2,1)}, bf16[2,128,512]{2,1,0:T(8,128)(2,1)S(1)}, u32[]{:S(2)}) copy-start(bf16[2,128,512]{2,1,0:T(8,128)(2,1)S(1)} %collective-permute-done.prev_hbm) | copy-start | bytes 786436
  17.7 1.7 %collective-permute-start.3 = (bf16[2,128,512]{2,1,0:T(8,128)(2,1)S(1)}, bf16[2,128,512]{2,1,0:T(8,128)(2,1)S(1)}, u32[]{:S(2)}, u32[]{:S(2)}) collective-permute-start(bf16[2,128,512]{2,1,0:T(8,128)(2,1)S(1)} %broadcast_select_fusion), channel_id=1, source_target_pairs={{0,1},{1,0},{2,3},{3,2},{4,5},{5,4},{6,7},{7,6},{8,9},{9,8},{10,11... | collective-permute-start | bytes 786440 | tf_op jit(solution)/shard_map/ppermute | solution.py:209
  18.2 1.2 %copy-start.3 = (bf16[2,128,512]{2,1,0:T(8,128)(2,1)}, bf16[2,128,512]{2,1,0:T(8,128)(2,1)S(1)}, u32[]{:S(2)}) copy-start(bf16[2,128,512]{2,1,0:T(8,128)(2,1)S(1)} %collective-permute-done.2.partner_hbm) | copy-start | bytes 786436
  19.4 0.7 %copy-start.4 = (bf16[2,128,512]{2,1,0:T(8,128)(2,1)}, bf16[2,128,512]{2,1,0:T(8,128)(2,1)S(1)}, u32[]{:S(2)}) copy-start(bf16[2,128,512]{2,1,0:T(8,128)(2,1)S(1)} %collective-permute-done.3.sel_hbm) | copy-start | bytes 786436
  27.3 7.5 %collective-permute-start.4 = (bf16[64,1024]{1,0:T(8,128)(2,1)}, bf16[64,1024]{1,0:T(8,128)(2,1)S(1)}, u32[]{:S(2)}, u32[]{:S(2)}) collective-permute-start(bf16[64,1024]{1,0:T(8,128)(2,1)} %get-tuple-element.18), channel_id=1, source_target_pairs={{1,2},{3,4},{5,6},{7,8},{9,10},{11,12},{13,14},{2,1},{4,3},{6,5},{... | collective-permute-start | bytes 393224 | tf_op jit(solution)/shard_map/ppermute | solution.py:247
  29.8 5.0 %collective-permute-start.5 = (bf16[64,1024]{1,0:T(8,128)(2,1)}, bf16[64,1024]{1,0:T(8,128)(2,1)S(1)}, u32[]{:S(2)}, u32[]{:S(2)}) collective-permute-start(bf16[64,1024]{1,0:T(8,128)(2,1)} %get-tuple-element.19), channel_id=1, source_target_pairs={{0,1},{1,0},{2,3},{3,2},{4,5},{5,4},{6,7},{7,6},{8,9},{9,8},{10,11... | collective-permute-start | bytes 393224 | tf_op jit(solution)/shard_map/ppermute | solution.py:248
  34.8 0.7 %copy-start.5 = (bf16[64,1024]{1,0:T(8,128)(2,1)}, bf16[64,1024]{1,0:T(8,128)(2,1)S(1)}, u32[]{:S(2)}) copy-start(bf16[64,1024]{1,0:T(8,128)(2,1)S(1)} %collective-permute-done.4.cross_ref) | copy-start | bytes 393220
  34.8 0.7 %copy-start.6 = (bf16[64,1024]{1,0:T(8,128)(2,1)}, bf16[64,1024]{1,0:T(8,128)(2,1)S(1)}, u32[]{:S(2)}) copy-start(bf16[64,1024]{1,0:T(8,128)(2,1)S(1)} %collective-permute-done.5.pairg_ref) | copy-start | bytes 393220

commit v11 on v10

--- a/solution.py
+++ b/solution.py
@@ -238,7 +238,7 @@
         ),
         name="attention_glu",
     )(
-        meta, utterance_lengths, table, bias_t, query_proj, from_prev, from_next, packed, partner, partner_sel,
+        meta, utterance_lengths, table, bias_t, query_proj, *[pltpu.with_memory_space_constraint(a, pltpu.VMEM) for a in (from_prev, from_next)], packed, *[pltpu.with_memory_space_constraint(a, pltpu.VMEM) for a in (partner, partner_sel)],
         frames_in, norm_gain.reshape(1, -1), out_weight, expand_weight,
     )
 
@@ -263,7 +263,7 @@
             flops=conv_flops, transcendentals=rows * model_width, bytes_accessed=conv_bytes
         ),
         name="conv_shrink",
-    )(meta, gated, cross_recv, partner_recv, depth_taps, inner_gain.reshape(1, -1), mid, shrink_weight)
+    )(meta, gated, pltpu.with_memory_space_constraint(cross_recv, pltpu.VMEM), pltpu.with_memory_space_constraint(partner_recv, pltpu.VMEM), depth_taps, inner_gain.reshape(1, -1), mid, shrink_weight)
 
 
 def solution(mesh):

time: 40.7 us -> 39 us (0.958)
  local copies, waits for them, and re-layouts: 2.67 us -> 1.29 us
    unnamed x14 -> x2, local copies, waits for them, and re-layouts: 1.38 us -> 0.01 us
where the time goes in v11:
time: 39 us; the launch traced here: 38.6 us
  waiting for transfers between devices  13.3 us (34%)
  Pallas kernels  11.7 us (30%)
  starting transfers between devices  10.6 us (27%)
  other arithmetic  1.67 us (4%)
  local copies, waits for them, and re-layouts  1.29 us (3%)
    ppermute x2, waiting for transfers between devices, lin_shift(): lax.ppermute(value, ('chip', 'core'), [(s, s + steps) for s in range(lead...  7.27 us
    pallas_call x1, Pallas kernels, on_device(): pl.pallas_call(attention_kernel, out_shape=(jax.ShapeDtypeStruct((rows, m...  6.89 us
    ppermute x2, starting transfers between devices, lin_shift(): lax.ppermute(value, ('chip', 'core'), [(s, s + steps) for s in range(lead...  6.18 us
    ppermute x1, waiting for transfers between devices, on_device(): cross_recv = lax.ppermute(cross_send, ('chip', 'core'), inward)  4.9 us
    pallas_call x1, Pallas kernels, on_device(): pl.pallas_call(conv_kernel, out_shape=jax.ShapeDtypeStruct((rows, model_w...  4.78 us
    ppermute x1, starting transfers between devices, on_device(): cross_recv = lax.ppermute(cross_send, ('chip', 'core'), inward)  2.51 us
    ppermute x1, starting transfers between devices, on_device(): partner = lax.ppermute(gated_input, 'core', swap)  1.24 us
    ppermute x1, waiting for transfers between devices, on_device(): partner_sel = lax.ppermute(sel, 'core', swap)  1.16 us
  transfers between devices with their start and end apart: 6, of which 4 were waited for; matrix products, arithmetic and copies ran while one was open for 5% of the time, Pallas kernels for 0%

profile of v11, /device:TPU:21, one launch (start us, length us, event | category | flops | bytes accessed | tf_op | source)
XLA Modules:
  0.0 38.6 jit_solution(13001232415005720914)
XLA Ops:
  0.0 1.0 %pad_maximum_fusion.own_hbm = bf16[2,128,512]{2,1,0:T(8,128)(2,1)S(1)} fusion(bf16[1,128,512]{2,1,0:T(8,128)(2,1)} %bitcast.7, bf16[1,128,512]{2,1,0:T(8,128)(2,1)} %bitcast.8), kind=kLoop, calls=%fused_computation | loop fusion | flops 131072 | bytes 524288 | tf_op jit(solution)/shard_map/stack | solution.py:202
  1.0 0.0 copy-start
  1.0 2.1 %collective-permute-start.1 = (bf16[2,128,512]{2,1,0:T(8,128)(2,1)S(1)}, bf16[2,128,512]{2,1,0:T(8,128)(2,1)S(1)}, u32[]{:S(2)}, u32[]{:S(2)}) collective-permute-start(bf16[2,128,512]{2,1,0:T(8,128)(2,1)S(1)} %pad_maximum_fusion.own_hbm), channel_id=1, source_target_pairs={{2,0},{3,1},{4,2},{5,3},{6,4},{7,5},{8,6},{9,7},{10,8},{11,9},{12,... | collective-permute-start | bytes 786440 | tf_op jit(solution)/shard_map/ppermute | solution.py:196
  3.2 4.0 %collective-permute-start = (bf16[2,128,512]{2,1,0:T(8,128)(2,1)S(1)}, bf16[2,128,512]{2,1,0:T(8,128)(2,1)S(1)}, u32[]{:S(2)}, u32[]{:S(2)}) collective-permute-start(bf16[2,128,512]{2,1,0:T(8,128)(2,1)S(1)} %pad_maximum_fusion.own_hbm), channel_id=1, source_target_pairs={{0,2},{1,3},{2,4},{3,5},{4,6},{5,7},{6,8},{7,9},{8,10},{9,11},{10,... | collective-permute-start | bytes 786440 | tf_op jit(solution)/shard_map/ppermute | solution.py:196
  7.2 0.7 %pad.4 = s32[768]{0:T(1024)S(1)} pad(s32[767]{0:T(1024)} %param.18, s32[]{:T(128)} %constant.5.clone.1), padding=0_1 | pad | bytes 6144 | tf_op jit(solution)/shard_map/jit(_pad)/pad | solution.py:199
  7.9 0.6 %reshape.9.table_ref = s32[1,768]{1,0:T(1,128)} reshape(s32[768]{0:T(1024)S(1)} %pad.4) | data formatting | bytes 6144 | tf_op jit(solution)/shard_map/reshape | solution.py:199
  8.5 0.6 %pad_add_fusion.meta_ref = s32[2]{0:T(128)} fusion(s32[1]{0:T(128)} %bitcast.3, s32[1]{0:T(128)} %bitcast.2), kind=kLoop, calls=%fused_computation.2 | loop fusion | flops 2 | bytes 16 | tf_op jit(solution)/shard_map/stack | solution.py:192
  9.1 1.2 %collective-permute-start.2 = (bf16[2,128,512]{2,1,0:T(8,128)(2,1)S(1)}, bf16[2,128,512]{2,1,0:T(8,128)(2,1)S(1)}, u32[]{:S(2)}, u32[]{:S(2)}) collective-permute-start(bf16[2,128,512]{2,1,0:T(8,128)(2,1)S(1)} %pad_maximum_fusion.own_hbm), channel_id=1, source_target_pairs={{0,1},{1,0},{2,3},{3,2},{4,5},{5,4},{6,7},{7,6},{8,9},{9,8},{10,11... | collective-permute-start | bytes 786440 | tf_op jit(solution)/shard_map/ppermute | solution.py:207
  10.4 3.2 %collective-permute-done.1.next_hbm = bf16[2,128,512]{2,1,0:T(8,128)(2,1)S(1)} collective-permute-done((bf16[2,128,512]{2,1,0:T(8,128)(2,1)S(1)}, bf16[2,128,512]{2,1,0:T(8,128)(2,1)S(1)}, u32[]{:S(2)}, u32[]{:S(2)}) %collective-permute-start.1) | collective-permute-done | bytes 262176 | tf_op jit(solution)/shard_map/ppermute | solution.py:196
  13.6 4.1 %collective-permute-done.prev_hbm = bf16[2,128,512]{2,1,0:T(8,128)(2,1)S(1)} collective-permute-done((bf16[2,128,512]{2,1,0:T(8,128)(2,1)S(1)}, bf16[2,128,512]{2,1,0:T(8,128)(2,1)S(1)}, u32[]{:S(2)}, u32[]{:S(2)}) %collective-permute-start) | collective-permute-done | bytes 262176 | tf_op jit(solution)/shard_map/ppermute | solution.py:196
  17.7 0.6 %collective-permute-start.3 = (bf16[2,128,512]{2,1,0:T(8,128)(2,1)S(1)}, bf16[2,128,512]{2,1,0:T(8,128)(2,1)S(1)}, u32[]{:S(2)}, u32[]{:S(2)}) collective-permute-start(bf16[2,128,512]{2,1,0:T(8,128)(2,1)S(1)} %broadcast_select_fusion), channel_id=1, source_target_pairs={{0,1},{1,0},{2,3},{3,2},{4,5},{5,4},{6,7},{7,6},{8,9},{9,8},{10,11... | collective-permute-start | bytes 786440 | tf_op jit(solution)/shard_map/ppermute | solution.py:209
  18.2 0.0 collective-permute-done.2.partner_hbm
  18.2 1.2 %collective-permute-done.3.sel_hbm = bf16[2,128,512]{2,1,0:T(8,128)(2,1)S(1)} collective-permute-done((bf16[2,128,512]{2,1,0:T(8,128)(2,1)S(1)}, bf16[2,128,512]{2,1,0:T(8,128)(2,1)S(1)}, u32[]{:S(2)}, u32[]{:S(2)}) %collective-permute-start.3) | collective-permute-done | bytes 262176 | tf_op jit(solution)/shard_map/ppermute | solution.py:209
  19.4 0.0 copy-done
  19.4 6.9 %attention_glu.1 = (bf16[128,1024]{1,0:T(8,128)(2,1)}, bf16[128,1024]{1,0:T(8,128)(2,1)}, bf16[64,1024]{1,0:T(8,128)(2,1)}, bf16[64,1024]{1,0:T(8,128)(2,1)}) custom-call(s32[2]{0:T(128)} %pad_add_fusion.meta_ref, s32[16]{0:T(128)} %len_ref.1, s32[1,768]{1,0:T(1,128)} %reshape.9.table_ref, f32[8,32]{1,0:T(8,128)} %bitcast.9, bf16[128,512]{1,0:T(8,128)(2,1)} %q_ref.1, ...), custom_call_target="tpu_custom_call" | custom-call | flops 1006632960 | bytes 7208960 | tf_op jit(solution)/shard_map/attention_glu/pallas_call | solution.py:219
  26.3 2.5 %collective-permute-start.4 = (bf16[64,1024]{1,0:T(8,128)(2,1)}, bf16[64,1024]{1,0:T(8,128)(2,1)S(1)}, u32[]{:S(2)}, u32[]{:S(2)}) collective-permute-start(bf16[64,1024]{1,0:T(8,128)(2,1)} %get-tuple-element.18), channel_id=1, source_target_pairs={{1,2},{3,4},{5,6},{7,8},{9,10},{11,12},{13,14},{2,1},{4,3},{6,5},{... | collective-permute-start | bytes 393224 | tf_op jit(solution)/shard_map/ppermute | solution.py:247
  28.8 0.1 collective-permute-start.5
  28.9 4.9 %collective-permute-done.4.cross_ref = bf16[64,1024]{1,0:T(8,128)(2,1)S(1)} collective-permute-done((bf16[64,1024]{1,0:T(8,128)(2,1)}, bf16[64,1024]{1,0:T(8,128)(2,1)S(1)}, u32[]{:S(2)}, u32[]{:S(2)}) %collective-permute-start.4) | collective-permute-done | bytes 131104 | tf_op jit(solution)/shard_map/ppermute | solution.py:247
  33.8 0.0 collective-permute-done.5.pairg_ref
  33.8 4.8 %conv_shrink.1 = bf16[128,1024]{1,0:T(8,128)(2,1)} custom-call(s32[2]{0:T(128)} %pad_add_fusion.meta_ref, bf16[128,1024]{1,0:T(8,128)(2,1)} %get-tuple-element.17.gated_ref, bf16[64,1024]{1,0:T(8,128)(2,1)S(1)} %collective-permute-done.4.cross_ref, bf16[64,1024]{1,0:T(8,128)(2,1)S(1)} %collective-permute-done.5.pairg_ref, f32[31,1024]{1,0:T(8,128)} %taps_ref.1, ...), custom_call_target="tpu_custom_call" | custom-call | flops 276561920 | bytes 3272704 | tf_op jit(solution)/shard_map/conv_shrink/pallas_call | solution.py:251
  (1 shorter events, 0.0 us)
Async XLA Ops:
  1.0 18.4 %copy-start = (bf16[2,128,512]{2,1,0:T(8,128)(2,1)}, bf16[2,128,512]{2,1,0:T(8,128)(2,1)S(1)}, u32[]{:S(2)}) copy-start(bf16[2,128,512]{2,1,0:T(8,128)(2,1)S(1)} %pad_maximum_fusion.own_hbm) | copy-start | bytes 786436
  1.0 12.6 %collective-permute-start.1 = (bf16[2,128,512]{2,1,0:T(8,128)(2,1)S(1)}, bf16[2,128,512]{2,1,0:T(8,128)(2,1)S(1)}, u32[]{:S(2)}, u32[]{:S(2)}) collective-permute-start(bf16[2,128,512]{2,1,0:T(8,128)(2,1)S(1)} %pad_maximum_fusion.own_hbm), channel_id=1, source_target_pairs={{2,0},{3,1},{4,2},{5,3},{6,4},{7,5},{8,6},{9,7},{10,8},{11,9},{12,... | collective-permute-start | bytes 786440 | tf_op jit(solution)/shard_map/ppermute | solution.py:196
  3.2 14.5 %collective-permute-start = (bf16[2,128,512]{2,1,0:T(8,128)(2,1)S(1)}, bf16[2,128,512]{2,1,0:T(8,128)(2,1)S(1)}, u32[]{:S(2)}, u32[]{:S(2)}) collective-permute-start(bf16[2,128,512]{2,1,0:T(8,128)(2,1)S(1)} %pad_maximum_fusion.own_hbm), channel_id=1, source_target_pairs={{0,2},{1,3},{2,4},{3,5},{4,6},{5,7},{6,8},{7,9},{8,10},{9,11},{10,... | collective-permute-start | bytes 786440 | tf_op jit(solution)/shard_map/ppermute | solution.py:196
  9.1 9.1 %collective-permute-start.2 = (bf16[2,128,512]{2,1,0:T(8,128)(2,1)S(1)}, bf16[2,128,512]{2,1,0:T(8,128)(2,1)S(1)}, u32[]{:S(2)}, u32[]{:S(2)}) collective-permute-start(bf16[2,128,512]{2,1,0:T(8,128)(2,1)S(1)} %pad_maximum_fusion.own_hbm), channel_id=1, source_target_pairs={{0,1},{1,0},{2,3},{3,2},{4,5},{5,4},{6,7},{7,6},{8,9},{9,8},{10,11... | collective-permute-start | bytes 786440 | tf_op jit(solution)/shard_map/ppermute | solution.py:207
  17.7 1.7 %collective-permute-start.3 = (bf16[2,128,512]{2,1,0:T(8,128)(2,1)S(1)}, bf16[2,128,512]{2,1,0:T(8,128)(2,1)S(1)}, u32[]{:S(2)}, u32[]{:S(2)}) collective-permute-start(bf16[2,128,512]{2,1,0:T(8,128)(2,1)S(1)} %broadcast_select_fusion), channel_id=1, source_target_pairs={{0,1},{1,0},{2,3},{3,2},{4,5},{5,4},{6,7},{7,6},{8,9},{9,8},{10,11... | collective-permute-start | bytes 786440 | tf_op jit(solution)/shard_map/ppermute | solution.py:209
  26.3 7.5 %collective-permute-start.4 = (bf16[64,1024]{1,0:T(8,128)(2,1)}, bf16[64,1024]{1,0:T(8,128)(2,1)S(1)}, u32[]{:S(2)}, u32[]{:S(2)}) collective-permute-start(bf16[64,1024]{1,0:T(8,128)(2,1)} %get-tuple-element.18), channel_id=1, source_target_pairs={{1,2},{3,4},{5,6},{7,8},{9,10},{11,12},{13,14},{2,1},{4,3},{6,5},{... | collective-permute-start | bytes 393224 | tf_op jit(solution)/shard_map/ppermute | solution.py:247
  28.8 5.0 %collective-permute-start.5 = (bf16[64,1024]{1,0:T(8,128)(2,1)}, bf16[64,1024]{1,0:T(8,128)(2,1)S(1)}, u32[]{:S(2)}, u32[]{:S(2)}) collective-permute-start(bf16[64,1024]{1,0:T(8,128)(2,1)} %get-tuple-element.19), channel_id=1, source_target_pairs={{0,1},{1,0},{2,3},{3,2},{4,5},{5,4},{6,7},{7,6},{8,9},{9,8},{10,11... | collective-permute-start | bytes 393224 | tf_op jit(solution)/shard_map/ppermute | solution.py:248

commit v12 on v11

--- a/solution.py
+++ b/solution.py
@@ -27,6 +27,21 @@
     return centred * lax.rsqrt(spread + norm_epsilon) * gain_vec
 
 
+class row_chunks:
+    def __init__(self, src, dst, sems, count):
+        step = src.shape[0] // count
+        self.copies = [
+            pltpu.make_async_copy(src.at[pl.ds(i * step, step)], dst.at[pl.ds(i * step, step)], sems.at[i])
+            for i in range(count)
+        ]
+        for copy in self.copies:
+            copy.start()
+
+    def wait(self):
+        for copy in self.copies:
+            copy.wait()
+
+
 def sigmoid(values):
     return 1.0 / (1.0 + jnp.exp(-values))
 
@@ -36,7 +51,7 @@
     prev_hbm, next_hbm, own_hbm, partner_hbm, sel_hbm,
     x_ref, gain_ref, ow_hbm, ew_hbm,
     mid_ref, gated_ref, cross_ref, partner_ref,
-    ow_vmem, ew_vmem, sems, att_ref, win_ref,
+    ow_vmem, ew_vmem, sems, att_ref, win_ref, chunk_sems,
 ):
     base = meta_ref[0]
     core = meta_ref[1]
@@ -54,10 +69,8 @@
     ]
     for copy in copies:
         copy.start()
-    ow_copy = pltpu.make_async_copy(ow_hbm, ow_vmem, sems.at[0])
-    ew_copy = pltpu.make_async_copy(ew_hbm, ew_vmem, sems.at[1])
-    ow_copy.start()
-    ew_copy.start()
+    ow_copy = row_chunks(ow_hbm, ow_vmem, chunk_sems.at[0], 2)
+    ew_copy = row_chunks(ew_hbm, ew_vmem, chunk_sems.at[1], 4)
     blocks = win_ref.shape[0] // planes
     rows, att_width = q_ref.shape
     heads = bias_t_ref.shape[0]
@@ -137,8 +150,7 @@
     meta_ref, gated_ref, cross_ref, pairg_ref, taps_ref, gain_ref, mid_ref, sw_hbm,
     out_ref, win_ref, conv_ref, sw_vmem, sems,
 ):
-    sw_copy = pltpu.make_async_copy(sw_hbm, sw_vmem, sems.at[0])
-    sw_copy.start()
+    sw_copy = row_chunks(sw_hbm, sw_vmem, sems.at[0], 4)
     half = cross_ref.shape[0]
     rows, model_width = mid_ref.shape
     first_core = meta_ref[1] == 0
@@ -232,6 +244,7 @@
             pltpu.SemaphoreType.DMA((7,)),
             pltpu.VMEM((rows, att_width), jnp.bfloat16),
             pltpu.VMEM((len(order) * packed.shape[0], rows, att_width), jnp.bfloat16),
+            pltpu.SemaphoreType.DMA((2, 4)),
         ],
         cost_estimate=pl.CostEstimate(
             flops=attn_flops, transcendentals=heads * rows * window + rows * model_width, bytes_accessed=attn_bytes
@@ -257,7 +270,7 @@
             pltpu.VMEM((rows + 2 * half, model_width), jnp.float32),
             pltpu.VMEM((rows, model_width), jnp.float32),
             pltpu.VMEM((model_width, model_width), jnp.bfloat16),
-            pltpu.SemaphoreType.DMA((1,)),
+            pltpu.SemaphoreType.DMA((1, 4)),
         ],
         cost_estimate=pl.CostEstimate(
             flops=conv_flops, transcendentals=rows * model_width, bytes_accessed=conv_bytes

time: 39 us -> 39.1 us (level)
  no operation moved by 1% of the time
where the time goes in v12:
time: 39.1 us; the launch traced here: 38.7 us
  waiting for transfers between devices  13.3 us (34%)
  Pallas kernels  11.8 us (30%)
  starting transfers between devices  10.6 us (27%)
  other arithmetic  1.67 us (4%)
  local copies, waits for them, and re-layouts  1.29 us (3%)
    ppermute x2, waiting for transfers between devices, lin_shift(): lax.ppermute(value, ('chip', 'core'), [(s, s + steps) for s in range(lead...  7.27 us
    pallas_call x1, Pallas kernels, on_device(): pl.pallas_call(attention_kernel, out_shape=(jax.ShapeDtypeStruct((rows, m...  6.97 us
    ppermute x2, starting transfers between devices, lin_shift(): lax.ppermute(value, ('chip', 'core'), [(s, s + steps) for s in range(lead...  6.18 us
    ppermute x1, waiting for transfers between devices, on_device(): cross_recv = lax.ppermute(cross_send, ('chip', 'core'), inward)  4.9 us
    pallas_call x1, Pallas kernels, on_device(): pl.pallas_call(conv_kernel, out_shape=jax.ShapeDtypeStruct((rows, model_w...  4.82 us
    ppermute x1, starting transfers between devices, on_device(): cross_recv = lax.ppermute(cross_send, ('chip', 'core'), inward)  2.51 us
    ppermute x1, starting transfers between devices, on_device(): partner = lax.ppermute(gated_input, 'core', swap)  1.24 us
    ppermute x1, waiting for transfers between devices, on_device(): partner_sel = lax.ppermute(sel, 'core', swap)  1.16 us
  transfers between devices with their start and end apart: 6, of which 4 were waited for; matrix products, arithmetic and copies ran while one was open for 5% of the time, Pallas kernels for 0%

profile of v12, /device:TPU:21, one launch (start us, length us, event | category | flops | bytes accessed | tf_op | source)
XLA Modules:
  0.0 38.7 jit_solution(6563443460978498115)
XLA Ops:
  0.0 1.0 %pad_maximum_fusion.own_hbm = bf16[2,128,512]{2,1,0:T(8,128)(2,1)S(1)} fusion(bf16[1,128,512]{2,1,0:T(8,128)(2,1)} %bitcast.7, bf16[1,128,512]{2,1,0:T(8,128)(2,1)} %bitcast.8), kind=kLoop, calls=%fused_computation | loop fusion | flops 131072 | bytes 524288 | tf_op jit(solution)/shard_map/stack | solution.py:214
  1.0 0.0 copy-start
  1.0 2.1 %collective-permute-start.1 = (bf16[2,128,512]{2,1,0:T(8,128)(2,1)S(1)}, bf16[2,128,512]{2,1,0:T(8,128)(2,1)S(1)}, u32[]{:S(2)}, u32[]{:S(2)}) collective-permute-start(bf16[2,128,512]{2,1,0:T(8,128)(2,1)S(1)} %pad_maximum_fusion.own_hbm), channel_id=1, source_target_pairs={{2,0},{3,1},{4,2},{5,3},{6,4},{7,5},{8,6},{9,7},{10,8},{11,9},{12,... | collective-permute-start | bytes 786440 | tf_op jit(solution)/shard_map/ppermute | solution.py:208
  3.2 4.0 %collective-permute-start = (bf16[2,128,512]{2,1,0:T(8,128)(2,1)S(1)}, bf16[2,128,512]{2,1,0:T(8,128)(2,1)S(1)}, u32[]{:S(2)}, u32[]{:S(2)}) collective-permute-start(bf16[2,128,512]{2,1,0:T(8,128)(2,1)S(1)} %pad_maximum_fusion.own_hbm), channel_id=1, source_target_pairs={{0,2},{1,3},{2,4},{3,5},{4,6},{5,7},{6,8},{7,9},{8,10},{9,11},{10,... | collective-permute-start | bytes 786440 | tf_op jit(solution)/shard_map/ppermute | solution.py:208
  7.2 0.7 %pad.4 = s32[768]{0:T(1024)S(1)} pad(s32[767]{0:T(1024)} %param.18, s32[]{:T(128)} %constant.5.clone.1), padding=0_1 | pad | bytes 6144 | tf_op jit(solution)/shard_map/jit(_pad)/pad | solution.py:211
  7.9 0.6 %reshape.9.table_ref = s32[1,768]{1,0:T(1,128)} reshape(s32[768]{0:T(1024)S(1)} %pad.4) | data formatting | bytes 6144 | tf_op jit(solution)/shard_map/reshape | solution.py:211
  8.5 0.6 %pad_add_fusion.meta_ref = s32[2]{0:T(128)} fusion(s32[1]{0:T(128)} %bitcast.3, s32[1]{0:T(128)} %bitcast.2), kind=kLoop, calls=%fused_computation.2 | loop fusion | flops 2 | bytes 16 | tf_op jit(solution)/shard_map/stack | solution.py:204
  9.1 1.2 %collective-permute-start.2 = (bf16[2,128,512]{2,1,0:T(8,128)(2,1)S(1)}, bf16[2,128,512]{2,1,0:T(8,128)(2,1)S(1)}, u32[]{:S(2)}, u32[]{:S(2)}) collective-permute-start(bf16[2,128,512]{2,1,0:T(8,128)(2,1)S(1)} %pad_maximum_fusion.own_hbm), channel_id=1, source_target_pairs={{0,1},{1,0},{2,3},{3,2},{4,5},{5,4},{6,7},{7,6},{8,9},{9,8},{10,11... | collective-permute-start | bytes 786440 | tf_op jit(solution)/shard_map/ppermute | solution.py:219
  10.4 3.2 %collective-permute-done.1.next_hbm = bf16[2,128,512]{2,1,0:T(8,128)(2,1)S(1)} collective-permute-done((bf16[2,128,512]{2,1,0:T(8,128)(2,1)S(1)}, bf16[2,128,512]{2,1,0:T(8,128)(2,1)S(1)}, u32[]{:S(2)}, u32[]{:S(2)}) %collective-permute-start.1) | collective-permute-done | bytes 262176 | tf_op jit(solution)/shard_map/ppermute | solution.py:208
  13.6 4.1 %collective-permute-done.prev_hbm = bf16[2,128,512]{2,1,0:T(8,128)(2,1)S(1)} collective-permute-done((bf16[2,128,512]{2,1,0:T(8,128)(2,1)S(1)}, bf16[2,128,512]{2,1,0:T(8,128)(2,1)S(1)}, u32[]{:S(2)}, u32[]{:S(2)}) %collective-permute-start) | collective-permute-done | bytes 262176 | tf_op jit(solution)/shard_map/ppermute | solution.py:208
  17.7 0.6 %collective-permute-start.3 = (bf16[2,128,512]{2,1,0:T(8,128)(2,1)S(1)}, bf16[2,128,512]{2,1,0:T(8,128)(2,1)S(1)}, u32[]{:S(2)}, u32[]{:S(2)}) collective-permute-start(bf16[2,128,512]{2,1,0:T(8,128)(2,1)S(1)} %broadcast_select_fusion), channel_id=1, source_target_pairs={{0,1},{1,0},{2,3},{3,2},{4,5},{5,4},{6,7},{7,6},{8,9},{9,8},{10,11... | collective-permute-start | bytes 786440 | tf_op jit(solution)/shard_map/ppermute | solution.py:221
  18.2 0.0 collective-permute-done.2.partner_hbm
  18.2 1.2 %collective-permute-done.3.sel_hbm = bf16[2,128,512]{2,1,0:T(8,128)(2,1)S(1)} collective-permute-done((bf16[2,128,512]{2,1,0:T(8,128)(2,1)S(1)}, bf16[2,128,512]{2,1,0:T(8,128)(2,1)S(1)}, u32[]{:S(2)}, u32[]{:S(2)}) %collective-permute-start.3) | collective-permute-done | bytes 262176 | tf_op jit(solution)/shard_map/ppermute | solution.py:221
  19.4 0.0 copy-done
  19.4 7.0 %attention_glu.1 = (bf16[128,1024]{1,0:T(8,128)(2,1)}, bf16[128,1024]{1,0:T(8,128)(2,1)}, bf16[64,1024]{1,0:T(8,128)(2,1)}, bf16[64,1024]{1,0:T(8,128)(2,1)}) custom-call(s32[2]{0:T(128)} %pad_add_fusion.meta_ref, s32[16]{0:T(128)} %len_ref.1, s32[1,768]{1,0:T(1,128)} %reshape.9.table_ref, f32[8,32]{1,0:T(8,128)} %bitcast.9, bf16[128,512]{1,0:T(8,128)(2,1)} %q_ref.1, ...), custom_call_target="tpu_custom_call" | custom-call | flops 1006632960 | bytes 7208960 | tf_op jit(solution)/shard_map/attention_glu/pallas_call | solution.py:231
  26.4 2.5 %collective-permute-start.4 = (bf16[64,1024]{1,0:T(8,128)(2,1)}, bf16[64,1024]{1,0:T(8,128)(2,1)S(1)}, u32[]{:S(2)}, u32[]{:S(2)}) collective-permute-start(bf16[64,1024]{1,0:T(8,128)(2,1)} %get-tuple-element.18), channel_id=1, source_target_pairs={{1,2},{3,4},{5,6},{7,8},{9,10},{11,12},{13,14},{2,1},{4,3},{6,5},{... | collective-permute-start | bytes 393224 | tf_op jit(solution)/shard_map/ppermute | solution.py:260
  28.9 0.1 collective-permute-start.5
  29.0 4.9 %collective-permute-done.4.cross_ref = bf16[64,1024]{1,0:T(8,128)(2,1)S(1)} collective-permute-done((bf16[64,1024]{1,0:T(8,128)(2,1)}, bf16[64,1024]{1,0:T(8,128)(2,1)S(1)}, u32[]{:S(2)}, u32[]{:S(2)}) %collective-permute-start.4) | collective-permute-done | bytes 131104 | tf_op jit(solution)/shard_map/ppermute | solution.py:260
  33.9 0.0 collective-permute-done.5.pairg_ref
  33.9 4.8 %conv_shrink.1 = bf16[128,1024]{1,0:T(8,128)(2,1)} custom-call(s32[2]{0:T(128)} %pad_add_fusion.meta_ref, bf16[128,1024]{1,0:T(8,128)(2,1)} %get-tuple-element.17.gated_ref, bf16[64,1024]{1,0:T(8,128)(2,1)S(1)} %collective-permute-done.4.cross_ref, bf16[64,1024]{1,0:T(8,128)(2,1)S(1)} %collective-permute-done.5.pairg_ref, f32[31,1024]{1,0:T(8,128)} %taps_ref.1, ...), custom_call_target="tpu_custom_call" | custom-call | flops 276561920 | bytes 3272704 | tf_op jit(solution)/shard_map/conv_shrink/pallas_call | solution.py:264
  (1 shorter events, 0.0 us)
Async XLA Ops:
  1.0 18.4 %copy-start = (bf16[2,128,512]{2,1,0:T(8,128)(2,1)}, bf16[2,128,512]{2,1,0:T(8,128)(2,1)S(1)}, u32[]{:S(2)}) copy-start(bf16[2,128,512]{2,1,0:T(8,128)(2,1)S(1)} %pad_maximum_fusion.own_hbm) | copy-start | bytes 786436
  1.0 12.6 %collective-permute-start.1 = (bf16[2,128,512]{2,1,0:T(8,128)(2,1)S(1)}, bf16[2,128,512]{2,1,0:T(8,128)(2,1)S(1)}, u32[]{:S(2)}, u32[]{:S(2)}) collective-permute-start(bf16[2,128,512]{2,1,0:T(8,128)(2,1)S(1)} %pad_maximum_fusion.own_hbm), channel_id=1, source_target_pairs={{2,0},{3,1},{4,2},{5,3},{6,4},{7,5},{8,6},{9,7},{10,8},{11,9},{12,... | collective-permute-start | bytes 786440 | tf_op jit(solution)/shard_map/ppermute | solution.py:208
  3.2 14.5 %collective-permute-start = (bf16[2,128,512]{2,1,0:T(8,128)(2,1)S(1)}, bf16[2,128,512]{2,1,0:T(8,128)(2,1)S(1)}, u32[]{:S(2)}, u32[]{:S(2)}) collective-permute-start(bf16[2,128,512]{2,1,0:T(8,128)(2,1)S(1)} %pad_maximum_fusion.own_hbm), channel_id=1, source_target_pairs={{0,2},{1,3},{2,4},{3,5},{4,6},{5,7},{6,8},{7,9},{8,10},{9,11},{10,... | collective-permute-start | bytes 786440 | tf_op jit(solution)/shard_map/ppermute | solution.py:208
  9.1 9.1 %collective-permute-start.2 = (bf16[2,128,512]{2,1,0:T(8,128)(2,1)S(1)}, bf16[2,128,512]{2,1,0:T(8,128)(2,1)S(1)}, u32[]{:S(2)}, u32[]{:S(2)}) collective-permute-start(bf16[2,128,512]{2,1,0:T(8,128)(2,1)S(1)} %pad_maximum_fusion.own_hbm), channel_id=1, source_target_pairs={{0,1},{1,0},{2,3},{3,2},{4,5},{5,4},{6,7},{7,6},{8,9},{9,8},{10,11... | collective-permute-start | bytes 786440 | tf_op jit(solution)/shard_map/ppermute | solution.py:219
  17.7 1.7 %collective-permute-start.3 = (bf16[2,128,512]{2,1,0:T(8,128)(2,1)S(1)}, bf16[2,128,512]{2,1,0:T(8,128)(2,1)S(1)}, u32[]{:S(2)}, u32[]{:S(2)}) collective-permute-start(bf16[2,128,512]{2,1,0:T(8,128)(2,1)S(1)} %broadcast_select_fusion), channel_id=1, source_target_pairs={{0,1},{1,0},{2,3},{3,2},{4,5},{5,4},{6,7},{7,6},{8,9},{9,8},{10,11... | collective-permute-start | bytes 786440 | tf_op jit(solution)/shard_map/ppermute | solution.py:221
  26.4 7.5 %collective-permute-start.4 = (bf16[64,1024]{1,0:T(8,128)(2,1)}, bf16[64,1024]{1,0:T(8,128)(2,1)S(1)}, u32[]{:S(2)}, u32[]{:S(2)}) collective-permute-start(bf16[64,1024]{1,0:T(8,128)(2,1)} %get-tuple-element.18), channel_id=1, source_target_pairs={{1,2},{3,4},{5,6},{7,8},{9,10},{11,12},{13,14},{2,1},{4,3},{6,5},{... | collective-permute-start | bytes 393224 | tf_op jit(solution)/shard_map/ppermute | solution.py:260
  28.9 5.0 %collective-permute-start.5 = (bf16[64,1024]{1,0:T(8,128)(2,1)}, bf16[64,1024]{1,0:T(8,128)(2,1)S(1)}, u32[]{:S(2)}, u32[]{:S(2)}) collective-permute-start(bf16[64,1024]{1,0:T(8,128)(2,1)} %get-tuple-element.19), channel_id=1, source_target_pairs={{0,1},{1,0},{2,3},{3,2},{4,5},{5,4},{6,7},{7,6},{8,9},{9,8},{10,11... | collective-permute-start | bytes 393224 | tf_op jit(solution)/shard_map/ppermute | solution.py:261

commit v13 on v11

--- a/solution.py
+++ b/solution.py
@@ -34,9 +34,9 @@
 def attention_kernel(
     meta_ref, len_ref, table_ref, bias_t_ref, q_ref,
     prev_hbm, next_hbm, own_hbm, partner_hbm, sel_hbm,
-    x_ref, gain_ref, ow_hbm, ew_hbm,
+    x_ref, gain_ref, ow_hbm, value_hbm, gate_w,
     mid_ref, gated_ref, cross_ref, partner_ref,
-    ow_vmem, ew_vmem, sems, att_ref, win_ref,
+    ow_vmem, value_w, sems, att_ref, win_ref,
 ):
     base = meta_ref[0]
     core = meta_ref[1]
@@ -55,9 +55,9 @@
     for copy in copies:
         copy.start()
     ow_copy = pltpu.make_async_copy(ow_hbm, ow_vmem, sems.at[0])
-    ew_copy = pltpu.make_async_copy(ew_hbm, ew_vmem, sems.at[1])
+    value_copy = pltpu.make_async_copy(value_hbm.at[:, pl.ds(0, value_w.shape[1])], value_w, sems.at[1])
     ow_copy.start()
-    ew_copy.start()
+    value_copy.start()
     blocks = win_ref.shape[0] // planes
     rows, att_width = q_ref.shape
     heads = bias_t_ref.shape[0]
@@ -123,9 +123,9 @@
     mid_ref[...] = mid
     normed = layer_norm(mid.astype(jnp.float32), gain_ref[...]).astype(jnp.bfloat16)
     model_width = mid.shape[1]
-    ew_copy.wait()
-    value_half = jnp.dot(normed, ew_vmem[:, :model_width], preferred_element_type=jnp.float32)
-    gate_half = jnp.dot(normed, ew_vmem[:, model_width:], preferred_element_type=jnp.float32)
+    value_copy.wait()
+    value_half = jnp.dot(normed, value_w[...], preferred_element_type=jnp.float32)
+    gate_half = jnp.dot(normed, gate_w[...], preferred_element_type=jnp.float32)
     gated = (value_half * sigmoid(gate_half)).astype(jnp.bfloat16)
     gated_ref[...] = gated
     half = cross_ref.shape[0]
@@ -203,7 +203,7 @@
     from_prev = lin_shift(packed, REACH)
     from_next = lin_shift(packed, -REACH)
     swap = [(0, 1), (1, 0)]
-    gated_input, table, meta, bias_t = lax.optimization_barrier((packed, table, meta, bias_t))
+    gated_input, table, meta, bias_t, gate_weight = lax.optimization_barrier((packed, table, meta, bias_t, expand_weight[:, model_width:]))
     partner = lax.ppermute(gated_input, "core", swap)
     sel = jnp.where(core == 0, from_next, from_prev)
     partner_sel = lax.ppermute(sel, "core", swap)
@@ -224,11 +224,11 @@
             jax.ShapeDtypeStruct((half, model_width), jnp.bfloat16),
             jax.ShapeDtypeStruct((half, model_width), jnp.bfloat16),
         ),
-        in_specs=[smem, smem, vmem, vmem, vmem] + [anywhere] * 5 + [vmem, vmem, anywhere, anywhere],
+        in_specs=[smem, smem, vmem, vmem, vmem] + [anywhere] * 5 + [vmem, vmem, anywhere, anywhere, vmem],
         out_specs=(vmem, vmem, vmem, vmem),
         scratch_shapes=[
             pltpu.VMEM((att_width, model_width), jnp.bfloat16),
-            pltpu.VMEM((model_width, 2 * model_width), jnp.bfloat16),
+            pltpu.VMEM((model_width, model_width), jnp.bfloat16),
             pltpu.SemaphoreType.DMA((7,)),
             pltpu.VMEM((rows, att_width), jnp.bfloat16),
             pltpu.VMEM((len(order) * packed.shape[0], rows, att_width), jnp.bfloat16),
@@ -239,7 +239,9 @@
         name="attention_glu",
     )(
         meta, utterance_lengths, table, bias_t, query_proj, *[pltpu.with_memory_space_constraint(a, pltpu.VMEM) for a in (from_prev, from_next)], packed, *[pltpu.with_memory_space_constraint(a, pltpu.VMEM) for a in (partner, partner_sel)],
-        frames_in, norm_gain.reshape(1, -1), out_weight, expand_weight,
+        frames_in, norm_gain.reshape(1, -1), out_weight,
+        expand_weight,
+        pltpu.with_memory_space_constraint(gate_weight, pltpu.VMEM),
     )
 
     chips = count // cores

time: 39 us -> 39 us (level)
  local copies, waits for them, and re-layouts: 1.29 us -> 3.05 us
  waiting for transfers between devices: 13.3 us -> 11.6 us
    ppermute x2, waiting for transfers between devices: 7.27 us -> 5.49 us  [lin_shift(): lax.ppermute(value, ('chip', 'core'), [(s, s + steps) for s in range(lead...]
    slice x0 -> x1, local copies, waits for them, and re-layouts: none -> 1.76 us  [on_device(): expand_weight[:, model_width:]]
  transfers between devices with their start and end apart: 6 -> 6, of which waited for: 4 -> 4; matrix products, arithmetic and copies ran while one was open for 5% -> 10% of each run, Pallas kernels for 0% -> 0%
where the time goes in v13:
time: 39 us; the launch traced here: 38.6 us
  Pallas kernels  11.7 us (30%)
  waiting for transfers between devices  11.6 us (30%)
  starting transfers between devices  10.6 us (27%)
  local copies, waits for them, and re-layouts  3.05 us (8%)
  other arithmetic  1.67 us (4%)
    pallas_call x1, Pallas kernels, on_device(): pl.pallas_call(attention_kernel, out_shape=(jax.ShapeDtypeStruct((rows, m...  6.88 us
    ppermute x2, starting transfers between devices, lin_shift(): lax.ppermute(value, ('chip', 'core'), [(s, s + steps) for s in range(lead...  6.18 us
    ppermute x2, waiting for transfers between devices, lin_shift(): lax.ppermute(value, ('chip', 'core'), [(s, s + steps) for s in range(lead...  5.49 us
    ppermute x1, waiting for transfers between devices, on_device(): cross_recv = lax.ppermute(cross_send, ('chip', 'core'), inward)  4.9 us
    pallas_call x1, Pallas kernels, on_device(): pl.pallas_call(conv_kernel, out_shape=jax.ShapeDtypeStruct((rows, model_w...  4.78 us
    ppermute x1, starting transfers between devices, on_device(): cross_recv = lax.ppermute(cross_send, ('chip', 'core'), inward)  2.51 us
    slice x1, local copies, waits for them, and re-layouts, on_device(): expand_weight[:, model_width:]  1.76 us
    ppermute x1, starting transfers between devices, on_device(): partner = lax.ppermute(gated_input, 'core', swap)  1.24 us
  transfers between devices with their start and end apart: 6, of which 4 were waited for; matrix products, arithmetic and copies ran while one was open for 10% of the time, Pallas kernels for 0%

profile of v13, /device:TPU:21, one launch (start us, length us, event | category | flops | bytes accessed | tf_op | source)
XLA Modules:
  0.0 38.6 jit_solution(8436086843726573466)
XLA Ops:
  0.0 1.0 %pad_maximum_fusion.own_hbm = bf16[2,128,512]{2,1,0:T(8,128)(2,1)S(1)} fusion(bf16[1,128,512]{2,1,0:T(8,128)(2,1)} %bitcast.7, bf16[1,128,512]{2,1,0:T(8,128)(2,1)} %bitcast.8), kind=kLoop, calls=%fused_computation | loop fusion | flops 131072 | bytes 524288 | tf_op jit(solution)/shard_map/stack | solution.py:202
  1.0 0.0 copy-start
  1.0 2.1 %collective-permute-start.1 = (bf16[2,128,512]{2,1,0:T(8,128)(2,1)S(1)}, bf16[2,128,512]{2,1,0:T(8,128)(2,1)S(1)}, u32[]{:S(2)}, u32[]{:S(2)}) collective-permute-start(bf16[2,128,512]{2,1,0:T(8,128)(2,1)S(1)} %pad_maximum_fusion.own_hbm), channel_id=1, source_target_pairs={{2,0},{3,1},{4,2},{5,3},{6,4},{7,5},{8,6},{9,7},{10,8},{11,9},{12,... | collective-permute-start | bytes 786440 | tf_op jit(solution)/shard_map/ppermute | solution.py:196
  3.2 4.0 %collective-permute-start = (bf16[2,128,512]{2,1,0:T(8,128)(2,1)S(1)}, bf16[2,128,512]{2,1,0:T(8,128)(2,1)S(1)}, u32[]{:S(2)}, u32[]{:S(2)}) collective-permute-start(bf16[2,128,512]{2,1,0:T(8,128)(2,1)S(1)} %pad_maximum_fusion.own_hbm), channel_id=1, source_target_pairs={{0,2},{1,3},{2,4},{3,5},{4,6},{5,7},{6,8},{7,9},{8,10},{9,11},{10,... | collective-permute-start | bytes 786440 | tf_op jit(solution)/shard_map/ppermute | solution.py:196
  7.2 0.7 %pad.4 = s32[768]{0:T(1024)S(1)} pad(s32[767]{0:T(1024)} %param.18, s32[]{:T(128)} %constant.5.clone.1), padding=0_1 | pad | bytes 6144 | tf_op jit(solution)/shard_map/jit(_pad)/pad | solution.py:199
  7.9 0.6 %reshape.9.table_ref = s32[1,768]{1,0:T(1,128)} reshape(s32[768]{0:T(1024)S(1)} %pad.4) | data formatting | bytes 6144 | tf_op jit(solution)/shard_map/reshape | solution.py:199
  8.5 1.8 %slice.3.gate_w = bf16[1024,1024]{1,0:T(8,128)(2,1)S(1)} slice(bf16[1024,2048]{1,0:T(8,128)(2,1)} %value_hbm.1), slice={[0:1024], [1024:2048]} | slice | bytes 4194304 | tf_op jit(solution)/shard_map/slice | solution.py:206
  10.3 0.6 %pad_add_fusion.meta_ref = s32[2]{0:T(128)} fusion(s32[1]{0:T(128)} %bitcast.3, s32[1]{0:T(128)} %bitcast.2), kind=kLoop, calls=%fused_computation.2 | loop fusion | flops 2 | bytes 16 | tf_op jit(solution)/shard_map/stack | solution.py:192
  10.9 0.0 copy-done
  10.9 1.2 %collective-permute-start.2 = (bf16[2,128,512]{2,1,0:T(8,128)(2,1)S(1)}, bf16[2,128,512]{2,1,0:T(8,128)(2,1)S(1)}, u32[]{:S(2)}, u32[]{:S(2)}) collective-permute-start(bf16[2,128,512]{2,1,0:T(8,128)(2,1)S(1)} %pad_maximum_fusion.own_hbm), channel_id=1, source_target_pairs={{0,1},{1,0},{2,3},{3,2},{4,5},{5,4},{6,7},{7,6},{8,9},{9,8},{10,11... | collective-permute-start | bytes 786440 | tf_op jit(solution)/shard_map/ppermute | solution.py:207
  12.2 1.4 %collective-permute-done.1.next_hbm = bf16[2,128,512]{2,1,0:T(8,128)(2,1)S(1)} collective-permute-done((bf16[2,128,512]{2,1,0:T(8,128)(2,1)S(1)}, bf16[2,128,512]{2,1,0:T(8,128)(2,1)S(1)}, u32[]{:S(2)}, u32[]{:S(2)}) %collective-permute-start.1) | collective-permute-done | bytes 262176 | tf_op jit(solution)/shard_map/ppermute | solution.py:196
  13.6 4.1 %collective-permute-done.prev_hbm = bf16[2,128,512]{2,1,0:T(8,128)(2,1)S(1)} collective-permute-done((bf16[2,128,512]{2,1,0:T(8,128)(2,1)S(1)}, bf16[2,128,512]{2,1,0:T(8,128)(2,1)S(1)}, u32[]{:S(2)}, u32[]{:S(2)}) %collective-permute-start) | collective-permute-done | bytes 262176 | tf_op jit(solution)/shard_map/ppermute | solution.py:196
  17.7 0.6 %collective-permute-start.3 = (bf16[2,128,512]{2,1,0:T(8,128)(2,1)S(1)}, bf16[2,128,512]{2,1,0:T(8,128)(2,1)S(1)}, u32[]{:S(2)}, u32[]{:S(2)}) collective-permute-start(bf16[2,128,512]{2,1,0:T(8,128)(2,1)S(1)} %broadcast_select_fusion), channel_id=1, source_target_pairs={{0,1},{1,0},{2,3},{3,2},{4,5},{5,4},{6,7},{7,6},{8,9},{9,8},{10,11... | collective-permute-start | bytes 786440 | tf_op jit(solution)/shard_map/ppermute | solution.py:209
  18.2 0.0 collective-permute-done.2.partner_hbm
  18.2 1.2 %collective-permute-done.3.sel_hbm = bf16[2,128,512]{2,1,0:T(8,128)(2,1)S(1)} collective-permute-done((bf16[2,128,512]{2,1,0:T(8,128)(2,1)S(1)}, bf16[2,128,512]{2,1,0:T(8,128)(2,1)S(1)}, u32[]{:S(2)}, u32[]{:S(2)}) %collective-permute-start.3) | collective-permute-done | bytes 262176 | tf_op jit(solution)/shard_map/ppermute | solution.py:209
  19.4 6.9 %attention_glu.1 = (bf16[128,1024]{1,0:T(8,128)(2,1)}, bf16[128,1024]{1,0:T(8,128)(2,1)}, bf16[64,1024]{1,0:T(8,128)(2,1)}, bf16[64,1024]{1,0:T(8,128)(2,1)}) custom-call(s32[2]{0:T(128)} %pad_add_fusion.meta_ref, s32[16]{0:T(128)} %len_ref.1, s32[1,768]{1,0:T(1,128)} %reshape.9.table_ref, f32[8,32]{1,0:T(8,128)} %bitcast.9, bf16[128,512]{1,0:T(8,128)(2,1)} %q_ref.1, ...), custom_call_target="tpu_custom_call" | custom-call | flops 1006632960 | bytes 7208960 | tf_op jit(solution)/shard_map/attention_glu/pallas_call | solution.py:219
  26.3 2.5 %collective-permute-start.4 = (bf16[64,1024]{1,0:T(8,128)(2,1)}, bf16[64,1024]{1,0:T(8,128)(2,1)S(1)}, u32[]{:S(2)}, u32[]{:S(2)}) collective-permute-start(bf16[64,1024]{1,0:T(8,128)(2,1)} %get-tuple-element.20), channel_id=1, source_target_pairs={{1,2},{3,4},{5,6},{7,8},{9,10},{11,12},{13,14},{2,1},{4,3},{6,5},{... | collective-permute-start | bytes 393224 | tf_op jit(solution)/shard_map/ppermute | solution.py:249
  28.8 0.1 collective-permute-start.5
  28.9 4.9 %collective-permute-done.4.cross_ref = bf16[64,1024]{1,0:T(8,128)(2,1)S(1)} collective-permute-done((bf16[64,1024]{1,0:T(8,128)(2,1)}, bf16[64,1024]{1,0:T(8,128)(2,1)S(1)}, u32[]{:S(2)}, u32[]{:S(2)}) %collective-permute-start.4) | collective-permute-done | bytes 131104 | tf_op jit(solution)/shard_map/ppermute | solution.py:249
  33.8 0.0 collective-permute-done.5.pairg_ref
  33.8 4.8 %conv_shrink.1 = bf16[128,1024]{1,0:T(8,128)(2,1)} custom-call(s32[2]{0:T(128)} %pad_add_fusion.meta_ref, bf16[128,1024]{1,0:T(8,128)(2,1)} %get-tuple-element.19.gated_ref, bf16[64,1024]{1,0:T(8,128)(2,1)S(1)} %collective-permute-done.4.cross_ref, bf16[64,1024]{1,0:T(8,128)(2,1)S(1)} %collective-permute-done.5.pairg_ref, f32[31,1024]{1,0:T(8,128)} %taps_ref.1, ...), custom_call_target="tpu_custom_call" | custom-call | flops 276561920 | bytes 3272704 | tf_op jit(solution)/shard_map/conv_shrink/pallas_call | solution.py:253
  (1 shorter events, 0.0 us)
Async XLA Ops:
  1.0 9.9 %copy-start = (bf16[2,128,512]{2,1,0:T(8,128)(2,1)}, bf16[2,128,512]{2,1,0:T(8,128)(2,1)S(1)}, u32[]{:S(2)}) copy-start(bf16[2,128,512]{2,1,0:T(8,128)(2,1)S(1)} %pad_maximum_fusion.own_hbm) | copy-start | bytes 786436
  1.0 12.6 %collective-permute-start.1 = (bf16[2,128,512]{2,1,0:T(8,128)(2,1)S(1)}, bf16[2,128,512]{2,1,0:T(8,128)(2,1)S(1)}, u32[]{:S(2)}, u32[]{:S(2)}) collective-permute-start(bf16[2,128,512]{2,1,0:T(8,128)(2,1)S(1)} %pad_maximum_fusion.own_hbm), channel_id=1, source_target_pairs={{2,0},{3,1},{4,2},{5,3},{6,4},{7,5},{8,6},{9,7},{10,8},{11,9},{12,... | collective-permute-start | bytes 786440 | tf_op jit(solution)/shard_map/ppermute | solution.py:196
  3.2 14.5 %collective-permute-start = (bf16[2,128,512]{2,1,0:T(8,128)(2,1)S(1)}, bf16[2,128,512]{2,1,0:T(8,128)(2,1)S(1)}, u32[]{:S(2)}, u32[]{:S(2)}) collective-permute-start(bf16[2,128,512]{2,1,0:T(8,128)(2,1)S(1)} %pad_maximum_fusion.own_hbm), channel_id=1, source_target_pairs={{0,2},{1,3},{2,4},{3,5},{4,6},{5,7},{6,8},{7,9},{8,10},{9,11},{10,... | collective-permute-start | bytes 786440 | tf_op jit(solution)/shard_map/ppermute | solution.py:196
  10.9 7.3 %collective-permute-start.2 = (bf16[2,128,512]{2,1,0:T(8,128)(2,1)S(1)}, bf16[2,128,512]{2,1,0:T(8,128)(2,1)S(1)}, u32[]{:S(2)}, u32[]{:S(2)}) collective-permute-start(bf16[2,128,512]{2,1,0:T(8,128)(2,1)S(1)} %pad_maximum_fusion.own_hbm), channel_id=1, source_target_pairs={{0,1},{1,0},{2,3},{3,2},{4,5},{5,4},{6,7},{7,6},{8,9},{9,8},{10,11... | collective-permute-start | bytes 786440 | tf_op jit(solution)/shard_map/ppermute | solution.py:207
  17.7 1.7 %collective-permute-start.3 = (bf16[2,128,512]{2,1,0:T(8,128)(2,1)S(1)}, bf16[2,128,512]{2,1,0:T(8,128)(2,1)S(1)}, u32[]{:S(2)}, u32[]{:S(2)}) collective-permute-start(bf16[2,128,512]{2,1,0:T(8,128)(2,1)S(1)} %broadcast_select_fusion), channel_id=1, source_target_pairs={{0,1},{1,0},{2,3},{3,2},{4,5},{5,4},{6,7},{7,6},{8,9},{9,8},{10,11... | collective-permute-start | bytes 786440 | tf_op jit(solution)/shard_map/ppermute | solution.py:209
  26.3 7.5 %collective-permute-start.4 = (bf16[64,1024]{1,0:T(8,128)(2,1)}, bf16[64,1024]{1,0:T(8,128)(2,1)S(1)}, u32[]{:S(2)}, u32[]{:S(2)}) collective-permute-start(bf16[64,1024]{1,0:T(8,128)(2,1)} %get-tuple-element.20), channel_id=1, source_target_pairs={{1,2},{3,4},{5,6},{7,8},{9,10},{11,12},{13,14},{2,1},{4,3},{6,5},{... | collective-permute-start | bytes 393224 | tf_op jit(solution)/shard_map/ppermute | solution.py:249
  28.8 5.0 %collective-permute-start.5 = (bf16[64,1024]{1,0:T(8,128)(2,1)}, bf16[64,1024]{1,0:T(8,128)(2,1)S(1)}, u32[]{:S(2)}, u32[]{:S(2)}) collective-permute-start(bf16[64,1024]{1,0:T(8,128)(2,1)} %get-tuple-element.21), channel_id=1, source_target_pairs={{0,1},{1,0},{2,3},{3,2},{4,5},{5,4},{6,7},{7,6},{8,9},{9,8},{10,11... | collective-permute-start | bytes 393224 | tf_op jit(solution)/shard_map/ppermute | solution.py:250

commit v14 on v13

--- a/solution.py
+++ b/solution.py
@@ -199,7 +199,7 @@
     table = jnp.pad(bucket_table, (0, line_len - bucket_table.shape[0])).reshape(1, line_len)
     bias_t = bucket_bias.T
 
-    packed = jnp.stack([key_proj, value_proj])
+    packed = jnp.concatenate([key_proj, value_proj], axis=0).reshape(2, rows, att_width)
     from_prev = lin_shift(packed, REACH)
     from_next = lin_shift(packed, -REACH)
     swap = [(0, 1), (1, 0)]

time: 39 us -> 39 us (level)
    another operation x1 -> x0, other arithmetic: 0.99 us -> none  [on_device(): packed = jnp.stack([key_proj, value_proj])]
    concatenate x0 -> x1, other arithmetic: none -> 0.99 us  [on_device(): jnp.concatenate([key_proj, value_proj], axis=0).reshape(2, rows, att_width)]
where the time goes in v14:
time: 39 us; the launch traced here: 38.6 us
  Pallas kernels  11.7 us (30%)
  waiting for transfers between devices  11.6 us (30%)
  starting transfers between devices  10.5 us (27%)
  local copies, waits for them, and re-layouts  3.05 us (8%)
  other arithmetic  1.66 us (4%)
    pallas_call x1, Pallas kernels, on_device(): pl.pallas_call(attention_kernel, out_shape=(jax.ShapeDtypeStruct((rows, m...  6.89 us
    ppermute x2, starting transfers between devices, lin_shift(): lax.ppermute(value, ('chip', 'core'), [(s, s + steps) for s in range(lead...  6.18 us
    ppermute x2, waiting for transfers between devices, lin_shift(): lax.ppermute(value, ('chip', 'core'), [(s, s + steps) for s in range(lead...  5.49 us
    ppermute x1, waiting for transfers between devices, on_device(): cross_recv = lax.ppermute(cross_send, ('chip', 'core'), inward)  4.91 us
    pallas_call x1, Pallas kernels, on_device(): pl.pallas_call(conv_kernel, out_shape=jax.ShapeDtypeStruct((rows, model_w...  4.78 us
    ppermute x1, starting transfers between devices, on_device(): cross_recv = lax.ppermute(cross_send, ('chip', 'core'), inward)  2.5 us
    slice x1, local copies, waits for them, and re-layouts, on_device(): expand_weight[:, model_width:]  1.76 us
    ppermute x1, starting transfers between devices, on_device(): partner = lax.ppermute(gated_input, 'core', swap)  1.24 us
  transfers between devices with their start and end apart: 6, of which 4 were waited for; matrix products, arithmetic and copies ran while one was open for 10% of the time, Pallas kernels for 0%

profile of v14, /device:TPU:21, one launch (start us, length us, event | category | flops | bytes accessed | tf_op | source)
XLA Modules:
  0.0 38.6 jit_solution(3122348717086472817)
XLA Ops:
  0.0 1.0 %pad_maximum_fusion = bf16[256,512]{1,0:T(8,128)(2,1)S(1)} fusion(bf16[128,512]{1,0:T(8,128)(2,1)} %param.16, bf16[128,512]{1,0:T(8,128)(2,1)} %param.15), kind=kLoop, calls=%fused_computation | loop fusion | flops 524288 | bytes 524288 | tf_op jit(solution)/shard_map/concatenate | solution.py:202
  1.0 0.0 copy-start
  1.0 2.1 %collective-permute-start.1 = (bf16[2,128,512]{2,1,0:T(8,128)(2,1)S(1)}, bf16[2,128,512]{2,1,0:T(8,128)(2,1)S(1)}, u32[]{:S(2)}, u32[]{:S(2)}) collective-permute-start(bf16[2,128,512]{2,1,0:T(8,128)(2,1)S(1)} %bitcast.6), channel_id=1, source_target_pairs={{2,0},{3,1},{4,2},{5,3},{6,4},{7,5},{8,6},{9,7},{10,8},{11,9},{12,... | collective-permute-start | bytes 786440 | tf_op jit(solution)/shard_map/ppermute | solution.py:196
  3.1 4.0 %collective-permute-start = (bf16[2,128,512]{2,1,0:T(8,128)(2,1)S(1)}, bf16[2,128,512]{2,1,0:T(8,128)(2,1)S(1)}, u32[]{:S(2)}, u32[]{:S(2)}) collective-permute-start(bf16[2,128,512]{2,1,0:T(8,128)(2,1)S(1)} %bitcast.7), channel_id=1, source_target_pairs={{0,2},{1,3},{2,4},{3,5},{4,6},{5,7},{6,8},{7,9},{8,10},{9,11},{10,... | collective-permute-start | bytes 786440 | tf_op jit(solution)/shard_map/ppermute | solution.py:196
  7.2 0.7 %pad.4 = s32[768]{0:T(1024)S(1)} pad(s32[767]{0:T(1024)} %param.18, s32[]{:T(128)} %constant.5.clone.1), padding=0_1 | pad | bytes 6144 | tf_op jit(solution)/shard_map/jit(_pad)/pad | solution.py:199
  7.9 0.6 %reshape.13.table_ref = s32[1,768]{1,0:T(1,128)} reshape(s32[768]{0:T(1024)S(1)} %pad.4) | data formatting | bytes 6144 | tf_op jit(solution)/shard_map/reshape | solution.py:199
  8.5 1.8 %slice.3.gate_w = bf16[1024,1024]{1,0:T(8,128)(2,1)S(1)} slice(bf16[1024,2048]{1,0:T(8,128)(2,1)} %value_hbm.1), slice={[0:1024], [1024:2048]} | slice | bytes 4194304 | tf_op jit(solution)/shard_map/slice | solution.py:206
  10.3 0.6 %pad_add_fusion.meta_ref = s32[2]{0:T(128)} fusion(s32[1]{0:T(128)} %bitcast.2, s32[1]{0:T(128)} %bitcast.1), kind=kLoop, calls=%fused_computation.2 | loop fusion | flops 2 | bytes 16 | tf_op jit(solution)/shard_map/stack | solution.py:192
  10.9 0.0 copy-done
  10.9 1.2 %collective-permute-start.2 = (bf16[2,128,512]{2,1,0:T(8,128)(2,1)S(1)}, bf16[2,128,512]{2,1,0:T(8,128)(2,1)S(1)}, u32[]{:S(2)}, u32[]{:S(2)}) collective-permute-start(bf16[2,128,512]{2,1,0:T(8,128)(2,1)S(1)} %bitcast.8), channel_id=1, source_target_pairs={{0,1},{1,0},{2,3},{3,2},{4,5},{5,4},{6,7},{7,6},{8,9},{9,8},{10,11... | collective-permute-start | bytes 786440 | tf_op jit(solution)/shard_map/ppermute | solution.py:207
  12.1 1.4 %collective-permute-done.1.next_hbm = bf16[2,128,512]{2,1,0:T(8,128)(2,1)S(1)} collective-permute-done((bf16[2,128,512]{2,1,0:T(8,128)(2,1)S(1)}, bf16[2,128,512]{2,1,0:T(8,128)(2,1)S(1)}, u32[]{:S(2)}, u32[]{:S(2)}) %collective-permute-start.1) | collective-permute-done | bytes 262176 | tf_op jit(solution)/shard_map/ppermute | solution.py:196
  13.6 4.1 %collective-permute-done.prev_hbm = bf16[2,128,512]{2,1,0:T(8,128)(2,1)S(1)} collective-permute-done((bf16[2,128,512]{2,1,0:T(8,128)(2,1)S(1)}, bf16[2,128,512]{2,1,0:T(8,128)(2,1)S(1)}, u32[]{:S(2)}, u32[]{:S(2)}) %collective-permute-start) | collective-permute-done | bytes 262176 | tf_op jit(solution)/shard_map/ppermute | solution.py:196
  17.7 0.6 %collective-permute-start.3 = (bf16[2,128,512]{2,1,0:T(8,128)(2,1)S(1)}, bf16[2,128,512]{2,1,0:T(8,128)(2,1)S(1)}, u32[]{:S(2)}, u32[]{:S(2)}) collective-permute-start(bf16[2,128,512]{2,1,0:T(8,128)(2,1)S(1)} %broadcast_select_fusion), channel_id=1, source_target_pairs={{0,1},{1,0},{2,3},{3,2},{4,5},{5,4},{6,7},{7,6},{8,9},{9,8},{10,11... | collective-permute-start | bytes 786440 | tf_op jit(solution)/shard_map/ppermute | solution.py:209
  18.2 0.0 collective-permute-done.2.partner_hbm
  18.2 1.2 %collective-permute-done.3.sel_hbm = bf16[2,128,512]{2,1,0:T(8,128)(2,1)S(1)} collective-permute-done((bf16[2,128,512]{2,1,0:T(8,128)(2,1)S(1)}, bf16[2,128,512]{2,1,0:T(8,128)(2,1)S(1)}, u32[]{:S(2)}, u32[]{:S(2)}) %collective-permute-start.3) | collective-permute-done | bytes 262176 | tf_op jit(solution)/shard_map/ppermute | solution.py:209
  19.4 6.9 %attention_glu.1 = (bf16[128,1024]{1,0:T(8,128)(2,1)}, bf16[128,1024]{1,0:T(8,128)(2,1)}, bf16[64,1024]{1,0:T(8,128)(2,1)}, bf16[64,1024]{1,0:T(8,128)(2,1)}) custom-call(s32[2]{0:T(128)} %pad_add_fusion.meta_ref, s32[16]{0:T(128)} %len_ref.1, s32[1,768]{1,0:T(1,128)} %reshape.13.table_ref, f32[8,32]{1,0:T(8,128)} %bitcast.10, bf16[128,512]{1,0:T(8,128)(2,1)} %q_ref.1, ...), custom_call_target="tpu_custom_call" | custom-call | flops 1006632960 | bytes 7208960 | tf_op jit(solution)/shard_map/attention_glu/pallas_call | solution.py:219
  26.3 2.5 %collective-permute-start.4 = (bf16[64,1024]{1,0:T(8,128)(2,1)}, bf16[64,1024]{1,0:T(8,128)(2,1)S(1)}, u32[]{:S(2)}, u32[]{:S(2)}) collective-permute-start(bf16[64,1024]{1,0:T(8,128)(2,1)} %get-tuple-element.20), channel_id=1, source_target_pairs={{1,2},{3,4},{5,6},{7,8},{9,10},{11,12},{13,14},{2,1},{4,3},{6,5},{... | collective-permute-start | bytes 393224 | tf_op jit(solution)/shard_map/ppermute | solution.py:249
  28.8 0.1 collective-permute-start.5
  28.9 4.9 %collective-permute-done.4.cross_ref = bf16[64,1024]{1,0:T(8,128)(2,1)S(1)} collective-permute-done((bf16[64,1024]{1,0:T(8,128)(2,1)}, bf16[64,1024]{1,0:T(8,128)(2,1)S(1)}, u32[]{:S(2)}, u32[]{:S(2)}) %collective-permute-start.4) | collective-permute-done | bytes 131104 | tf_op jit(solution)/shard_map/ppermute | solution.py:249
  33.8 0.0 collective-permute-done.5.pairg_ref
  33.8 4.8 %conv_shrink.1 = bf16[128,1024]{1,0:T(8,128)(2,1)} custom-call(s32[2]{0:T(128)} %pad_add_fusion.meta_ref, bf16[128,1024]{1,0:T(8,128)(2,1)} %get-tuple-element.19.gated_ref, bf16[64,1024]{1,0:T(8,128)(2,1)S(1)} %collective-permute-done.4.cross_ref, bf16[64,1024]{1,0:T(8,128)(2,1)S(1)} %collective-permute-done.5.pairg_ref, f32[31,1024]{1,0:T(8,128)} %taps_ref.1, ...), custom_call_target="tpu_custom_call" | custom-call | flops 276561920 | bytes 3272704 | tf_op jit(solution)/shard_map/conv_shrink/pallas_call | solution.py:253
  (1 shorter events, 0.0 us)
Async XLA Ops:
  1.0 9.9 %copy-start = (bf16[256,512]{1,0:T(8,128)(2,1)}, bf16[256,512]{1,0:T(8,128)(2,1)S(1)}, u32[]{:S(2)}) copy-start(bf16[256,512]{1,0:T(8,128)(2,1)S(1)} %pad_maximum_fusion) | copy-start | bytes 786436
  1.0 12.6 %collective-permute-start.1 = (bf16[2,128,512]{2,1,0:T(8,128)(2,1)S(1)}, bf16[2,128,512]{2,1,0:T(8,128)(2,1)S(1)}, u32[]{:S(2)}, u32[]{:S(2)}) collective-permute-start(bf16[2,128,512]{2,1,0:T(8,128)(2,1)S(1)} %bitcast.6), channel_id=1, source_target_pairs={{2,0},{3,1},{4,2},{5,3},{6,4},{7,5},{8,6},{9,7},{10,8},{11,9},{12,... | collective-permute-start | bytes 786440 | tf_op jit(solution)/shard_map/ppermute | solution.py:196
  3.1 14.5 %collective-permute-start = (bf16[2,128,512]{2,1,0:T(8,128)(2,1)S(1)}, bf16[2,128,512]{2,1,0:T(8,128)(2,1)S(1)}, u32[]{:S(2)}, u32[]{:S(2)}) collective-permute-start(bf16[2,128,512]{2,1,0:T(8,128)(2,1)S(1)} %bitcast.7), channel_id=1, source_target_pairs={{0,2},{1,3},{2,4},{3,5},{4,6},{5,7},{6,8},{7,9},{8,10},{9,11},{10,... | collective-permute-start | bytes 786440 | tf_op jit(solution)/shard_map/ppermute | solution.py:196
  10.9 7.3 %collective-permute-start.2 = (bf16[2,128,512]{2,1,0:T(8,128)(2,1)S(1)}, bf16[2,128,512]{2,1,0:T(8,128)(2,1)S(1)}, u32[]{:S(2)}, u32[]{:S(2)}) collective-permute-start(bf16[2,128,512]{2,1,0:T(8,128)(2,1)S(1)} %bitcast.8), channel_id=1, source_target_pairs={{0,1},{1,0},{2,3},{3,2},{4,5},{5,4},{6,7},{7,6},{8,9},{9,8},{10,11... | collective-permute-start | bytes 786440 | tf_op jit(solution)/shard_map/ppermute | solution.py:207
  17.7 1.7 %collective-permute-start.3 = (bf16[2,128,512]{2,1,0:T(8,128)(2,1)S(1)}, bf16[2,128,512]{2,1,0:T(8,128)(2,1)S(1)}, u32[]{:S(2)}, u32[]{:S(2)}) collective-permute-start(bf16[2,128,512]{2,1,0:T(8,128)(2,1)S(1)} %broadcast_select_fusion), channel_id=1, source_target_pairs={{0,1},{1,0},{2,3},{3,2},{4,5},{5,4},{6,7},{7,6},{8,9},{9,8},{10,11... | collective-permute-start | bytes 786440 | tf_op jit(solution)/shard_map/ppermute | solution.py:209
  26.3 7.5 %collective-permute-start.4 = (bf16[64,1024]{1,0:T(8,128)(2,1)}, bf16[64,1024]{1,0:T(8,128)(2,1)S(1)}, u32[]{:S(2)}, u32[]{:S(2)}) collective-permute-start(bf16[64,1024]{1,0:T(8,128)(2,1)} %get-tuple-element.20), channel_id=1, source_target_pairs={{1,2},{3,4},{5,6},{7,8},{9,10},{11,12},{13,14},{2,1},{4,3},{6,5},{... | collective-permute-start | bytes 393224 | tf_op jit(solution)/shard_map/ppermute | solution.py:249
  28.8 5.0 %collective-permute-start.5 = (bf16[64,1024]{1,0:T(8,128)(2,1)}, bf16[64,1024]{1,0:T(8,128)(2,1)S(1)}, u32[]{:S(2)}, u32[]{:S(2)}) collective-permute-start(bf16[64,1024]{1,0:T(8,128)(2,1)} %get-tuple-element.21), channel_id=1, source_target_pairs={{0,1},{1,0},{2,3},{3,2},{4,5},{5,4},{6,7},{7,6},{8,9},{9,8},{10,11... | collective-permute-start | bytes 393224 | tf_op jit(solution)/shard_map/ppermute | solution.py:250

commit v15 on v13

--- a/solution.py
+++ b/solution.py
@@ -28,7 +28,7 @@
 
 
 def sigmoid(values):
-    return 1.0 / (1.0 + jnp.exp(-values))
+    return 0.5 * jnp.tanh(0.5 * values) + 0.5
 
 
 def attention_kernel(
@@ -113,7 +113,7 @@
             weights = jnp.exp(scores - top)
             total = jnp.sum(weights, axis=1, keepdims=True)
             summed = jnp.dot(weights.astype(jnp.bfloat16), v_pair, preferred_element_type=jnp.float32)
-            part = summed / total
+            part = summed * (1.0 / total)
             result = part if result is None else jnp.where(in_head, part, result)
         att_ref[:, cols] = result.astype(jnp.bfloat16)
 

time: 39 us -> 39 us (level)
  no operation moved by 1% of the time
where the time goes in v15:
time: 39 us; the launch traced here: 38.6 us
  waiting for transfers between devices  11.6 us (30%)
  Pallas kernels  11.6 us (30%)
  starting transfers between devices  10.6 us (27%)
  local copies, waits for them, and re-layouts  3.05 us (8%)
  other arithmetic  1.67 us (4%)
    pallas_call x1, Pallas kernels, on_device(): pl.pallas_call(attention_kernel, out_shape=(jax.ShapeDtypeStruct((rows, m...  6.87 us
    ppermute x2, starting transfers between devices, lin_shift(): lax.ppermute(value, ('chip', 'core'), [(s, s + steps) for s in range(lead...  6.18 us
    ppermute x2, waiting for transfers between devices, lin_shift(): lax.ppermute(value, ('chip', 'core'), [(s, s + steps) for s in range(lead...  5.49 us
    ppermute x1, waiting for transfers between devices, on_device(): cross_recv = lax.ppermute(cross_send, ('chip', 'core'), inward)  4.9 us
    pallas_call x1, Pallas kernels, on_device(): pl.pallas_call(conv_kernel, out_shape=jax.ShapeDtypeStruct((rows, model_w...  4.77 us
    ppermute x1, starting transfers between devices, on_device(): cross_recv = lax.ppermute(cross_send, ('chip', 'core'), inward)  2.51 us
    slice x1, local copies, waits for them, and re-layouts, on_device(): expand_weight[:, model_width:]  1.76 us
    ppermute x1, starting transfers between devices, on_device(): partner = lax.ppermute(gated_input, 'core', swap)  1.24 us
  transfers between devices with their start and end apart: 6, of which 4 were waited for; matrix products, arithmetic and copies ran while one was open for 10% of the time, Pallas kernels for 0%

profile of v15, /device:TPU:21, one launch (start us, length us, event | category | flops | bytes accessed | tf_op | source)
XLA Modules:
  0.0 38.6 jit_solution(9528931981875749710)
XLA Ops:
  0.0 1.0 %pad_maximum_fusion.own_hbm = bf16[2,128,512]{2,1,0:T(8,128)(2,1)S(1)} fusion(bf16[1,128,512]{2,1,0:T(8,128)(2,1)} %bitcast.7, bf16[1,128,512]{2,1,0:T(8,128)(2,1)} %bitcast.8), kind=kLoop, calls=%fused_computation | loop fusion | flops 131072 | bytes 524288 | tf_op jit(solution)/shard_map/stack | solution.py:202
  1.0 0.0 copy-start
  1.0 2.1 %collective-permute-start.1 = (bf16[2,128,512]{2,1,0:T(8,128)(2,1)S(1)}, bf16[2,128,512]{2,1,0:T(8,128)(2,1)S(1)}, u32[]{:S(2)}, u32[]{:S(2)}) collective-permute-start(bf16[2,128,512]{2,1,0:T(8,128)(2,1)S(1)} %pad_maximum_fusion.own_hbm), channel_id=1, source_target_pairs={{2,0},{3,1},{4,2},{5,3},{6,4},{7,5},{8,6},{9,7},{10,8},{11,9},{12,... | collective-permute-start | bytes 786440 | tf_op jit(solution)/shard_map/ppermute | solution.py:196
  3.2 4.0 %collective-permute-start = (bf16[2,128,512]{2,1,0:T(8,128)(2,1)S(1)}, bf16[2,128,512]{2,1,0:T(8,128)(2,1)S(1)}, u32[]{:S(2)}, u32[]{:S(2)}) collective-permute-start(bf16[2,128,512]{2,1,0:T(8,128)(2,1)S(1)} %pad_maximum_fusion.own_hbm), channel_id=1, source_target_pairs={{0,2},{1,3},{2,4},{3,5},{4,6},{5,7},{6,8},{7,9},{8,10},{9,11},{10,... | collective-permute-start | bytes 786440 | tf_op jit(solution)/shard_map/ppermute | solution.py:196
  7.2 0.7 %pad.4 = s32[768]{0:T(1024)S(1)} pad(s32[767]{0:T(1024)} %param.18, s32[]{:T(128)} %constant.5.clone.1), padding=0_1 | pad | bytes 6144 | tf_op jit(solution)/shard_map/jit(_pad)/pad | solution.py:199
  7.9 0.6 %reshape.9.table_ref = s32[1,768]{1,0:T(1,128)} reshape(s32[768]{0:T(1024)S(1)} %pad.4) | data formatting | bytes 6144 | tf_op jit(solution)/shard_map/reshape | solution.py:199
  8.5 1.8 %slice.3.gate_w = bf16[1024,1024]{1,0:T(8,128)(2,1)S(1)} slice(bf16[1024,2048]{1,0:T(8,128)(2,1)} %value_hbm.1), slice={[0:1024], [1024:2048]} | slice | bytes 4194304 | tf_op jit(solution)/shard_map/slice | solution.py:206
  10.3 0.6 %pad_add_fusion.meta_ref = s32[2]{0:T(128)} fusion(s32[1]{0:T(128)} %bitcast.3, s32[1]{0:T(128)} %bitcast.2), kind=kLoop, calls=%fused_computation.2 | loop fusion | flops 2 | bytes 16 | tf_op jit(solution)/shard_map/stack | solution.py:192
  10.9 0.0 copy-done
  10.9 1.2 %collective-permute-start.2 = (bf16[2,128,512]{2,1,0:T(8,128)(2,1)S(1)}, bf16[2,128,512]{2,1,0:T(8,128)(2,1)S(1)}, u32[]{:S(2)}, u32[]{:S(2)}) collective-permute-start(bf16[2,128,512]{2,1,0:T(8,128)(2,1)S(1)} %pad_maximum_fusion.own_hbm), channel_id=1, source_target_pairs={{0,1},{1,0},{2,3},{3,2},{4,5},{5,4},{6,7},{7,6},{8,9},{9,8},{10,11... | collective-permute-start | bytes 786440 | tf_op jit(solution)/shard_map/ppermute | solution.py:207
  12.2 1.4 %collective-permute-done.1.next_hbm = bf16[2,128,512]{2,1,0:T(8,128)(2,1)S(1)} collective-permute-done((bf16[2,128,512]{2,1,0:T(8,128)(2,1)S(1)}, bf16[2,128,512]{2,1,0:T(8,128)(2,1)S(1)}, u32[]{:S(2)}, u32[]{:S(2)}) %collective-permute-start.1) | collective-permute-done | bytes 262176 | tf_op jit(solution)/shard_map/ppermute | solution.py:196
  13.6 4.1 %collective-permute-done.prev_hbm = bf16[2,128,512]{2,1,0:T(8,128)(2,1)S(1)} collective-permute-done((bf16[2,128,512]{2,1,0:T(8,128)(2,1)S(1)}, bf16[2,128,512]{2,1,0:T(8,128)(2,1)S(1)}, u32[]{:S(2)}, u32[]{:S(2)}) %collective-permute-start) | collective-permute-done | bytes 262176 | tf_op jit(solution)/shard_map/ppermute | solution.py:196
  17.7 0.6 %collective-permute-start.3 = (bf16[2,128,512]{2,1,0:T(8,128)(2,1)S(1)}, bf16[2,128,512]{2,1,0:T(8,128)(2,1)S(1)}, u32[]{:S(2)}, u32[]{:S(2)}) collective-permute-start(bf16[2,128,512]{2,1,0:T(8,128)(2,1)S(1)} %broadcast_select_fusion), channel_id=1, source_target_pairs={{0,1},{1,0},{2,3},{3,2},{4,5},{5,4},{6,7},{7,6},{8,9},{9,8},{10,11... | collective-permute-start | bytes 786440 | tf_op jit(solution)/shard_map/ppermute | solution.py:209
  18.2 0.0 collective-permute-done.2.partner_hbm
  18.2 1.2 %collective-permute-done.3.sel_hbm = bf16[2,128,512]{2,1,0:T(8,128)(2,1)S(1)} collective-permute-done((bf16[2,128,512]{2,1,0:T(8,128)(2,1)S(1)}, bf16[2,128,512]{2,1,0:T(8,128)(2,1)S(1)}, u32[]{:S(2)}, u32[]{:S(2)}) %collective-permute-start.3) | collective-permute-done | bytes 262176 | tf_op jit(solution)/shard_map/ppermute | solution.py:209
  19.4 6.9 %attention_glu.1 = (bf16[128,1024]{1,0:T(8,128)(2,1)}, bf16[128,1024]{1,0:T(8,128)(2,1)}, bf16[64,1024]{1,0:T(8,128)(2,1)}, bf16[64,1024]{1,0:T(8,128)(2,1)}) custom-call(s32[2]{0:T(128)} %pad_add_fusion.meta_ref, s32[16]{0:T(128)} %len_ref.1, s32[1,768]{1,0:T(1,128)} %reshape.9.table_ref, f32[8,32]{1,0:T(8,128)} %bitcast.9, bf16[128,512]{1,0:T(8,128)(2,1)} %q_ref.1, ...), custom_call_target="tpu_custom_call" | custom-call | flops 1006632960 | bytes 7208960 | tf_op jit(solution)/shard_map/attention_glu/pallas_call | solution.py:219
  26.3 2.5 %collective-permute-start.4 = (bf16[64,1024]{1,0:T(8,128)(2,1)}, bf16[64,1024]{1,0:T(8,128)(2,1)S(1)}, u32[]{:S(2)}, u32[]{:S(2)}) collective-permute-start(bf16[64,1024]{1,0:T(8,128)(2,1)} %get-tuple-element.20), channel_id=1, source_target_pairs={{1,2},{3,4},{5,6},{7,8},{9,10},{11,12},{13,14},{2,1},{4,3},{6,5},{... | collective-permute-start | bytes 393224 | tf_op jit(solution)/shard_map/ppermute | solution.py:249
  28.8 0.1 collective-permute-start.5
  28.9 4.9 %collective-permute-done.4.cross_ref = bf16[64,1024]{1,0:T(8,128)(2,1)S(1)} collective-permute-done((bf16[64,1024]{1,0:T(8,128)(2,1)}, bf16[64,1024]{1,0:T(8,128)(2,1)S(1)}, u32[]{:S(2)}, u32[]{:S(2)}) %collective-permute-start.4) | collective-permute-done | bytes 131104 | tf_op jit(solution)/shard_map/ppermute | solution.py:249
  33.8 0.0 collective-permute-done.5.pairg_ref
  33.8 4.8 %conv_shrink.1 = bf16[128,1024]{1,0:T(8,128)(2,1)} custom-call(s32[2]{0:T(128)} %pad_add_fusion.meta_ref, bf16[128,1024]{1,0:T(8,128)(2,1)} %get-tuple-element.19.gated_ref, bf16[64,1024]{1,0:T(8,128)(2,1)S(1)} %collective-permute-done.4.cross_ref, bf16[64,1024]{1,0:T(8,128)(2,1)S(1)} %collective-permute-done.5.pairg_ref, f32[31,1024]{1,0:T(8,128)} %taps_ref.1, ...), custom_call_target="tpu_custom_call" | custom-call | flops 276561920 | bytes 3272704 | tf_op jit(solution)/shard_map/conv_shrink/pallas_call | solution.py:253
  (1 shorter events, 0.0 us)
Async XLA Ops:
  1.0 9.9 %copy-start = (bf16[2,128,512]{2,1,0:T(8,128)(2,1)}, bf16[2,128,512]{2,1,0:T(8,128)(2,1)S(1)}, u32[]{:S(2)}) copy-start(bf16[2,128,512]{2,1,0:T(8,128)(2,1)S(1)} %pad_maximum_fusion.own_hbm) | copy-start | bytes 786436
  1.0 12.6 %collective-permute-start.1 = (bf16[2,128,512]{2,1,0:T(8,128)(2,1)S(1)}, bf16[2,128,512]{2,1,0:T(8,128)(2,1)S(1)}, u32[]{:S(2)}, u32[]{:S(2)}) collective-permute-start(bf16[2,128,512]{2,1,0:T(8,128)(2,1)S(1)} %pad_maximum_fusion.own_hbm), channel_id=1, source_target_pairs={{2,0},{3,1},{4,2},{5,3},{6,4},{7,5},{8,6},{9,7},{10,8},{11,9},{12,... | collective-permute-start | bytes 786440 | tf_op jit(solution)/shard_map/ppermute | solution.py:196
  3.2 14.5 %collective-permute-start = (bf16[2,128,512]{2,1,0:T(8,128)(2,1)S(1)}, bf16[2,128,512]{2,1,0:T(8,128)(2,1)S(1)}, u32[]{:S(2)}, u32[]{:S(2)}) collective-permute-start(bf16[2,128,512]{2,1,0:T(8,128)(2,1)S(1)} %pad_maximum_fusion.own_hbm), channel_id=1, source_target_pairs={{0,2},{1,3},{2,4},{3,5},{4,6},{5,7},{6,8},{7,9},{8,10},{9,11},{10,... | collective-permute-start | bytes 786440 | tf_op jit(solution)/shard_map/ppermute | solution.py:196
  10.9 7.3 %collective-permute-start.2 = (bf16[2,128,512]{2,1,0:T(8,128)(2,1)S(1)}, bf16[2,128,512]{2,1,0:T(8,128)(2,1)S(1)}, u32[]{:S(2)}, u32[]{:S(2)}) collective-permute-start(bf16[2,128,512]{2,1,0:T(8,128)(2,1)S(1)} %pad_maximum_fusion.own_hbm), channel_id=1, source_target_pairs={{0,1},{1,0},{2,3},{3,2},{4,5},{5,4},{6,7},{7,6},{8,9},{9,8},{10,11... | collective-permute-start | bytes 786440 | tf_op jit(solution)/shard_map/ppermute | solution.py:207
  17.7 1.7 %collective-permute-start.3 = (bf16[2,128,512]{2,1,0:T(8,128)(2,1)S(1)}, bf16[2,128,512]{2,1,0:T(8,128)(2,1)S(1)}, u32[]{:S(2)}, u32[]{:S(2)}) collective-permute-start(bf16[2,128,512]{2,1,0:T(8,128)(2,1)S(1)} %broadcast_select_fusion), channel_id=1, source_target_pairs={{0,1},{1,0},{2,3},{3,2},{4,5},{5,4},{6,7},{7,6},{8,9},{9,8},{10,11... | collective-permute-start | bytes 786440 | tf_op jit(solution)/shard_map/ppermute | solution.py:209
  26.3 7.5 %collective-permute-start.4 = (bf16[64,1024]{1,0:T(8,128)(2,1)}, bf16[64,1024]{1,0:T(8,128)(2,1)S(1)}, u32[]{:S(2)}, u32[]{:S(2)}) collective-permute-start(bf16[64,1024]{1,0:T(8,128)(2,1)} %get-tuple-element.20), channel_id=1, source_target_pairs={{1,2},{3,4},{5,6},{7,8},{9,10},{11,12},{13,14},{2,1},{4,3},{6,5},{... | collective-permute-start | bytes 393224 | tf_op jit(solution)/shard_map/ppermute | solution.py:249
  28.8 5.0 %collective-permute-start.5 = (bf16[64,1024]{1,0:T(8,128)(2,1)}, bf16[64,1024]{1,0:T(8,128)(2,1)S(1)}, u32[]{:S(2)}, u32[]{:S(2)}) collective-permute-start(bf16[64,1024]{1,0:T(8,128)(2,1)} %get-tuple-element.21), channel_id=1, source_target_pairs={{0,1},{1,0},{2,3},{3,2},{4,5},{5,4},{6,7},{7,6},{8,9},{9,8},{10,11... | collective-permute-start | bytes 393224 | tf_op jit(solution)/shard_map/ppermute | solution.py:250

commit v16 on v13

--- a/solution.py
+++ b/solution.py
@@ -35,8 +35,8 @@
     meta_ref, len_ref, table_ref, bias_t_ref, q_ref,
     prev_hbm, next_hbm, own_hbm, partner_hbm, sel_hbm,
     x_ref, gain_ref, ow_hbm, value_hbm, gate_w,
-    mid_ref, gated_ref, cross_ref, partner_ref,
-    ow_vmem, value_w, sems, att_ref, win_ref,
+    mid_ref, cross_ref, partner_ref,
+    ow_vmem, value_w, sems, att_ref, win_ref, gated_ref,
 ):
     base = meta_ref[0]
     core = meta_ref[1]
@@ -134,7 +134,7 @@
 
 
 def conv_kernel(
-    meta_ref, gated_ref, cross_ref, pairg_ref, taps_ref, gain_ref, mid_ref, sw_hbm,
+    meta_ref, own_cross_ref, own_partner_ref, cross_ref, pairg_ref, taps_ref, gain_ref, mid_ref, sw_hbm,
     out_ref, win_ref, conv_ref, sw_vmem, sems,
 ):
     sw_copy = pltpu.make_async_copy(sw_hbm, sw_vmem, sems.at[0])
@@ -145,7 +145,10 @@
     cross = cross_ref[...]
     partner = pairg_ref[...]
     win_ref[0:half, :] = jnp.where(first_core, cross, partner).astype(jnp.float32)
-    win_ref[half:half + rows, :] = gated_ref[...].astype(jnp.float32)
+    own_cross = own_cross_ref[...]
+    own_partner = own_partner_ref[...]
+    win_ref[half:2 * half, :] = jnp.where(first_core, own_cross, own_partner).astype(jnp.float32)
+    win_ref[2 * half:3 * half, :] = jnp.where(first_core, own_partner, own_cross).astype(jnp.float32)
     win_ref[half + rows:2 * half + rows, :] = jnp.where(first_core, partner, cross).astype(jnp.float32)
     reach = DILATION * (KERNEL - 1) // 2
     start = half - reach
@@ -216,22 +219,22 @@
     window = len(order) * rows
     attn_flops = 2 * 2 * heads * rows * window * LANES + 2 * rows * att_width * model_width + 2 * rows * model_width * 2 * model_width
     attn_bytes = 2 * (rows * att_width * (1 + 2 * len(order)) + rows * model_width * 2 + att_width * model_width + model_width * 2 * model_width)
-    mid, gated, cross_send, partner_send = pl.pallas_call(
+    mid, cross_send, partner_send = pl.pallas_call(
         attention_kernel,
         out_shape=(
             jax.ShapeDtypeStruct((rows, model_width), jnp.bfloat16),
-            jax.ShapeDtypeStruct((rows, model_width), jnp.bfloat16),
             jax.ShapeDtypeStruct((half, model_width), jnp.bfloat16),
             jax.ShapeDtypeStruct((half, model_width), jnp.bfloat16),
         ),
         in_specs=[smem, smem, vmem, vmem, vmem] + [anywhere] * 5 + [vmem, vmem, anywhere, anywhere, vmem],
-        out_specs=(vmem, vmem, vmem, vmem),
+        out_specs=(vmem, vmem, vmem),
         scratch_shapes=[
             pltpu.VMEM((att_width, model_width), jnp.bfloat16),
             pltpu.VMEM((model_width, model_width), jnp.bfloat16),
             pltpu.SemaphoreType.DMA((7,)),
             pltpu.VMEM((rows, att_width), jnp.bfloat16),
             pltpu.VMEM((len(order) * packed.shape[0], rows, att_width), jnp.bfloat16),
+            pltpu.VMEM((rows, model_width), jnp.bfloat16),
         ],
         cost_estimate=pl.CostEstimate(
             flops=attn_flops, transcendentals=heads * rows * window + rows * model_width, bytes_accessed=attn_bytes
@@ -253,7 +256,7 @@
     return pl.pallas_call(
         conv_kernel,
         out_shape=jax.ShapeDtypeStruct((rows, model_width), jnp.bfloat16),
-        in_specs=[smem] + [vmem] * 6 + [anywhere],
+        in_specs=[smem] + [vmem] * 7 + [anywhere],
         out_specs=vmem,
         scratch_shapes=[
             pltpu.VMEM((rows + 2 * half, model_width), jnp.float32),
@@ -265,7 +268,7 @@
             flops=conv_flops, transcendentals=rows * model_width, bytes_accessed=conv_bytes
         ),
         name="conv_shrink",
-    )(meta, gated, pltpu.with_memory_space_constraint(cross_recv, pltpu.VMEM), pltpu.with_memory_space_constraint(partner_recv, pltpu.VMEM), depth_taps, inner_gain.reshape(1, -1), mid, shrink_weight)
+    )(meta, cross_send, partner_send, pltpu.with_memory_space_constraint(cross_recv, pltpu.VMEM), pltpu.with_memory_space_constraint(partner_recv, pltpu.VMEM), depth_taps, inner_gain.reshape(1, -1), mid, shrink_weight)
 
 
 def solution(mesh):

time: 39 us -> 38.9 us (level)
  no operation moved by 1% of the time
where the time goes in v16:
time: 38.9 us; the launch traced here: 38.6 us
  waiting for transfers between devices  11.6 us (30%)
  Pallas kernels  11.6 us (30%)
  starting transfers between devices  10.6 us (27%)
  local copies, waits for them, and re-layouts  3.04 us (8%)
  other arithmetic  1.66 us (4%)
    pallas_call x1, Pallas kernels, on_device(): pl.pallas_call(attention_kernel, out_shape=(jax.ShapeDtypeStruct((rows, m...  6.8 us
    ppermute x2, starting transfers between devices, lin_shift(): lax.ppermute(value, ('chip', 'core'), [(s, s + steps) for s in range(lead...  6.18 us
    ppermute x2, waiting for transfers between devices, lin_shift(): lax.ppermute(value, ('chip', 'core'), [(s, s + steps) for s in range(lead...  5.51 us
    ppermute x1, waiting for transfers between devices, on_device(): cross_recv = lax.ppermute(cross_send, ('chip', 'core'), inward)  4.9 us
    pallas_call x1, Pallas kernels, on_device(): pl.pallas_call(conv_kernel, out_shape=jax.ShapeDtypeStruct((rows, model_w...  4.84 us
    ppermute x1, starting transfers between devices, on_device(): cross_recv = lax.ppermute(cross_send, ('chip', 'core'), inward)  2.51 us
    slice x1, local copies, waits for them, and re-layouts, on_device(): expand_weight[:, model_width:]  1.76 us
    ppermute x1, starting transfers between devices, on_device(): partner = lax.ppermute(gated_input, 'core', swap)  1.24 us
  transfers between devices with their start and end apart: 6, of which 4 were waited for; matrix products, arithmetic and copies ran while one was open for 10% of the time, Pallas kernels for 0%

profile of v16, /device:TPU:21, one launch (start us, length us, event | category | flops | bytes accessed | tf_op | source)
XLA Modules:
  0.0 38.6 jit_solution(3218503339882167683)
XLA Ops:
  0.0 1.0 %pad_maximum_fusion.own_hbm = bf16[2,128,512]{2,1,0:T(8,128)(2,1)S(1)} fusion(bf16[1,128,512]{2,1,0:T(8,128)(2,1)} %bitcast.7, bf16[1,128,512]{2,1,0:T(8,128)(2,1)} %bitcast.8), kind=kLoop, calls=%fused_computation | loop fusion | flops 131072 | bytes 524288 | tf_op jit(solution)/shard_map/stack | solution.py:205
  1.0 0.0 copy-start
  1.0 2.1 %collective-permute-start.1 = (bf16[2,128,512]{2,1,0:T(8,128)(2,1)S(1)}, bf16[2,128,512]{2,1,0:T(8,128)(2,1)S(1)}, u32[]{:S(2)}, u32[]{:S(2)}) collective-permute-start(bf16[2,128,512]{2,1,0:T(8,128)(2,1)S(1)} %pad_maximum_fusion.own_hbm), channel_id=1, source_target_pairs={{2,0},{3,1},{4,2},{5,3},{6,4},{7,5},{8,6},{9,7},{10,8},{11,9},{12,... | collective-permute-start | bytes 786440 | tf_op jit(solution)/shard_map/ppermute | solution.py:199
  3.2 4.0 %collective-permute-start = (bf16[2,128,512]{2,1,0:T(8,128)(2,1)S(1)}, bf16[2,128,512]{2,1,0:T(8,128)(2,1)S(1)}, u32[]{:S(2)}, u32[]{:S(2)}) collective-permute-start(bf16[2,128,512]{2,1,0:T(8,128)(2,1)S(1)} %pad_maximum_fusion.own_hbm), channel_id=1, source_target_pairs={{0,2},{1,3},{2,4},{3,5},{4,6},{5,7},{6,8},{7,9},{8,10},{9,11},{10,... | collective-permute-start | bytes 786440 | tf_op jit(solution)/shard_map/ppermute | solution.py:199
  7.2 0.7 %pad.4 = s32[768]{0:T(1024)S(1)} pad(s32[767]{0:T(1024)} %param.18, s32[]{:T(128)} %constant.5.clone.1), padding=0_1 | pad | bytes 6144 | tf_op jit(solution)/shard_map/jit(_pad)/pad | solution.py:202
  7.9 0.6 %reshape.9.table_ref = s32[1,768]{1,0:T(1,128)} reshape(s32[768]{0:T(1024)S(1)} %pad.4) | data formatting | bytes 6144 | tf_op jit(solution)/shard_map/reshape | solution.py:202
  8.5 1.8 %slice.3.gate_w = bf16[1024,1024]{1,0:T(8,128)(2,1)S(1)} slice(bf16[1024,2048]{1,0:T(8,128)(2,1)} %value_hbm.1), slice={[0:1024], [1024:2048]} | slice | bytes 4194304 | tf_op jit(solution)/shard_map/slice | solution.py:209
  10.3 0.6 %pad_add_fusion.meta_ref = s32[2]{0:T(128)} fusion(s32[1]{0:T(128)} %bitcast.3, s32[1]{0:T(128)} %bitcast.2), kind=kLoop, calls=%fused_computation.2 | loop fusion | flops 2 | bytes 16 | tf_op jit(solution)/shard_map/stack | solution.py:195
  10.9 0.0 copy-done
  10.9 1.2 %collective-permute-start.2 = (bf16[2,128,512]{2,1,0:T(8,128)(2,1)S(1)}, bf16[2,128,512]{2,1,0:T(8,128)(2,1)S(1)}, u32[]{:S(2)}, u32[]{:S(2)}) collective-permute-start(bf16[2,128,512]{2,1,0:T(8,128)(2,1)S(1)} %pad_maximum_fusion.own_hbm), channel_id=1, source_target_pairs={{0,1},{1,0},{2,3},{3,2},{4,5},{5,4},{6,7},{7,6},{8,9},{9,8},{10,11... | collective-permute-start | bytes 786440 | tf_op jit(solution)/shard_map/ppermute | solution.py:210
  12.1 1.4 %collective-permute-done.1.next_hbm = bf16[2,128,512]{2,1,0:T(8,128)(2,1)S(1)} collective-permute-done((bf16[2,128,512]{2,1,0:T(8,128)(2,1)S(1)}, bf16[2,128,512]{2,1,0:T(8,128)(2,1)S(1)}, u32[]{:S(2)}, u32[]{:S(2)}) %collective-permute-start.1) | collective-permute-done | bytes 262176 | tf_op jit(solution)/shard_map/ppermute | solution.py:199
  13.6 4.1 %collective-permute-done.prev_hbm = bf16[2,128,512]{2,1,0:T(8,128)(2,1)S(1)} collective-permute-done((bf16[2,128,512]{2,1,0:T(8,128)(2,1)S(1)}, bf16[2,128,512]{2,1,0:T(8,128)(2,1)S(1)}, u32[]{:S(2)}, u32[]{:S(2)}) %collective-permute-start) | collective-permute-done | bytes 262176 | tf_op jit(solution)/shard_map/ppermute | solution.py:199
  17.7 0.6 %collective-permute-start.3 = (bf16[2,128,512]{2,1,0:T(8,128)(2,1)S(1)}, bf16[2,128,512]{2,1,0:T(8,128)(2,1)S(1)}, u32[]{:S(2)}, u32[]{:S(2)}) collective-permute-start(bf16[2,128,512]{2,1,0:T(8,128)(2,1)S(1)} %broadcast_select_fusion), channel_id=1, source_target_pairs={{0,1},{1,0},{2,3},{3,2},{4,5},{5,4},{6,7},{7,6},{8,9},{9,8},{10,11... | collective-permute-start | bytes 786440 | tf_op jit(solution)/shard_map/ppermute | solution.py:212
  18.2 0.0 collective-permute-done.2.partner_hbm
  18.2 1.2 %collective-permute-done.3.sel_hbm = bf16[2,128,512]{2,1,0:T(8,128)(2,1)S(1)} collective-permute-done((bf16[2,128,512]{2,1,0:T(8,128)(2,1)S(1)}, bf16[2,128,512]{2,1,0:T(8,128)(2,1)S(1)}, u32[]{:S(2)}, u32[]{:S(2)}) %collective-permute-start.3) | collective-permute-done | bytes 262176 | tf_op jit(solution)/shard_map/ppermute | solution.py:212
  19.4 6.8 %attention_glu.1 = (bf16[128,1024]{1,0:T(8,128)(2,1)}, bf16[64,1024]{1,0:T(8,128)(2,1)}, bf16[64,1024]{1,0:T(8,128)(2,1)}) custom-call(s32[2]{0:T(128)} %pad_add_fusion.meta_ref, s32[16]{0:T(128)} %len_ref.1, s32[1,768]{1,0:T(1,128)} %reshape.9.table_ref, f32[8,32]{1,0:T(8,128)} %bitcast.9, bf16[128,512]{1,0:T(8,128)(2,1)} %q_ref.1, ...), custom_call_target="tpu_custom_call" | custom-call | flops 1006632960 | bytes 7208960 | tf_op jit(solution)/shard_map/attention_glu/pallas_call | solution.py:222
  26.2 2.5 %collective-permute-start.4 = (bf16[64,1024]{1,0:T(8,128)(2,1)}, bf16[64,1024]{1,0:T(8,128)(2,1)S(1)}, u32[]{:S(2)}, u32[]{:S(2)}) collective-permute-start(bf16[64,1024]{1,0:T(8,128)(2,1)} %get-tuple-element.18.own_cross_ref), channel_id=1, source_target_pairs={{1,2},{3,4},{5,6},{7,8},{9,10},{11,12},{13,14},{2,1},{4,3},{6,5},{... | collective-permute-start | bytes 393224 | tf_op jit(solution)/shard_map/ppermute | solution.py:252
  28.7 0.1 collective-permute-start.5
  28.8 4.9 %collective-permute-done.4.cross_ref = bf16[64,1024]{1,0:T(8,128)(2,1)S(1)} collective-permute-done((bf16[64,1024]{1,0:T(8,128)(2,1)}, bf16[64,1024]{1,0:T(8,128)(2,1)S(1)}, u32[]{:S(2)}, u32[]{:S(2)}) %collective-permute-start.4) | collective-permute-done | bytes 131104 | tf_op jit(solution)/shard_map/ppermute | solution.py:252
  33.7 0.0 collective-permute-done.5.pairg_ref
  33.7 4.8 %conv_shrink.1 = bf16[128,1024]{1,0:T(8,128)(2,1)} custom-call(s32[2]{0:T(128)} %pad_add_fusion.meta_ref, bf16[64,1024]{1,0:T(8,128)(2,1)} %get-tuple-element.18.own_cross_ref, bf16[64,1024]{1,0:T(8,128)(2,1)} %get-tuple-element.19.own_partner_ref, bf16[64,1024]{1,0:T(8,128)(2,1)S(1)} %collective-permute-done.4.cross_ref, ...), custom_call_target="tpu_custom_call" | custom-call | flops 276561920 | bytes 3272704 | tf_op jit(solution)/shard_map/conv_shrink/pallas_call | solution.py:256
  (1 shorter events, 0.0 us)
Async XLA Ops:
  1.0 9.9 %copy-start = (bf16[2,128,512]{2,1,0:T(8,128)(2,1)}, bf16[2,128,512]{2,1,0:T(8,128)(2,1)S(1)}, u32[]{:S(2)}) copy-start(bf16[2,128,512]{2,1,0:T(8,128)(2,1)S(1)} %pad_maximum_fusion.own_hbm) | copy-start | bytes 786436
  1.0 12.6 %collective-permute-start.1 = (bf16[2,128,512]{2,1,0:T(8,128)(2,1)S(1)}, bf16[2,128,512]{2,1,0:T(8,128)(2,1)S(1)}, u32[]{:S(2)}, u32[]{:S(2)}) collective-permute-start(bf16[2,128,512]{2,1,0:T(8,128)(2,1)S(1)} %pad_maximum_fusion.own_hbm), channel_id=1, source_target_pairs={{2,0},{3,1},{4,2},{5,3},{6,4},{7,5},{8,6},{9,7},{10,8},{11,9},{12,... | collective-permute-start | bytes 786440 | tf_op jit(solution)/shard_map/ppermute | solution.py:199
  3.2 14.5 %collective-permute-start = (bf16[2,128,512]{2,1,0:T(8,128)(2,1)S(1)}, bf16[2,128,512]{2,1,0:T(8,128)(2,1)S(1)}, u32[]{:S(2)}, u32[]{:S(2)}) collective-permute-start(bf16[2,128,512]{2,1,0:T(8,128)(2,1)S(1)} %pad_maximum_fusion.own_hbm), channel_id=1, source_target_pairs={{0,2},{1,3},{2,4},{3,5},{4,6},{5,7},{6,8},{7,9},{8,10},{9,11},{10,... | collective-permute-start | bytes 786440 | tf_op jit(solution)/shard_map/ppermute | solution.py:199
  10.9 7.3 %collective-permute-start.2 = (bf16[2,128,512]{2,1,0:T(8,128)(2,1)S(1)}, bf16[2,128,512]{2,1,0:T(8,128)(2,1)S(1)}, u32[]{:S(2)}, u32[]{:S(2)}) collective-permute-start(bf16[2,128,512]{2,1,0:T(8,128)(2,1)S(1)} %pad_maximum_fusion.own_hbm), channel_id=1, source_target_pairs={{0,1},{1,0},{2,3},{3,2},{4,5},{5,4},{6,7},{7,6},{8,9},{9,8},{10,11... | collective-permute-start | bytes 786440 | tf_op jit(solution)/shard_map/ppermute | solution.py:210
  17.7 1.7 %collective-permute-start.3 = (bf16[2,128,512]{2,1,0:T(8,128)(2,1)S(1)}, bf16[2,128,512]{2,1,0:T(8,128)(2,1)S(1)}, u32[]{:S(2)}, u32[]{:S(2)}) collective-permute-start(bf16[2,128,512]{2,1,0:T(8,128)(2,1)S(1)} %broadcast_select_fusion), channel_id=1, source_target_pairs={{0,1},{1,0},{2,3},{3,2},{4,5},{5,4},{6,7},{7,6},{8,9},{9,8},{10,11... | collective-permute-start | bytes 786440 | tf_op jit(solution)/shard_map/ppermute | solution.py:212
  26.2 7.5 %collective-permute-start.4 = (bf16[64,1024]{1,0:T(8,128)(2,1)}, bf16[64,1024]{1,0:T(8,128)(2,1)S(1)}, u32[]{:S(2)}, u32[]{:S(2)}) collective-permute-start(bf16[64,1024]{1,0:T(8,128)(2,1)} %get-tuple-element.18.own_cross_ref), channel_id=1, source_target_pairs={{1,2},{3,4},{5,6},{7,8},{9,10},{11,12},{13,14},{2,1},{4,3},{6,5},{... | collective-permute-start | bytes 393224 | tf_op jit(solution)/shard_map/ppermute | solution.py:252
  28.7 5.0 %collective-permute-start.5 = (bf16[64,1024]{1,0:T(8,128)(2,1)}, bf16[64,1024]{1,0:T(8,128)(2,1)S(1)}, u32[]{:S(2)}, u32[]{:S(2)}) collective-permute-start(bf16[64,1024]{1,0:T(8,128)(2,1)} %get-tuple-element.19.own_partner_ref), channel_id=1, source_target_pairs={{0,1},{1,0},{2,3},{3,2},{4,5},{5,4},{6,7},{7,6},{8,9},{9,8},{10,11... | collective-permute-start | bytes 393224 | tf_op jit(solution)/shard_map/ppermute | solution.py:253

commit v17 on v16

--- a/solution.py
+++ b/solution.py
@@ -268,7 +268,7 @@
             flops=conv_flops, transcendentals=rows * model_width, bytes_accessed=conv_bytes
         ),
         name="conv_shrink",
-    )(meta, cross_send, partner_send, pltpu.with_memory_space_constraint(cross_recv, pltpu.VMEM), pltpu.with_memory_space_constraint(partner_recv, pltpu.VMEM), depth_taps, inner_gain.reshape(1, -1), mid, shrink_weight)
+    )(meta, cross_send, partner_send, pltpu.with_memory_space_constraint(cross_recv, pltpu.VMEM), pltpu.with_memory_space_constraint(partner_recv, pltpu.VMEM), pltpu.with_memory_space_constraint(depth_taps, pltpu.VMEM), pltpu.with_memory_space_constraint(inner_gain.reshape(1, -1), pltpu.VMEM), mid, shrink_weight)
 
 
 def solution(mesh):

time: 38.9 us -> 38.9 us (level)
  no operation moved by 1% of the time
where the time goes in v17:
time: 38.9 us; the launch traced here: 38.5 us
  waiting for transfers between devices  11.6 us (30%)
  Pallas kernels  11.6 us (30%)
  starting transfers between devices  10.6 us (27%)
  local copies, waits for them, and re-layouts  3.05 us (8%)
  other arithmetic  1.61 us (4%)
    pallas_call x1, Pallas kernels, on_device(): pl.pallas_call(attention_kernel, out_shape=(jax.ShapeDtypeStruct((rows, m...  6.83 us
    ppermute x2, starting transfers between devices, lin_shift(): lax.ppermute(value, ('chip', 'core'), [(s, s + steps) for s in range(lead...  6.18 us
    ppermute x2, waiting for transfers between devices, lin_shift(): lax.ppermute(value, ('chip', 'core'), [(s, s + steps) for s in range(lead...  5.55 us
    ppermute x1, waiting for transfers between devices, on_device(): cross_recv = lax.ppermute(cross_send, ('chip', 'core'), inward)  4.9 us
    pallas_call x1, Pallas kernels, on_device(): pl.pallas_call(conv_kernel, out_shape=jax.ShapeDtypeStruct((rows, model_w...  4.76 us
    ppermute x1, starting transfers between devices, on_device(): cross_recv = lax.ppermute(cross_send, ('chip', 'core'), inward)  2.51 us
    slice x1, local copies, waits for them, and re-layouts, on_device(): expand_weight[:, model_width:]  1.76 us
    ppermute x1, starting transfers between devices, on_device(): partner = lax.ppermute(gated_input, 'core', swap)  1.24 us
  transfers between devices with their start and end apart: 6, of which 4 were waited for; matrix products, arithmetic and copies ran while one was open for 10% of the time, Pallas kernels for 0%

profile of v17, /device:TPU:21, one launch (start us, length us, event | category | flops | bytes accessed | tf_op | source)
XLA Modules:
  0.0 38.5 jit_solution(5156548427735568300)
XLA Ops:
  0.0 1.0 %pad_maximum_fusion.own_hbm = bf16[2,128,512]{2,1,0:T(8,128)(2,1)S(1)} fusion(bf16[1,128,512]{2,1,0:T(8,128)(2,1)} %bitcast.8, bf16[1,128,512]{2,1,0:T(8,128)(2,1)} %bitcast.9), kind=kLoop, calls=%fused_computation | loop fusion | flops 131072 | bytes 524288 | tf_op jit(solution)/shard_map/stack | solution.py:205
  1.0 0.0 copy-start.2
  1.0 2.1 %collective-permute-start.1 = (bf16[2,128,512]{2,1,0:T(8,128)(2,1)S(1)}, bf16[2,128,512]{2,1,0:T(8,128)(2,1)S(1)}, u32[]{:S(2)}, u32[]{:S(2)}) collective-permute-start(bf16[2,128,512]{2,1,0:T(8,128)(2,1)S(1)} %pad_maximum_fusion.own_hbm), channel_id=1, source_target_pairs={{2,0},{3,1},{4,2},{5,3},{6,4},{7,5},{8,6},{9,7},{10,8},{11,9},{12,... | collective-permute-start | bytes 786440 | tf_op jit(solution)/shard_map/ppermute | solution.py:199
  3.2 4.0 %collective-permute-start = (bf16[2,128,512]{2,1,0:T(8,128)(2,1)S(1)}, bf16[2,128,512]{2,1,0:T(8,128)(2,1)S(1)}, u32[]{:S(2)}, u32[]{:S(2)}) collective-permute-start(bf16[2,128,512]{2,1,0:T(8,128)(2,1)S(1)} %pad_maximum_fusion.own_hbm), channel_id=1, source_target_pairs={{0,2},{1,3},{2,4},{3,5},{4,6},{5,7},{6,8},{7,9},{8,10},{9,11},{10,... | collective-permute-start | bytes 786440 | tf_op jit(solution)/shard_map/ppermute | solution.py:199
  7.2 0.7 %pad.4 = s32[768]{0:T(1024)S(1)} pad(s32[767]{0:T(1024)} %param.18, s32[]{:T(128)} %constant.5.clone.1), padding=0_1 | pad | bytes 6144 | tf_op jit(solution)/shard_map/jit(_pad)/pad | solution.py:202
  7.9 0.6 %reshape.9.table_ref = s32[1,768]{1,0:T(1,128)} reshape(s32[768]{0:T(1024)S(1)} %pad.4) | data formatting | bytes 6144 | tf_op jit(solution)/shard_map/reshape | solution.py:202
  8.5 1.8 %slice.3.gate_w = bf16[1024,1024]{1,0:T(8,128)(2,1)S(1)} slice(bf16[1024,2048]{1,0:T(8,128)(2,1)} %value_hbm.1), slice={[0:1024], [1024:2048]} | slice | bytes 4194304 | tf_op jit(solution)/shard_map/slice | solution.py:209
  10.3 0.6 %pad_add_fusion.meta_ref = s32[2]{0:T(128)} fusion(s32[1]{0:T(128)} %bitcast.3, s32[1]{0:T(128)} %bitcast.2), kind=kLoop, calls=%fused_computation.2 | loop fusion | flops 2 | bytes 16 | tf_op jit(solution)/shard_map/stack | solution.py:195
  10.9 0.0 copy-done.2
  10.9 1.2 %collective-permute-start.2 = (bf16[2,128,512]{2,1,0:T(8,128)(2,1)S(1)}, bf16[2,128,512]{2,1,0:T(8,128)(2,1)S(1)}, u32[]{:S(2)}, u32[]{:S(2)}) collective-permute-start(bf16[2,128,512]{2,1,0:T(8,128)(2,1)S(1)} %pad_maximum_fusion.own_hbm), channel_id=1, source_target_pairs={{0,1},{1,0},{2,3},{3,2},{4,5},{5,4},{6,7},{7,6},{8,9},{9,8},{10,11... | collective-permute-start | bytes 786440 | tf_op jit(solution)/shard_map/ppermute | solution.py:210
  12.1 1.5 %collective-permute-done.1.next_hbm = bf16[2,128,512]{2,1,0:T(8,128)(2,1)S(1)} collective-permute-done((bf16[2,128,512]{2,1,0:T(8,128)(2,1)S(1)}, bf16[2,128,512]{2,1,0:T(8,128)(2,1)S(1)}, u32[]{:S(2)}, u32[]{:S(2)}) %collective-permute-start.1) | collective-permute-done | bytes 262176 | tf_op jit(solution)/shard_map/ppermute | solution.py:199
  13.6 4.1 %collective-permute-done.prev_hbm = bf16[2,128,512]{2,1,0:T(8,128)(2,1)S(1)} collective-permute-done((bf16[2,128,512]{2,1,0:T(8,128)(2,1)S(1)}, bf16[2,128,512]{2,1,0:T(8,128)(2,1)S(1)}, u32[]{:S(2)}, u32[]{:S(2)}) %collective-permute-start) | collective-permute-done | bytes 262176 | tf_op jit(solution)/shard_map/ppermute | solution.py:199
  17.7 0.6 %collective-permute-start.3 = (bf16[2,128,512]{2,1,0:T(8,128)(2,1)S(1)}, bf16[2,128,512]{2,1,0:T(8,128)(2,1)S(1)}, u32[]{:S(2)}, u32[]{:S(2)}) collective-permute-start(bf16[2,128,512]{2,1,0:T(8,128)(2,1)S(1)} %broadcast_select_fusion), channel_id=1, source_target_pairs={{0,1},{1,0},{2,3},{3,2},{4,5},{5,4},{6,7},{7,6},{8,9},{9,8},{10,11... | collective-permute-start | bytes 786440 | tf_op jit(solution)/shard_map/ppermute | solution.py:212
  18.2 0.0 collective-permute-done.2.partner_hbm
  18.2 1.2 %collective-permute-done.3.sel_hbm = bf16[2,128,512]{2,1,0:T(8,128)(2,1)S(1)} collective-permute-done((bf16[2,128,512]{2,1,0:T(8,128)(2,1)S(1)}, bf16[2,128,512]{2,1,0:T(8,128)(2,1)S(1)}, u32[]{:S(2)}, u32[]{:S(2)}) %collective-permute-start.3) | collective-permute-done | bytes 262176 | tf_op jit(solution)/shard_map/ppermute | solution.py:212
  19.4 0.0 copy-start
  19.4 0.0 copy-start.1
  19.4 6.8 %attention_glu.1 = (bf16[128,1024]{1,0:T(8,128)(2,1)}, bf16[64,1024]{1,0:T(8,128)(2,1)}, bf16[64,1024]{1,0:T(8,128)(2,1)}) custom-call(s32[2]{0:T(128)} %pad_add_fusion.meta_ref, s32[16]{0:T(128)} %len_ref.1, s32[1,768]{1,0:T(1,128)} %reshape.9.table_ref, f32[8,32]{1,0:T(8,128)} %bitcast.10, bf16[128,512]{1,0:T(8,128)(2,1)} %q_ref.1, ...), custom_call_target="tpu_custom_call" | custom-call | flops 1006632960 | bytes 7208960 | tf_op jit(solution)/shard_map/attention_glu/pallas_call | solution.py:222
  26.2 2.5 %collective-permute-start.4 = (bf16[64,1024]{1,0:T(8,128)(2,1)}, bf16[64,1024]{1,0:T(8,128)(2,1)S(1)}, u32[]{:S(2)}, u32[]{:S(2)}) collective-permute-start(bf16[64,1024]{1,0:T(8,128)(2,1)} %get-tuple-element.18.own_cross_ref), channel_id=1, source_target_pairs={{1,2},{3,4},{5,6},{7,8},{9,10},{11,12},{13,14},{2,1},{4,3},{6,5},{... | collective-permute-start | bytes 393224 | tf_op jit(solution)/shard_map/ppermute | solution.py:252
  28.8 0.1 collective-permute-start.5
  28.8 4.9 %collective-permute-done.4.cross_ref = bf16[64,1024]{1,0:T(8,128)(2,1)S(1)} collective-permute-done((bf16[64,1024]{1,0:T(8,128)(2,1)}, bf16[64,1024]{1,0:T(8,128)(2,1)S(1)}, u32[]{:S(2)}, u32[]{:S(2)}) %collective-permute-start.4) | collective-permute-done | bytes 131104 | tf_op jit(solution)/shard_map/ppermute | solution.py:252
  33.7 0.0 collective-permute-done.5.pairg_ref
  33.7 0.0 copy-done
  33.8 0.0 copy-done.1
  33.8 4.8 %conv_shrink.1 = bf16[128,1024]{1,0:T(8,128)(2,1)} custom-call(s32[2]{0:T(128)} %pad_add_fusion.meta_ref, bf16[64,1024]{1,0:T(8,128)(2,1)} %get-tuple-element.18.own_cross_ref, bf16[64,1024]{1,0:T(8,128)(2,1)} %get-tuple-element.19.own_partner_ref, bf16[64,1024]{1,0:T(8,128)(2,1)S(1)} %collective-permute-done.4.cross_ref, ...), custom_call_target="tpu_custom_call" | custom-call | flops 276561920 | bytes 3272704 | tf_op jit(solution)/shard_map/conv_shrink/pallas_call | solution.py:256
  (1 shorter events, 0.0 us)
Async XLA Ops:
  1.0 9.9 %copy-start.2 = (bf16[2,128,512]{2,1,0:T(8,128)(2,1)}, bf16[2,128,512]{2,1,0:T(8,128)(2,1)S(1)}, u32[]{:S(2)}) copy-start(bf16[2,128,512]{2,1,0:T(8,128)(2,1)S(1)} %pad_maximum_fusion.own_hbm) | copy-start | bytes 786436
  1.0 12.6 %collective-permute-start.1 = (bf16[2,128,512]{2,1,0:T(8,128)(2,1)S(1)}, bf16[2,128,512]{2,1,0:T(8,128)(2,1)S(1)}, u32[]{:S(2)}, u32[]{:S(2)}) collective-permute-start(bf16[2,128,512]{2,1,0:T(8,128)(2,1)S(1)} %pad_maximum_fusion.own_hbm), channel_id=1, source_target_pairs={{2,0},{3,1},{4,2},{5,3},{6,4},{7,5},{8,6},{9,7},{10,8},{11,9},{12,... | collective-permute-start | bytes 786440 | tf_op jit(solution)/shard_map/ppermute | solution.py:199
  3.2 14.5 %collective-permute-start = (bf16[2,128,512]{2,1,0:T(8,128)(2,1)S(1)}, bf16[2,128,512]{2,1,0:T(8,128)(2,1)S(1)}, u32[]{:S(2)}, u32[]{:S(2)}) collective-permute-start(bf16[2,128,512]{2,1,0:T(8,128)(2,1)S(1)} %pad_maximum_fusion.own_hbm), channel_id=1, source_target_pairs={{0,2},{1,3},{2,4},{3,5},{4,6},{5,7},{6,8},{7,9},{8,10},{9,11},{10,... | collective-permute-start | bytes 786440 | tf_op jit(solution)/shard_map/ppermute | solution.py:199
  10.9 7.4 %collective-permute-start.2 = (bf16[2,128,512]{2,1,0:T(8,128)(2,1)S(1)}, bf16[2,128,512]{2,1,0:T(8,128)(2,1)S(1)}, u32[]{:S(2)}, u32[]{:S(2)}) collective-permute-start(bf16[2,128,512]{2,1,0:T(8,128)(2,1)S(1)} %pad_maximum_fusion.own_hbm), channel_id=1, source_target_pairs={{0,1},{1,0},{2,3},{3,2},{4,5},{5,4},{6,7},{7,6},{8,9},{9,8},{10,11... | collective-permute-start | bytes 786440 | tf_op jit(solution)/shard_map/ppermute | solution.py:210
  17.7 1.7 %collective-permute-start.3 = (bf16[2,128,512]{2,1,0:T(8,128)(2,1)S(1)}, bf16[2,128,512]{2,1,0:T(8,128)(2,1)S(1)}, u32[]{:S(2)}, u32[]{:S(2)}) collective-permute-start(bf16[2,128,512]{2,1,0:T(8,128)(2,1)S(1)} %broadcast_select_fusion), channel_id=1, source_target_pairs={{0,1},{1,0},{2,3},{3,2},{4,5},{5,4},{6,7},{7,6},{8,9},{9,8},{10,11... | collective-permute-start | bytes 786440 | tf_op jit(solution)/shard_map/ppermute | solution.py:212
  19.4 14.3 %copy-start = (f32[31,1024]{1,0:T(8,128)S(1)}, f32[31,1024]{1,0:T(8,128)}, u32[]{:S(2)}) copy-start(f32[31,1024]{1,0:T(8,128)} %taps_ref.1) | copy-start | bytes 380932
  19.4 14.4 %copy-start.1 = (f32[1024]{0:T(1024)S(1)}, f32[1024]{0:T(1024)}, u32[]{:S(2)}) copy-start(f32[1024]{0:T(1024)} %param.24) | copy-start | bytes 12292
  26.2 7.5 %collective-permute-start.4 = (bf16[64,1024]{1,0:T(8,128)(2,1)}, bf16[64,1024]{1,0:T(8,128)(2,1)S(1)}, u32[]{:S(2)}, u32[]{:S(2)}) collective-permute-start(bf16[64,1024]{1,0:T(8,128)(2,1)} %get-tuple-element.18.own_cross_ref), channel_id=1, source_target_pairs={{1,2},{3,4},{5,6},{7,8},{9,10},{11,12},{13,14},{2,1},{4,3},{6,5},{... | collective-permute-start | bytes 393224 | tf_op jit(solution)/shard_map/ppermute | solution.py:252
  28.8 5.0 %collective-permute-start.5 = (bf16[64,1024]{1,0:T(8,128)(2,1)}, bf16[64,1024]{1,0:T(8,128)(2,1)S(1)}, u32[]{:S(2)}, u32[]{:S(2)}) collective-permute-start(bf16[64,1024]{1,0:T(8,128)(2,1)} %get-tuple-element.19.own_partner_ref), channel_id=1, source_target_pairs={{0,1},{1,0},{2,3},{3,2},{4,5},{5,4},{6,7},{7,6},{8,9},{9,8},{10,11... | collective-permute-start | bytes 393224 | tf_op jit(solution)/shard_map/ppermute | solution.py:253

commit v18 on v17

--- a/solution.py
+++ b/solution.py
@@ -90,32 +90,35 @@
     for copy in copies:
         copy.wait()
     scaling = head_width ** (-0.5)
-    lane = lax.broadcasted_iota(jnp.int32, (rows, LANES), 1)
+    band = rows // 2
+    band_lane = lax.broadcasted_iota(jnp.int32, (band, LANES), 1)
     per_pair = LANES // head_width
     for pair in range(att_width // LANES):
         cols = slice(pair * LANES, (pair + 1) * LANES)
         q_pair = q_ref[:, cols]
         k_pair = jnp.concatenate([win_ref[planes * j, :, cols] for j in range(blocks)], axis=0)
         v_pair = jnp.concatenate([win_ref[planes * j + 1, :, cols] for j in range(blocks)], axis=0)
-        result = None
-        for sub in range(per_pair):
-            head = pair * per_pair + sub
-            in_head = (lane >= sub * head_width) & (lane < (sub + 1) * head_width)
-            q_head = jnp.where(in_head, q_pair, jnp.zeros_like(q_pair))
-            spread = jnp.broadcast_to(line[head:head + 1, :], (rows, line_len))
-            skew = pltpu.roll(spread, line_len - rows + 1, 1, stride=1, stride_axis=0)[:, :width]
-            bias = jnp.where(same, skew, masked_score)
-            scores = lax.dot_general(
-                q_head, k_pair, (((1,), (1,)), ((), ())), preferred_element_type=jnp.float32
-            )
-            scores = scores * scaling + bias
-            top = jnp.max(scores, axis=1, keepdims=True)
-            weights = jnp.exp(scores - top)
-            total = jnp.sum(weights, axis=1, keepdims=True)
-            summed = jnp.dot(weights.astype(jnp.bfloat16), v_pair, preferred_element_type=jnp.float32)
-            part = summed / total
-            result = part if result is None else jnp.where(in_head, part, result)
-        att_ref[:, cols] = result.astype(jnp.bfloat16)
+        for first in range(0, rows, band):
+            band_rows = slice(first, first + band)
+            result = None
+            for sub in range(per_pair):
+                head = pair * per_pair + sub
+                in_head = (band_lane >= sub * head_width) & (band_lane < (sub + 1) * head_width)
+                q_head = jnp.where(in_head, q_pair[band_rows], jnp.zeros_like(q_pair[band_rows]))
+                spread = jnp.broadcast_to(line[head:head + 1, :], (band, line_len))
+                skew = pltpu.roll(spread, (line_len - rows + 1 + first) % line_len, 1, stride=1, stride_axis=0)[:, :width]
+                bias = jnp.where(same[band_rows], skew, masked_score)
+                scores = lax.dot_general(
+                    q_head, k_pair, (((1,), (1,)), ((), ())), preferred_element_type=jnp.float32
+                )
+                scores = scores * scaling + bias
+                top = jnp.max(scores, axis=1, keepdims=True)
+                weights = jnp.exp(scores - top)
+                total = jnp.sum(weights, axis=1, keepdims=True)
+                summed = jnp.dot(weights.astype(jnp.bfloat16), v_pair, preferred_element_type=jnp.float32)
+                part = summed / total
+                result = part if result is None else jnp.where(in_head, part, result)
+            att_ref[band_rows, cols] = result.astype(jnp.bfloat16)
 
     ow_copy.wait()
     projected = jnp.dot(att_ref[...], ow_vmem[...], preferred_element_type=jnp.float32)

time: 38.9 us -> 41.2 us (1.059)
  Pallas kernels: 11.6 us -> 13.9 us
    pallas_call x1, Pallas kernels: 6.83 us -> 9.16 us  [on_device(): pl.pallas_call(attention_kernel, out_shape=(jax.ShapeDtypeStruct((rows, m...]
  transfers between devices with their start and end apart: 6 -> 6, of which waited for: 4 -> 4; matrix products, arithmetic and copies ran while one was open for 10% -> 9% of each run, Pallas kernels for 0% -> 0%
where the time goes in v18:
time: 41.2 us; the launch traced here: 40.8 us
  Pallas kernels  13.9 us (34%)
  waiting for transfers between devices  11.6 us (28%)
  starting transfers between devices  10.6 us (26%)
  local copies, waits for them, and re-layouts  3.05 us (7%)
  other arithmetic  1.61 us (4%)
    pallas_call x1, Pallas kernels, on_device(): pl.pallas_call(attention_kernel, out_shape=(jax.ShapeDtypeStruct((rows, m...  9.16 us
    ppermute x2, starting transfers between devices, lin_shift(): lax.ppermute(value, ('chip', 'core'), [(s, s + steps) for s in range(lead...  6.18 us
    ppermute x2, waiting for transfers between devices, lin_shift(): lax.ppermute(value, ('chip', 'core'), [(s, s + steps) for s in range(lead...  5.55 us
    ppermute x1, waiting for transfers between devices, on_device(): cross_recv = lax.ppermute(cross_send, ('chip', 'core'), inward)  4.9 us
    pallas_call x1, Pallas kernels, on_device(): pl.pallas_call(conv_kernel, out_shape=jax.ShapeDtypeStruct((rows, model_w...  4.76 us
    ppermute x1, starting transfers between devices, on_device(): cross_recv = lax.ppermute(cross_send, ('chip', 'core'), inward)  2.51 us
    slice x1, local copies, waits for them, and re-layouts, on_device(): expand_weight[:, model_width:]  1.76 us
    ppermute x1, starting transfers between devices, on_device(): partner = lax.ppermute(gated_input, 'core', swap)  1.24 us
  transfers between devices with their start and end apart: 6, of which 4 were waited for; matrix products, arithmetic and copies ran while one was open for 9% of the time, Pallas kernels for 0%

profile of v18, /device:TPU:21, one launch (start us, length us, event | category | flops | bytes accessed | tf_op | source)
XLA Modules:
  0.0 40.8 jit_solution(5531666701643144378)
XLA Ops:
  0.0 1.0 %pad_maximum_fusion.own_hbm = bf16[2,128,512]{2,1,0:T(8,128)(2,1)S(1)} fusion(bf16[1,128,512]{2,1,0:T(8,128)(2,1)} %bitcast.8, bf16[1,128,512]{2,1,0:T(8,128)(2,1)} %bitcast.9), kind=kLoop, calls=%fused_computation | loop fusion | flops 131072 | bytes 524288 | tf_op jit(solution)/shard_map/stack | solution.py:208
  1.0 0.0 copy-start.2
  1.0 2.1 %collective-permute-start.1 = (bf16[2,128,512]{2,1,0:T(8,128)(2,1)S(1)}, bf16[2,128,512]{2,1,0:T(8,128)(2,1)S(1)}, u32[]{:S(2)}, u32[]{:S(2)}) collective-permute-start(bf16[2,128,512]{2,1,0:T(8,128)(2,1)S(1)} %pad_maximum_fusion.own_hbm), channel_id=1, source_target_pairs={{2,0},{3,1},{4,2},{5,3},{6,4},{7,5},{8,6},{9,7},{10,8},{11,9},{12,... | collective-permute-start | bytes 786440 | tf_op jit(solution)/shard_map/ppermute | solution.py:202
  3.2 4.0 %collective-permute-start = (bf16[2,128,512]{2,1,0:T(8,128)(2,1)S(1)}, bf16[2,128,512]{2,1,0:T(8,128)(2,1)S(1)}, u32[]{:S(2)}, u32[]{:S(2)}) collective-permute-start(bf16[2,128,512]{2,1,0:T(8,128)(2,1)S(1)} %pad_maximum_fusion.own_hbm), channel_id=1, source_target_pairs={{0,2},{1,3},{2,4},{3,5},{4,6},{5,7},{6,8},{7,9},{8,10},{9,11},{10,... | collective-permute-start | bytes 786440 | tf_op jit(solution)/shard_map/ppermute | solution.py:202
  7.2 0.7 %pad.4 = s32[768]{0:T(1024)S(1)} pad(s32[767]{0:T(1024)} %param.18, s32[]{:T(128)} %constant.5.clone.1), padding=0_1 | pad | bytes 6144 | tf_op jit(solution)/shard_map/jit(_pad)/pad | solution.py:205
  7.9 0.6 %reshape.9.table_ref = s32[1,768]{1,0:T(1,128)} reshape(s32[768]{0:T(1024)S(1)} %pad.4) | data formatting | bytes 6144 | tf_op jit(solution)/shard_map/reshape | solution.py:205
  8.5 1.8 %slice.3.gate_w = bf16[1024,1024]{1,0:T(8,128)(2,1)S(1)} slice(bf16[1024,2048]{1,0:T(8,128)(2,1)} %value_hbm.1), slice={[0:1024], [1024:2048]} | slice | bytes 4194304 | tf_op jit(solution)/shard_map/slice | solution.py:212
  10.3 0.6 %pad_add_fusion.meta_ref = s32[2]{0:T(128)} fusion(s32[1]{0:T(128)} %bitcast.3, s32[1]{0:T(128)} %bitcast.2), kind=kLoop, calls=%fused_computation.2 | loop fusion | flops 2 | bytes 16 | tf_op jit(solution)/shard_map/stack | solution.py:198
  10.9 0.0 copy-done.2
  10.9 1.2 %collective-permute-start.2 = (bf16[2,128,512]{2,1,0:T(8,128)(2,1)S(1)}, bf16[2,128,512]{2,1,0:T(8,128)(2,1)S(1)}, u32[]{:S(2)}, u32[]{:S(2)}) collective-permute-start(bf16[2,128,512]{2,1,0:T(8,128)(2,1)S(1)} %pad_maximum_fusion.own_hbm), channel_id=1, source_target_pairs={{0,1},{1,0},{2,3},{3,2},{4,5},{5,4},{6,7},{7,6},{8,9},{9,8},{10,11... | collective-permute-start | bytes 786440 | tf_op jit(solution)/shard_map/ppermute | solution.py:213
  12.1 1.5 %collective-permute-done.1.next_hbm = bf16[2,128,512]{2,1,0:T(8,128)(2,1)S(1)} collective-permute-done((bf16[2,128,512]{2,1,0:T(8,128)(2,1)S(1)}, bf16[2,128,512]{2,1,0:T(8,128)(2,1)S(1)}, u32[]{:S(2)}, u32[]{:S(2)}) %collective-permute-start.1) | collective-permute-done | bytes 262176 | tf_op jit(solution)/shard_map/ppermute | solution.py:202
  13.6 4.1 %collective-permute-done.prev_hbm = bf16[2,128,512]{2,1,0:T(8,128)(2,1)S(1)} collective-permute-done((bf16[2,128,512]{2,1,0:T(8,128)(2,1)S(1)}, bf16[2,128,512]{2,1,0:T(8,128)(2,1)S(1)}, u32[]{:S(2)}, u32[]{:S(2)}) %collective-permute-start) | collective-permute-done | bytes 262176 | tf_op jit(solution)/shard_map/ppermute | solution.py:202
  17.7 0.6 %collective-permute-start.3 = (bf16[2,128,512]{2,1,0:T(8,128)(2,1)S(1)}, bf16[2,128,512]{2,1,0:T(8,128)(2,1)S(1)}, u32[]{:S(2)}, u32[]{:S(2)}) collective-permute-start(bf16[2,128,512]{2,1,0:T(8,128)(2,1)S(1)} %broadcast_select_fusion), channel_id=1, source_target_pairs={{0,1},{1,0},{2,3},{3,2},{4,5},{5,4},{6,7},{7,6},{8,9},{9,8},{10,11... | collective-permute-start | bytes 786440 | tf_op jit(solution)/shard_map/ppermute | solution.py:215
  18.2 0.0 collective-permute-done.2.partner_hbm
  18.2 1.2 %collective-permute-done.3.sel_hbm = bf16[2,128,512]{2,1,0:T(8,128)(2,1)S(1)} collective-permute-done((bf16[2,128,512]{2,1,0:T(8,128)(2,1)S(1)}, bf16[2,128,512]{2,1,0:T(8,128)(2,1)S(1)}, u32[]{:S(2)}, u32[]{:S(2)}) %collective-permute-start.3) | collective-permute-done | bytes 262176 | tf_op jit(solution)/shard_map/ppermute | solution.py:215
  19.4 0.0 copy-start
  19.4 0.0 copy-start.1
  19.4 9.2 %attention_glu.1 = (bf16[128,1024]{1,0:T(8,128)(2,1)}, bf16[64,1024]{1,0:T(8,128)(2,1)}, bf16[64,1024]{1,0:T(8,128)(2,1)}) custom-call(s32[2]{0:T(128)} %pad_add_fusion.meta_ref, s32[16]{0:T(128)} %len_ref.1, s32[1,768]{1,0:T(1,128)} %reshape.9.table_ref, f32[8,32]{1,0:T(8,128)} %bitcast.10, bf16[128,512]{1,0:T(8,128)(2,1)} %q_ref.1, ...), custom_call_target="tpu_custom_call" | custom-call | flops 1006632960 | bytes 7208960 | tf_op jit(solution)/shard_map/attention_glu/pallas_call | solution.py:225
  28.6 2.5 %collective-permute-start.4 = (bf16[64,1024]{1,0:T(8,128)(2,1)}, bf16[64,1024]{1,0:T(8,128)(2,1)S(1)}, u32[]{:S(2)}, u32[]{:S(2)}) collective-permute-start(bf16[64,1024]{1,0:T(8,128)(2,1)} %get-tuple-element.18.own_cross_ref), channel_id=1, source_target_pairs={{1,2},{3,4},{5,6},{7,8},{9,10},{11,12},{13,14},{2,1},{4,3},{6,5},{... | collective-permute-start | bytes 393224 | tf_op jit(solution)/shard_map/ppermute | solution.py:255
  31.1 0.1 collective-permute-start.5
  31.2 4.9 %collective-permute-done.4.cross_ref = bf16[64,1024]{1,0:T(8,128)(2,1)S(1)} collective-permute-done((bf16[64,1024]{1,0:T(8,128)(2,1)}, bf16[64,1024]{1,0:T(8,128)(2,1)S(1)}, u32[]{:S(2)}, u32[]{:S(2)}) %collective-permute-start.4) | collective-permute-done | bytes 131104 | tf_op jit(solution)/shard_map/ppermute | solution.py:255
  36.1 0.0 collective-permute-done.5.pairg_ref
  36.1 0.0 copy-done
  36.1 0.0 copy-done.1
  36.1 4.8 %conv_shrink.1 = bf16[128,1024]{1,0:T(8,128)(2,1)} custom-call(s32[2]{0:T(128)} %pad_add_fusion.meta_ref, bf16[64,1024]{1,0:T(8,128)(2,1)} %get-tuple-element.18.own_cross_ref, bf16[64,1024]{1,0:T(8,128)(2,1)} %get-tuple-element.19.own_partner_ref, bf16[64,1024]{1,0:T(8,128)(2,1)S(1)} %collective-permute-done.4.cross_ref, ...), custom_call_target="tpu_custom_call" | custom-call | flops 276561920 | bytes 3272704 | tf_op jit(solution)/shard_map/conv_shrink/pallas_call | solution.py:259
  (1 shorter events, 0.0 us)
Async XLA Ops:
  1.0 9.9 %copy-start.2 = (bf16[2,128,512]{2,1,0:T(8,128)(2,1)}, bf16[2,128,512]{2,1,0:T(8,128)(2,1)S(1)}, u32[]{:S(2)}) copy-start(bf16[2,128,512]{2,1,0:T(8,128)(2,1)S(1)} %pad_maximum_fusion.own_hbm) | copy-start | bytes 786436
  1.0 12.6 %collective-permute-start.1 = (bf16[2,128,512]{2,1,0:T(8,128)(2,1)S(1)}, bf16[2,128,512]{2,1,0:T(8,128)(2,1)S(1)}, u32[]{:S(2)}, u32[]{:S(2)}) collective-permute-start(bf16[2,128,512]{2,1,0:T(8,128)(2,1)S(1)} %pad_maximum_fusion.own_hbm), channel_id=1, source_target_pairs={{2,0},{3,1},{4,2},{5,3},{6,4},{7,5},{8,6},{9,7},{10,8},{11,9},{12,... | collective-permute-start | bytes 786440 | tf_op jit(solution)/shard_map/ppermute | solution.py:202
  3.2 14.5 %collective-permute-start = (bf16[2,128,512]{2,1,0:T(8,128)(2,1)S(1)}, bf16[2,128,512]{2,1,0:T(8,128)(2,1)S(1)}, u32[]{:S(2)}, u32[]{:S(2)}) collective-permute-start(bf16[2,128,512]{2,1,0:T(8,128)(2,1)S(1)} %pad_maximum_fusion.own_hbm), channel_id=1, source_target_pairs={{0,2},{1,3},{2,4},{3,5},{4,6},{5,7},{6,8},{7,9},{8,10},{9,11},{10,... | collective-permute-start | bytes 786440 | tf_op jit(solution)/shard_map/ppermute | solution.py:202
  10.9 7.4 %collective-permute-start.2 = (bf16[2,128,512]{2,1,0:T(8,128)(2,1)S(1)}, bf16[2,128,512]{2,1,0:T(8,128)(2,1)S(1)}, u32[]{:S(2)}, u32[]{:S(2)}) collective-permute-start(bf16[2,128,512]{2,1,0:T(8,128)(2,1)S(1)} %pad_maximum_fusion.own_hbm), channel_id=1, source_target_pairs={{0,1},{1,0},{2,3},{3,2},{4,5},{5,4},{6,7},{7,6},{8,9},{9,8},{10,11... | collective-permute-start | bytes 786440 | tf_op jit(solution)/shard_map/ppermute | solution.py:213
  17.7 1.7 %collective-permute-start.3 = (bf16[2,128,512]{2,1,0:T(8,128)(2,1)S(1)}, bf16[2,128,512]{2,1,0:T(8,128)(2,1)S(1)}, u32[]{:S(2)}, u32[]{:S(2)}) collective-permute-start(bf16[2,128,512]{2,1,0:T(8,128)(2,1)S(1)} %broadcast_select_fusion), channel_id=1, source_target_pairs={{0,1},{1,0},{2,3},{3,2},{4,5},{5,4},{6,7},{7,6},{8,9},{9,8},{10,11... | collective-permute-start | bytes 786440 | tf_op jit(solution)/shard_map/ppermute | solution.py:215
  19.4 16.7 %copy-start = (f32[31,1024]{1,0:T(8,128)S(1)}, f32[31,1024]{1,0:T(8,128)}, u32[]{:S(2)}) copy-start(f32[31,1024]{1,0:T(8,128)} %taps_ref.1) | copy-start | bytes 380932
  19.4 16.7 %copy-start.1 = (f32[1024]{0:T(1024)S(1)}, f32[1024]{0:T(1024)}, u32[]{:S(2)}) copy-start(f32[1024]{0:T(1024)} %param.24) | copy-start | bytes 12292
  28.6 7.5 %collective-permute-start.4 = (bf16[64,1024]{1,0:T(8,128)(2,1)}, bf16[64,1024]{1,0:T(8,128)(2,1)S(1)}, u32[]{:S(2)}, u32[]{:S(2)}) collective-permute-start(bf16[64,1024]{1,0:T(8,128)(2,1)} %get-tuple-element.18.own_cross_ref), channel_id=1, source_target_pairs={{1,2},{3,4},{5,6},{7,8},{9,10},{11,12},{13,14},{2,1},{4,3},{6,5},{... | collective-permute-start | bytes 393224 | tf_op jit(solution)/shard_map/ppermute | solution.py:255
  31.1 5.0 %collective-permute-start.5 = (bf16[64,1024]{1,0:T(8,128)(2,1)}, bf16[64,1024]{1,0:T(8,128)(2,1)S(1)}, u32[]{:S(2)}, u32[]{:S(2)}) collective-permute-start(bf16[64,1024]{1,0:T(8,128)(2,1)} %get-tuple-element.19.own_partner_ref), channel_id=1, source_target_pairs={{0,1},{1,0},{2,3},{3,2},{4,5},{5,4},{6,7},{7,6},{8,9},{9,8},{10,11... | collective-permute-start | bytes 393224 | tf_op jit(solution)/shard_map/ppermute | solution.py:256

commit v19 on v17

--- a/solution.py
+++ b/solution.py
@@ -97,24 +97,27 @@
         q_pair = q_ref[:, cols]
         k_pair = jnp.concatenate([win_ref[planes * j, :, cols] for j in range(blocks)], axis=0)
         v_pair = jnp.concatenate([win_ref[planes * j + 1, :, cols] for j in range(blocks)], axis=0)
-        result = None
+        q_rows, biases, masks = [], [], []
         for sub in range(per_pair):
             head = pair * per_pair + sub
             in_head = (lane >= sub * head_width) & (lane < (sub + 1) * head_width)
-            q_head = jnp.where(in_head, q_pair, jnp.zeros_like(q_pair))
+            q_rows.append(jnp.where(in_head, q_pair, jnp.zeros_like(q_pair)))
             spread = jnp.broadcast_to(line[head:head + 1, :], (rows, line_len))
             skew = pltpu.roll(spread, line_len - rows + 1, 1, stride=1, stride_axis=0)[:, :width]
-            bias = jnp.where(same, skew, masked_score)
-            scores = lax.dot_general(
-                q_head, k_pair, (((1,), (1,)), ((), ())), preferred_element_type=jnp.float32
-            )
-            scores = scores * scaling + bias
-            top = jnp.max(scores, axis=1, keepdims=True)
-            weights = jnp.exp(scores - top)
-            total = jnp.sum(weights, axis=1, keepdims=True)
-            summed = jnp.dot(weights.astype(jnp.bfloat16), v_pair, preferred_element_type=jnp.float32)
-            part = summed / total
-            result = part if result is None else jnp.where(in_head, part, result)
+            biases.append(jnp.where(same, skew, masked_score))
+            masks.append(in_head)
+        scores = lax.dot_general(
+            jnp.concatenate(q_rows, axis=0), k_pair, (((1,), (1,)), ((), ())), preferred_element_type=jnp.float32
+        )
+        scores = scores * scaling + jnp.concatenate(biases, axis=0)
+        top = jnp.max(scores, axis=1, keepdims=True)
+        weights = jnp.exp(scores - top)
+        total = jnp.sum(weights, axis=1, keepdims=True)
+        summed = jnp.dot(weights.astype(jnp.bfloat16), v_pair, preferred_element_type=jnp.float32)
+        part = summed / total
+        result = part[0:rows]
+        for sub in range(1, per_pair):
+            result = jnp.where(masks[sub], part[sub * rows:(sub + 1) * rows], result)
         att_ref[:, cols] = result.astype(jnp.bfloat16)
 
     ow_copy.wait()

time: 38.9 us -> 38.7 us (level)
  no operation moved by 1% of the time
where the time goes in v19:
time: 38.7 us; the launch traced here: 38.3 us
  waiting for transfers between devices  11.6 us (30%)
  Pallas kernels  11.4 us (29%)
  starting transfers between devices  10.6 us (27%)
  local copies, waits for them, and re-layouts  3.05 us (8%)
  other arithmetic  1.61 us (4%)
    pallas_call x1, Pallas kernels, on_device(): pl.pallas_call(attention_kernel, out_shape=(jax.ShapeDtypeStruct((rows, m...  6.66 us
    ppermute x2, starting transfers between devices, lin_shift(): lax.ppermute(value, ('chip', 'core'), [(s, s + steps) for s in range(lead...  6.18 us
    ppermute x2, waiting for transfers between devices, lin_shift(): lax.ppermute(value, ('chip', 'core'), [(s, s + steps) for s in range(lead...  5.55 us
    ppermute x1, waiting for transfers between devices, on_device(): cross_recv = lax.ppermute(cross_send, ('chip', 'core'), inward)  4.9 us
    pallas_call x1, Pallas kernels, on_device(): pl.pallas_call(conv_kernel, out_shape=jax.ShapeDtypeStruct((rows, model_w...  4.76 us
    ppermute x1, starting transfers between devices, on_device(): cross_recv = lax.ppermute(cross_send, ('chip', 'core'), inward)  2.51 us
    slice x1, local copies, waits for them, and re-layouts, on_device(): expand_weight[:, model_width:]  1.76 us
    ppermute x1, starting transfers between devices, on_device(): partner = lax.ppermute(gated_input, 'core', swap)  1.24 us
  transfers between devices with their start and end apart: 6, of which 4 were waited for; matrix products, arithmetic and copies ran while one was open for 10% of the time, Pallas kernels for 0%

profile of v19, /device:TPU:21, one launch (start us, length us, event | category | flops | bytes accessed | tf_op | source)
XLA Modules:
  0.0 38.3 jit_solution(12003688924774110104)
XLA Ops:
  0.0 1.0 %pad_maximum_fusion.own_hbm = bf16[2,128,512]{2,1,0:T(8,128)(2,1)S(1)} fusion(bf16[1,128,512]{2,1,0:T(8,128)(2,1)} %bitcast.8, bf16[1,128,512]{2,1,0:T(8,128)(2,1)} %bitcast.9), kind=kLoop, calls=%fused_computation | loop fusion | flops 131072 | bytes 524288 | tf_op jit(solution)/shard_map/stack | solution.py:208
  1.0 0.0 copy-start.2
  1.0 2.1 %collective-permute-start.1 = (bf16[2,128,512]{2,1,0:T(8,128)(2,1)S(1)}, bf16[2,128,512]{2,1,0:T(8,128)(2,1)S(1)}, u32[]{:S(2)}, u32[]{:S(2)}) collective-permute-start(bf16[2,128,512]{2,1,0:T(8,128)(2,1)S(1)} %pad_maximum_fusion.own_hbm), channel_id=1, source_target_pairs={{2,0},{3,1},{4,2},{5,3},{6,4},{7,5},{8,6},{9,7},{10,8},{11,9},{12,... | collective-permute-start | bytes 786440 | tf_op jit(solution)/shard_map/ppermute | solution.py:202
  3.2 4.0 %collective-permute-start = (bf16[2,128,512]{2,1,0:T(8,128)(2,1)S(1)}, bf16[2,128,512]{2,1,0:T(8,128)(2,1)S(1)}, u32[]{:S(2)}, u32[]{:S(2)}) collective-permute-start(bf16[2,128,512]{2,1,0:T(8,128)(2,1)S(1)} %pad_maximum_fusion.own_hbm), channel_id=1, source_target_pairs={{0,2},{1,3},{2,4},{3,5},{4,6},{5,7},{6,8},{7,9},{8,10},{9,11},{10,... | collective-permute-start | bytes 786440 | tf_op jit(solution)/shard_map/ppermute | solution.py:202
  7.2 0.7 %pad.4 = s32[768]{0:T(1024)S(1)} pad(s32[767]{0:T(1024)} %param.18, s32[]{:T(128)} %constant.5.clone.1), padding=0_1 | pad | bytes 6144 | tf_op jit(solution)/shard_map/jit(_pad)/pad | solution.py:205
  7.9 0.6 %reshape.9.table_ref = s32[1,768]{1,0:T(1,128)} reshape(s32[768]{0:T(1024)S(1)} %pad.4) | data formatting | bytes 6144 | tf_op jit(solution)/shard_map/reshape | solution.py:205
  8.5 1.8 %slice.3.gate_w = bf16[1024,1024]{1,0:T(8,128)(2,1)S(1)} slice(bf16[1024,2048]{1,0:T(8,128)(2,1)} %value_hbm.1), slice={[0:1024], [1024:2048]} | slice | bytes 4194304 | tf_op jit(solution)/shard_map/slice | solution.py:212
  10.3 0.6 %pad_add_fusion.meta_ref = s32[2]{0:T(128)} fusion(s32[1]{0:T(128)} %bitcast.3, s32[1]{0:T(128)} %bitcast.2), kind=kLoop, calls=%fused_computation.2 | loop fusion | flops 2 | bytes 16 | tf_op jit(solution)/shard_map/stack | solution.py:198
  10.9 0.0 copy-done.2
  10.9 1.2 %collective-permute-start.2 = (bf16[2,128,512]{2,1,0:T(8,128)(2,1)S(1)}, bf16[2,128,512]{2,1,0:T(8,128)(2,1)S(1)}, u32[]{:S(2)}, u32[]{:S(2)}) collective-permute-start(bf16[2,128,512]{2,1,0:T(8,128)(2,1)S(1)} %pad_maximum_fusion.own_hbm), channel_id=1, source_target_pairs={{0,1},{1,0},{2,3},{3,2},{4,5},{5,4},{6,7},{7,6},{8,9},{9,8},{10,11... | collective-permute-start | bytes 786440 | tf_op jit(solution)/shard_map/ppermute | solution.py:213
  12.1 1.5 %collective-permute-done.1.next_hbm = bf16[2,128,512]{2,1,0:T(8,128)(2,1)S(1)} collective-permute-done((bf16[2,128,512]{2,1,0:T(8,128)(2,1)S(1)}, bf16[2,128,512]{2,1,0:T(8,128)(2,1)S(1)}, u32[]{:S(2)}, u32[]{:S(2)}) %collective-permute-start.1) | collective-permute-done | bytes 262176 | tf_op jit(solution)/shard_map/ppermute | solution.py:202
  13.6 4.1 %collective-permute-done.prev_hbm = bf16[2,128,512]{2,1,0:T(8,128)(2,1)S(1)} collective-permute-done((bf16[2,128,512]{2,1,0:T(8,128)(2,1)S(1)}, bf16[2,128,512]{2,1,0:T(8,128)(2,1)S(1)}, u32[]{:S(2)}, u32[]{:S(2)}) %collective-permute-start) | collective-permute-done | bytes 262176 | tf_op jit(solution)/shard_map/ppermute | solution.py:202
  17.7 0.6 %collective-permute-start.3 = (bf16[2,128,512]{2,1,0:T(8,128)(2,1)S(1)}, bf16[2,128,512]{2,1,0:T(8,128)(2,1)S(1)}, u32[]{:S(2)}, u32[]{:S(2)}) collective-permute-start(bf16[2,128,512]{2,1,0:T(8,128)(2,1)S(1)} %broadcast_select_fusion), channel_id=1, source_target_pairs={{0,1},{1,0},{2,3},{3,2},{4,5},{5,4},{6,7},{7,6},{8,9},{9,8},{10,11... | collective-permute-start | bytes 786440 | tf_op jit(solution)/shard_map/ppermute | solution.py:215
  18.2 0.0 collective-permute-done.2.partner_hbm
  18.2 1.2 %collective-permute-done.3.sel_hbm = bf16[2,128,512]{2,1,0:T(8,128)(2,1)S(1)} collective-permute-done((bf16[2,128,512]{2,1,0:T(8,128)(2,1)S(1)}, bf16[2,128,512]{2,1,0:T(8,128)(2,1)S(1)}, u32[]{:S(2)}, u32[]{:S(2)}) %collective-permute-start.3) | collective-permute-done | bytes 262176 | tf_op jit(solution)/shard_map/ppermute | solution.py:215
  19.4 0.0 copy-start
  19.4 0.0 copy-start.1
  19.4 6.7 %attention_glu.1 = (bf16[128,1024]{1,0:T(8,128)(2,1)}, bf16[64,1024]{1,0:T(8,128)(2,1)}, bf16[64,1024]{1,0:T(8,128)(2,1)}) custom-call(s32[2]{0:T(128)} %pad_add_fusion.meta_ref, s32[16]{0:T(128)} %len_ref.1, s32[1,768]{1,0:T(1,128)} %reshape.9.table_ref, f32[8,32]{1,0:T(8,128)} %bitcast.10, bf16[128,512]{1,0:T(8,128)(2,1)} %q_ref.1, ...), custom_call_target="tpu_custom_call" | custom-call | flops 1006632960 | bytes 7208960 | tf_op jit(solution)/shard_map/attention_glu/pallas_call | solution.py:225
  26.1 2.5 %collective-permute-start.4 = (bf16[64,1024]{1,0:T(8,128)(2,1)}, bf16[64,1024]{1,0:T(8,128)(2,1)S(1)}, u32[]{:S(2)}, u32[]{:S(2)}) collective-permute-start(bf16[64,1024]{1,0:T(8,128)(2,1)} %get-tuple-element.18.own_cross_ref), channel_id=1, source_target_pairs={{1,2},{3,4},{5,6},{7,8},{9,10},{11,12},{13,14},{2,1},{4,3},{6,5},{... | collective-permute-start | bytes 393224 | tf_op jit(solution)/shard_map/ppermute | solution.py:255
  28.6 0.1 collective-permute-start.5
  28.7 4.9 %collective-permute-done.4.cross_ref = bf16[64,1024]{1,0:T(8,128)(2,1)S(1)} collective-permute-done((bf16[64,1024]{1,0:T(8,128)(2,1)}, bf16[64,1024]{1,0:T(8,128)(2,1)S(1)}, u32[]{:S(2)}, u32[]{:S(2)}) %collective-permute-start.4) | collective-permute-done | bytes 131104 | tf_op jit(solution)/shard_map/ppermute | solution.py:255
  33.6 0.0 collective-permute-done.5.pairg_ref
  33.6 0.0 copy-done
  33.6 0.0 copy-done.1
  33.6 4.8 %conv_shrink.1 = bf16[128,1024]{1,0:T(8,128)(2,1)} custom-call(s32[2]{0:T(128)} %pad_add_fusion.meta_ref, bf16[64,1024]{1,0:T(8,128)(2,1)} %get-tuple-element.18.own_cross_ref, bf16[64,1024]{1,0:T(8,128)(2,1)} %get-tuple-element.19.own_partner_ref, bf16[64,1024]{1,0:T(8,128)(2,1)S(1)} %collective-permute-done.4.cross_ref, ...), custom_call_target="tpu_custom_call" | custom-call | flops 276561920 | bytes 3272704 | tf_op jit(solution)/shard_map/conv_shrink/pallas_call | solution.py:259
  (1 shorter events, 0.0 us)
Async XLA Ops:
  1.0 9.9 %copy-start.2 = (bf16[2,128,512]{2,1,0:T(8,128)(2,1)}, bf16[2,128,512]{2,1,0:T(8,128)(2,1)S(1)}, u32[]{:S(2)}) copy-start(bf16[2,128,512]{2,1,0:T(8,128)(2,1)S(1)} %pad_maximum_fusion.own_hbm) | copy-start | bytes 786436
  1.0 12.6 %collective-permute-start.1 = (bf16[2,128,512]{2,1,0:T(8,128)(2,1)S(1)}, bf16[2,128,512]{2,1,0:T(8,128)(2,1)S(1)}, u32[]{:S(2)}, u32[]{:S(2)}) collective-permute-start(bf16[2,128,512]{2,1,0:T(8,128)(2,1)S(1)} %pad_maximum_fusion.own_hbm), channel_id=1, source_target_pairs={{2,0},{3,1},{4,2},{5,3},{6,4},{7,5},{8,6},{9,7},{10,8},{11,9},{12,... | collective-permute-start | bytes 786440 | tf_op jit(solution)/shard_map/ppermute | solution.py:202
  3.2 14.5 %collective-permute-start = (bf16[2,128,512]{2,1,0:T(8,128)(2,1)S(1)}, bf16[2,128,512]{2,1,0:T(8,128)(2,1)S(1)}, u32[]{:S(2)}, u32[]{:S(2)}) collective-permute-start(bf16[2,128,512]{2,1,0:T(8,128)(2,1)S(1)} %pad_maximum_fusion.own_hbm), channel_id=1, source_target_pairs={{0,2},{1,3},{2,4},{3,5},{4,6},{5,7},{6,8},{7,9},{8,10},{9,11},{10,... | collective-permute-start | bytes 786440 | tf_op jit(solution)/shard_map/ppermute | solution.py:202
  10.9 7.4 %collective-permute-start.2 = (bf16[2,128,512]{2,1,0:T(8,128)(2,1)S(1)}, bf16[2,128,512]{2,1,0:T(8,128)(2,1)S(1)}, u32[]{:S(2)}, u32[]{:S(2)}) collective-permute-start(bf16[2,128,512]{2,1,0:T(8,128)(2,1)S(1)} %pad_maximum_fusion.own_hbm), channel_id=1, source_target_pairs={{0,1},{1,0},{2,3},{3,2},{4,5},{5,4},{6,7},{7,6},{8,9},{9,8},{10,11... | collective-permute-start | bytes 786440 | tf_op jit(solution)/shard_map/ppermute | solution.py:213
  17.7 1.7 %collective-permute-start.3 = (bf16[2,128,512]{2,1,0:T(8,128)(2,1)S(1)}, bf16[2,128,512]{2,1,0:T(8,128)(2,1)S(1)}, u32[]{:S(2)}, u32[]{:S(2)}) collective-permute-start(bf16[2,128,512]{2,1,0:T(8,128)(2,1)S(1)} %broadcast_select_fusion), channel_id=1, source_target_pairs={{0,1},{1,0},{2,3},{3,2},{4,5},{5,4},{6,7},{7,6},{8,9},{9,8},{10,11... | collective-permute-start | bytes 786440 | tf_op jit(solution)/shard_map/ppermute | solution.py:215
  19.4 14.2 %copy-start = (f32[31,1024]{1,0:T(8,128)S(1)}, f32[31,1024]{1,0:T(8,128)}, u32[]{:S(2)}) copy-start(f32[31,1024]{1,0:T(8,128)} %taps_ref.1) | copy-start | bytes 380932
  19.4 14.2 %copy-start.1 = (f32[1024]{0:T(1024)S(1)}, f32[1024]{0:T(1024)}, u32[]{:S(2)}) copy-start(f32[1024]{0:T(1024)} %param.24) | copy-start | bytes 12292
  26.1 7.5 %collective-permute-start.4 = (bf16[64,1024]{1,0:T(8,128)(2,1)}, bf16[64,1024]{1,0:T(8,128)(2,1)S(1)}, u32[]{:S(2)}, u32[]{:S(2)}) collective-permute-start(bf16[64,1024]{1,0:T(8,128)(2,1)} %get-tuple-element.18.own_cross_ref), channel_id=1, source_target_pairs={{1,2},{3,4},{5,6},{7,8},{9,10},{11,12},{13,14},{2,1},{4,3},{6,5},{... | collective-permute-start | bytes 393224 | tf_op jit(solution)/shard_map/ppermute | solution.py:255
  28.6 5.0 %collective-permute-start.5 = (bf16[64,1024]{1,0:T(8,128)(2,1)}, bf16[64,1024]{1,0:T(8,128)(2,1)S(1)}, u32[]{:S(2)}, u32[]{:S(2)}) collective-permute-start(bf16[64,1024]{1,0:T(8,128)(2,1)} %get-tuple-element.19.own_partner_ref), channel_id=1, source_target_pairs={{0,1},{1,0},{2,3},{3,2},{4,5},{5,4},{6,7},{7,6},{8,9},{9,8},{10,11... | collective-permute-start | bytes 393224 | tf_op jit(solution)/shard_map/ppermute | solution.py:256

commit v20 on v19

--- a/solution.py
+++ b/solution.py
@@ -144,15 +144,16 @@
     sw_copy.start()
     half = cross_ref.shape[0]
     rows, model_width = mid_ref.shape
-    first_core = meta_ref[1] == 0
-    cross = cross_ref[...]
-    partner = pairg_ref[...]
-    win_ref[0:half, :] = jnp.where(first_core, cross, partner).astype(jnp.float32)
-    own_cross = own_cross_ref[...]
-    own_partner = own_partner_ref[...]
-    win_ref[half:2 * half, :] = jnp.where(first_core, own_cross, own_partner).astype(jnp.float32)
-    win_ref[2 * half:3 * half, :] = jnp.where(first_core, own_partner, own_cross).astype(jnp.float32)
-    win_ref[half + rows:2 * half + rows, :] = jnp.where(first_core, partner, cross).astype(jnp.float32)
+    core = meta_ref[1]
+    outer = rows + half
+
+    def place(first, ref):
+        win_ref[pl.ds(pl.multiple_of(first, half), half), :] = ref[...].astype(jnp.float32)
+
+    place(core * outer, cross_ref)
+    place((1 - core) * outer, pairg_ref)
+    place(half + core * half, own_cross_ref)
+    place(2 * half - core * half, own_partner_ref)
     reach = DILATION * (KERNEL - 1) // 2
     start = half - reach
 

time: 38.7 us -> 38.7 us (level)
  no operation moved by 1% of the time
where the time goes in v20:
time: 38.7 us; the launch traced here: 38.3 us
  waiting for transfers between devices  11.6 us (30%)
  Pallas kernels  11.4 us (29%)
  starting transfers between devices  10.6 us (27%)
  local copies, waits for them, and re-layouts  3.05 us (8%)
  other arithmetic  1.61 us (4%)
    pallas_call x1, Pallas kernels, on_device(): pl.pallas_call(attention_kernel, out_shape=(jax.ShapeDtypeStruct((rows, m...  6.66 us
    ppermute x2, starting transfers between devices, lin_shift(): lax.ppermute(value, ('chip', 'core'), [(s, s + steps) for s in range(lead...  6.18 us
    ppermute x2, waiting for transfers between devices, lin_shift(): lax.ppermute(value, ('chip', 'core'), [(s, s + steps) for s in range(lead...  5.55 us
    ppermute x1, waiting for transfers between devices, on_device(): cross_recv = lax.ppermute(cross_send, ('chip', 'core'), inward)  4.9 us
    pallas_call x1, Pallas kernels, on_device(): pl.pallas_call(conv_kernel, out_shape=jax.ShapeDtypeStruct((rows, model_w...  4.75 us
    ppermute x1, starting transfers between devices, on_device(): cross_recv = lax.ppermute(cross_send, ('chip', 'core'), inward)  2.51 us
    slice x1, local copies, waits for them, and re-layouts, on_device(): expand_weight[:, model_width:]  1.76 us
    ppermute x1, starting transfers between devices, on_device(): partner = lax.ppermute(gated_input, 'core', swap)  1.24 us
  transfers between devices with their start and end apart: 6, of which 4 were waited for; matrix products, arithmetic and copies ran while one was open for 10% of the time, Pallas kernels for 0%

profile of v20, /device:TPU:21, one launch (start us, length us, event | category | flops | bytes accessed | tf_op | source)
XLA Modules:
  0.0 38.3 jit_solution(1344085518490044670)
XLA Ops:
  0.0 1.0 %pad_maximum_fusion.own_hbm = bf16[2,128,512]{2,1,0:T(8,128)(2,1)S(1)} fusion(bf16[1,128,512]{2,1,0:T(8,128)(2,1)} %bitcast.8, bf16[1,128,512]{2,1,0:T(8,128)(2,1)} %bitcast.9), kind=kLoop, calls=%fused_computation | loop fusion | flops 131072 | bytes 524288 | tf_op jit(solution)/shard_map/stack | solution.py:209
  1.0 0.0 copy-start.2
  1.0 2.1 %collective-permute-start.1 = (bf16[2,128,512]{2,1,0:T(8,128)(2,1)S(1)}, bf16[2,128,512]{2,1,0:T(8,128)(2,1)S(1)}, u32[]{:S(2)}, u32[]{:S(2)}) collective-permute-start(bf16[2,128,512]{2,1,0:T(8,128)(2,1)S(1)} %pad_maximum_fusion.own_hbm), channel_id=1, source_target_pairs={{2,0},{3,1},{4,2},{5,3},{6,4},{7,5},{8,6},{9,7},{10,8},{11,9},{12,... | collective-permute-start | bytes 786440 | tf_op jit(solution)/shard_map/ppermute | solution.py:203
  3.2 4.0 %collective-permute-start = (bf16[2,128,512]{2,1,0:T(8,128)(2,1)S(1)}, bf16[2,128,512]{2,1,0:T(8,128)(2,1)S(1)}, u32[]{:S(2)}, u32[]{:S(2)}) collective-permute-start(bf16[2,128,512]{2,1,0:T(8,128)(2,1)S(1)} %pad_maximum_fusion.own_hbm), channel_id=1, source_target_pairs={{0,2},{1,3},{2,4},{3,5},{4,6},{5,7},{6,8},{7,9},{8,10},{9,11},{10,... | collective-permute-start | bytes 786440 | tf_op jit(solution)/shard_map/ppermute | solution.py:203
  7.2 0.7 %pad.4 = s32[768]{0:T(1024)S(1)} pad(s32[767]{0:T(1024)} %param.18, s32[]{:T(128)} %constant.5.clone.1), padding=0_1 | pad | bytes 6144 | tf_op jit(solution)/shard_map/jit(_pad)/pad | solution.py:206
  7.9 0.6 %reshape.9.table_ref = s32[1,768]{1,0:T(1,128)} reshape(s32[768]{0:T(1024)S(1)} %pad.4) | data formatting | bytes 6144 | tf_op jit(solution)/shard_map/reshape | solution.py:206
  8.5 1.8 %slice.3.gate_w = bf16[1024,1024]{1,0:T(8,128)(2,1)S(1)} slice(bf16[1024,2048]{1,0:T(8,128)(2,1)} %value_hbm.1), slice={[0:1024], [1024:2048]} | slice | bytes 4194304 | tf_op jit(solution)/shard_map/slice | solution.py:213
  10.3 0.6 %pad_add_fusion.meta_ref = s32[2]{0:T(128)} fusion(s32[1]{0:T(128)} %bitcast.3, s32[1]{0:T(128)} %bitcast.2), kind=kLoop, calls=%fused_computation.2 | loop fusion | flops 2 | bytes 16 | tf_op jit(solution)/shard_map/stack | solution.py:199
  10.9 0.0 copy-done.2
  10.9 1.2 %collective-permute-start.2 = (bf16[2,128,512]{2,1,0:T(8,128)(2,1)S(1)}, bf16[2,128,512]{2,1,0:T(8,128)(2,1)S(1)}, u32[]{:S(2)}, u32[]{:S(2)}) collective-permute-start(bf16[2,128,512]{2,1,0:T(8,128)(2,1)S(1)} %pad_maximum_fusion.own_hbm), channel_id=1, source_target_pairs={{0,1},{1,0},{2,3},{3,2},{4,5},{5,4},{6,7},{7,6},{8,9},{9,8},{10,11... | collective-permute-start | bytes 786440 | tf_op jit(solution)/shard_map/ppermute | solution.py:214
  12.1 1.5 %collective-permute-done.1.next_hbm = bf16[2,128,512]{2,1,0:T(8,128)(2,1)S(1)} collective-permute-done((bf16[2,128,512]{2,1,0:T(8,128)(2,1)S(1)}, bf16[2,128,512]{2,1,0:T(8,128)(2,1)S(1)}, u32[]{:S(2)}, u32[]{:S(2)}) %collective-permute-start.1) | collective-permute-done | bytes 262176 | tf_op jit(solution)/shard_map/ppermute | solution.py:203
  13.6 4.1 %collective-permute-done.prev_hbm = bf16[2,128,512]{2,1,0:T(8,128)(2,1)S(1)} collective-permute-done((bf16[2,128,512]{2,1,0:T(8,128)(2,1)S(1)}, bf16[2,128,512]{2,1,0:T(8,128)(2,1)S(1)}, u32[]{:S(2)}, u32[]{:S(2)}) %collective-permute-start) | collective-permute-done | bytes 262176 | tf_op jit(solution)/shard_map/ppermute | solution.py:203
  17.7 0.6 %collective-permute-start.3 = (bf16[2,128,512]{2,1,0:T(8,128)(2,1)S(1)}, bf16[2,128,512]{2,1,0:T(8,128)(2,1)S(1)}, u32[]{:S(2)}, u32[]{:S(2)}) collective-permute-start(bf16[2,128,512]{2,1,0:T(8,128)(2,1)S(1)} %broadcast_select_fusion), channel_id=1, source_target_pairs={{0,1},{1,0},{2,3},{3,2},{4,5},{5,4},{6,7},{7,6},{8,9},{9,8},{10,11... | collective-permute-start | bytes 786440 | tf_op jit(solution)/shard_map/ppermute | solution.py:216
  18.2 0.0 collective-permute-done.2.partner_hbm
  18.2 1.2 %collective-permute-done.3.sel_hbm = bf16[2,128,512]{2,1,0:T(8,128)(2,1)S(1)} collective-permute-done((bf16[2,128,512]{2,1,0:T(8,128)(2,1)S(1)}, bf16[2,128,512]{2,1,0:T(8,128)(2,1)S(1)}, u32[]{:S(2)}, u32[]{:S(2)}) %collective-permute-start.3) | collective-permute-done | bytes 262176 | tf_op jit(solution)/shard_map/ppermute | solution.py:216
  19.4 0.0 copy-start
  19.4 0.0 copy-start.1
  19.4 6.7 %attention_glu.1 = (bf16[128,1024]{1,0:T(8,128)(2,1)}, bf16[64,1024]{1,0:T(8,128)(2,1)}, bf16[64,1024]{1,0:T(8,128)(2,1)}) custom-call(s32[2]{0:T(128)} %pad_add_fusion.meta_ref, s32[16]{0:T(128)} %len_ref.1, s32[1,768]{1,0:T(1,128)} %reshape.9.table_ref, f32[8,32]{1,0:T(8,128)} %bitcast.10, bf16[128,512]{1,0:T(8,128)(2,1)} %q_ref.1, ...), custom_call_target="tpu_custom_call" | custom-call | flops 1006632960 | bytes 7208960 | tf_op jit(solution)/shard_map/attention_glu/pallas_call | solution.py:226
  26.1 2.5 %collective-permute-start.4 = (bf16[64,1024]{1,0:T(8,128)(2,1)}, bf16[64,1024]{1,0:T(8,128)(2,1)S(1)}, u32[]{:S(2)}, u32[]{:S(2)}) collective-permute-start(bf16[64,1024]{1,0:T(8,128)(2,1)} %get-tuple-element.18.own_cross_ref), channel_id=1, source_target_pairs={{1,2},{3,4},{5,6},{7,8},{9,10},{11,12},{13,14},{2,1},{4,3},{6,5},{... | collective-permute-start | bytes 393224 | tf_op jit(solution)/shard_map/ppermute | solution.py:256
  28.6 0.1 collective-permute-start.5
  28.7 4.9 %collective-permute-done.4.cross_ref = bf16[64,1024]{1,0:T(8,128)(2,1)S(1)} collective-permute-done((bf16[64,1024]{1,0:T(8,128)(2,1)}, bf16[64,1024]{1,0:T(8,128)(2,1)S(1)}, u32[]{:S(2)}, u32[]{:S(2)}) %collective-permute-start.4) | collective-permute-done | bytes 131104 | tf_op jit(solution)/shard_map/ppermute | solution.py:256
  33.6 0.0 collective-permute-done.5.pairg_ref
  33.6 0.0 copy-done
  33.6 0.0 copy-done.1
  33.6 4.8 %conv_shrink.1 = bf16[128,1024]{1,0:T(8,128)(2,1)} custom-call(s32[2]{0:T(128)} %pad_add_fusion.meta_ref, bf16[64,1024]{1,0:T(8,128)(2,1)} %get-tuple-element.18.own_cross_ref, bf16[64,1024]{1,0:T(8,128)(2,1)} %get-tuple-element.19.own_partner_ref, bf16[64,1024]{1,0:T(8,128)(2,1)S(1)} %collective-permute-done.4.cross_ref, ...), custom_call_target="tpu_custom_call" | custom-call | flops 276561920 | bytes 3272704 | tf_op jit(solution)/shard_map/conv_shrink/pallas_call | solution.py:260
  (1 shorter events, 0.0 us)
Async XLA Ops:
  1.0 9.9 %copy-start.2 = (bf16[2,128,512]{2,1,0:T(8,128)(2,1)}, bf16[2,128,512]{2,1,0:T(8,128)(2,1)S(1)}, u32[]{:S(2)}) copy-start(bf16[2,128,512]{2,1,0:T(8,128)(2,1)S(1)} %pad_maximum_fusion.own_hbm) | copy-start | bytes 786436
  1.0 12.6 %collective-permute-start.1 = (bf16[2,128,512]{2,1,0:T(8,128)(2,1)S(1)}, bf16[2,128,512]{2,1,0:T(8,128)(2,1)S(1)}, u32[]{:S(2)}, u32[]{:S(2)}) collective-permute-start(bf16[2,128,512]{2,1,0:T(8,128)(2,1)S(1)} %pad_maximum_fusion.own_hbm), channel_id=1, source_target_pairs={{2,0},{3,1},{4,2},{5,3},{6,4},{7,5},{8,6},{9,7},{10,8},{11,9},{12,... | collective-permute-start | bytes 786440 | tf_op jit(solution)/shard_map/ppermute | solution.py:203
  3.2 14.5 %collective-permute-start = (bf16[2,128,512]{2,1,0:T(8,128)(2,1)S(1)}, bf16[2,128,512]{2,1,0:T(8,128)(2,1)S(1)}, u32[]{:S(2)}, u32[]{:S(2)}) collective-permute-start(bf16[2,128,512]{2,1,0:T(8,128)(2,1)S(1)} %pad_maximum_fusion.own_hbm), channel_id=1, source_target_pairs={{0,2},{1,3},{2,4},{3,5},{4,6},{5,7},{6,8},{7,9},{8,10},{9,11},{10,... | collective-permute-start | bytes 786440 | tf_op jit(solution)/shard_map/ppermute | solution.py:203
  10.9 7.4 %collective-permute-start.2 = (bf16[2,128,512]{2,1,0:T(8,128)(2,1)S(1)}, bf16[2,128,512]{2,1,0:T(8,128)(2,1)S(1)}, u32[]{:S(2)}, u32[]{:S(2)}) collective-permute-start(bf16[2,128,512]{2,1,0:T(8,128)(2,1)S(1)} %pad_maximum_fusion.own_hbm), channel_id=1, source_target_pairs={{0,1},{1,0},{2,3},{3,2},{4,5},{5,4},{6,7},{7,6},{8,9},{9,8},{10,11... | collective-permute-start | bytes 786440 | tf_op jit(solution)/shard_map/ppermute | solution.py:214
  17.7 1.7 %collective-permute-start.3 = (bf16[2,128,512]{2,1,0:T(8,128)(2,1)S(1)}, bf16[2,128,512]{2,1,0:T(8,128)(2,1)S(1)}, u32[]{:S(2)}, u32[]{:S(2)}) collective-permute-start(bf16[2,128,512]{2,1,0:T(8,128)(2,1)S(1)} %broadcast_select_fusion), channel_id=1, source_target_pairs={{0,1},{1,0},{2,3},{3,2},{4,5},{5,4},{6,7},{7,6},{8,9},{9,8},{10,11... | collective-permute-start | bytes 786440 | tf_op jit(solution)/shard_map/ppermute | solution.py:216
  19.4 14.2 %copy-start = (f32[31,1024]{1,0:T(8,128)S(1)}, f32[31,1024]{1,0:T(8,128)}, u32[]{:S(2)}) copy-start(f32[31,1024]{1,0:T(8,128)} %taps_ref.1) | copy-start | bytes 380932
  19.4 14.2 %copy-start.1 = (f32[1024]{0:T(1024)S(1)}, f32[1024]{0:T(1024)}, u32[]{:S(2)}) copy-start(f32[1024]{0:T(1024)} %param.24) | copy-start | bytes 12292
  26.1 7.5 %collective-permute-start.4 = (bf16[64,1024]{1,0:T(8,128)(2,1)}, bf16[64,1024]{1,0:T(8,128)(2,1)S(1)}, u32[]{:S(2)}, u32[]{:S(2)}) collective-permute-start(bf16[64,1024]{1,0:T(8,128)(2,1)} %get-tuple-element.18.own_cross_ref), channel_id=1, source_target_pairs={{1,2},{3,4},{5,6},{7,8},{9,10},{11,12},{13,14},{2,1},{4,3},{6,5},{... | collective-permute-start | bytes 393224 | tf_op jit(solution)/shard_map/ppermute | solution.py:256
  28.6 5.0 %collective-permute-start.5 = (bf16[64,1024]{1,0:T(8,128)(2,1)}, bf16[64,1024]{1,0:T(8,128)(2,1)S(1)}, u32[]{:S(2)}, u32[]{:S(2)}) collective-permute-start(bf16[64,1024]{1,0:T(8,128)(2,1)} %get-tuple-element.19.own_partner_ref), channel_id=1, source_target_pairs={{0,1},{1,0},{2,3},{3,2},{4,5},{5,4},{6,7},{7,6},{8,9},{9,8},{10,11... | collective-permute-start | bytes 393224 | tf_op jit(solution)/shard_map/ppermute | solution.py:257
